TPU v7x, 32 devices: a whole 2x2x4 slice. The times are simulated.
32 devices in a mesh: clips: 2 (over y), frame: 4 (over x, core), row: 4 (over z).
Axes of the slice: x: 2, y: 2, z: 4, core: 2. Of those that a mesh axis runs over, the one named last changes fastest.
Arguments:
- frames: bfloat16 [16, 512, 640], P(('clips', 'frame'), 'row'), parts along dimension 0, may hold values from -16 to 16
- key_index: int32 [4], P('clips'), parts along dimension 0, may hold values from 0 to 7, as said below
- w_query: bfloat16 [640, 640], replicated, may hold values from -0.25 to 0.25
- w_keyval: bfloat16 [640, 1280], replicated, may hold values from -0.25 to 0.25
- w_out: bfloat16 [640, 640], replicated, may hold values from -0.25 to 0.25
- norm_gain: float32 [640], replicated, may hold values from 0.1 to 1.9
- w_first: bfloat16 [3, 640, 640], replicated, may hold values from -0.125 to 0.125
- w_second: bfloat16 [3, 640, 640], replicated, may hold values from -0.125 to 0.125
Outputs:
- edited: bfloat16 [16, 512, 640], P(('clips', 'frame'), 'row'), parts along dimension 0
There are 2 independent parts, one for each index of `clips`. A program takes and returns all parts, laid end to end along the dimension named above; an argument that names none is the same for every part. Nothing has to cross between parts.
Inputs may be any that keep to these rules, and one draw needn't show every extreme that they name: `key_index`: two different frame indices of the window, in either order; one of them is the window's last frame 8 - 1.
All inputs are finite; a program needn't handle non-finite values.
Results may differ from a plain program's by a relative error of at most 0.0067.
Values may be sent and summed in bfloat16 or wider, within the bound.
No kernel may reach another device: no remote copies, remote signals or barrier semaphores. Data moves between devices by JAX's collectives and lax.ppermute only.
A program may use at most 128 MiB of HBM per device.

v0:
```python
from functools import partial

import jax
import jax.numpy as jnp
from jax import lax
from jax.sharding import PartitionSpec as P

HEADS = 10
HEAD_DIM = 64


def from_root(value, axis, source):
    kept = jnp.where(lax.axis_index(axis) == source, value, 0).astype(value.dtype)
    return lax.psum(kept, axis)


def extended(array, sides, width):
    for axis, dim in sides:
        size, length = (lax.axis_size(axis), array.shape[dim])
        up = [(i, (i + 1) % size) for i in range(size - 1)]
        down = [(j, i) for i, j in up]
        last = lax.slice_in_dim(array, length - width, length, axis=dim)
        first = lax.slice_in_dim(array, 0, width, axis=dim)
        before = lax.ppermute(last, axis, up)
        after = lax.ppermute(first, axis, down)
        array = jnp.concatenate([before, array, after], axis=dim)
    return array


def temporal_mix(padded, weights, count):
    result = jnp.zeros((count * padded.shape[1], padded.shape[2]), jnp.float32)
    for offset in range(3):
        window = padded[offset : offset + count].reshape(-1, padded.shape[2])
        result = result + jnp.dot(window, weights[offset], preferred_element_type=jnp.float32)
    return result


def absorb_keys(query_heads, channels, state_now, kv_pieces, piece_start):
    highest, denominator, accumulated = state_now
    joined = jnp.concatenate(kv_pieces, axis=0)
    key_heads = joined[:, :channels].reshape(-1, HEADS, HEAD_DIM)
    value_heads = joined[:, channels:].reshape(-1, HEADS, HEAD_DIM)
    scores = jnp.einsum(
        "qhd,khd->hqk", query_heads, key_heads, preferred_element_type=jnp.float32
    ) * HEAD_DIM ** (-0.5)
    raised = jnp.maximum(highest, jnp.max(scores, axis=-1))
    kept_frac = jnp.exp(highest - raised)
    exponent = jnp.exp(scores - raised[:, :, None])
    denominator = jnp.sum(exponent, axis=-1)
    contrib = jnp.einsum(
        "hqk,khd->qhd",
        exponent.astype(jnp.bfloat16),
        value_heads,
        preferred_element_type=jnp.float32,
    )
    accumulated = accumulated * jnp.repeat(kept_frac.T, HEAD_DIM, axis=1) + contrib.reshape(
        contrib.shape[0], -1
    )
    return (raised, denominator, accumulated)


def shards(frames, key_index, w_query, w_keyval, w_out, norm_gain, w_first, w_second):
    frame_count, row_count, channels = frames.shape
    flattened = frames.reshape(-1, channels)
    queries = jnp.dot(flattened, w_query, preferred_element_type=jnp.float32).astype(jnp.bfloat16)
    query_heads = queries.reshape(-1, HEADS, HEAD_DIM)
    query_total = queries.shape[0]
    owners = key_index // frame_count
    chosen = frames[key_index % frame_count].reshape(-1, channels)
    keyval = jnp.dot(chosen, w_keyval, preferred_element_type=jnp.float32).astype(jnp.bfloat16)
    own_parts = (keyval[:row_count], keyval[row_count:])
    initial = (
        jnp.full((HEADS, query_total), -1e30, jnp.float32),
        jnp.zeros((HEADS, query_total), jnp.float32),
        jnp.zeros((query_total, channels), jnp.float32),
    )
    absorb = partial(absorb_keys, query_heads, channels)
    spread_parts = []
    for key_slot in range(2):
        spread_parts.append(from_root(own_parts[key_slot], "frame", owners[key_slot]))
    final = absorb(
        initial,
        (
            lax.all_gather(spread_parts[0], "row", axis=0, tiled=True),
            lax.all_gather(spread_parts[1], "row", axis=0, tiled=True),
        ),
        jnp.int32(0),
    )
    highest, denominator, accumulated = final
    mixed = accumulated.reshape(query_total, HEADS, HEAD_DIM) / denominator.T[:, :, None]
    attended = mixed.reshape(query_total, channels).astype(jnp.bfloat16)
    residual = flattened.astype(jnp.float32) + jnp.dot(
        attended, w_out, preferred_element_type=jnp.float32
    )
    mean_square = jnp.mean(residual * residual, axis=-1, keepdims=True)
    normed = (residual * lax.rsqrt(mean_square + 1e-06) * norm_gain).astype(jnp.bfloat16)
    normed = normed.reshape(frame_count, row_count, channels)
    padded = extended(normed, (("frame", 0),), 1)
    hidden = jax.nn.silu(temporal_mix(padded, w_first, frame_count)).astype(jnp.bfloat16)
    hidden = hidden.reshape(frame_count, row_count, channels)
    padded = extended(hidden, (("frame", 0),), 1)
    second = temporal_mix(padded, w_second, frame_count)
    return (residual + second).astype(jnp.bfloat16).reshape(frame_count, row_count, channels)


def solution(mesh):
    return jax.shard_map(
        shards,
        mesh=mesh,
        in_specs=(P(("clips", "frame"), "row", None), P("clips"), P(), P(), P(), P(), P(), P()),
        out_specs=P(("clips", "frame"), "row", None),
        check_vma=False,
    )
```

profile of v0, /device:TPU:9, one launch (start us, length us, event | category | flops | bytes accessed | tf_op | source)
XLA Modules:
  0.0 160.8 jit_solution(13678371207064377667)
XLA Ops:
  6.5 0.8 and_select_fusion.1
  7.3 0.6 fusion.42
  9.2 1.6 gather_fusion
  10.8 0.7 convolution_convert_fusion
  11.5 0.9 slice_select_fusion
  12.5 34.3 %all-reduce.3.cloned.1.call-done = (bf16[128,1280]{1,0:T(8,128)(2,1)}, bf16[128,1280]{1,0:T(8,128)(2,1)}) async-done(((bf16[128,1280]{1,0:T(8,128)(2,1)}, bf16[128,1280]{1,0:T(8,128)(2,1)}), (bf16[128,1280]{1,0:T(8,128)(2,1)}, bf16[128,1280]{1,0:T(8,128)(2,1)})) %all-reduce.3.cloned.1.call-update) | async-done | bytes 655376 | tf_op jit(solution)/shard_map/psum | solution.py:14
  46.8 0.7 all-gather.5.cloned.1.call-update
  47.5 0.5 convolution_convert_fusion.1
  48.0 0.9 copy.12
  48.9 32.1 %all-gather.3.cloned.1.call-done = bf16[512,1280]{1,0:T(8,128)(2,1)} async-done(((bf16[128,1280]{1,0:T(8,128)(2,1)}), bf16[512,1280]{1,0:T(8,128)(2,1)}) %all-gather.3.cloned.1.call-update) | async-done | bytes 1310736 | tf_op jit(solution)/shard_map/all_gather | solution.py:84
  81.1 2.5 %constant_dynamic-update-slice_fusion.1 = bf16[1024,1280]{1,0:T(8,128)(2,1)} fusion(bf16[512,1280]{1,0:T(8,128)(2,1)} %all-gather.3.cloned.1.call-done), kind=kLoop, calls=%fused_computation.54 | loop fusion | bytes 2621440
  83.5 30.8 %all-gather.5.cloned.1.call-done = bf16[512,1280]{1,0:T(8,128)(2,1)} async-done(((bf16[128,1280]{1,0:T(8,128)(2,1)}), bf16[512,1280]{1,0:T(8,128)(2,1)}) %all-gather.5.cloned.1.call-update) | async-done | bytes 1310736 | tf_op jit(solution)/shard_map/all_gather | solution.py:85
  114.4 2.5 %constant_dynamic-update-slice_fusion = bf16[1024,1280]{1,0:T(8,128)(2,1)} fusion(bf16[1024,1280]{1,0:T(8,128)(2,1)} %constant_dynamic-update-slice_fusion.1, bf16[512,1280]{1,0:T(8,128)(2,1)} %all-gather.5.cloned.1.call-done), kind=kLoop, calls=%fused_computation.53 | loop fusion | bytes 2621440 | tf_op jit(solution)/shard_map/concatenate | solution.py:40
  116.8 3.5 %fusion.41 = (bf16[1024,640]{1,0:T(8,128)(2,1)}, bf16[1024,640]{1,0:T(8,128)(2,1)}) fusion(bf16[1024,1280]{1,0:T(8,128)(2,1)} %constant_dynamic-update-slice_fusion), kind=kLoop, calls=%fused_computation.63 | loop fusion | bytes 5242880 | tf_op jit(solution)/shard_map/slice | solution.py:41
  120.3 1.6 copy.13
  121.9 2.5 %copy.14 = bf16[1024,640]{0,1:T(8,128)(2,1)} copy(bf16[1024,640]{1,0:T(8,128)(2,1)} %get-tuple-element.8) | data formatting | bytes 2621440 | tf_op jit(solution)/shard_map/slice | solution.py:42
  124.3 2.6 %multiply_reduce_fusion = (f32[10,256]{1,0:T(8,128)S(1)}, f32[10,256,1024]{2,1,0:T(8,128)S(1)}) fusion(bf16[256,10,64]{0,2,1:T(8,128)(2,1)} %bitcast.74, bf16[1024,10,64]{0,2,1:T(8,128)(2,1)S(1)} %bitcast.69), kind=kOutput, calls=%fused_computation.2 | convolution fusion | flops 340784640 | bytes 12134400 | tf_op jit(solution)/shard_map/qhd,khd->hqk/dot_general | solution.py:43
  127.0 2.1 %fusion = f32[10,256]{1,0:T(8,128)S(1)} fusion(f32[10,256,1024]{2,1,0:T(8,128)S(1)} %get-tuple-element.26, f32[10,256]{1,0:T(8,128)S(1)} %get-tuple-element.20), kind=kLoop, calls=%fused_computation.3 | loop fusion | flops 7861760 | bytes 10506240 | tf_op jit(solution)/shard_map/reduce_sum | solution.py:49
  129.1 2.3 %fusion.19 = bf16[256,10,64]{0,2,1:T(8,128)(2,1)S(1)} fusion(bf16[1024,10,64]{0,2,1:T(8,128)(2,1)S(1)} %bitcast.77, f32[10,256,1024]{2,1,0:T(8,128)S(1)} %get-tuple-element.26, f32[10,256]{1,0:T(8,128)S(1)} %get-tuple-element.20, f32[256,10]{0,1:T(8,128)S(1)} %bitcast.82, f32[256,10]{0,1:T(8,128)S(1)} %get-tuple-element.19), kind=kOutput, calls=%fused_computation.20 | convolution fusion | flops 343900160 | bytes 12154880 | tf_op jit(solution)/shard_map/hqk,khd->qhd/dot_general | solution.py:50
  131.4 0.6 multiply_reduce_fusion.1
  132.2 3.9 %collective-permute-start = (bf16[1,128,640]{2,1,0:T(8,128)(2,1)S(1)}, bf16[1,128,640]{2,1,0:T(8,128)(2,1)S(1)}, u32[]{:S(2)}, u32[]{:S(2)}) collective-permute-start(bf16[1,128,640]{2,1,0:T(8,128)(2,1)S(1)} %get-tuple-element.17), channel_id=1, source_target_pairs={{0,4},{4,8},{8,12},{1,5},{5,9},{9,13},{2,6},{6,10},{10,14},{3,7},{... | collective-permute-start | bytes 491528 | tf_op jit(solution)/shard_map/ppermute | solution.py:24
  136.1 1.9 %collective-permute-start.1 = (bf16[1,128,640]{2,1,0:T(8,128)(2,1)S(1)}, bf16[1,128,640]{2,1,0:T(8,128)(2,1)S(1)}, u32[]{:S(2)}, u32[]{:S(2)}) collective-permute-start(bf16[1,128,640]{2,1,0:T(8,128)(2,1)S(1)} %get-tuple-element.18), channel_id=1, source_target_pairs={{4,0},{8,4},{12,8},{5,1},{9,5},{13,9},{6,2},{10,6},{14,10},{7,3},{... | collective-permute-start | bytes 491528 | tf_op jit(solution)/shard_map/ppermute | solution.py:25
  138.0 0.5 fusion.29
  138.5 4.2 %collective-permute-done.1 = bf16[1,128,640]{2,1,0:T(8,128)(2,1)S(1)} collective-permute-done((bf16[1,128,640]{2,1,0:T(8,128)(2,1)S(1)}, bf16[1,128,640]{2,1,0:T(8,128)(2,1)S(1)}, u32[]{:S(2)}, u32[]{:S(2)}) %collective-permute-start.1) | collective-permute-done | bytes 163872 | tf_op jit(solution)/shard_map/ppermute | solution.py:25
  142.8 0.5 fusion.27
  143.3 0.5 multiply_convert_fusion
  143.8 2.1 %collective-permute-start.2 = (bf16[1,128,640]{2,1,0:T(8,128)(2,1)S(1)}, bf16[1,128,640]{2,1,0:T(8,128)(2,1)S(1)}, u32[]{:S(2)}, u32[]{:S(2)}) collective-permute-start(bf16[1,128,640]{2,1,0:T(8,128)(2,1)S(1)} %get-tuple-element.13), channel_id=1, source_target_pairs={{0,4},{4,8},{8,12},{1,5},{5,9},{9,13},{2,6},{6,10},{10,14},{3,7},{... | collective-permute-start | bytes 491528 | tf_op jit(solution)/shard_map/ppermute | solution.py:24
  145.9 2.4 %collective-permute-start.3 = (bf16[1,128,640]{2,1,0:T(8,128)(2,1)S(1)}, bf16[1,128,640]{2,1,0:T(8,128)(2,1)S(1)}, u32[]{:S(2)}, u32[]{:S(2)}) collective-permute-start(bf16[1,128,640]{2,1,0:T(8,128)(2,1)S(1)} %get-tuple-element.14), channel_id=1, source_target_pairs={{4,0},{8,4},{12,8},{5,1},{9,5},{13,9},{6,2},{10,6},{14,10},{7,3},{... | collective-permute-start | bytes 491528 | tf_op jit(solution)/shard_map/ppermute | solution.py:25
  148.3 0.5 fusion.24
  148.8 3.7 %collective-permute-done.3 = bf16[1,128,640]{2,1,0:T(8,128)(2,1)S(1)} collective-permute-done((bf16[1,128,640]{2,1,0:T(8,128)(2,1)S(1)}, bf16[1,128,640]{2,1,0:T(8,128)(2,1)S(1)}, u32[]{:S(2)}, u32[]{:S(2)}) %collective-permute-start.3) | collective-permute-done | bytes 163872 | tf_op jit(solution)/shard_map/ppermute | solution.py:25
  152.6 0.5 fusion.22
  153.0 1.2 fusion.15
  (31 shorter events, 0.5 us)
Async XLA Ops:
  6.5 4.3 %copy-start = (bf16[640,1280]{1,0:T(8,128)(2,1)S(1)}, bf16[640,1280]{1,0:T(8,128)(2,1)}, u32[]{:S(2)}) copy-start(bf16[640,1280]{1,0:T(8,128)(2,1)} %param.11) | copy-start | bytes 4915204
  6.5 40.2 %all-reduce.3.cloned.1.call-start = ((), (), s32[]{:S(2)}) async-start(), calls=%async_computation.2 | async-start | bytes 1310720 | tf_op jit(solution)/shard_map/psum | solution.py:14
  10.8 36.7 %copy-start.1 = (bf16[2,128,640]{2,1,0:T(8,128)(2,1)S(1)}, bf16[2,128,640]{2,1,0:T(8,128)(2,1)}, u32[]{:S(2)}) copy-start(bf16[2,128,640]{2,1,0:T(8,128)(2,1)} %param.8) | copy-start | bytes 983044
  10.8 36.7 %copy-start.5 = (bf16[640,640]{1,0:T(8,128)(2,1)S(1)}, bf16[640,640]{1,0:T(8,128)(2,1)}, u32[]{:S(2)}) copy-start(bf16[640,640]{1,0:T(8,128)(2,1)} %param.10) | copy-start | bytes 2457604
  12.5 68.6 %all-gather.3.cloned.1.call-start = ((), (), s32[]{:S(2)}) async-start(), calls=%async_computation | async-start | bytes 1638400 | tf_op jit(solution)/shard_map/all_gather | solution.py:84
  46.8 67.6 %all-gather.5.cloned.1.call-start = ((), (), s32[]{:S(2)}) async-start(), calls=%async_computation.1 | async-start | bytes 1638400 | tf_op jit(solution)/shard_map/all_gather | solution.py:85
  127.0 2.1 %copy-start.3 = (bf16[1024,640]{0,1:T(8,128)(2,1)S(1)}, bf16[1024,640]{0,1:T(8,128)(2,1)}, u32[]{:S(2)}) copy-start(bf16[1024,640]{0,1:T(8,128)(2,1)} %copy.14) | copy-start | bytes 3932164
  129.0 2.4 %copy-start.6 = (bf16[640,640]{1,0:T(8,128)(2,1)S(1)}, bf16[640,640]{1,0:T(8,128)(2,1)}, u32[]{:S(2)}) copy-start(bf16[640,640]{1,0:T(8,128)(2,1)} %param.12) | copy-start | bytes 2457604
  129.1 2.9 %copy-start.7 = (f32[640]{0:T(1024)S(1)}, f32[640]{0:T(1024)}, u32[]{:S(2)}) copy-start(f32[640]{0:T(1024)} %param.13) | copy-start | bytes 7684
  131.4 6.6 %copy-start.4 = (bf16[3,640,640]{2,1,0:T(8,128)(2,1)S(1)}, bf16[3,640,640]{2,1,0:T(8,128)(2,1)}, u32[]{:S(2)}) copy-start(bf16[3,640,640]{2,1,0:T(8,128)(2,1)} %param.14) | copy-start | bytes 7372804
  132.2 6.3 %collective-permute-start = (bf16[1,128,640]{2,1,0:T(8,128)(2,1)S(1)}, bf16[1,128,640]{2,1,0:T(8,128)(2,1)S(1)}, u32[]{:S(2)}, u32[]{:S(2)}) collective-permute-start(bf16[1,128,640]{2,1,0:T(8,128)(2,1)S(1)} %get-tuple-element.17), channel_id=1, source_target_pairs={{0,4},{4,8},{8,12},{1,5},{5,9},{9,13},{2,6},{6,10},{10,14},{3,7},{... | collective-permute-start | bytes 491528 | tf_op jit(solution)/shard_map/ppermute | solution.py:24
  136.1 6.6 %collective-permute-start.1 = (bf16[1,128,640]{2,1,0:T(8,128)(2,1)S(1)}, bf16[1,128,640]{2,1,0:T(8,128)(2,1)S(1)}, u32[]{:S(2)}, u32[]{:S(2)}) collective-permute-start(bf16[1,128,640]{2,1,0:T(8,128)(2,1)S(1)} %get-tuple-element.18), channel_id=1, source_target_pairs={{4,0},{8,4},{12,8},{5,1},{9,5},{13,9},{6,2},{10,6},{14,10},{7,3},{... | collective-permute-start | bytes 491528 | tf_op jit(solution)/shard_map/ppermute | solution.py:25
  143.2 5.1 %copy-start.2 = (bf16[3,640,640]{2,1,0:T(8,128)(2,1)S(1)}, bf16[3,640,640]{2,1,0:T(8,128)(2,1)}, u32[]{:S(2)}) copy-start(bf16[3,640,640]{2,1,0:T(8,128)(2,1)} %param.15) | copy-start | bytes 7372804
  143.8 5.0 %collective-permute-start.2 = (bf16[1,128,640]{2,1,0:T(8,128)(2,1)S(1)}, bf16[1,128,640]{2,1,0:T(8,128)(2,1)S(1)}, u32[]{:S(2)}, u32[]{:S(2)}) collective-permute-start(bf16[1,128,640]{2,1,0:T(8,128)(2,1)S(1)} %get-tuple-element.13), channel_id=1, source_target_pairs={{0,4},{4,8},{8,12},{1,5},{5,9},{9,13},{2,6},{6,10},{10,14},{3,7},{... | collective-permute-start | bytes 491528 | tf_op jit(solution)/shard_map/ppermute | solution.py:24
  145.9 6.6 %collective-permute-start.3 = (bf16[1,128,640]{2,1,0:T(8,128)(2,1)S(1)}, bf16[1,128,640]{2,1,0:T(8,128)(2,1)S(1)}, u32[]{:S(2)}, u32[]{:S(2)}) collective-permute-start(bf16[1,128,640]{2,1,0:T(8,128)(2,1)S(1)} %get-tuple-element.14), channel_id=1, source_target_pairs={{4,0},{8,4},{12,8},{5,1},{9,5},{13,9},{6,2},{10,6},{14,10},{7,3},{... | collective-permute-start | bytes 491528 | tf_op jit(solution)/shard_map/ppermute | solution.py:25
Sparse Core Ops, SparseCore 0:
  12.6 34.1 all-reduce.2
  48.3 32.6 all-gather.2
  82.6 31.6 all-gather.4
where the time goes:
time: 163 us; the launch traced here: 161 us
  waiting for transfers between devices  106 us (65%)
  local copies, waits for them, and re-layouts  15.6 us (10%)
  between operations  14.7 us (9%)
  starting transfers between devices  10.3 us (6%)
  matrix products  10.2 us (6%)
  other arithmetic  4.05 us (2%)
    psum x1, waiting for transfers between devices, from_root(): return lax.psum(kept, axis)  34.3 us
    all_gather x1, waiting for transfers between devices, shards(): lax.all_gather(spread_parts[0], 'row', axis=0, tiled=True)  32.1 us
    all_gather x1, waiting for transfers between devices, shards(): lax.all_gather(spread_parts[1], 'row', axis=0, tiled=True)  30.8 us
    ppermute x2, waiting for transfers between devices, extended(): after = lax.ppermute(first, axis, down)  7.96 us
    ppermute x2, starting transfers between devices, extended(): before = lax.ppermute(last, axis, up)  5.92 us
    slice x2, local copies, waits for them, and re-layouts, absorb_keys(): key_heads = joined[:, :channels].reshape(-1, HEADS, HEAD_DIM)  5.06 us
    ppermute x2, starting transfers between devices, extended(): after = lax.ppermute(first, axis, down)  4.33 us
    dot_general x6, matrix products, temporal_mix(): jnp.dot(window, weights[offset], preferred_element_type=jnp.float32)  3.53 us
  transfers between devices with their start and end apart: 7, of which 5 were waited for; matrix products, arithmetic and copies ran while one was open for 3% of the time, Pallas kernels for 0%

commit v1 on v0

v1 whole, which is shorter than its diff:
```python
import jax
import jax.numpy as jnp
from jax import lax
from jax.sharding import PartitionSpec as P

HEADS = 10
HEAD_DIM = 64


def extended(array, axis, width):
    size, length = (lax.axis_size(axis), array.shape[0])
    up = [(i, i + 1) for i in range(size - 1)]
    down = [(j, i) for i, j in up]
    last = lax.slice_in_dim(array, length - width, length, axis=0)
    first = lax.slice_in_dim(array, 0, width, axis=0)
    before = lax.ppermute(last, axis, up)
    after = lax.ppermute(first, axis, down)
    return jnp.concatenate([before, array, after], axis=0)


def temporal_mix(padded, weights, count):
    result = jnp.zeros((count * padded.shape[1], padded.shape[2]), jnp.float32)
    for offset in range(3):
        window = padded[offset : offset + count].reshape(-1, padded.shape[2])
        result = result + jnp.dot(window, weights[offset], preferred_element_type=jnp.float32)
    return result


def gather_keyframes(frames, key_index):
    n_loc, rows, channels = frames.shape
    fsize = lax.axis_size("frame")
    rsize = lax.axis_size("row")
    me = lax.axis_index("frame")
    last = n_loc * fsize - 1
    other = key_index[0] + key_index[1] - last
    owner_a = other // n_loc
    cand_a = lax.dynamic_index_in_dim(frames, other % n_loc, 0, keepdims=False)
    cand_b = frames[n_loc - 1]
    owner_b = fsize - 1
    half = rows // 2

    def half_of(x, h):
        return lax.dynamic_slice_in_dim(x, h * half, half, 0)

    got_a = jnp.where(me == owner_a, half_of(cand_a, me % 2), jnp.zeros((half, channels), frames.dtype))
    got_b = half_of(cand_b, me % 2)
    for s in range(1, fsize):
        recv_a = lax.ppermute(
            half_of(cand_a, (me + s) % 2), "frame", [(i, (i + s) % fsize) for i in range(fsize)]
        )
        got_a = jnp.where((me - s) % fsize == owner_a, recv_a, got_a)
        dest = (owner_b + s) % fsize
        recv_b = lax.ppermute(cand_b[(dest % 2) * half : (dest % 2 + 1) * half], "frame", [(owner_b, dest)])
        got_b = jnp.where(me == dest, recv_b, got_b)
    piece = jnp.stack([got_a, got_b])
    pieces = [piece]
    for s in range(1, rsize):
        pieces.append(lax.ppermute(piece, "row", [(i, (i + s) % rsize) for i in range(rsize)]))
    mine = jnp.stack(pieces).reshape(-1, channels)
    sibling = lax.ppermute(mine, "frame", [(i, i ^ 1) for i in range(fsize)])
    return jnp.concatenate([mine, sibling], axis=0)


def shards(frames, key_index, w_query, w_keyval, w_out, norm_gain, w_first, w_second):
    frame_count, row_count, channels = frames.shape
    flattened = frames.reshape(-1, channels)
    queries = jnp.dot(flattened, w_query, preferred_element_type=jnp.float32).astype(jnp.bfloat16)
    query_heads = queries.reshape(-1, HEADS, HEAD_DIM)
    query_total = queries.shape[0]
    key_tokens = gather_keyframes(frames, key_index)
    keyval = jnp.dot(key_tokens, w_keyval, preferred_element_type=jnp.float32).astype(jnp.bfloat16)
    key_heads = keyval[:, :channels].reshape(-1, HEADS, HEAD_DIM)
    value_heads = keyval[:, channels:].reshape(-1, HEADS, HEAD_DIM)
    scores = jnp.einsum(
        "qhd,khd->hqk", query_heads, key_heads, preferred_element_type=jnp.float32
    ) * HEAD_DIM ** (-0.5)
    highest = jnp.max(scores, axis=-1, keepdims=True)
    exponent = jnp.exp(scores - highest)
    denominator = jnp.sum(exponent, axis=-1)
    mixed = jnp.einsum(
        "hqk,khd->qhd", exponent.astype(jnp.bfloat16), value_heads, preferred_element_type=jnp.float32
    )
    mixed = mixed / denominator.T[:, :, None]
    attended = mixed.reshape(query_total, channels).astype(jnp.bfloat16)
    residual = flattened.astype(jnp.float32) + jnp.dot(
        attended, w_out, preferred_element_type=jnp.float32
    )
    mean_square = jnp.mean(residual * residual, axis=-1, keepdims=True)
    normed = (residual * lax.rsqrt(mean_square + 1e-06) * norm_gain).astype(jnp.bfloat16)
    normed = normed.reshape(frame_count, row_count, channels)
    padded = extended(normed, "frame", 1)
    hidden = jax.nn.silu(temporal_mix(padded, w_first, frame_count)).astype(jnp.bfloat16)
    hidden = hidden.reshape(frame_count, row_count, channels)
    padded = extended(hidden, "frame", 1)
    second = temporal_mix(padded, w_second, frame_count)
    return (residual + second).astype(jnp.bfloat16).reshape(frame_count, row_count, channels)


def solution(mesh):
    return jax.shard_map(
        shards,
        mesh=mesh,
        in_specs=(P(("clips", "frame"), "row", None), P("clips"), P(), P(), P(), P(), P(), P()),
        out_specs=P(("clips", "frame"), "row", None),
        check_vma=False,
    )
```

time: 163 us -> 77.3 us (0.47)
  waiting for transfers between devices: 106 us -> 23.4 us
  between operations: 14.7 us -> 1.72 us
  starting transfers between devices: 10.3 us -> 22.2 us
  local copies, waits for them, and re-layouts: 15.6 us -> 10.3 us
  matrix products: 10.2 us -> 13 us
    all_gather x2 -> x0, waiting for transfers between devices: 63 us -> none  [the longest x1 32.1 us: shards(): lax.all_gather(spread_parts[0], 'row', axis=0, tiled=True)]
    psum x1 -> x0, waiting for transfers between devices: 34.3 us -> none  [from_root(): return lax.psum(kept, axis)]
    ppermute x0 -> x10, waiting for transfers between devices: none -> 15.5 us  [the longest x3 12.6 us: gather_keyframes(): lax.ppermute(piece, 'row', [(i, (i + s) % rsize) for i in range(rsize)])]
    ppermute x0 -> x10, starting transfers between devices: none -> 12.8 us  [the longest x3 4.79 us: gather_keyframes(): lax.ppermute(half_of(cand_a, (me + s) % 2), 'frame', [(i, (i + s) % fsize...]
    another operation x1 -> x4, other arithmetic: 0.01 us -> 2.89 us  [the longest x2 1.89 us: gather_keyframes(): piece = jnp.stack([got_a, got_b])]
    dot_general x3, matrix products: 5.6 us -> 8.39 us  [the longest x1 3.49 us: shards(): jnp.dot(key_tokens, w_keyval, preferred_element_type=jnp.float32)]
    unnamed x17 -> x16, local copies, waits for them, and re-layouts: 2.52 us -> 0.04 us
    concatenate x1 -> x0, local copies, waits for them, and re-layouts: 2.46 us -> none  [absorb_keys(): joined = jnp.concatenate(kv_pieces, axis=0)]
  transfers between devices with their start and end apart: 7 -> 14, of which waited for: 5 -> 7; matrix products, arithmetic and copies ran while one was open for 3% -> 5% of each run, Pallas kernels for 0% -> 0%
where the time goes in v1:
time: 77.3 us; the launch traced here: 75.8 us
  waiting for transfers between devices  23.4 us (30%)
  starting transfers between devices  22.2 us (29%)
  matrix products  13 us (17%)
  local copies, waits for them, and re-layouts  10.3 us (13%)
  other arithmetic  5.22 us (7%)
  between operations  1.72 us (2%)
    ppermute x3, waiting for transfers between devices, gather_keyframes(): lax.ppermute(piece, 'row', [(i, (i + s) % rsize) for i in range(rsize)])  12.6 us
    ppermute x2, waiting for transfers between devices, extended(): after = lax.ppermute(first, axis, down)  7.96 us
    ppermute x2, starting transfers between devices, extended(): before = lax.ppermute(last, axis, up)  5.04 us
    ppermute x3, starting transfers between devices, gather_keyframes(): lax.ppermute(half_of(cand_a, (me + s) % 2), 'frame', [(i, (i + s) % fsize...  4.79 us
    ppermute x2, starting transfers between devices, extended(): after = lax.ppermute(first, axis, down)  4.33 us
    ppermute x3, starting transfers between devices, gather_keyframes(): lax.ppermute(cand_b[dest % 2 * half:(dest % 2 + 1) * half], 'frame', [(ow...  3.87 us
    ppermute x3, starting transfers between devices, gather_keyframes(): lax.ppermute(piece, 'row', [(i, (i + s) % rsize) for i in range(rsize)])  3.84 us
    dot_general x6, matrix products, temporal_mix(): jnp.dot(window, weights[offset], preferred_element_type=jnp.float32)  3.53 us
  transfers between devices with their start and end apart: 14, of which 7 were waited for; matrix products, arithmetic and copies ran while one was open for 5% of the time, Pallas kernels for 0%

profile of v1, /device:TPU:9, one launch (start us, length us, event | category | flops | bytes accessed | tf_op | source)
XLA Modules:
  0.0 75.8 jit_solution(7660117601117662754)
XLA Ops:
  0.0 1.4 %fusion.50 = (s32[1]{0:T(128)}, s32[1]{0:T(128)}) fusion(s32[2]{0:T(128)} %param.9), kind=kLoop, calls=%fused_computation.69 | loop fusion | bytes 16 | tf_op jit(solution)/shard_map/slice | solution.py:35
  2.8 1.1 %dynamic-slice_bitcast_fusion = (bf16[64,640]{1,0:T(8,128)(2,1)S(1)}, bf16[64,640]{1,0:T(8,128)(2,1)S(1)}, bf16[64,640]{1,0:T(8,128)(2,1)S(1)}, bf16[64,640]{1,0:T(8,128)(2,1)S(1)}, bf16[64,640]{1,0:T(8,128)(2,1)S(1)}) fusion(bf16[2,128,640]{2,1,0:T(8,128)(2,1)} %param.8, s32[]{:T(128)S(6)} %select_n.120, s32[]{:T(128)S(6)} %select_n.133, s32[]{:T(128)S(6)} %select_n.128, ...), kind=kLoop, calls=%fused_computation.61 | loop fusion | bytes 819216 | tf_op jit(solution)/shard_map/dynamic_slice | solution.py:43
  3.9 1.3 %collective-permute-start.4 = (bf16[64,640]{1,0:T(8,128)(2,1)S(1)}, bf16[64,640]{1,0:T(8,128)(2,1)}, u32[]{:S(2)}, u32[]{:S(2)}) collective-permute-start(bf16[64,640]{1,0:T(8,128)(2,1)S(1)} %get-tuple-element.19), channel_id=1, source_target_pairs={{12,4},{13,5},{14,6},{15,7},{28,20},{29,21},{30,22},{31,23}} | collective-permute-start | bytes 245768 | tf_op jit(solution)/shard_map/ppermute | solution.py:53
  5.2 1.3 %collective-permute-start.5 = (bf16[64,640]{1,0:T(8,128)(2,1)S(1)}, bf16[64,640]{1,0:T(8,128)(2,1)}, u32[]{:S(2)}, u32[]{:S(2)}) collective-permute-start(bf16[64,640]{1,0:T(8,128)(2,1)S(1)} %get-tuple-element.16), channel_id=1, source_target_pairs={{12,0},{13,1},{14,2},{15,3},{28,16},{29,17},{30,18},{31,19}} | collective-permute-start | bytes 245768 | tf_op jit(solution)/shard_map/ppermute | solution.py:53
  6.5 1.3 %collective-permute-start.3 = (bf16[64,640]{1,0:T(8,128)(2,1)S(1)}, bf16[64,640]{1,0:T(8,128)(2,1)}, u32[]{:S(2)}, u32[]{:S(2)}) collective-permute-start(bf16[64,640]{1,0:T(8,128)(2,1)S(1)} %get-tuple-element.16), channel_id=1, source_target_pairs={{12,8},{13,9},{14,10},{15,11},{28,24},{29,25},{30,26},{31,27}} | collective-permute-start | bytes 245768 | tf_op jit(solution)/shard_map/ppermute | solution.py:53
  7.8 1.8 %collective-permute-start.2 = (bf16[64,640]{1,0:T(8,128)(2,1)S(1)}, bf16[64,640]{1,0:T(8,128)(2,1)S(1)}, u32[]{:S(2)}, u32[]{:S(2)}) collective-permute-start(bf16[64,640]{1,0:T(8,128)(2,1)S(1)} %get-tuple-element.15), channel_id=1, source_target_pairs={{0,4},{4,8},{8,12},{12,0},{1,5},{5,9},{9,13},{13,1},{2,6},{6,10},{... | collective-permute-start | bytes 245768 | tf_op jit(solution)/shard_map/ppermute | solution.py:48
  9.6 2.2 %collective-permute-start.1 = (bf16[64,640]{1,0:T(8,128)(2,1)S(1)}, bf16[64,640]{1,0:T(8,128)(2,1)S(1)}, u32[]{:S(2)}, u32[]{:S(2)}) collective-permute-start(bf16[64,640]{1,0:T(8,128)(2,1)S(1)} %get-tuple-element.17), channel_id=1, source_target_pairs={{0,8},{4,12},{8,0},{12,4},{1,9},{5,13},{9,1},{13,5},{2,10},{6,14},... | collective-permute-start | bytes 245768 | tf_op jit(solution)/shard_map/ppermute | solution.py:48
  11.8 0.9 %slice.94 = bf16[1,128,640]{2,1,0:T(8,128)(2,1)S(1)} slice(bf16[2,128,640]{2,1,0:T(8,128)(2,1)} %param.8), slice={[1:2], [0:128], [0:640]} | slice | bytes 327680 | tf_op jit(solution)/shard_map/slice | solution.py:38
  12.8 0.8 %collective-permute-start = (bf16[64,640]{1,0:T(8,128)(2,1)S(1)}, bf16[64,640]{1,0:T(8,128)(2,1)S(1)}, u32[]{:S(2)}, u32[]{:S(2)}) collective-permute-start(bf16[64,640]{1,0:T(8,128)(2,1)S(1)} %get-tuple-element.18), channel_id=1, source_target_pairs={{0,12},{4,0},{8,4},{12,8},{1,13},{5,1},{9,5},{13,9},{2,14},{6,2},{... | collective-permute-start | bytes 245768 | tf_op jit(solution)/shard_map/ppermute | solution.py:48
  13.6 0.9 %fusion.42 = bf16[1,64,640]{2,1,0:T(8,128)(2,1)S(1)} fusion(bf16[64,640]{1,0:T(8,128)(2,1)} %collective-permute-done.3, bf16[64,640]{1,0:T(8,128)(2,1)} %collective-permute-done.4, bf16[64,640]{1,0:T(8,128)(2,1)} %collective-permute-done.5, bf16[1,128,640]{2,1,0:T(8,128)(2,1)S(1)} %slice.94, s32[]{:T(128)S(6)} %select_n.136, pred[]{:T(512)S(6)} %eq.37, ...), kind=kLoop, calls=%fused_computation.54 | loop fusion | flops 122880 | bytes 409607 | tf_op jit(solution)/shard_map/stack | solution.py:55
  15.4 1.3 %collective-permute-done = bf16[64,640]{1,0:T(8,128)(2,1)S(1)} collective-permute-done((bf16[64,640]{1,0:T(8,128)(2,1)S(1)}, bf16[64,640]{1,0:T(8,128)(2,1)S(1)}, u32[]{:S(2)}, u32[]{:S(2)}) %collective-permute-start) | collective-permute-done | bytes 81952 | tf_op jit(solution)/shard_map/ppermute | solution.py:48
  16.7 0.9 %fusion.45 = bf16[1,64,640]{2,1,0:T(8,128)(2,1)S(1)} fusion(bf16[64,640]{1,0:T(8,128)(2,1)S(1)} %collective-permute-done, bf16[64,640]{1,0:T(8,128)(2,1)S(1)} %collective-permute-done.1, bf16[64,640]{1,0:T(8,128)(2,1)S(1)} %collective-permute-done.2, bf16[2,128,640]{2,1,0:T(8,128)(2,1)} %param.8, s32[]{:T(128)S(6)} %select_n.120, s32[]{:T(128)S(6)} %select_n.137, ...), kind=kLoop, calls=%fused_computation.58 | loop fusion | flops 163840 | bytes 409612 | tf_op jit(solution)/shard_map/stack | solution.py:55
  17.7 2.4 %collective-permute-start.7 = (bf16[2,64,640]{2,1,0:T(8,128)(2,1)S(1)}, bf16[2,64,640]{2,1,0:T(8,128)(2,1)S(1)}, u32[]{:S(2)}, u32[]{:S(2)}) collective-permute-start(bf16[2,64,640]{2,1,0:T(8,128)(2,1)S(1)} %get-tuple-element.21), channel_id=1, source_target_pairs={{0,2},{1,3},{2,0},{3,1},{4,6},{5,7},{6,4},{7,5},{8,10},{9,11},{10,... | collective-permute-start | bytes 491528 | tf_op jit(solution)/shard_map/ppermute | solution.py:58
  20.1 1.5 %collective-permute-start.8 = (bf16[2,64,640]{2,1,0:T(8,128)(2,1)S(1)}, bf16[2,64,640]{2,1,0:T(8,128)(2,1)S(1)}, u32[]{:S(2)}, u32[]{:S(2)}) collective-permute-start(bf16[2,64,640]{2,1,0:T(8,128)(2,1)S(1)} %get-tuple-element.21), channel_id=1, source_target_pairs={{0,3},{1,0},{2,1},{3,2},{4,7},{5,4},{6,5},{7,6},{8,11},{9,8},{10,9... | collective-permute-start | bytes 491528 | tf_op jit(solution)/shard_map/ppermute | solution.py:58
  21.5 5.7 %collective-permute-done.7 = bf16[2,64,640]{2,1,0:T(8,128)(2,1)S(1)} collective-permute-done((bf16[2,64,640]{2,1,0:T(8,128)(2,1)S(1)}, bf16[2,64,640]{2,1,0:T(8,128)(2,1)S(1)}, u32[]{:S(2)}, u32[]{:S(2)}) %collective-permute-start.7) | collective-permute-done | bytes 163872 | tf_op jit(solution)/shard_map/ppermute | solution.py:58
  27.2 6.9 %collective-permute-done.6 = bf16[2,64,640]{2,1,0:T(8,128)(2,1)S(1)} collective-permute-done((bf16[2,64,640]{2,1,0:T(8,128)(2,1)S(1)}, bf16[2,64,640]{2,1,0:T(8,128)(2,1)S(1)}, u32[]{:S(2)}, u32[]{:S(2)}) %collective-permute-start.6) | collective-permute-done | bytes 163872 | tf_op jit(solution)/shard_map/ppermute | solution.py:58
  34.1 1.0 %pad_maximum_fusion = bf16[4,2,64,640]{3,2,1,0:T(8,128)(2,1)} fusion(bf16[1,2,64,640]{3,2,1,0:T(8,128)(2,1)S(1)} %bitcast.112, bf16[1,2,64,640]{3,2,1,0:T(8,128)(2,1)S(1)} %bitcast.110, bf16[1,2,64,640]{3,2,1,0:T(8,128)(2,1)S(1)} %bitcast.111, bf16[1,2,64,640]{3,2,1,0:T(8,128)(2,1)S(1)} %get-tuple-element.20), kind=kLoop, calls=%fused_computation.38 | loop fusion | flops 983040 | bytes 1310720 | tf_op jit(solution)/shard_map/stack | solution.py:59
  35.9 0.9 %copy.13 = bf16[256,640]{0,1:T(8,128)(2,1)} copy(bf16[256,640]{1,0:T(8,128)(2,1)S(1)} %convolution_convert_fusion.1) | data formatting | bytes 655360 | tf_op jit(solution)/shard_map/convert_element_type | solution.py:67
  37.5 3.5 %convolution_convert_fusion = bf16[1024,1280]{1,0:T(8,128)(2,1)S(1)} fusion(bf16[640,1280]{1,0:T(8,128)(2,1)S(1)} %copy-done, bf16[512,640]{1,0:T(8,128)(2,1)} %collective-permute-done.9, bf16[512,640]{1,0:T(8,128)(2,1)} %bitcast.15), kind=kOutput, calls=%fused_computation.7 | convolution fusion | flops 1681653760 | bytes 5570560 | tf_op jit(solution)/shard_map/dot_general | solution.py:71
  41.0 1.7 %fusion.49 = (bf16[1024,640]{1,0:T(8,128)(2,1)}, bf16[1024,640]{1,0:T(8,128)(2,1)}) fusion(bf16[1024,1280]{1,0:T(8,128)(2,1)S(1)} %convolution_convert_fusion), kind=kLoop, calls=%fused_computation.68 | loop fusion | bytes 5242880 | tf_op jit(solution)/shard_map/slice | solution.py:72
  42.7 1.6 %copy.14 = bf16[1024,640]{0,1:T(8,128)(2,1)S(1)} copy(bf16[1024,640]{1,0:T(8,128)(2,1)} %get-tuple-element.5) | data formatting | bytes 2621440 | tf_op jit(solution)/shard_map/slice | solution.py:72
  44.3 2.5 %copy.12 = bf16[1024,640]{0,1:T(8,128)(2,1)} copy(bf16[1024,640]{1,0:T(8,128)(2,1)} %get-tuple-element.6) | data formatting | bytes 2621440 | tf_op jit(solution)/shard_map/slice | solution.py:73
  46.8 2.6 %multiply_reduce_fusion = (f32[10,256]{1,0:T(8,128)S(1)}, f32[10,256,1024]{2,1,0:T(8,128)S(1)}) fusion(bf16[256,10,64]{0,2,1:T(8,128)(2,1)} %bitcast.103, bf16[1024,10,64]{0,2,1:T(8,128)(2,1)S(1)} %bitcast.98), kind=kOutput, calls=%fused_computation.1 | convolution fusion | flops 340784640 | bytes 12134400 | tf_op jit(solution)/shard_map/qhd,khd->hqk/dot_general | solution.py:74
  49.5 2.1 %fusion = f32[10,256]{1,0:T(8,128)S(1)} fusion(f32[10,256,1024]{2,1,0:T(8,128)S(1)} %get-tuple-element.25, f32[10,256]{1,0:T(8,128)S(1)} %get-tuple-element.24), kind=kLoop, calls=%fused_computation.2 | loop fusion | flops 7861760 | bytes 10506240 | tf_op jit(solution)/shard_map/reduce_sum | solution.py:79
  51.5 2.3 %fusion.19 = bf16[256,10,64]{0,2,1:T(8,128)(2,1)S(1)} fusion(bf16[1024,10,64]{0,2,1:T(8,128)(2,1)S(1)} %bitcast.106, f32[10,256,1024]{2,1,0:T(8,128)S(1)} %get-tuple-element.25, f32[10,256]{1,0:T(8,128)S(1)} %get-tuple-element.24, f32[256,10]{0,1:T(8,128)S(1)} %bitcast.113), kind=kOutput, calls=%fused_computation.21 | convolution fusion | flops 343736320 | bytes 12144640 | tf_op jit(solution)/shard_map/hqk,khd->qhd/dot_general | solution.py:80
  54.6 3.0 %collective-permute-start.10 = (bf16[1,128,640]{2,1,0:T(8,128)(2,1)S(1)}, bf16[1,128,640]{2,1,0:T(8,128)(2,1)S(1)}, u32[]{:S(2)}, u32[]{:S(2)}) collective-permute-start(bf16[1,128,640]{2,1,0:T(8,128)(2,1)S(1)} %get-tuple-element.13), channel_id=1, source_target_pairs={{0,4},{4,8},{8,12},{1,5},{5,9},{9,13},{2,6},{6,10},{10,14},{3,7},{... | collective-permute-start | bytes 491528 | tf_op jit(solution)/shard_map/ppermute | solution.py:16
  57.6 1.9 %collective-permute-start.11 = (bf16[1,128,640]{2,1,0:T(8,128)(2,1)S(1)}, bf16[1,128,640]{2,1,0:T(8,128)(2,1)S(1)}, u32[]{:S(2)}, u32[]{:S(2)}) collective-permute-start(bf16[1,128,640]{2,1,0:T(8,128)(2,1)S(1)} %get-tuple-element.14), channel_id=1, source_target_pairs={{4,0},{8,4},{12,8},{5,1},{9,5},{13,9},{6,2},{10,6},{14,10},{7,3},{... | collective-permute-start | bytes 491528 | tf_op jit(solution)/shard_map/ppermute | solution.py:17
  60.0 4.2 %collective-permute-done.11 = bf16[1,128,640]{2,1,0:T(8,128)(2,1)S(1)} collective-permute-done((bf16[1,128,640]{2,1,0:T(8,128)(2,1)S(1)}, bf16[1,128,640]{2,1,0:T(8,128)(2,1)S(1)}, u32[]{:S(2)}, u32[]{:S(2)}) %collective-permute-start.11) | collective-permute-done | bytes 163872 | tf_op jit(solution)/shard_map/ppermute | solution.py:17
  65.4 2.1 %collective-permute-start.12 = (bf16[1,128,640]{2,1,0:T(8,128)(2,1)S(1)}, bf16[1,128,640]{2,1,0:T(8,128)(2,1)S(1)}, u32[]{:S(2)}, u32[]{:S(2)}) collective-permute-start(bf16[1,128,640]{2,1,0:T(8,128)(2,1)S(1)} %get-tuple-element.9), channel_id=1, source_target_pairs={{0,4},{4,8},{8,12},{1,5},{5,9},{9,13},{2,6},{6,10},{10,14},{3,7},{... | collective-permute-start | bytes 491528 | tf_op jit(solution)/shard_map/ppermute | solution.py:16
  67.4 2.4 %collective-permute-start.13 = (bf16[1,128,640]{2,1,0:T(8,128)(2,1)S(1)}, bf16[1,128,640]{2,1,0:T(8,128)(2,1)S(1)}, u32[]{:S(2)}, u32[]{:S(2)}) collective-permute-start(bf16[1,128,640]{2,1,0:T(8,128)(2,1)S(1)} %get-tuple-element.10), channel_id=1, source_target_pairs={{4,0},{8,4},{12,8},{5,1},{9,5},{13,9},{6,2},{10,6},{14,10},{7,3},{... | collective-permute-start | bytes 491528 | tf_op jit(solution)/shard_map/ppermute | solution.py:17
  70.3 3.7 %collective-permute-done.13 = bf16[1,128,640]{2,1,0:T(8,128)(2,1)S(1)} collective-permute-done((bf16[1,128,640]{2,1,0:T(8,128)(2,1)S(1)}, bf16[1,128,640]{2,1,0:T(8,128)(2,1)S(1)}, u32[]{:S(2)}, u32[]{:S(2)}) %collective-permute-start.13) | collective-permute-done | bytes 163872 | tf_op jit(solution)/shard_map/ppermute | solution.py:17
  74.6 1.2 %fusion.15 = bf16[256,640]{1,0:T(8,128)(2,1)} fusion(f32[256,640]{1,0:T(8,128)S(1)} %get-tuple-element.27, f32[256,640]{1,0:T(8,128)S(1)} %fusion.22, f32[256,640]{1,0:T(8,128)S(1)} %fusion.24, bf16[256,640]{1,0:T(8,128)(2,1)S(1)} %bitcast.107, bf16[3,640,640]{2,1,0:T(8,128)(2,1)S(1)} %copy-done.2), kind=kOutput, calls=%fused_computation.18 | convolution fusion | flops 210370560 | bytes 3440640 | tf_op jit(solution)/shard_map/dot_general | solution.py:25
  (41 shorter events, 5.7 us)
Async XLA Ops:
  0.0 37.5 %copy-start = (bf16[640,1280]{1,0:T(8,128)(2,1)S(1)}, bf16[640,1280]{1,0:T(8,128)(2,1)}, u32[]{:S(2)}) copy-start(bf16[640,1280]{1,0:T(8,128)(2,1)} %param.11) | copy-start | bytes 4915204
  0.0 35.4 %copy-start.1 = (bf16[2,128,640]{2,1,0:T(8,128)(2,1)S(1)}, bf16[2,128,640]{2,1,0:T(8,128)(2,1)}, u32[]{:S(2)}) copy-start(bf16[2,128,640]{2,1,0:T(8,128)(2,1)} %param.8) | copy-start | bytes 983044
  0.0 35.4 %copy-start.5 = (bf16[640,640]{1,0:T(8,128)(2,1)S(1)}, bf16[640,640]{1,0:T(8,128)(2,1)}, u32[]{:S(2)}) copy-start(bf16[640,640]{1,0:T(8,128)(2,1)} %param.10) | copy-start | bytes 2457604
  3.9 8.8 %collective-permute-start.4 = (bf16[64,640]{1,0:T(8,128)(2,1)S(1)}, bf16[64,640]{1,0:T(8,128)(2,1)}, u32[]{:S(2)}, u32[]{:S(2)}) collective-permute-start(bf16[64,640]{1,0:T(8,128)(2,1)S(1)} %get-tuple-element.19), channel_id=1, source_target_pairs={{12,4},{13,5},{14,6},{15,7},{28,20},{29,21},{30,22},{31,23}} | collective-permute-start | bytes 245768 | tf_op jit(solution)/shard_map/ppermute | solution.py:53
  5.2 8.4 %collective-permute-start.5 = (bf16[64,640]{1,0:T(8,128)(2,1)S(1)}, bf16[64,640]{1,0:T(8,128)(2,1)}, u32[]{:S(2)}, u32[]{:S(2)}) collective-permute-start(bf16[64,640]{1,0:T(8,128)(2,1)S(1)} %get-tuple-element.16), channel_id=1, source_target_pairs={{12,0},{13,1},{14,2},{15,3},{28,16},{29,17},{30,18},{31,19}} | collective-permute-start | bytes 245768 | tf_op jit(solution)/shard_map/ppermute | solution.py:53
  6.5 7.1 %collective-permute-start.3 = (bf16[64,640]{1,0:T(8,128)(2,1)S(1)}, bf16[64,640]{1,0:T(8,128)(2,1)}, u32[]{:S(2)}, u32[]{:S(2)}) collective-permute-start(bf16[64,640]{1,0:T(8,128)(2,1)S(1)} %get-tuple-element.16), channel_id=1, source_target_pairs={{12,8},{13,9},{14,10},{15,11},{28,24},{29,25},{30,26},{31,27}} | collective-permute-start | bytes 245768 | tf_op jit(solution)/shard_map/ppermute | solution.py:53
  7.8 6.8 %collective-permute-start.2 = (bf16[64,640]{1,0:T(8,128)(2,1)S(1)}, bf16[64,640]{1,0:T(8,128)(2,1)S(1)}, u32[]{:S(2)}, u32[]{:S(2)}) collective-permute-start(bf16[64,640]{1,0:T(8,128)(2,1)S(1)} %get-tuple-element.15), channel_id=1, source_target_pairs={{0,4},{4,8},{8,12},{12,0},{1,5},{5,9},{9,13},{13,1},{2,6},{6,10},{... | collective-permute-start | bytes 245768 | tf_op jit(solution)/shard_map/ppermute | solution.py:48
  9.6 5.8 %collective-permute-start.1 = (bf16[64,640]{1,0:T(8,128)(2,1)S(1)}, bf16[64,640]{1,0:T(8,128)(2,1)S(1)}, u32[]{:S(2)}, u32[]{:S(2)}) collective-permute-start(bf16[64,640]{1,0:T(8,128)(2,1)S(1)} %get-tuple-element.17), channel_id=1, source_target_pairs={{0,8},{4,12},{8,0},{12,4},{1,9},{5,13},{9,1},{13,5},{2,10},{6,14},... | collective-permute-start | bytes 245768 | tf_op jit(solution)/shard_map/ppermute | solution.py:48
  12.8 3.9 %collective-permute-start = (bf16[64,640]{1,0:T(8,128)(2,1)S(1)}, bf16[64,640]{1,0:T(8,128)(2,1)S(1)}, u32[]{:S(2)}, u32[]{:S(2)}) collective-permute-start(bf16[64,640]{1,0:T(8,128)(2,1)S(1)} %get-tuple-element.18), channel_id=1, source_target_pairs={{0,12},{4,0},{8,4},{12,8},{1,13},{5,1},{9,5},{13,9},{2,14},{6,2},{... | collective-permute-start | bytes 245768 | tf_op jit(solution)/shard_map/ppermute | solution.py:48
  17.7 9.5 %collective-permute-start.7 = (bf16[2,64,640]{2,1,0:T(8,128)(2,1)S(1)}, bf16[2,64,640]{2,1,0:T(8,128)(2,1)S(1)}, u32[]{:S(2)}, u32[]{:S(2)}) collective-permute-start(bf16[2,64,640]{2,1,0:T(8,128)(2,1)S(1)} %get-tuple-element.21), channel_id=1, source_target_pairs={{0,2},{1,3},{2,0},{3,1},{4,6},{5,7},{6,4},{7,5},{8,10},{9,11},{10,... | collective-permute-start | bytes 491528 | tf_op jit(solution)/shard_map/ppermute | solution.py:58
  20.1 14.0 %collective-permute-start.6 = (bf16[2,64,640]{2,1,0:T(8,128)(2,1)S(1)}, bf16[2,64,640]{2,1,0:T(8,128)(2,1)S(1)}, u32[]{:S(2)}, u32[]{:S(2)}) collective-permute-start(bf16[2,64,640]{2,1,0:T(8,128)(2,1)S(1)} %get-tuple-element.21), channel_id=1, source_target_pairs={{0,1},{1,2},{2,3},{3,0},{4,5},{5,6},{6,7},{7,4},{8,9},{9,10},{10,1... | collective-permute-start | bytes 491528 | tf_op jit(solution)/shard_map/ppermute | solution.py:58
  20.1 14.0 %collective-permute-start.8 = (bf16[2,64,640]{2,1,0:T(8,128)(2,1)S(1)}, bf16[2,64,640]{2,1,0:T(8,128)(2,1)S(1)}, u32[]{:S(2)}, u32[]{:S(2)}) collective-permute-start(bf16[2,64,640]{2,1,0:T(8,128)(2,1)S(1)} %get-tuple-element.21), channel_id=1, source_target_pairs={{0,3},{1,0},{2,1},{3,2},{4,7},{5,4},{6,5},{7,6},{8,11},{9,8},{10,9... | collective-permute-start | bytes 491528 | tf_op jit(solution)/shard_map/ppermute | solution.py:58
  35.1 2.4 %collective-permute-start.9 = (bf16[512,640]{1,0:T(8,128)(2,1)}, bf16[512,640]{1,0:T(8,128)(2,1)}, u32[]{:S(2)}, u32[]{:S(2)}) collective-permute-start(bf16[512,640]{1,0:T(8,128)(2,1)} %bitcast.15), channel_id=1, source_target_pairs={{0,4},{4,0},{8,12},{12,8},{1,5},{5,1},{9,13},{13,9},{2,6},{6,2},{1... | collective-permute-start | bytes 1966088 | tf_op jit(solution)/shard_map/ppermute | solution.py:60
  49.4 2.1 %copy-start.3 = (bf16[1024,640]{0,1:T(8,128)(2,1)S(1)}, bf16[1024,640]{0,1:T(8,128)(2,1)}, u32[]{:S(2)}) copy-start(bf16[1024,640]{0,1:T(8,128)(2,1)} %copy.12) | copy-start | bytes 3932164
  51.5 2.3 %copy-start.6 = (bf16[640,640]{1,0:T(8,128)(2,1)S(1)}, bf16[640,640]{1,0:T(8,128)(2,1)}, u32[]{:S(2)}) copy-start(bf16[640,640]{1,0:T(8,128)(2,1)} %param.12) | copy-start | bytes 2457604
  51.5 2.9 %copy-start.7 = (f32[640]{0:T(1024)S(1)}, f32[640]{0:T(1024)}, u32[]{:S(2)}) copy-start(f32[640]{0:T(1024)} %param.13) | copy-start | bytes 7684
  53.8 5.7 %copy-start.4 = (bf16[3,640,640]{2,1,0:T(8,128)(2,1)S(1)}, bf16[3,640,640]{2,1,0:T(8,128)(2,1)}, u32[]{:S(2)}) copy-start(bf16[3,640,640]{2,1,0:T(8,128)(2,1)} %param.14) | copy-start | bytes 7372804
  54.6 5.4 %collective-permute-start.10 = (bf16[1,128,640]{2,1,0:T(8,128)(2,1)S(1)}, bf16[1,128,640]{2,1,0:T(8,128)(2,1)S(1)}, u32[]{:S(2)}, u32[]{:S(2)}) collective-permute-start(bf16[1,128,640]{2,1,0:T(8,128)(2,1)S(1)} %get-tuple-element.13), channel_id=1, source_target_pairs={{0,4},{4,8},{8,12},{1,5},{5,9},{9,13},{2,6},{6,10},{10,14},{3,7},{... | collective-permute-start | bytes 491528 | tf_op jit(solution)/shard_map/ppermute | solution.py:16
  57.6 6.6 %collective-permute-start.11 = (bf16[1,128,640]{2,1,0:T(8,128)(2,1)S(1)}, bf16[1,128,640]{2,1,0:T(8,128)(2,1)S(1)}, u32[]{:S(2)}, u32[]{:S(2)}) collective-permute-start(bf16[1,128,640]{2,1,0:T(8,128)(2,1)S(1)} %get-tuple-element.14), channel_id=1, source_target_pairs={{4,0},{8,4},{12,8},{5,1},{9,5},{13,9},{6,2},{10,6},{14,10},{7,3},{... | collective-permute-start | bytes 491528 | tf_op jit(solution)/shard_map/ppermute | solution.py:17
  64.8 5.1 %copy-start.2 = (bf16[3,640,640]{2,1,0:T(8,128)(2,1)S(1)}, bf16[3,640,640]{2,1,0:T(8,128)(2,1)}, u32[]{:S(2)}) copy-start(bf16[3,640,640]{2,1,0:T(8,128)(2,1)} %param.15) | copy-start | bytes 7372804
  65.4 5.0 %collective-permute-start.12 = (bf16[1,128,640]{2,1,0:T(8,128)(2,1)S(1)}, bf16[1,128,640]{2,1,0:T(8,128)(2,1)S(1)}, u32[]{:S(2)}, u32[]{:S(2)}) collective-permute-start(bf16[1,128,640]{2,1,0:T(8,128)(2,1)S(1)} %get-tuple-element.9), channel_id=1, source_target_pairs={{0,4},{4,8},{8,12},{1,5},{5,9},{9,13},{2,6},{6,10},{10,14},{3,7},{... | collective-permute-start | bytes 491528 | tf_op jit(solution)/shard_map/ppermute | solution.py:16
  67.4 6.6 %collective-permute-start.13 = (bf16[1,128,640]{2,1,0:T(8,128)(2,1)S(1)}, bf16[1,128,640]{2,1,0:T(8,128)(2,1)S(1)}, u32[]{:S(2)}, u32[]{:S(2)}) collective-permute-start(bf16[1,128,640]{2,1,0:T(8,128)(2,1)S(1)} %get-tuple-element.10), channel_id=1, source_target_pairs={{4,0},{8,4},{12,8},{5,1},{9,5},{13,9},{6,2},{10,6},{14,10},{7,3},{... | collective-permute-start | bytes 491528 | tf_op jit(solution)/shard_map/ppermute | solution.py:17

commit v2 on v1

--- a/solution.py
+++ b/solution.py
@@ -42,16 +42,15 @@
     def half_of(x, h):
         return lax.dynamic_slice_in_dim(x, h * half, half, 0)
 
-    got_a = jnp.where(me == owner_a, half_of(cand_a, me % 2), jnp.zeros((half, channels), frames.dtype))
-    got_b = half_of(cand_b, me % 2)
+    own = jnp.stack([half_of(cand_a, me % 2), half_of(cand_b, me % 2)])
+    got_a = jnp.where(me == owner_a, own[0], jnp.zeros((half, channels), frames.dtype))
+    got_b = own[1]
     for s in range(1, fsize):
-        recv_a = lax.ppermute(
-            half_of(cand_a, (me + s) % 2), "frame", [(i, (i + s) % fsize) for i in range(fsize)]
-        )
-        got_a = jnp.where((me - s) % fsize == owner_a, recv_a, got_a)
-        dest = (owner_b + s) % fsize
-        recv_b = lax.ppermute(cand_b[(dest % 2) * half : (dest % 2 + 1) * half], "frame", [(owner_b, dest)])
-        got_b = jnp.where(me == dest, recv_b, got_b)
+        sent = jnp.stack([half_of(cand_a, (me + s) % 2), half_of(cand_b, (me + s) % 2)])
+        recv = lax.ppermute(sent, "frame", [(i, (i + s) % fsize) for i in range(fsize)])
+        source = (me - s) % fsize
+        got_a = jnp.where(source == owner_a, recv[0], got_a)
+        got_b = jnp.where(source == owner_b, recv[1], got_b)
     piece = jnp.stack([got_a, got_b])
     pieces = [piece]
     for s in range(1, rsize):
@@ -63,6 +62,7 @@
 
 def shards(frames, key_index, w_query, w_keyval, w_out, norm_gain, w_first, w_second):
     frame_count, row_count, channels = frames.shape
+    assert frame_count >= 2
     flattened = frames.reshape(-1, channels)
     queries = jnp.dot(flattened, w_query, preferred_element_type=jnp.float32).astype(jnp.bfloat16)
     query_heads = queries.reshape(-1, HEADS, HEAD_DIM)
@@ -88,11 +88,20 @@
     mean_square = jnp.mean(residual * residual, axis=-1, keepdims=True)
     normed = (residual * lax.rsqrt(mean_square + 1e-06) * norm_gain).astype(jnp.bfloat16)
     normed = normed.reshape(frame_count, row_count, channels)
-    padded = extended(normed, "frame", 1)
-    hidden = jax.nn.silu(temporal_mix(padded, w_first, frame_count)).astype(jnp.bfloat16)
-    hidden = hidden.reshape(frame_count, row_count, channels)
-    padded = extended(hidden, "frame", 1)
-    second = temporal_mix(padded, w_second, frame_count)
+    padded = extended(normed, "frame", 2)
+    hidden = jax.nn.silu(temporal_mix(padded, w_first, frame_count + 2)).astype(jnp.bfloat16)
+    hidden = hidden.reshape(frame_count + 2, row_count, channels)
+    me = lax.axis_index("frame")
+    outside = jnp.zeros((1, row_count, channels), hidden.dtype)
+    hidden = jnp.concatenate(
+        [
+            jnp.where(me == 0, outside, hidden[:1]),
+            hidden[1:-1],
+            jnp.where(me == lax.axis_size("frame") - 1, outside, hidden[-1:]),
+        ],
+        axis=0,
+    )
+    second = temporal_mix(hidden, w_second, frame_count)
     return (residual + second).astype(jnp.bfloat16).reshape(frame_count, row_count, channels)
 
 

time: 77.3 us -> 72.9 us (0.943)
  the two profiles are of different devices: /device:TPU:9 before, /device:TPU:1 now
where the time goes in v2:
time: 72.9 us; the launch traced here: 72.5 us
  waiting for transfers between devices  27 us (37%)
  matrix products  14.3 us (20%)
  starting transfers between devices  12.8 us (18%)
  local copies, waits for them, and re-layouts  11.3 us (16%)
  other arithmetic  5.43 us (7%)
  between operations  1.64 us (2%)
    ppermute x3, waiting for transfers between devices, gather_keyframes(): lax.ppermute(piece, 'row', [(i, (i + s) % rsize) for i in range(rsize)])  13.8 us
    ppermute x3, waiting for transfers between devices, gather_keyframes(): lax.ppermute(sent, 'frame', [(i, (i + s) % fsize) for i in range(fsize)])  6.33 us
    ppermute x3, starting transfers between devices, gather_keyframes(): lax.ppermute(piece, 'row', [(i, (i + s) % rsize) for i in range(rsize)])  4.63 us
    dot_general x6, matrix products, temporal_mix(): jnp.dot(window, weights[offset], preferred_element_type=jnp.float32)  4.45 us
    ppermute x1, waiting for transfers between devices, extended(): after = lax.ppermute(first, axis, down)  4.4 us
    dot_general x1, matrix products, shards(): jnp.dot(key_tokens, w_keyval, preferred_element_type=jnp.float32)  3.48 us
    ppermute x3, starting transfers between devices, gather_keyframes(): lax.ppermute(sent, 'frame', [(i, (i + s) % fsize) for i in range(fsize)])  3.12 us
    dot_general x1, matrix products, shards(): jnp.einsum('qhd,khd->hqk', query_heads, key_heads, preferred_element_type...  3.07 us
  transfers between devices with their start and end apart: 9, of which 8 were waited for; matrix products, arithmetic and copies ran while one was open for 3% of the time, Pallas kernels for 0%

profile of v2, /device:TPU:1, one launch (start us, length us, event | category | flops | bytes accessed | tf_op | source)
XLA Modules:
  0.0 72.5 jit_solution(18267043431447855835)
XLA Ops:
  0.0 1.4 %fusion.47 = (s32[1]{0:T(128)}, s32[1]{0:T(128)}) fusion(s32[2]{0:T(128)} %param.9), kind=kLoop, calls=%fused_computation.73 | loop fusion | bytes 16 | tf_op jit(solution)/shard_map/slice | solution.py:35
  2.8 0.9 %slice.82 = bf16[1,128,640]{2,1,0:T(8,128)(2,1)S(1)} slice(bf16[2,128,640]{2,1,0:T(8,128)(2,1)} %param.8), slice={[1:2], [0:128], [0:640]} | slice | bytes 327680 | tf_op jit(solution)/shard_map/slice | solution.py:38
  3.7 1.1 %constant_dynamic-slice_fusion.4 = (bf16[1,64,640]{2,1,0:T(8,128)(2,1)S(1)}, bf16[1,64,640]{2,1,0:T(8,128)(2,1)S(1)}, bf16[1,64,640]{2,1,0:T(8,128)(2,1)S(1)}, b...) fusion(bf16[1,128,640]{2,1,0:T(8,128)(2,1)S(1)} %slice.82, ...), kind=kLoop, calls=%fused_computation.65 | loop fusion | bytes 983068 | tf_op jit(solution)/shard_map/dynamic_slice | solution.py:43
  4.9 2.6 %collective-permute-start.2 = (bf16[2,64,640]{2,1,0:T(8,128)(2,1)S(1)}, bf16[2,64,640]{2,1,0:T(8,128)(2,1)}, u32[]{:S(2)}, u32[]{:S(2)}) collective-permute-start(bf16[2,64,640]{2,1,0:T(8,128)(2,1)S(1)} %pad_maximum_fusion.9), channel_id=1, source_target_pairs={{0,4},{4,8},{8,12},{12,0},{1,5},{5,9},{9,13},{13,1},{2,6},{6,10},{... | collective-permute-start | bytes 491528 | tf_op jit(solution)/shard_map/ppermute | solution.py:50
  7.7 0.7 pad_maximum_fusion.7
  8.7 2.2 %collective-permute-done.2 = bf16[2,64,640]{2,1,0:T(8,128)(2,1)} collective-permute-done((bf16[2,64,640]{2,1,0:T(8,128)(2,1)S(1)}, bf16[2,64,640]{2,1,0:T(8,128)(2,1)}, u32[]{:S(2)}, u32[]{:S(2)}) %collective-permute-start.2) | collective-permute-done | bytes 163872 | tf_op jit(solution)/shard_map/ppermute | solution.py:50
  10.9 3.5 %collective-permute-done.1 = bf16[2,64,640]{2,1,0:T(8,128)(2,1)} collective-permute-done((bf16[2,64,640]{2,1,0:T(8,128)(2,1)S(1)}, bf16[2,64,640]{2,1,0:T(8,128)(2,1)}, u32[]{:S(2)}, u32[]{:S(2)}) %collective-permute-start.1) | collective-permute-done | bytes 163872 | tf_op jit(solution)/shard_map/ppermute | solution.py:50
  14.4 0.6 collective-permute-done
  15.1 1.2 %fusion.41 = (bf16[1,64,640]{2,1,0:T(8,128)(2,1)S(1)}, bf16[1,64,640]{2,1,0:T(8,128)(2,1)S(1)}) fusion(bf16[2,64,640]{2,1,0:T(8,128)(2,1)} %collective-permute-done.2, bf16[2,64,640]{2,1,0:T(8,128)(2,1)} %collective-permute-done.1, bf16[2,64,640]{2,1,0:T(8,128)(2,1)} %collective-permute-done, bf16[2,128,640]{2,1,0:T(8,128)(2,1)S(1)} %copy-done.1, ...), kind=kLoop, calls=%fused_computation.60 | loop fusion | flops 286720 | bytes 819219 | tf_op jit(solution)/shard_map/jit(_where)/select_n | solution.py:52
  16.3 4.2 %collective-permute-start.5 = (bf16[2,64,640]{2,1,0:T(8,128)(2,1)S(1)}, bf16[2,64,640]{2,1,0:T(8,128)(2,1)S(1)}, u32[]{:S(2)}, u32[]{:S(2)}) collective-permute-start(bf16[2,64,640]{2,1,0:T(8,128)(2,1)S(1)} %get-tuple-element.20), channel_id=1, source_target_pairs={{0,3},{1,0},{2,1},{3,2},{4,7},{5,4},{6,5},{7,6},{8,11},{9,8},{10,9... | collective-permute-start | bytes 491528 | tf_op jit(solution)/shard_map/ppermute | solution.py:57
  20.9 3.5 %collective-permute-done.5 = bf16[2,64,640]{2,1,0:T(8,128)(2,1)S(1)} collective-permute-done((bf16[2,64,640]{2,1,0:T(8,128)(2,1)S(1)}, bf16[2,64,640]{2,1,0:T(8,128)(2,1)S(1)}, u32[]{:S(2)}, u32[]{:S(2)}) %collective-permute-start.5) | collective-permute-done | bytes 163872 | tf_op jit(solution)/shard_map/ppermute | solution.py:57
  24.4 10.3 %collective-permute-done.4 = bf16[2,64,640]{2,1,0:T(8,128)(2,1)S(1)} collective-permute-done((bf16[2,64,640]{2,1,0:T(8,128)(2,1)S(1)}, bf16[2,64,640]{2,1,0:T(8,128)(2,1)S(1)}, u32[]{:S(2)}, u32[]{:S(2)}) %collective-permute-start.4) | collective-permute-done | bytes 163872 | tf_op jit(solution)/shard_map/ppermute | solution.py:57
  34.8 0.9 %pad_maximum_fusion.2 = bf16[4,2,64,640]{3,2,1,0:T(8,128)(2,1)} fusion(bf16[1,2,64,640]{3,2,1,0:T(8,128)(2,1)S(1)} %bitcast.77, bf16[1,2,64,640]{3,2,1,0:T(8,128)(2,1)S(1)} %bitcast.78, bf16[1,2,64,640]{3,2,1,0:T(8,128)(2,1)S(1)} %bitcast.79, bf16[1,2,64,640]{3,2,1,0:T(8,128)(2,1)S(1)} %get-tuple-element.19), kind=kLoop, calls=%fused_computation.40 | loop fusion | flops 983040 | bytes 1310720 | tf_op jit(solution)/shard_map/stack | solution.py:58
  36.7 0.9 %copy.13 = bf16[256,640]{0,1:T(8,128)(2,1)} copy(bf16[256,640]{1,0:T(8,128)(2,1)S(1)} %convolution_convert_fusion.1) | data formatting | bytes 655360 | tf_op jit(solution)/shard_map/convert_element_type | solution.py:67
  37.6 0.7 collective-permute-done.6
  38.3 3.5 %convolution_convert_fusion = bf16[1024,1280]{1,0:T(8,128)(2,1)S(1)} fusion(bf16[640,1280]{1,0:T(8,128)(2,1)S(1)} %copy-done, bf16[512,640]{1,0:T(8,128)(2,1)} %collective-permute-done.6, bf16[512,640]{1,0:T(8,128)(2,1)} %bitcast.6), kind=kOutput, calls=%fused_computation.7 | convolution fusion | flops 1681653760 | bytes 5570560 | tf_op jit(solution)/shard_map/dot_general | solution.py:71
  41.8 1.3 %fusion.46 = (bf16[1024,640]{1,0:T(8,128)(2,1)S(1)}, bf16[1024,640]{1,0:T(8,128)(2,1)}) fusion(bf16[1024,1280]{1,0:T(8,128)(2,1)S(1)} %convolution_convert_fusion), kind=kLoop, calls=%fused_computation.72 | loop fusion | bytes 5242880 | tf_op jit(solution)/shard_map/slice | solution.py:72
  43.1 2.5 %copy.12 = bf16[1024,640]{0,1:T(8,128)(2,1)} copy(bf16[1024,640]{1,0:T(8,128)(2,1)} %get-tuple-element.6) | data formatting | bytes 2621440 | tf_op jit(solution)/shard_map/slice | solution.py:73
  45.6 1.5 %copy.14 = bf16[1024,640]{0,1:T(8,128)(2,1)} copy(bf16[1024,640]{1,0:T(8,128)(2,1)S(1)} %get-tuple-element.5) | data formatting | bytes 2621440 | tf_op jit(solution)/shard_map/slice | solution.py:72
  47.1 3.1 %multiply_reduce_fusion = (f32[10,256]{1,0:T(8,128)S(1)}, f32[10,256,1024]{2,1,0:T(8,128)S(1)}) fusion(bf16[256,10,64]{0,2,1:T(8,128)(2,1)} %bitcast.67, bf16[1024,10,64]{0,2,1:T(8,128)(2,1)} %bitcast.62), kind=kOutput, calls=%fused_computation.1 | convolution fusion | flops 340784640 | bytes 12134400 | tf_op jit(solution)/shard_map/qhd,khd->hqk/dot_general | solution.py:74
  50.2 2.1 %fusion = f32[10,256]{1,0:T(8,128)S(1)} fusion(f32[10,256,1024]{2,1,0:T(8,128)S(1)} %get-tuple-element.27, f32[10,256]{1,0:T(8,128)S(1)} %get-tuple-element.26), kind=kLoop, calls=%fused_computation.2 | loop fusion | flops 7861760 | bytes 10506240 | tf_op jit(solution)/shard_map/reduce_sum | solution.py:79
  52.3 2.3 %fusion.18 = bf16[256,10,64]{0,2,1:T(8,128)(2,1)S(1)} fusion(bf16[1024,10,64]{0,2,1:T(8,128)(2,1)S(1)} %bitcast.70, f32[10,256,1024]{2,1,0:T(8,128)S(1)} %get-tuple-element.27, f32[10,256]{1,0:T(8,128)S(1)} %get-tuple-element.26, f32[256,10]{0,1:T(8,128)S(1)} %bitcast.80), kind=kOutput, calls=%fused_computation.22 | convolution fusion | flops 343736320 | bytes 12144640 | tf_op jit(solution)/shard_map/hqk,khd->qhd/dot_general | solution.py:80
  54.6 0.6 multiply_reduce_fusion.1
  55.4 2.3 %collective-permute-start.7 = (bf16[2,128,640]{2,1,0:T(8,128)(2,1)S(1)}, bf16[2,128,640]{2,1,0:T(8,128)(2,1)S(1)}, u32[]{:S(2)}, u32[]{:S(2)}) collective-permute-start(bf16[2,128,640]{2,1,0:T(8,128)(2,1)S(1)} %bitcast.72), channel_id=1, source_target_pairs={{0,4},{4,8},{8,12},{1,5},{5,9},{9,13},{2,6},{6,10},{10,14},{3,7},{... | collective-permute-start | bytes 983048 | tf_op jit(solution)/shard_map/ppermute | solution.py:16
  57.6 2.2 %collective-permute-start.8 = (bf16[2,128,640]{2,1,0:T(8,128)(2,1)S(1)}, bf16[2,128,640]{2,1,0:T(8,128)(2,1)S(1)}, u32[]{:S(2)}, u32[]{:S(2)}) collective-permute-start(bf16[2,128,640]{2,1,0:T(8,128)(2,1)S(1)} %bitcast.73), channel_id=1, source_target_pairs={{4,0},{8,4},{12,8},{5,1},{9,5},{13,9},{6,2},{10,6},{14,10},{7,3},{... | collective-permute-start | bytes 983048 | tf_op jit(solution)/shard_map/ppermute | solution.py:17
  59.9 1.7 %collective-permute-done.7 = bf16[2,128,640]{2,1,0:T(8,128)(2,1)S(1)} collective-permute-done((bf16[2,128,640]{2,1,0:T(8,128)(2,1)S(1)}, bf16[2,128,640]{2,1,0:T(8,128)(2,1)S(1)}, u32[]{:S(2)}, u32[]{:S(2)}) %collective-permute-start.7) | collective-permute-done | bytes 327712 | tf_op jit(solution)/shard_map/ppermute | solution.py:16
  61.6 4.4 %collective-permute-done.8 = bf16[2,128,640]{2,1,0:T(8,128)(2,1)S(1)} collective-permute-done((bf16[2,128,640]{2,1,0:T(8,128)(2,1)S(1)}, bf16[2,128,640]{2,1,0:T(8,128)(2,1)S(1)}, u32[]{:S(2)}, u32[]{:S(2)}) %collective-permute-start.8) | collective-permute-done | bytes 327712 | tf_op jit(solution)/shard_map/ppermute | solution.py:17
  66.3 0.7 %fusion.25 = f32[512,640]{1,0:T(8,128)S(1)} fusion(bf16[512,640]{1,0:T(8,128)(2,1)S(1)} %bitcast.66, bf16[3,640,640]{2,1,0:T(8,128)(2,1)S(1)} %copy-done.4), kind=kOutput, calls=%fused_computation.27 | convolution fusion | flops 419430400 | bytes 2785280 | tf_op jit(solution)/shard_map/dot_general | solution.py:25
  67.0 0.7 %fusion.27 = f32[512,640]{1,0:T(8,128)S(1)} fusion(bf16[512,640]{1,0:T(8,128)(2,1)S(1)} %bitcast.65, bf16[3,640,640]{2,1,0:T(8,128)(2,1)S(1)} %copy-done.4), kind=kOutput, calls=%fused_computation.29 | convolution fusion | flops 419430400 | bytes 2785280 | tf_op jit(solution)/shard_map/dot_general | solution.py:25
  67.8 0.8 %multiply_convert_fusion = bf16[512,640]{1,0:T(8,128)(2,1)S(1)} fusion(f32[512,640]{1,0:T(8,128)S(1)} %fusion.25, f32[512,640]{1,0:T(8,128)S(1)} %fusion.27, bf16[512,640]{1,0:T(8,128)(2,1)S(1)} %bitcast.75, bf16[3,640,640]{2,1,0:T(8,128)(2,1)S(1)} %copy-done.4), kind=kOutput, calls=%fused_computation.13 | convolution fusion | flops 421724160 | bytes 4751360 | tf_op jit(solution)/shard_map/dot_general | solution.py:25
  68.8 1.5 %copy-done.2 = bf16[3,640,640]{2,1,0:T(8,128)(2,1)S(1)} copy-done((bf16[3,640,640]{2,1,0:T(8,128)(2,1)S(1)}, bf16[3,640,640]{2,1,0:T(8,128)(2,1)}, u32[]{:S(2)}) %copy-start.2) | copy-done | bytes 2457624
  71.3 1.2 %fusion.14 = bf16[256,640]{1,0:T(8,128)(2,1)} fusion(f32[256,640]{1,0:T(8,128)S(1)} %get-tuple-element.29, f32[256,640]{1,0:T(8,128)S(1)} %convolution_add_fusion.2, bf16[256,640]{1,0:T(8,128)(2,1)S(1)} %bitcast.71, bf16[3,640,640]{2,1,0:T(8,128)(2,1)S(1)} %copy-done.2), kind=kOutput, calls=%fused_computation.19 | convolution fusion | flops 210206720 | bytes 2785280 | tf_op jit(solution)/shard_map/dot_general | solution.py:25
  (33 shorter events, 3.5 us)
Async XLA Ops:
  0.0 38.3 %copy-start = (bf16[640,1280]{1,0:T(8,128)(2,1)S(1)}, bf16[640,1280]{1,0:T(8,128)(2,1)}, u32[]{:S(2)}) copy-start(bf16[640,1280]{1,0:T(8,128)(2,1)} %param.11) | copy-start | bytes 4915204
  0.0 15.1 %copy-start.1 = (bf16[2,128,640]{2,1,0:T(8,128)(2,1)S(1)}, bf16[2,128,640]{2,1,0:T(8,128)(2,1)}, u32[]{:S(2)}) copy-start(bf16[2,128,640]{2,1,0:T(8,128)(2,1)} %param.8) | copy-start | bytes 983044
  3.7 32.6 %copy-start.5 = (bf16[640,640]{1,0:T(8,128)(2,1)S(1)}, bf16[640,640]{1,0:T(8,128)(2,1)}, u32[]{:S(2)}) copy-start(bf16[640,640]{1,0:T(8,128)(2,1)} %param.10) | copy-start | bytes 2457604
  4.9 6.0 %collective-permute-start.2 = (bf16[2,64,640]{2,1,0:T(8,128)(2,1)S(1)}, bf16[2,64,640]{2,1,0:T(8,128)(2,1)}, u32[]{:S(2)}, u32[]{:S(2)}) collective-permute-start(bf16[2,64,640]{2,1,0:T(8,128)(2,1)S(1)} %pad_maximum_fusion.9), channel_id=1, source_target_pairs={{0,4},{4,8},{8,12},{12,0},{1,5},{5,9},{9,13},{13,1},{2,6},{6,10},{... | collective-permute-start | bytes 491528 | tf_op jit(solution)/shard_map/ppermute | solution.py:50
  7.6 6.9 %collective-permute-start.1 = (bf16[2,64,640]{2,1,0:T(8,128)(2,1)S(1)}, bf16[2,64,640]{2,1,0:T(8,128)(2,1)}, u32[]{:S(2)}, u32[]{:S(2)}) collective-permute-start(bf16[2,64,640]{2,1,0:T(8,128)(2,1)S(1)} %pad_maximum_fusion.8), channel_id=1, source_target_pairs={{0,8},{4,12},{8,0},{12,4},{1,9},{5,13},{9,1},{13,5},{2,10},{6,14},... | collective-permute-start | bytes 491528 | tf_op jit(solution)/shard_map/ppermute | solution.py:50
  8.3 6.7 %collective-permute-start = (bf16[2,64,640]{2,1,0:T(8,128)(2,1)}, bf16[2,64,640]{2,1,0:T(8,128)(2,1)}, u32[]{:S(2)}, u32[]{:S(2)}) collective-permute-start(bf16[2,64,640]{2,1,0:T(8,128)(2,1)} %pad_maximum_fusion.7), channel_id=1, source_target_pairs={{0,12},{4,0},{8,4},{12,8},{1,13},{5,1},{9,5},{13,9},{2,14},{6,2},{... | collective-permute-start | bytes 491528 | tf_op jit(solution)/shard_map/ppermute | solution.py:50
  16.3 8.1 %collective-permute-start.5 = (bf16[2,64,640]{2,1,0:T(8,128)(2,1)S(1)}, bf16[2,64,640]{2,1,0:T(8,128)(2,1)S(1)}, u32[]{:S(2)}, u32[]{:S(2)}) collective-permute-start(bf16[2,64,640]{2,1,0:T(8,128)(2,1)S(1)} %get-tuple-element.20), channel_id=1, source_target_pairs={{0,3},{1,0},{2,1},{3,2},{4,7},{5,4},{6,5},{7,6},{8,11},{9,8},{10,9... | collective-permute-start | bytes 491528 | tf_op jit(solution)/shard_map/ppermute | solution.py:57
  20.5 14.3 %collective-permute-start.4 = (bf16[2,64,640]{2,1,0:T(8,128)(2,1)S(1)}, bf16[2,64,640]{2,1,0:T(8,128)(2,1)S(1)}, u32[]{:S(2)}, u32[]{:S(2)}) collective-permute-start(bf16[2,64,640]{2,1,0:T(8,128)(2,1)S(1)} %get-tuple-element.20), channel_id=1, source_target_pairs={{0,2},{1,3},{2,0},{3,1},{4,6},{5,7},{6,4},{7,5},{8,10},{9,11},{10,... | collective-permute-start | bytes 491528 | tf_op jit(solution)/shard_map/ppermute | solution.py:57
  20.5 14.3 %collective-permute-start.3 = (bf16[2,64,640]{2,1,0:T(8,128)(2,1)S(1)}, bf16[2,64,640]{2,1,0:T(8,128)(2,1)S(1)}, u32[]{:S(2)}, u32[]{:S(2)}) collective-permute-start(bf16[2,64,640]{2,1,0:T(8,128)(2,1)S(1)} %get-tuple-element.20), channel_id=1, source_target_pairs={{0,1},{1,2},{2,3},{3,0},{4,5},{5,6},{6,7},{7,4},{8,9},{9,10},{10,1... | collective-permute-start | bytes 491528 | tf_op jit(solution)/shard_map/ppermute | solution.py:57
  35.7 2.6 %collective-permute-start.6 = (bf16[512,640]{1,0:T(8,128)(2,1)}, bf16[512,640]{1,0:T(8,128)(2,1)}, u32[]{:S(2)}, u32[]{:S(2)}) collective-permute-start(bf16[512,640]{1,0:T(8,128)(2,1)} %bitcast.6), channel_id=1, source_target_pairs={{0,4},{4,0},{8,12},{12,8},{1,5},{5,1},{9,13},{13,9},{2,6},{6,2},{1... | collective-permute-start | bytes 1966088 | tf_op jit(solution)/shard_map/ppermute | solution.py:59
  50.2 2.1 %copy-start.3 = (bf16[1024,640]{0,1:T(8,128)(2,1)S(1)}, bf16[1024,640]{0,1:T(8,128)(2,1)}, u32[]{:S(2)}) copy-start(bf16[1024,640]{0,1:T(8,128)(2,1)} %copy.12) | copy-start | bytes 3932164
  52.3 2.3 %copy-start.6 = (bf16[640,640]{1,0:T(8,128)(2,1)S(1)}, bf16[640,640]{1,0:T(8,128)(2,1)}, u32[]{:S(2)}) copy-start(bf16[640,640]{1,0:T(8,128)(2,1)} %param.12) | copy-start | bytes 2457604
  52.3 2.9 %copy-start.7 = (f32[640]{0:T(1024)S(1)}, f32[640]{0:T(1024)}, u32[]{:S(2)}) copy-start(f32[640]{0:T(1024)} %param.13) | copy-start | bytes 7684
  55.4 6.3 %collective-permute-start.7 = (bf16[2,128,640]{2,1,0:T(8,128)(2,1)S(1)}, bf16[2,128,640]{2,1,0:T(8,128)(2,1)S(1)}, u32[]{:S(2)}, u32[]{:S(2)}) collective-permute-start(bf16[2,128,640]{2,1,0:T(8,128)(2,1)S(1)} %bitcast.72), channel_id=1, source_target_pairs={{0,4},{4,8},{8,12},{1,5},{5,9},{9,13},{2,6},{6,10},{10,14},{3,7},{... | collective-permute-start | bytes 983048 | tf_op jit(solution)/shard_map/ppermute | solution.py:16
  57.6 8.4 %collective-permute-start.8 = (bf16[2,128,640]{2,1,0:T(8,128)(2,1)S(1)}, bf16[2,128,640]{2,1,0:T(8,128)(2,1)S(1)}, u32[]{:S(2)}, u32[]{:S(2)}) collective-permute-start(bf16[2,128,640]{2,1,0:T(8,128)(2,1)S(1)} %bitcast.73), channel_id=1, source_target_pairs={{4,0},{8,4},{12,8},{5,1},{9,5},{13,9},{6,2},{10,6},{14,10},{7,3},{... | collective-permute-start | bytes 983048 | tf_op jit(solution)/shard_map/ppermute | solution.py:17
  59.9 6.4 %copy-start.4 = (bf16[3,640,640]{2,1,0:T(8,128)(2,1)S(1)}, bf16[3,640,640]{2,1,0:T(8,128)(2,1)}, u32[]{:S(2)}) copy-start(bf16[3,640,640]{2,1,0:T(8,128)(2,1)} %param.14) | copy-start | bytes 7372804
  68.6 1.7 %copy-start.2 = (bf16[3,640,640]{2,1,0:T(8,128)(2,1)S(1)}, bf16[3,640,640]{2,1,0:T(8,128)(2,1)}, u32[]{:S(2)}) copy-start(bf16[3,640,640]{2,1,0:T(8,128)(2,1)} %param.15) | copy-start | bytes 7372804

commit v3 on v2

--- a/solution.py
+++ b/solution.py
@@ -1,11 +1,43 @@
 import jax
 import jax.numpy as jnp
 from jax import lax
+from jax.experimental import pallas as pl
 from jax.sharding import PartitionSpec as P
 
 HEADS = 10
 HEAD_DIM = 64
 
+
+def attention_kernel(q_ref, k_ref, v_ref, o_ref):
+    outs = []
+    for hh in range(2):
+        cols = slice(hh * HEAD_DIM, (hh + 1) * HEAD_DIM)
+        scores = lax.dot_general(
+            q_ref[:, cols], k_ref[:, cols], (((1,), (1,)), ((), ())),
+            preferred_element_type=jnp.float32) * HEAD_DIM ** (-0.5)
+        highest = jnp.max(scores, axis=1, keepdims=True)
+        exponent = jnp.exp(scores - highest)
+        denominator = jnp.sum(exponent, axis=1, keepdims=True)
+        mixed = jnp.dot(exponent.astype(jnp.bfloat16), v_ref[:, cols], preferred_element_type=jnp.float32)
+        outs.append(mixed / denominator)
+    o_ref[...] = jnp.concatenate(outs, axis=1).astype(o_ref.dtype)
+
+def attend(queries, keyval, q_tile=128):
+    total, channels = queries.shape
+    keys = keyval.shape[0]
+    pairs = channels // (2 * HEAD_DIM)
+    width = 2 * HEAD_DIM
+    return pl.pallas_call(
+        attention_kernel,
+        grid=(pairs, total // q_tile),
+        in_specs=[
+            pl.BlockSpec((q_tile, width), lambda j, i: (i, j)),
+            pl.BlockSpec((keys, width), lambda j, i: (0, j)),
+            pl.BlockSpec((keys, width), lambda j, i: (0, pairs + j)),
+        ],
+        out_specs=pl.BlockSpec((q_tile, width), lambda j, i: (i, j)),
+        out_shape=jax.ShapeDtypeStruct((total, channels), jnp.bfloat16),
+    )(queries, keyval, keyval)
 
 def extended(array, axis, width):
     size, length = (lax.axis_size(axis), array.shape[0])
@@ -65,23 +97,10 @@
     assert frame_count >= 2
     flattened = frames.reshape(-1, channels)
     queries = jnp.dot(flattened, w_query, preferred_element_type=jnp.float32).astype(jnp.bfloat16)
-    query_heads = queries.reshape(-1, HEADS, HEAD_DIM)
     query_total = queries.shape[0]
     key_tokens = gather_keyframes(frames, key_index)
     keyval = jnp.dot(key_tokens, w_keyval, preferred_element_type=jnp.float32).astype(jnp.bfloat16)
-    key_heads = keyval[:, :channels].reshape(-1, HEADS, HEAD_DIM)
-    value_heads = keyval[:, channels:].reshape(-1, HEADS, HEAD_DIM)
-    scores = jnp.einsum(
-        "qhd,khd->hqk", query_heads, key_heads, preferred_element_type=jnp.float32
-    ) * HEAD_DIM ** (-0.5)
-    highest = jnp.max(scores, axis=-1, keepdims=True)
-    exponent = jnp.exp(scores - highest)
-    denominator = jnp.sum(exponent, axis=-1)
-    mixed = jnp.einsum(
-        "hqk,khd->qhd", exponent.astype(jnp.bfloat16), value_heads, preferred_element_type=jnp.float32
-    )
-    mixed = mixed / denominator.T[:, :, None]
-    attended = mixed.reshape(query_total, channels).astype(jnp.bfloat16)
+    attended = attend(queries, keyval)
     residual = flattened.astype(jnp.float32) + jnp.dot(
         attended, w_out, preferred_element_type=jnp.float32
     )

time: 72.9 us -> 70.9 us (0.973)
  the two profiles are of different devices: /device:TPU:1 before, /device:TPU:9 now
where the time goes in v3:
time: 70.9 us; the launch traced here: 70.5 us
  waiting for transfers between devices  26.6 us (38%)
  Pallas kernels  12.3 us (17%)
  starting transfers between devices  12.2 us (17%)
  matrix products  10.9 us (15%)
  local copies, waits for them, and re-layouts  5.04 us (7%)
  other arithmetic  1.87 us (3%)
  between operations  1.54 us (2%)
    ppermute x3, waiting for transfers between devices, gather_keyframes(): lax.ppermute(piece, 'row', [(i, (i + s) % rsize) for i in range(rsize)])  13.7 us
    pallas_call x1, Pallas kernels, attend(): pl.pallas_call(attention_kernel, grid=(pairs, total // q_tile), in_specs=...  12.3 us
    ppermute x3, waiting for transfers between devices, gather_keyframes(): lax.ppermute(sent, 'frame', [(i, (i + s) % fsize) for i in range(fsize)])  5.91 us
    dot_general x6, matrix products, temporal_mix(): jnp.dot(window, weights[offset], preferred_element_type=jnp.float32)  4.44 us
    ppermute x1, waiting for transfers between devices, extended(): after = lax.ppermute(first, axis, down)  4.4 us
    ppermute x3, starting transfers between devices, gather_keyframes(): lax.ppermute(piece, 'row', [(i, (i + s) % rsize) for i in range(rsize)])  3.83 us
    dot_general x1, matrix products, shards(): jnp.dot(key_tokens, w_keyval, preferred_element_type=jnp.float32)  3.72 us
    ppermute x3, starting transfers between devices, gather_keyframes(): lax.ppermute(sent, 'frame', [(i, (i + s) % fsize) for i in range(fsize)])  3.4 us
  transfers between devices with their start and end apart: 9, of which 9 were waited for; matrix products, arithmetic and copies ran while one was open for 2% of the time, Pallas kernels for 0%

profile of v3, /device:TPU:9, one launch (start us, length us, event | category | flops | bytes accessed | tf_op | source)
XLA Modules:
  0.0 70.5 jit_solution(4813245953505785835)
XLA Ops:
  0.0 1.4 %fusion.30 = (s32[1]{0:T(128)}, s32[1]{0:T(128)}) fusion(s32[2]{0:T(128)} %param.9), kind=kLoop, calls=%fused_computation.61 | loop fusion | bytes 16 | tf_op jit(solution)/shard_map/slice | solution.py:67
  2.8 0.9 %slice.76 = bf16[1,128,640]{2,1,0:T(8,128)(2,1)S(1)} slice(bf16[2,128,640]{2,1,0:T(8,128)(2,1)} %param.8), slice={[1:2], [0:128], [0:640]} | slice | bytes 327680 | tf_op jit(solution)/shard_map/slice | solution.py:70
  3.7 1.1 %constant_dynamic-slice_fusion.4 = (bf16[1,64,640]{2,1,0:T(8,128)(2,1)S(1)}, bf16[1,64,640]{2,1,0:T(8,128)(2,1)S(1)}, bf16[1,64,640]{2,1,0:T(8,128)(2,1)S(1)}, b...) fusion(bf16[1,128,640]{2,1,0:T(8,128)(2,1)S(1)} %slice.76, ...), kind=kLoop, calls=%fused_computation.55 | loop fusion | bytes 983068 | tf_op jit(solution)/shard_map/dynamic_slice | solution.py:75
  4.9 0.7 %collective-permute-start = (bf16[2,64,640]{2,1,0:T(8,128)(2,1)S(1)}, bf16[2,64,640]{2,1,0:T(8,128)(2,1)}, u32[]{:S(2)}, u32[]{:S(2)}) collective-permute-start(bf16[2,64,640]{2,1,0:T(8,128)(2,1)S(1)} %pad_maximum_fusion.7), channel_id=1, source_target_pairs={{0,12},{4,0},{8,4},{12,8},{1,13},{5,1},{9,5},{13,9},{2,14},{6,2},{... | collective-permute-start | bytes 491528 | tf_op jit(solution)/shard_map/ppermute | solution.py:82
  5.6 1.3 %collective-permute-start.1 = (bf16[2,64,640]{2,1,0:T(8,128)(2,1)S(1)}, bf16[2,64,640]{2,1,0:T(8,128)(2,1)}, u32[]{:S(2)}, u32[]{:S(2)}) collective-permute-start(bf16[2,64,640]{2,1,0:T(8,128)(2,1)S(1)} %pad_maximum_fusion.8), channel_id=1, source_target_pairs={{0,8},{4,12},{8,0},{12,4},{1,9},{5,13},{9,1},{13,5},{2,10},{6,14},... | collective-permute-start | bytes 491528 | tf_op jit(solution)/shard_map/ppermute | solution.py:82
  6.9 1.4 %collective-permute-start.2 = (bf16[2,64,640]{2,1,0:T(8,128)(2,1)S(1)}, bf16[2,64,640]{2,1,0:T(8,128)(2,1)}, u32[]{:S(2)}, u32[]{:S(2)}) collective-permute-start(bf16[2,64,640]{2,1,0:T(8,128)(2,1)S(1)} %pad_maximum_fusion.9), channel_id=1, source_target_pairs={{0,4},{4,8},{8,12},{12,0},{1,5},{5,9},{9,13},{13,1},{2,6},{6,10},{... | collective-permute-start | bytes 491528 | tf_op jit(solution)/shard_map/ppermute | solution.py:82
  8.3 3.1 %collective-permute-done = bf16[2,64,640]{2,1,0:T(8,128)(2,1)} collective-permute-done((bf16[2,64,640]{2,1,0:T(8,128)(2,1)S(1)}, bf16[2,64,640]{2,1,0:T(8,128)(2,1)}, u32[]{:S(2)}, u32[]{:S(2)}) %collective-permute-start) | collective-permute-done | bytes 163872 | tf_op jit(solution)/shard_map/ppermute | solution.py:82
  11.4 0.6 collective-permute-done.1
  12.0 2.2 %collective-permute-done.2 = bf16[2,64,640]{2,1,0:T(8,128)(2,1)} collective-permute-done((bf16[2,64,640]{2,1,0:T(8,128)(2,1)S(1)}, bf16[2,64,640]{2,1,0:T(8,128)(2,1)}, u32[]{:S(2)}, u32[]{:S(2)}) %collective-permute-start.2) | collective-permute-done | bytes 163872 | tf_op jit(solution)/shard_map/ppermute | solution.py:82
  14.2 1.2 %fusion.26 = (bf16[1,64,640]{2,1,0:T(8,128)(2,1)S(1)}, bf16[1,64,640]{2,1,0:T(8,128)(2,1)S(1)}) fusion(bf16[2,64,640]{2,1,0:T(8,128)(2,1)} %collective-permute-done.2, bf16[2,64,640]{2,1,0:T(8,128)(2,1)} %collective-permute-done.1, bf16[2,64,640]{2,1,0:T(8,128)(2,1)} %collective-permute-done, bf16[2,128,640]{2,1,0:T(8,128)(2,1)S(1)} %copy-done.1, ...), kind=kLoop, calls=%fused_computation.50 | loop fusion | flops 286720 | bytes 819219 | tf_op jit(solution)/shard_map/jit(_where)/select_n | solution.py:84
  15.5 1.4 %collective-permute-start.3 = (bf16[2,64,640]{2,1,0:T(8,128)(2,1)S(1)}, bf16[2,64,640]{2,1,0:T(8,128)(2,1)S(1)}, u32[]{:S(2)}, u32[]{:S(2)}) collective-permute-start(bf16[2,64,640]{2,1,0:T(8,128)(2,1)S(1)} %get-tuple-element.18), channel_id=1, source_target_pairs={{0,1},{1,2},{2,3},{3,0},{4,5},{5,6},{6,7},{7,4},{8,9},{9,10},{10,1... | collective-permute-start | bytes 491528 | tf_op jit(solution)/shard_map/ppermute | solution.py:89
  16.8 1.1 %collective-permute-start.4 = (bf16[2,64,640]{2,1,0:T(8,128)(2,1)S(1)}, bf16[2,64,640]{2,1,0:T(8,128)(2,1)S(1)}, u32[]{:S(2)}, u32[]{:S(2)}) collective-permute-start(bf16[2,64,640]{2,1,0:T(8,128)(2,1)S(1)} %get-tuple-element.18), channel_id=1, source_target_pairs={{0,2},{1,3},{2,0},{3,1},{4,6},{5,7},{6,4},{7,5},{8,10},{9,11},{10,... | collective-permute-start | bytes 491528 | tf_op jit(solution)/shard_map/ppermute | solution.py:89
  17.9 1.4 %collective-permute-start.5 = (bf16[2,64,640]{2,1,0:T(8,128)(2,1)S(1)}, bf16[2,64,640]{2,1,0:T(8,128)(2,1)S(1)}, u32[]{:S(2)}, u32[]{:S(2)}) collective-permute-start(bf16[2,64,640]{2,1,0:T(8,128)(2,1)S(1)} %get-tuple-element.18), channel_id=1, source_target_pairs={{0,3},{1,0},{2,1},{3,2},{4,7},{5,4},{6,5},{7,6},{8,11},{9,8},{10,9... | collective-permute-start | bytes 491528 | tf_op jit(solution)/shard_map/ppermute | solution.py:89
  19.7 9.6 %collective-permute-done.4 = bf16[2,64,640]{2,1,0:T(8,128)(2,1)S(1)} collective-permute-done((bf16[2,64,640]{2,1,0:T(8,128)(2,1)S(1)}, bf16[2,64,640]{2,1,0:T(8,128)(2,1)S(1)}, u32[]{:S(2)}, u32[]{:S(2)}) %collective-permute-start.4) | collective-permute-done | bytes 163872 | tf_op jit(solution)/shard_map/ppermute | solution.py:89
  29.3 3.7 %collective-permute-done.5 = bf16[2,64,640]{2,1,0:T(8,128)(2,1)S(1)} collective-permute-done((bf16[2,64,640]{2,1,0:T(8,128)(2,1)S(1)}, bf16[2,64,640]{2,1,0:T(8,128)(2,1)S(1)}, u32[]{:S(2)}, u32[]{:S(2)}) %collective-permute-start.5) | collective-permute-done | bytes 163872 | tf_op jit(solution)/shard_map/ppermute | solution.py:89
  33.1 0.6 collective-permute-start.6
  33.7 1.2 %convolution_convert_fusion.1.q_ref = bf16[256,640]{1,0:T(8,128)(2,1)} fusion(bf16[256,640]{1,0:T(8,128)(2,1)S(1)} %bitcast.48, bf16[640,640]{1,0:T(8,128)(2,1)S(1)} %copy-done.4), kind=kOutput, calls=%fused_computation.12 | convolution fusion | flops 209879040 | bytes 1474560 | tf_op jit(solution)/shard_map/dot_general | solution.py:99
  34.9 0.5 collective-permute-done.6
  35.4 3.7 %convolution_convert_fusion.k_ref.v_ref = bf16[1024,1280]{1,0:T(8,128)(2,1)} fusion(bf16[640,1280]{1,0:T(8,128)(2,1)S(1)} %copy-done, bf16[512,640]{1,0:T(8,128)(2,1)S(1)} %collective-permute-done.6, bf16[512,640]{1,0:T(8,128)(2,1)S(1)} %bitcast.59), kind=kOutput, calls=%fused_computation | convolution fusion | flops 1681653760 | bytes 5570560 | tf_op jit(solution)/shard_map/dot_general | solution.py:102
  39.1 12.3 %shard_map.82 = bf16[256,640]{1,0:T(8,128)(2,1)} custom-call(bf16[256,640]{1,0:T(8,128)(2,1)} %convolution_convert_fusion.1.q_ref, bf16[1024,1280]{1,0:T(8,128)(2,1)} %convolution_convert_fusion.k_ref.v_ref, bf16[1024,1280]{1,0:T(8,128)(2,1)} %convolution_convert_fusion.k_ref.v_ref), custom_call_target="tpu_custom_call" | custom-call | tf_op jit(solution)/shard_map/pallas_call | solution.py:30
  51.5 1.5 %multiply_reduce_fusion = (f32[256]{0:T(256)S(1)}, f32[256,640]{1,0:T(8,128)S(1)}) fusion(bf16[256,640]{1,0:T(8,128)(2,1)} %shard_map.82, bf16[640,640]{1,0:T(8,128)(2,1)S(1)} %copy-done.5, bf16[256,640]{1,0:T(8,128)(2,1)S(1)} %bitcast.49), kind=kOutput, calls=%fused_computation.34 | convolution fusion | flops 210370304 | bytes 2130944 | tf_op jit(solution)/shard_map/dot_general | solution.py:104
  53.2 2.5 %collective-permute-start.7 = (bf16[2,128,640]{2,1,0:T(8,128)(2,1)S(1)}, bf16[2,128,640]{2,1,0:T(8,128)(2,1)S(1)}, u32[]{:S(2)}, u32[]{:S(2)}) collective-permute-start(bf16[2,128,640]{2,1,0:T(8,128)(2,1)S(1)} %bitcast.55), channel_id=1, source_target_pairs={{0,4},{4,8},{8,12},{1,5},{5,9},{9,13},{2,6},{6,10},{10,14},{3,7},{... | collective-permute-start | bytes 983048 | tf_op jit(solution)/shard_map/ppermute | solution.py:48
  55.6 1.9 %collective-permute-start.8 = (bf16[2,128,640]{2,1,0:T(8,128)(2,1)S(1)}, bf16[2,128,640]{2,1,0:T(8,128)(2,1)S(1)}, u32[]{:S(2)}, u32[]{:S(2)}) collective-permute-start(bf16[2,128,640]{2,1,0:T(8,128)(2,1)S(1)} %bitcast.56), channel_id=1, source_target_pairs={{4,0},{8,4},{12,8},{5,1},{9,5},{13,9},{6,2},{10,6},{14,10},{7,3},{... | collective-permute-start | bytes 983048 | tf_op jit(solution)/shard_map/ppermute | solution.py:49
  57.6 2.0 %collective-permute-done.7 = bf16[2,128,640]{2,1,0:T(8,128)(2,1)S(1)} collective-permute-done((bf16[2,128,640]{2,1,0:T(8,128)(2,1)S(1)}, bf16[2,128,640]{2,1,0:T(8,128)(2,1)S(1)}, u32[]{:S(2)}, u32[]{:S(2)}) %collective-permute-start.7) | collective-permute-done | bytes 327712 | tf_op jit(solution)/shard_map/ppermute | solution.py:48
  59.6 4.4 %collective-permute-done.8 = bf16[2,128,640]{2,1,0:T(8,128)(2,1)S(1)} collective-permute-done((bf16[2,128,640]{2,1,0:T(8,128)(2,1)S(1)}, bf16[2,128,640]{2,1,0:T(8,128)(2,1)S(1)}, u32[]{:S(2)}, u32[]{:S(2)}) %collective-permute-start.8) | collective-permute-done | bytes 327712 | tf_op jit(solution)/shard_map/ppermute | solution.py:49
  64.3 0.7 %fusion.10 = f32[512,640]{1,0:T(8,128)S(1)} fusion(bf16[512,640]{1,0:T(8,128)(2,1)S(1)} %bitcast.51, bf16[3,640,640]{2,1,0:T(8,128)(2,1)S(1)} %copy-done.3), kind=kOutput, calls=%fused_computation.17 | convolution fusion | flops 419430400 | bytes 2785280 | tf_op jit(solution)/shard_map/dot_general | solution.py:57
  65.0 0.7 %fusion.12 = f32[512,640]{1,0:T(8,128)S(1)} fusion(bf16[512,640]{1,0:T(8,128)(2,1)S(1)} %bitcast.50, bf16[3,640,640]{2,1,0:T(8,128)(2,1)S(1)} %copy-done.3), kind=kOutput, calls=%fused_computation.19 | convolution fusion | flops 419430400 | bytes 2785280 | tf_op jit(solution)/shard_map/dot_general | solution.py:57
  65.8 0.8 %multiply_convert_fusion = bf16[512,640]{1,0:T(8,128)(2,1)S(1)} fusion(f32[512,640]{1,0:T(8,128)S(1)} %fusion.10, f32[512,640]{1,0:T(8,128)S(1)} %fusion.12, bf16[512,640]{1,0:T(8,128)(2,1)S(1)} %bitcast.60, bf16[3,640,640]{2,1,0:T(8,128)(2,1)S(1)} %copy-done.3), kind=kOutput, calls=%fused_computation.6 | convolution fusion | flops 421724160 | bytes 4751360 | tf_op jit(solution)/shard_map/dot_general | solution.py:57
  66.8 1.5 %copy-done.2 = bf16[3,640,640]{2,1,0:T(8,128)(2,1)S(1)} copy-done((bf16[3,640,640]{2,1,0:T(8,128)(2,1)S(1)}, bf16[3,640,640]{2,1,0:T(8,128)(2,1)}, u32[]{:S(2)}) %copy-start.2) | copy-done | bytes 2457624
  68.3 0.5 fusion.8
  68.8 0.5 convolution_add_fusion.2
  69.3 1.2 %fusion.5 = bf16[256,640]{1,0:T(8,128)(2,1)} fusion(f32[256,640]{1,0:T(8,128)S(1)} %get-tuple-element.25, f32[256,640]{1,0:T(8,128)S(1)} %convolution_add_fusion.2, bf16[256,640]{1,0:T(8,128)(2,1)S(1)} %bitcast.54, bf16[3,640,640]{2,1,0:T(8,128)(2,1)S(1)} %copy-done.2), kind=kOutput, calls=%fused_computation.11 | convolution fusion | flops 210206720 | bytes 2785280 | tf_op jit(solution)/shard_map/dot_general | solution.py:57
  (25 shorter events, 1.1 us)
Async XLA Ops:
  0.0 35.4 %copy-start = (bf16[640,1280]{1,0:T(8,128)(2,1)S(1)}, bf16[640,1280]{1,0:T(8,128)(2,1)}, u32[]{:S(2)}) copy-start(bf16[640,1280]{1,0:T(8,128)(2,1)} %param.11) | copy-start | bytes 4915204
  0.0 14.2 %copy-start.1 = (bf16[2,128,640]{2,1,0:T(8,128)(2,1)S(1)}, bf16[2,128,640]{2,1,0:T(8,128)(2,1)}, u32[]{:S(2)}) copy-start(bf16[2,128,640]{2,1,0:T(8,128)(2,1)} %param.8) | copy-start | bytes 983044
  4.9 6.5 %collective-permute-start = (bf16[2,64,640]{2,1,0:T(8,128)(2,1)S(1)}, bf16[2,64,640]{2,1,0:T(8,128)(2,1)}, u32[]{:S(2)}, u32[]{:S(2)}) collective-permute-start(bf16[2,64,640]{2,1,0:T(8,128)(2,1)S(1)} %pad_maximum_fusion.7), channel_id=1, source_target_pairs={{0,12},{4,0},{8,4},{12,8},{1,13},{5,1},{9,5},{13,9},{2,14},{6,2},{... | collective-permute-start | bytes 491528 | tf_op jit(solution)/shard_map/ppermute | solution.py:82
  5.6 28.1 %copy-start.4 = (bf16[640,640]{1,0:T(8,128)(2,1)S(1)}, bf16[640,640]{1,0:T(8,128)(2,1)}, u32[]{:S(2)}) copy-start(bf16[640,640]{1,0:T(8,128)(2,1)} %param.10) | copy-start | bytes 2457604
  5.6 6.4 %collective-permute-start.1 = (bf16[2,64,640]{2,1,0:T(8,128)(2,1)S(1)}, bf16[2,64,640]{2,1,0:T(8,128)(2,1)}, u32[]{:S(2)}, u32[]{:S(2)}) collective-permute-start(bf16[2,64,640]{2,1,0:T(8,128)(2,1)S(1)} %pad_maximum_fusion.8), channel_id=1, source_target_pairs={{0,8},{4,12},{8,0},{12,4},{1,9},{5,13},{9,1},{13,5},{2,10},{6,14},... | collective-permute-start | bytes 491528 | tf_op jit(solution)/shard_map/ppermute | solution.py:82
  6.9 7.3 %collective-permute-start.2 = (bf16[2,64,640]{2,1,0:T(8,128)(2,1)S(1)}, bf16[2,64,640]{2,1,0:T(8,128)(2,1)}, u32[]{:S(2)}, u32[]{:S(2)}) collective-permute-start(bf16[2,64,640]{2,1,0:T(8,128)(2,1)S(1)} %pad_maximum_fusion.9), channel_id=1, source_target_pairs={{0,4},{4,8},{8,12},{12,0},{1,5},{5,9},{9,13},{13,1},{2,6},{6,10},{... | collective-permute-start | bytes 491528 | tf_op jit(solution)/shard_map/ppermute | solution.py:82
  15.5 4.2 %collective-permute-start.3 = (bf16[2,64,640]{2,1,0:T(8,128)(2,1)S(1)}, bf16[2,64,640]{2,1,0:T(8,128)(2,1)S(1)}, u32[]{:S(2)}, u32[]{:S(2)}) collective-permute-start(bf16[2,64,640]{2,1,0:T(8,128)(2,1)S(1)} %get-tuple-element.18), channel_id=1, source_target_pairs={{0,1},{1,2},{2,3},{3,0},{4,5},{5,6},{6,7},{7,4},{8,9},{9,10},{10,1... | collective-permute-start | bytes 491528 | tf_op jit(solution)/shard_map/ppermute | solution.py:89
  16.8 12.5 %collective-permute-start.4 = (bf16[2,64,640]{2,1,0:T(8,128)(2,1)S(1)}, bf16[2,64,640]{2,1,0:T(8,128)(2,1)S(1)}, u32[]{:S(2)}, u32[]{:S(2)}) collective-permute-start(bf16[2,64,640]{2,1,0:T(8,128)(2,1)S(1)} %get-tuple-element.18), channel_id=1, source_target_pairs={{0,2},{1,3},{2,0},{3,1},{4,6},{5,7},{6,4},{7,5},{8,10},{9,11},{10,... | collective-permute-start | bytes 491528 | tf_op jit(solution)/shard_map/ppermute | solution.py:89
  17.9 15.1 %collective-permute-start.5 = (bf16[2,64,640]{2,1,0:T(8,128)(2,1)S(1)}, bf16[2,64,640]{2,1,0:T(8,128)(2,1)S(1)}, u32[]{:S(2)}, u32[]{:S(2)}) collective-permute-start(bf16[2,64,640]{2,1,0:T(8,128)(2,1)S(1)} %get-tuple-element.18), channel_id=1, source_target_pairs={{0,3},{1,0},{2,1},{3,2},{4,7},{5,4},{6,5},{7,6},{8,11},{9,8},{10,9... | collective-permute-start | bytes 491528 | tf_op jit(solution)/shard_map/ppermute | solution.py:89
  33.1 2.3 %collective-permute-start.6 = (bf16[512,640]{1,0:T(8,128)(2,1)S(1)}, bf16[512,640]{1,0:T(8,128)(2,1)S(1)}, u32[]{:S(2)}, u32[]{:S(2)}) collective-permute-start(bf16[512,640]{1,0:T(8,128)(2,1)S(1)} %bitcast.58), channel_id=1, source_target_pairs={{0,4},{4,0},{8,12},{12,8},{1,5},{5,1},{9,13},{13,9},{2,6},{6,2},{1... | collective-permute-start | bytes 1966088 | tf_op jit(solution)/shard_map/ppermute | solution.py:91
  39.1 12.3 %copy-start.5 = (bf16[640,640]{1,0:T(8,128)(2,1)S(1)}, bf16[640,640]{1,0:T(8,128)(2,1)}, u32[]{:S(2)}) copy-start(bf16[640,640]{1,0:T(8,128)(2,1)} %param.12) | copy-start | bytes 2457604
  51.5 1.6 %copy-start.6 = (f32[640]{0:T(1024)S(1)}, f32[640]{0:T(1024)}, u32[]{:S(2)}) copy-start(f32[640]{0:T(1024)} %param.13) | copy-start | bytes 7684
  53.2 6.5 %collective-permute-start.7 = (bf16[2,128,640]{2,1,0:T(8,128)(2,1)S(1)}, bf16[2,128,640]{2,1,0:T(8,128)(2,1)S(1)}, u32[]{:S(2)}, u32[]{:S(2)}) collective-permute-start(bf16[2,128,640]{2,1,0:T(8,128)(2,1)S(1)} %bitcast.55), channel_id=1, source_target_pairs={{0,4},{4,8},{8,12},{1,5},{5,9},{9,13},{2,6},{6,10},{10,14},{3,7},{... | collective-permute-start | bytes 983048 | tf_op jit(solution)/shard_map/ppermute | solution.py:48
  55.6 8.4 %collective-permute-start.8 = (bf16[2,128,640]{2,1,0:T(8,128)(2,1)S(1)}, bf16[2,128,640]{2,1,0:T(8,128)(2,1)S(1)}, u32[]{:S(2)}, u32[]{:S(2)}) collective-permute-start(bf16[2,128,640]{2,1,0:T(8,128)(2,1)S(1)} %bitcast.56), channel_id=1, source_target_pairs={{4,0},{8,4},{12,8},{5,1},{9,5},{13,9},{6,2},{10,6},{14,10},{7,3},{... | collective-permute-start | bytes 983048 | tf_op jit(solution)/shard_map/ppermute | solution.py:49
  57.6 6.7 %copy-start.3 = (bf16[3,640,640]{2,1,0:T(8,128)(2,1)S(1)}, bf16[3,640,640]{2,1,0:T(8,128)(2,1)}, u32[]{:S(2)}) copy-start(bf16[3,640,640]{2,1,0:T(8,128)(2,1)} %param.14) | copy-start | bytes 7372804
  66.6 1.7 %copy-start.2 = (bf16[3,640,640]{2,1,0:T(8,128)(2,1)S(1)}, bf16[3,640,640]{2,1,0:T(8,128)(2,1)}, u32[]{:S(2)}) copy-start(bf16[3,640,640]{2,1,0:T(8,128)(2,1)} %param.15) | copy-start | bytes 7372804

commit v4 on v3

--- a/solution.py
+++ b/solution.py
@@ -8,13 +8,12 @@
 HEAD_DIM = 64
 
 
-def attention_kernel(q_ref, k_ref, v_ref, o_ref):
+def attention_kernel(q_ref, kt_ref, v_ref, o_ref):
     outs = []
     for hh in range(2):
         cols = slice(hh * HEAD_DIM, (hh + 1) * HEAD_DIM)
-        scores = lax.dot_general(
-            q_ref[:, cols], k_ref[:, cols], (((1,), (1,)), ((), ())),
-            preferred_element_type=jnp.float32) * HEAD_DIM ** (-0.5)
+        scores = jnp.dot(q_ref[:, cols], kt_ref[cols, :], preferred_element_type=jnp.float32)
+        scores = scores * HEAD_DIM ** (-0.5)
         highest = jnp.max(scores, axis=1, keepdims=True)
         exponent = jnp.exp(scores - highest)
         denominator = jnp.sum(exponent, axis=1, keepdims=True)
@@ -22,9 +21,10 @@
         outs.append(mixed / denominator)
     o_ref[...] = jnp.concatenate(outs, axis=1).astype(o_ref.dtype)
 
-def attend(queries, keyval, q_tile=128):
+
+def attend(queries, keys_t, values, q_tile=256):
     total, channels = queries.shape
-    keys = keyval.shape[0]
+    count = values.shape[0]
     pairs = channels // (2 * HEAD_DIM)
     width = 2 * HEAD_DIM
     return pl.pallas_call(
@@ -32,12 +32,12 @@
         grid=(pairs, total // q_tile),
         in_specs=[
             pl.BlockSpec((q_tile, width), lambda j, i: (i, j)),
-            pl.BlockSpec((keys, width), lambda j, i: (0, j)),
-            pl.BlockSpec((keys, width), lambda j, i: (0, pairs + j)),
+            pl.BlockSpec((width, count), lambda j, i: (j, 0)),
+            pl.BlockSpec((count, width), lambda j, i: (0, j)),
         ],
         out_specs=pl.BlockSpec((q_tile, width), lambda j, i: (i, j)),
         out_shape=jax.ShapeDtypeStruct((total, channels), jnp.bfloat16),
-    )(queries, keyval, keyval)
+    )(queries, keys_t, values)
 
 def extended(array, axis, width):
     size, length = (lax.axis_size(axis), array.shape[0])
@@ -99,8 +99,11 @@
     queries = jnp.dot(flattened, w_query, preferred_element_type=jnp.float32).astype(jnp.bfloat16)
     query_total = queries.shape[0]
     key_tokens = gather_keyframes(frames, key_index)
-    keyval = jnp.dot(key_tokens, w_keyval, preferred_element_type=jnp.float32).astype(jnp.bfloat16)
-    attended = attend(queries, keyval)
+    keys_t = lax.dot_general(
+        w_keyval[:, :channels], key_tokens, (((0,), (1,)), ((), ())), preferred_element_type=jnp.float32
+    ).astype(jnp.bfloat16)
+    values = jnp.dot(key_tokens, w_keyval[:, channels:], preferred_element_type=jnp.float32).astype(jnp.bfloat16)
+    attended = attend(queries, keys_t, values)
     residual = flattened.astype(jnp.float32) + jnp.dot(
         attended, w_out, preferred_element_type=jnp.float32
     )

time: 70.9 us -> 66.4 us (0.937)
  Pallas kernels: 12.3 us -> 8.02 us
  other arithmetic: 1.87 us -> 0.82 us
  matrix products: 10.9 us -> 11.9 us
    pallas_call x1, Pallas kernels: 12.3 us -> 8.02 us  [attend(): pl.pallas_call(attention_kernel, grid=(pairs, total // q_tile), in_specs=...]
    select_n x1, other arithmetic: 1.19 us -> 0.14 us  [gather_keyframes(): got_a = jnp.where(source == owner_a, recv[0], got_a)]
    dot_general x1 -> x2, matrix products: 3.72 us -> 4.7 us  [the longest x1 2.38 us: shards(): jnp.dot(key_tokens, w_keyval[:, channels:], preferred_element_type=jnp.fl...]
where the time goes in v4:
time: 66.4 us; the launch traced here: 66 us
  waiting for transfers between devices  26.6 us (40%)
  starting transfers between devices  12.2 us (18%)
  matrix products  11.9 us (18%)
  Pallas kernels  8.02 us (12%)
  local copies, waits for them, and re-layouts  4.99 us (8%)
  between operations  1.54 us (2%)
  other arithmetic  0.82 us (1%)
    ppermute x3, waiting for transfers between devices, gather_keyframes(): lax.ppermute(piece, 'row', [(i, (i + s) % rsize) for i in range(rsize)])  13.7 us
    pallas_call x1, Pallas kernels, attend(): pl.pallas_call(attention_kernel, grid=(pairs, total // q_tile), in_specs=...  8.02 us
    ppermute x3, waiting for transfers between devices, gather_keyframes(): lax.ppermute(sent, 'frame', [(i, (i + s) % fsize) for i in range(fsize)])  5.91 us
    dot_general x6, matrix products, temporal_mix(): jnp.dot(window, weights[offset], preferred_element_type=jnp.float32)  4.44 us
    ppermute x1, waiting for transfers between devices, extended(): after = lax.ppermute(first, axis, down)  4.4 us
    ppermute x3, starting transfers between devices, gather_keyframes(): lax.ppermute(piece, 'row', [(i, (i + s) % rsize) for i in range(rsize)])  3.83 us
    ppermute x3, starting transfers between devices, gather_keyframes(): lax.ppermute(sent, 'frame', [(i, (i + s) % fsize) for i in range(fsize)])  3.4 us
    ppermute x1, starting transfers between devices, extended(): before = lax.ppermute(last, axis, up)  2.49 us
  transfers between devices with their start and end apart: 9, of which 9 were waited for; matrix products, arithmetic and copies ran while one was open for 2% of the time, Pallas kernels for 0%

profile of v4, /device:TPU:9, one launch (start us, length us, event | category | flops | bytes accessed | tf_op | source)
XLA Modules:
  0.0 66.0 jit_solution(15058919235558443996)
XLA Ops:
  0.0 1.3 %fusion.31 = (s32[1]{0:T(128)}, s32[1]{0:T(128)}) fusion(s32[2]{0:T(128)} %param.9), kind=kLoop, calls=%fused_computation.64 | loop fusion | bytes 16 | tf_op jit(solution)/shard_map/slice | solution.py:67
  2.7 0.9 %slice.82 = bf16[1,128,640]{2,1,0:T(8,128)(2,1)S(1)} slice(bf16[2,128,640]{2,1,0:T(8,128)(2,1)} %param.8), slice={[1:2], [0:128], [0:640]} | slice | bytes 327680 | tf_op jit(solution)/shard_map/slice | solution.py:70
  3.6 1.1 %constant_dynamic-slice_fusion.4 = (bf16[1,64,640]{2,1,0:T(8,128)(2,1)S(1)}, bf16[1,64,640]{2,1,0:T(8,128)(2,1)S(1)}, bf16[1,64,640]{2,1,0:T(8,128)(2,1)S(1)}, b...) fusion(bf16[1,128,640]{2,1,0:T(8,128)(2,1)S(1)} %slice.82, ...), kind=kLoop, calls=%fused_computation.57 | loop fusion | bytes 983068 | tf_op jit(solution)/shard_map/dynamic_slice | solution.py:75
  4.8 0.7 %collective-permute-start = (bf16[2,64,640]{2,1,0:T(8,128)(2,1)S(1)}, bf16[2,64,640]{2,1,0:T(8,128)(2,1)S(1)}, u32[]{:S(2)}, u32[]{:S(2)}) collective-permute-start(bf16[2,64,640]{2,1,0:T(8,128)(2,1)S(1)} %pad_maximum_fusion.10), channel_id=1, source_target_pairs={{0,12},{4,0},{8,4},{12,8},{1,13},{5,1},{9,5},{13,9},{2,14},{6,2},{... | collective-permute-start | bytes 491528 | tf_op jit(solution)/shard_map/ppermute | solution.py:82
  5.6 1.3 %collective-permute-start.1 = (bf16[2,64,640]{2,1,0:T(8,128)(2,1)S(1)}, bf16[2,64,640]{2,1,0:T(8,128)(2,1)S(1)}, u32[]{:S(2)}, u32[]{:S(2)}) collective-permute-start(bf16[2,64,640]{2,1,0:T(8,128)(2,1)S(1)} %pad_maximum_fusion.11), channel_id=1, source_target_pairs={{0,8},{4,12},{8,0},{12,4},{1,9},{5,13},{9,1},{13,5},{2,10},{6,14},... | collective-permute-start | bytes 491528 | tf_op jit(solution)/shard_map/ppermute | solution.py:82
  6.9 1.4 %collective-permute-start.2 = (bf16[2,64,640]{2,1,0:T(8,128)(2,1)S(1)}, bf16[2,64,640]{2,1,0:T(8,128)(2,1)S(1)}, u32[]{:S(2)}, u32[]{:S(2)}) collective-permute-start(bf16[2,64,640]{2,1,0:T(8,128)(2,1)S(1)} %pad_maximum_fusion.12), channel_id=1, source_target_pairs={{0,4},{4,8},{8,12},{12,0},{1,5},{5,9},{9,13},{13,1},{2,6},{6,10},{... | collective-permute-start | bytes 491528 | tf_op jit(solution)/shard_map/ppermute | solution.py:82
  8.3 3.0 %collective-permute-done = bf16[2,64,640]{2,1,0:T(8,128)(2,1)S(1)} collective-permute-done((bf16[2,64,640]{2,1,0:T(8,128)(2,1)S(1)}, bf16[2,64,640]{2,1,0:T(8,128)(2,1)S(1)}, u32[]{:S(2)}, u32[]{:S(2)}) %collective-permute-start) | collective-permute-done | bytes 163872 | tf_op jit(solution)/shard_map/ppermute | solution.py:82
  11.2 0.6 collective-permute-done.1
  11.8 2.3 %collective-permute-done.2 = bf16[2,64,640]{2,1,0:T(8,128)(2,1)S(1)} collective-permute-done((bf16[2,64,640]{2,1,0:T(8,128)(2,1)S(1)}, bf16[2,64,640]{2,1,0:T(8,128)(2,1)S(1)}, u32[]{:S(2)}, u32[]{:S(2)}) %collective-permute-start.2) | collective-permute-done | bytes 163872 | tf_op jit(solution)/shard_map/ppermute | solution.py:82
  14.4 1.4 %collective-permute-start.3 = (bf16[2,64,640]{2,1,0:T(8,128)(2,1)S(1)}, bf16[2,64,640]{2,1,0:T(8,128)(2,1)S(1)}, u32[]{:S(2)}, u32[]{:S(2)}) collective-permute-start(bf16[2,64,640]{2,1,0:T(8,128)(2,1)S(1)} %get-tuple-element.18), channel_id=1, source_target_pairs={{0,1},{1,2},{2,3},{3,0},{4,5},{5,6},{6,7},{7,4},{8,9},{9,10},{10,1... | collective-permute-start | bytes 491528 | tf_op jit(solution)/shard_map/ppermute | solution.py:89
  15.7 1.1 %collective-permute-start.4 = (bf16[2,64,640]{2,1,0:T(8,128)(2,1)S(1)}, bf16[2,64,640]{2,1,0:T(8,128)(2,1)S(1)}, u32[]{:S(2)}, u32[]{:S(2)}) collective-permute-start(bf16[2,64,640]{2,1,0:T(8,128)(2,1)S(1)} %get-tuple-element.18), channel_id=1, source_target_pairs={{0,2},{1,3},{2,0},{3,1},{4,6},{5,7},{6,4},{7,5},{8,10},{9,11},{10,... | collective-permute-start | bytes 491528 | tf_op jit(solution)/shard_map/ppermute | solution.py:89
  16.8 1.4 %collective-permute-start.5 = (bf16[2,64,640]{2,1,0:T(8,128)(2,1)S(1)}, bf16[2,64,640]{2,1,0:T(8,128)(2,1)S(1)}, u32[]{:S(2)}, u32[]{:S(2)}) collective-permute-start(bf16[2,64,640]{2,1,0:T(8,128)(2,1)S(1)} %get-tuple-element.18), channel_id=1, source_target_pairs={{0,3},{1,0},{2,1},{3,2},{4,7},{5,4},{6,5},{7,6},{8,11},{9,8},{10,9... | collective-permute-start | bytes 491528 | tf_op jit(solution)/shard_map/ppermute | solution.py:89
  18.6 9.7 %collective-permute-done.4 = bf16[2,64,640]{2,1,0:T(8,128)(2,1)S(1)} collective-permute-done((bf16[2,64,640]{2,1,0:T(8,128)(2,1)S(1)}, bf16[2,64,640]{2,1,0:T(8,128)(2,1)S(1)}, u32[]{:S(2)}, u32[]{:S(2)}) %collective-permute-start.4) | collective-permute-done | bytes 163872 | tf_op jit(solution)/shard_map/ppermute | solution.py:89
  28.3 3.6 %collective-permute-done.5 = bf16[2,64,640]{2,1,0:T(8,128)(2,1)S(1)} collective-permute-done((bf16[2,64,640]{2,1,0:T(8,128)(2,1)S(1)}, bf16[2,64,640]{2,1,0:T(8,128)(2,1)S(1)}, u32[]{:S(2)}, u32[]{:S(2)}) %collective-permute-start.5) | collective-permute-done | bytes 163872 | tf_op jit(solution)/shard_map/ppermute | solution.py:89
  32.0 0.6 collective-permute-start.6
  32.6 1.2 %convolution_convert_fusion.2.q_ref = bf16[256,640]{1,0:T(8,128)(2,1)} fusion(bf16[256,640]{1,0:T(8,128)(2,1)S(1)} %bitcast.49, bf16[640,640]{1,0:T(8,128)(2,1)S(1)} %copy-done.4), kind=kOutput, calls=%fused_computation.12 | convolution fusion | flops 209879040 | bytes 1474560 | tf_op jit(solution)/shard_map/dot_general | solution.py:99
  33.8 0.5 collective-permute-done.6
  34.3 2.4 %convolution_convert_fusion.v_ref = bf16[1024,640]{1,0:T(8,128)(2,1)} fusion(bf16[512,640]{1,0:T(8,128)(2,1)S(1)} %collective-permute-done.6, bf16[512,640]{1,0:T(8,128)(2,1)S(1)} %bitcast.60, bf16[640,1280]{1,0:T(8,128)(2,1)S(1)} %copy-done.6), kind=kOutput, calls=%fused_computation | convolution fusion | flops 842137600 | bytes 3440640 | tf_op jit(solution)/shard_map/dot_general | solution.py:105
  36.7 2.3 %fusion.kt_ref = bf16[640,1024]{1,0:T(8,128)(2,1)} fusion(bf16[512,640]{1,0:T(8,128)(2,1)S(1)} %collective-permute-done.6, bf16[512,640]{1,0:T(8,128)(2,1)S(1)} %bitcast.61, bf16[640,1280]{1,0:T(8,128)(2,1)S(1)} %copy-done.6), kind=kOutput, calls=%fused_computation.2 | convolution fusion | flops 842137600 | bytes 3440640 | tf_op jit(solution)/shard_map/dot_general | solution.py:102
  39.0 8.0 %shard_map.82 = bf16[256,640]{1,0:T(8,128)(2,1)} custom-call(bf16[256,640]{1,0:T(8,128)(2,1)} %convolution_convert_fusion.2.q_ref, bf16[640,1024]{1,0:T(8,128)(2,1)} %fusion.kt_ref, bf16[1024,640]{1,0:T(8,128)(2,1)} %convolution_convert_fusion.v_ref), custom_call_target="tpu_custom_call" | custom-call | tf_op jit(solution)/shard_map/pallas_call | solution.py:30
  47.0 1.5 %multiply_reduce_fusion = (f32[256]{0:T(256)S(1)}, f32[256,640]{1,0:T(8,128)S(1)}) fusion(bf16[256,640]{1,0:T(8,128)(2,1)} %shard_map.82, bf16[640,640]{1,0:T(8,128)(2,1)S(1)} %copy-done, bf16[256,640]{1,0:T(8,128)(2,1)S(1)} %bitcast.50), kind=kOutput, calls=%fused_computation.36 | convolution fusion | flops 210370304 | bytes 2130944 | tf_op jit(solution)/shard_map/dot_general | solution.py:107
  48.7 2.5 %collective-permute-start.7 = (bf16[2,128,640]{2,1,0:T(8,128)(2,1)S(1)}, bf16[2,128,640]{2,1,0:T(8,128)(2,1)S(1)}, u32[]{:S(2)}, u32[]{:S(2)}) collective-permute-start(bf16[2,128,640]{2,1,0:T(8,128)(2,1)S(1)} %bitcast.56), channel_id=1, source_target_pairs={{0,4},{4,8},{8,12},{1,5},{5,9},{9,13},{2,6},{6,10},{10,14},{3,7},{... | collective-permute-start | bytes 983048 | tf_op jit(solution)/shard_map/ppermute | solution.py:48
  51.2 1.9 %collective-permute-start.8 = (bf16[2,128,640]{2,1,0:T(8,128)(2,1)S(1)}, bf16[2,128,640]{2,1,0:T(8,128)(2,1)S(1)}, u32[]{:S(2)}, u32[]{:S(2)}) collective-permute-start(bf16[2,128,640]{2,1,0:T(8,128)(2,1)S(1)} %bitcast.57), channel_id=1, source_target_pairs={{4,0},{8,4},{12,8},{5,1},{9,5},{13,9},{6,2},{10,6},{14,10},{7,3},{... | collective-permute-start | bytes 983048 | tf_op jit(solution)/shard_map/ppermute | solution.py:49
  53.2 2.0 %collective-permute-done.7 = bf16[2,128,640]{2,1,0:T(8,128)(2,1)S(1)} collective-permute-done((bf16[2,128,640]{2,1,0:T(8,128)(2,1)S(1)}, bf16[2,128,640]{2,1,0:T(8,128)(2,1)S(1)}, u32[]{:S(2)}, u32[]{:S(2)}) %collective-permute-start.7) | collective-permute-done | bytes 327712 | tf_op jit(solution)/shard_map/ppermute | solution.py:48
  55.2 4.4 %collective-permute-done.8 = bf16[2,128,640]{2,1,0:T(8,128)(2,1)S(1)} collective-permute-done((bf16[2,128,640]{2,1,0:T(8,128)(2,1)S(1)}, bf16[2,128,640]{2,1,0:T(8,128)(2,1)S(1)}, u32[]{:S(2)}, u32[]{:S(2)}) %collective-permute-start.8) | collective-permute-done | bytes 327712 | tf_op jit(solution)/shard_map/ppermute | solution.py:49
  59.9 0.7 %fusion.10 = f32[512,640]{1,0:T(8,128)S(1)} fusion(bf16[512,640]{1,0:T(8,128)(2,1)S(1)} %bitcast.52, bf16[3,640,640]{2,1,0:T(8,128)(2,1)S(1)} %copy-done.3), kind=kOutput, calls=%fused_computation.19 | convolution fusion | flops 419430400 | bytes 2785280 | tf_op jit(solution)/shard_map/dot_general | solution.py:57
  60.6 0.7 %fusion.8 = f32[512,640]{1,0:T(8,128)S(1)} fusion(bf16[512,640]{1,0:T(8,128)(2,1)S(1)} %bitcast.51, bf16[3,640,640]{2,1,0:T(8,128)(2,1)S(1)} %copy-done.3), kind=kOutput, calls=%fused_computation.17 | convolution fusion | flops 419430400 | bytes 2785280 | tf_op jit(solution)/shard_map/dot_general | solution.py:57
  61.4 0.8 %multiply_convert_fusion = bf16[512,640]{1,0:T(8,128)(2,1)S(1)} fusion(f32[512,640]{1,0:T(8,128)S(1)} %fusion.8, f32[512,640]{1,0:T(8,128)S(1)} %fusion.10, bf16[512,640]{1,0:T(8,128)(2,1)S(1)} %bitcast.62, bf16[3,640,640]{2,1,0:T(8,128)(2,1)S(1)} %copy-done.3), kind=kOutput, calls=%fused_computation.6 | convolution fusion | flops 421724160 | bytes 4751360 | tf_op jit(solution)/shard_map/dot_general | solution.py:57
  62.4 1.5 %copy-done.2 = bf16[3,640,640]{2,1,0:T(8,128)(2,1)S(1)} copy-done((bf16[3,640,640]{2,1,0:T(8,128)(2,1)S(1)}, bf16[3,640,640]{2,1,0:T(8,128)(2,1)}, u32[]{:S(2)}) %copy-start.2) | copy-done | bytes 2457624
  63.9 0.5 fusion.6
  64.4 0.5 convolution_add_fusion.2
  64.9 1.2 %fusion.3 = bf16[256,640]{1,0:T(8,128)(2,1)} fusion(f32[256,640]{1,0:T(8,128)S(1)} %get-tuple-element.25, f32[256,640]{1,0:T(8,128)S(1)} %convolution_add_fusion.2, bf16[256,640]{1,0:T(8,128)(2,1)S(1)} %bitcast.55, bf16[3,640,640]{2,1,0:T(8,128)(2,1)S(1)} %copy-done.2), kind=kOutput, calls=%fused_computation.11 | convolution fusion | flops 210206720 | bytes 2785280 | tf_op jit(solution)/shard_map/dot_general | solution.py:57
  (26 shorter events, 1.3 us)
Async XLA Ops:
  0.0 47.0 %copy-start = (bf16[640,640]{1,0:T(8,128)(2,1)S(1)}, bf16[640,640]{1,0:T(8,128)(2,1)}, u32[]{:S(2)}) copy-start(bf16[640,640]{1,0:T(8,128)(2,1)} %param.12) | copy-start | bytes 2457604
  0.0 14.2 %copy-start.1 = (bf16[2,128,640]{2,1,0:T(8,128)(2,1)S(1)}, bf16[2,128,640]{2,1,0:T(8,128)(2,1)}, u32[]{:S(2)}) copy-start(bf16[2,128,640]{2,1,0:T(8,128)(2,1)} %param.8) | copy-start | bytes 983044
  4.8 6.4 %collective-permute-start = (bf16[2,64,640]{2,1,0:T(8,128)(2,1)S(1)}, bf16[2,64,640]{2,1,0:T(8,128)(2,1)S(1)}, u32[]{:S(2)}, u32[]{:S(2)}) collective-permute-start(bf16[2,64,640]{2,1,0:T(8,128)(2,1)S(1)} %pad_maximum_fusion.10), channel_id=1, source_target_pairs={{0,12},{4,0},{8,4},{12,8},{1,13},{5,1},{9,5},{13,9},{2,14},{6,2},{... | collective-permute-start | bytes 491528 | tf_op jit(solution)/shard_map/ppermute | solution.py:82
  5.5 27.1 %copy-start.4 = (bf16[640,640]{1,0:T(8,128)(2,1)S(1)}, bf16[640,640]{1,0:T(8,128)(2,1)}, u32[]{:S(2)}) copy-start(bf16[640,640]{1,0:T(8,128)(2,1)} %param.10) | copy-start | bytes 2457604
  5.6 6.3 %collective-permute-start.1 = (bf16[2,64,640]{2,1,0:T(8,128)(2,1)S(1)}, bf16[2,64,640]{2,1,0:T(8,128)(2,1)S(1)}, u32[]{:S(2)}, u32[]{:S(2)}) collective-permute-start(bf16[2,64,640]{2,1,0:T(8,128)(2,1)S(1)} %pad_maximum_fusion.11), channel_id=1, source_target_pairs={{0,8},{4,12},{8,0},{12,4},{1,9},{5,13},{9,1},{13,5},{2,10},{6,14},... | collective-permute-start | bytes 491528 | tf_op jit(solution)/shard_map/ppermute | solution.py:82
  6.9 7.3 %collective-permute-start.2 = (bf16[2,64,640]{2,1,0:T(8,128)(2,1)S(1)}, bf16[2,64,640]{2,1,0:T(8,128)(2,1)S(1)}, u32[]{:S(2)}, u32[]{:S(2)}) collective-permute-start(bf16[2,64,640]{2,1,0:T(8,128)(2,1)S(1)} %pad_maximum_fusion.12), channel_id=1, source_target_pairs={{0,4},{4,8},{8,12},{12,0},{1,5},{5,9},{9,13},{13,1},{2,6},{6,10},{... | collective-permute-start | bytes 491528 | tf_op jit(solution)/shard_map/ppermute | solution.py:82
  14.3 20.0 %copy-start.6 = (bf16[640,1280]{1,0:T(8,128)(2,1)S(1)}, bf16[640,1280]{1,0:T(8,128)(2,1)}, u32[]{:S(2)}) copy-start(bf16[640,1280]{1,0:T(8,128)(2,1)} %param.11) | copy-start | bytes 4915204
  14.4 4.2 %collective-permute-start.3 = (bf16[2,64,640]{2,1,0:T(8,128)(2,1)S(1)}, bf16[2,64,640]{2,1,0:T(8,128)(2,1)S(1)}, u32[]{:S(2)}, u32[]{:S(2)}) collective-permute-start(bf16[2,64,640]{2,1,0:T(8,128)(2,1)S(1)} %get-tuple-element.18), channel_id=1, source_target_pairs={{0,1},{1,2},{2,3},{3,0},{4,5},{5,6},{6,7},{7,4},{8,9},{9,10},{10,1... | collective-permute-start | bytes 491528 | tf_op jit(solution)/shard_map/ppermute | solution.py:89
  15.7 12.6 %collective-permute-start.4 = (bf16[2,64,640]{2,1,0:T(8,128)(2,1)S(1)}, bf16[2,64,640]{2,1,0:T(8,128)(2,1)S(1)}, u32[]{:S(2)}, u32[]{:S(2)}) collective-permute-start(bf16[2,64,640]{2,1,0:T(8,128)(2,1)S(1)} %get-tuple-element.18), channel_id=1, source_target_pairs={{0,2},{1,3},{2,0},{3,1},{4,6},{5,7},{6,4},{7,5},{8,10},{9,11},{10,... | collective-permute-start | bytes 491528 | tf_op jit(solution)/shard_map/ppermute | solution.py:89
  16.8 15.1 %collective-permute-start.5 = (bf16[2,64,640]{2,1,0:T(8,128)(2,1)S(1)}, bf16[2,64,640]{2,1,0:T(8,128)(2,1)S(1)}, u32[]{:S(2)}, u32[]{:S(2)}) collective-permute-start(bf16[2,64,640]{2,1,0:T(8,128)(2,1)S(1)} %get-tuple-element.18), channel_id=1, source_target_pairs={{0,3},{1,0},{2,1},{3,2},{4,7},{5,4},{6,5},{7,6},{8,11},{9,8},{10,9... | collective-permute-start | bytes 491528 | tf_op jit(solution)/shard_map/ppermute | solution.py:89
  32.0 2.3 %collective-permute-start.6 = (bf16[512,640]{1,0:T(8,128)(2,1)S(1)}, bf16[512,640]{1,0:T(8,128)(2,1)S(1)}, u32[]{:S(2)}, u32[]{:S(2)}) collective-permute-start(bf16[512,640]{1,0:T(8,128)(2,1)S(1)} %bitcast.59), channel_id=1, source_target_pairs={{0,4},{4,0},{8,12},{12,8},{1,5},{5,1},{9,13},{13,9},{2,6},{6,2},{1... | collective-permute-start | bytes 1966088 | tf_op jit(solution)/shard_map/ppermute | solution.py:91
  47.0 1.6 %copy-start.5 = (f32[640]{0:T(1024)S(1)}, f32[640]{0:T(1024)}, u32[]{:S(2)}) copy-start(f32[640]{0:T(1024)} %param.13) | copy-start | bytes 7684
  48.7 6.5 %collective-permute-start.7 = (bf16[2,128,640]{2,1,0:T(8,128)(2,1)S(1)}, bf16[2,128,640]{2,1,0:T(8,128)(2,1)S(1)}, u32[]{:S(2)}, u32[]{:S(2)}) collective-permute-start(bf16[2,128,640]{2,1,0:T(8,128)(2,1)S(1)} %bitcast.56), channel_id=1, source_target_pairs={{0,4},{4,8},{8,12},{1,5},{5,9},{9,13},{2,6},{6,10},{10,14},{3,7},{... | collective-permute-start | bytes 983048 | tf_op jit(solution)/shard_map/ppermute | solution.py:48
  51.2 8.4 %collective-permute-start.8 = (bf16[2,128,640]{2,1,0:T(8,128)(2,1)S(1)}, bf16[2,128,640]{2,1,0:T(8,128)(2,1)S(1)}, u32[]{:S(2)}, u32[]{:S(2)}) collective-permute-start(bf16[2,128,640]{2,1,0:T(8,128)(2,1)S(1)} %bitcast.57), channel_id=1, source_target_pairs={{4,0},{8,4},{12,8},{5,1},{9,5},{13,9},{6,2},{10,6},{14,10},{7,3},{... | collective-permute-start | bytes 983048 | tf_op jit(solution)/shard_map/ppermute | solution.py:49
  53.2 6.7 %copy-start.3 = (bf16[3,640,640]{2,1,0:T(8,128)(2,1)S(1)}, bf16[3,640,640]{2,1,0:T(8,128)(2,1)}, u32[]{:S(2)}) copy-start(bf16[3,640,640]{2,1,0:T(8,128)(2,1)} %param.14) | copy-start | bytes 7372804
  62.2 1.7 %copy-start.2 = (bf16[3,640,640]{2,1,0:T(8,128)(2,1)S(1)}, bf16[3,640,640]{2,1,0:T(8,128)(2,1)}, u32[]{:S(2)}) copy-start(bf16[3,640,640]{2,1,0:T(8,128)(2,1)} %param.15) | copy-start | bytes 7372804

commit v5 on v4

--- a/solution.py
+++ b/solution.py
@@ -8,36 +8,32 @@
 HEAD_DIM = 64
 
 
-def attention_kernel(q_ref, kt_ref, v_ref, o_ref):
-    outs = []
+def attention_kernel(k_ref, qt_ref, vt_ref, o_ref):
     for hh in range(2):
         cols = slice(hh * HEAD_DIM, (hh + 1) * HEAD_DIM)
-        scores = jnp.dot(q_ref[:, cols], kt_ref[cols, :], preferred_element_type=jnp.float32)
-        scores = scores * HEAD_DIM ** (-0.5)
-        highest = jnp.max(scores, axis=1, keepdims=True)
+        scores = jnp.dot(k_ref[:, cols], qt_ref[cols, :], preferred_element_type=jnp.float32)
+        highest = jnp.max(scores, axis=0, keepdims=True)
         exponent = jnp.exp(scores - highest)
-        denominator = jnp.sum(exponent, axis=1, keepdims=True)
-        mixed = jnp.dot(exponent.astype(jnp.bfloat16), v_ref[:, cols], preferred_element_type=jnp.float32)
-        outs.append(mixed / denominator)
-    o_ref[...] = jnp.concatenate(outs, axis=1).astype(o_ref.dtype)
+        denominator = jnp.sum(exponent, axis=0, keepdims=True)
+        mixed = jnp.dot(vt_ref[cols, :], exponent.astype(jnp.bfloat16), preferred_element_type=jnp.float32)
+        o_ref[cols, :] = (mixed / denominator).astype(o_ref.dtype)
 
 
-def attend(queries, keys_t, values, q_tile=256):
-    total, channels = queries.shape
-    count = values.shape[0]
-    pairs = channels // (2 * HEAD_DIM)
+def attend(keys, queries_t, values_t):
+    channels, total = queries_t.shape
+    count = keys.shape[0]
     width = 2 * HEAD_DIM
     return pl.pallas_call(
         attention_kernel,
-        grid=(pairs, total // q_tile),
+        grid=(channels // width,),
         in_specs=[
-            pl.BlockSpec((q_tile, width), lambda j, i: (i, j)),
-            pl.BlockSpec((width, count), lambda j, i: (j, 0)),
-            pl.BlockSpec((count, width), lambda j, i: (0, j)),
+            pl.BlockSpec((count, width), lambda j: (0, j)),
+            pl.BlockSpec((width, total), lambda j: (j, 0)),
+            pl.BlockSpec((width, count), lambda j: (j, 0)),
         ],
-        out_specs=pl.BlockSpec((q_tile, width), lambda j, i: (i, j)),
-        out_shape=jax.ShapeDtypeStruct((total, channels), jnp.bfloat16),
-    )(queries, keys_t, values)
+        out_specs=pl.BlockSpec((width, total), lambda j: (j, 0)),
+        out_shape=jax.ShapeDtypeStruct((channels, total), jnp.bfloat16),
+    )(keys, queries_t, values_t)
 
 def extended(array, axis, width):
     size, length = (lax.axis_size(axis), array.shape[0])
@@ -96,16 +92,16 @@
     frame_count, row_count, channels = frames.shape
     assert frame_count >= 2
     flattened = frames.reshape(-1, channels)
-    queries = jnp.dot(flattened, w_query, preferred_element_type=jnp.float32).astype(jnp.bfloat16)
-    query_total = queries.shape[0]
+    queries_t = lax.dot_general(w_query, flattened, (((0,), (1,)), ((), ())), preferred_element_type=jnp.float32)
+    queries_t = (queries_t * HEAD_DIM ** (-0.5)).astype(jnp.bfloat16)
     key_tokens = gather_keyframes(frames, key_index)
-    keys_t = lax.dot_general(
-        w_keyval[:, :channels], key_tokens, (((0,), (1,)), ((), ())), preferred_element_type=jnp.float32
+    keys = jnp.dot(key_tokens, w_keyval[:, :channels], preferred_element_type=jnp.float32).astype(jnp.bfloat16)
+    values_t = lax.dot_general(
+        w_keyval[:, channels:], key_tokens, (((0,), (1,)), ((), ())), preferred_element_type=jnp.float32
     ).astype(jnp.bfloat16)
-    values = jnp.dot(key_tokens, w_keyval[:, channels:], preferred_element_type=jnp.float32).astype(jnp.bfloat16)
-    attended = attend(queries, keys_t, values)
-    residual = flattened.astype(jnp.float32) + jnp.dot(
-        attended, w_out, preferred_element_type=jnp.float32
+    attended_t = attend(keys, queries_t, values_t)
+    residual = flattened.astype(jnp.float32) + lax.dot_general(
+        attended_t, w_out, (((0,), (0,)), ((), ())), preferred_element_type=jnp.float32
     )
     mean_square = jnp.mean(residual * residual, axis=-1, keepdims=True)
     normed = (residual * lax.rsqrt(mean_square + 1e-06) * norm_gain).astype(jnp.bfloat16)

time: 66.4 us -> 67.1 us (1.011)
  Pallas kernels: 8.02 us -> 8.77 us
    pallas_call x1, Pallas kernels: 8.02 us -> 8.77 us  [attend(): pl.pallas_call(attention_kernel, grid=(channels // width,), in_specs=[pl....]
where the time goes in v5:
time: 67.1 us; the launch traced here: 66.8 us
  waiting for transfers between devices  26.6 us (40%)
  starting transfers between devices  12.2 us (18%)
  matrix products  11.9 us (18%)
  Pallas kernels  8.77 us (13%)
  local copies, waits for them, and re-layouts  4.99 us (7%)
  between operations  1.54 us (2%)
  other arithmetic  0.82 us (1%)
    ppermute x3, waiting for transfers between devices, gather_keyframes(): lax.ppermute(piece, 'row', [(i, (i + s) % rsize) for i in range(rsize)])  13.7 us
    pallas_call x1, Pallas kernels, attend(): pl.pallas_call(attention_kernel, grid=(channels // width,), in_specs=[pl....  8.77 us
    ppermute x3, waiting for transfers between devices, gather_keyframes(): lax.ppermute(sent, 'frame', [(i, (i + s) % fsize) for i in range(fsize)])  5.91 us
    dot_general x6, matrix products, temporal_mix(): jnp.dot(window, weights[offset], preferred_element_type=jnp.float32)  4.43 us
    ppermute x1, waiting for transfers between devices, extended(): after = lax.ppermute(first, axis, down)  4.4 us
    ppermute x3, starting transfers between devices, gather_keyframes(): lax.ppermute(piece, 'row', [(i, (i + s) % rsize) for i in range(rsize)])  3.83 us
    ppermute x3, starting transfers between devices, gather_keyframes(): lax.ppermute(sent, 'frame', [(i, (i + s) % fsize) for i in range(fsize)])  3.4 us
    ppermute x1, starting transfers between devices, extended(): before = lax.ppermute(last, axis, up)  2.49 us
  transfers between devices with their start and end apart: 9, of which 9 were waited for; matrix products, arithmetic and copies ran while one was open for 2% of the time, Pallas kernels for 0%

profile of v5, /device:TPU:9, one launch (start us, length us, event | category | flops | bytes accessed | tf_op | source)
XLA Modules:
  0.0 66.8 jit_solution(17782038948492800566)
XLA Ops:
  0.0 1.3 %fusion.32 = (s32[1]{0:T(128)}, s32[1]{0:T(128)}) fusion(s32[2]{0:T(128)} %param.9), kind=kLoop, calls=%fused_computation.65 | loop fusion | bytes 16 | tf_op jit(solution)/shard_map/slice | solution.py:63
  2.7 0.9 %slice.82 = bf16[1,128,640]{2,1,0:T(8,128)(2,1)S(1)} slice(bf16[2,128,640]{2,1,0:T(8,128)(2,1)} %param.8), slice={[1:2], [0:128], [0:640]} | slice | bytes 327680 | tf_op jit(solution)/shard_map/slice | solution.py:66
  3.6 1.1 %constant_dynamic-slice_fusion.4 = (bf16[1,64,640]{2,1,0:T(8,128)(2,1)S(1)}, bf16[1,64,640]{2,1,0:T(8,128)(2,1)S(1)}, bf16[1,64,640]{2,1,0:T(8,128)(2,1)S(1)}, b...) fusion(bf16[1,128,640]{2,1,0:T(8,128)(2,1)S(1)} %slice.82, ...), kind=kLoop, calls=%fused_computation.58 | loop fusion | bytes 983068 | tf_op jit(solution)/shard_map/dynamic_slice | solution.py:71
  4.8 0.7 %collective-permute-start = (bf16[2,64,640]{2,1,0:T(8,128)(2,1)S(1)}, bf16[2,64,640]{2,1,0:T(8,128)(2,1)S(1)}, u32[]{:S(2)}, u32[]{:S(2)}) collective-permute-start(bf16[2,64,640]{2,1,0:T(8,128)(2,1)S(1)} %pad_maximum_fusion.10), channel_id=1, source_target_pairs={{0,12},{4,0},{8,4},{12,8},{1,13},{5,1},{9,5},{13,9},{2,14},{6,2},{... | collective-permute-start | bytes 491528 | tf_op jit(solution)/shard_map/ppermute | solution.py:78
  5.6 1.3 %collective-permute-start.1 = (bf16[2,64,640]{2,1,0:T(8,128)(2,1)S(1)}, bf16[2,64,640]{2,1,0:T(8,128)(2,1)S(1)}, u32[]{:S(2)}, u32[]{:S(2)}) collective-permute-start(bf16[2,64,640]{2,1,0:T(8,128)(2,1)S(1)} %pad_maximum_fusion.11), channel_id=1, source_target_pairs={{0,8},{4,12},{8,0},{12,4},{1,9},{5,13},{9,1},{13,5},{2,10},{6,14},... | collective-permute-start | bytes 491528 | tf_op jit(solution)/shard_map/ppermute | solution.py:78
  6.9 1.4 %collective-permute-start.2 = (bf16[2,64,640]{2,1,0:T(8,128)(2,1)S(1)}, bf16[2,64,640]{2,1,0:T(8,128)(2,1)S(1)}, u32[]{:S(2)}, u32[]{:S(2)}) collective-permute-start(bf16[2,64,640]{2,1,0:T(8,128)(2,1)S(1)} %pad_maximum_fusion.12), channel_id=1, source_target_pairs={{0,4},{4,8},{8,12},{12,0},{1,5},{5,9},{9,13},{13,1},{2,6},{6,10},{... | collective-permute-start | bytes 491528 | tf_op jit(solution)/shard_map/ppermute | solution.py:78
  8.3 3.0 %collective-permute-done = bf16[2,64,640]{2,1,0:T(8,128)(2,1)S(1)} collective-permute-done((bf16[2,64,640]{2,1,0:T(8,128)(2,1)S(1)}, bf16[2,64,640]{2,1,0:T(8,128)(2,1)S(1)}, u32[]{:S(2)}, u32[]{:S(2)}) %collective-permute-start) | collective-permute-done | bytes 163872 | tf_op jit(solution)/shard_map/ppermute | solution.py:78
  11.2 0.6 collective-permute-done.1
  11.8 2.3 %collective-permute-done.2 = bf16[2,64,640]{2,1,0:T(8,128)(2,1)S(1)} collective-permute-done((bf16[2,64,640]{2,1,0:T(8,128)(2,1)S(1)}, bf16[2,64,640]{2,1,0:T(8,128)(2,1)S(1)}, u32[]{:S(2)}, u32[]{:S(2)}) %collective-permute-start.2) | collective-permute-done | bytes 163872 | tf_op jit(solution)/shard_map/ppermute | solution.py:78
  14.4 1.4 %collective-permute-start.3 = (bf16[2,64,640]{2,1,0:T(8,128)(2,1)S(1)}, bf16[2,64,640]{2,1,0:T(8,128)(2,1)S(1)}, u32[]{:S(2)}, u32[]{:S(2)}) collective-permute-start(bf16[2,64,640]{2,1,0:T(8,128)(2,1)S(1)} %get-tuple-element.18), channel_id=1, source_target_pairs={{0,1},{1,2},{2,3},{3,0},{4,5},{5,6},{6,7},{7,4},{8,9},{9,10},{10,1... | collective-permute-start | bytes 491528 | tf_op jit(solution)/shard_map/ppermute | solution.py:85
  15.7 1.1 %collective-permute-start.4 = (bf16[2,64,640]{2,1,0:T(8,128)(2,1)S(1)}, bf16[2,64,640]{2,1,0:T(8,128)(2,1)S(1)}, u32[]{:S(2)}, u32[]{:S(2)}) collective-permute-start(bf16[2,64,640]{2,1,0:T(8,128)(2,1)S(1)} %get-tuple-element.18), channel_id=1, source_target_pairs={{0,2},{1,3},{2,0},{3,1},{4,6},{5,7},{6,4},{7,5},{8,10},{9,11},{10,... | collective-permute-start | bytes 491528 | tf_op jit(solution)/shard_map/ppermute | solution.py:85
  16.8 1.4 %collective-permute-start.5 = (bf16[2,64,640]{2,1,0:T(8,128)(2,1)S(1)}, bf16[2,64,640]{2,1,0:T(8,128)(2,1)S(1)}, u32[]{:S(2)}, u32[]{:S(2)}) collective-permute-start(bf16[2,64,640]{2,1,0:T(8,128)(2,1)S(1)} %get-tuple-element.18), channel_id=1, source_target_pairs={{0,3},{1,0},{2,1},{3,2},{4,7},{5,4},{6,5},{7,6},{8,11},{9,8},{10,9... | collective-permute-start | bytes 491528 | tf_op jit(solution)/shard_map/ppermute | solution.py:85
  18.6 9.7 %collective-permute-done.4 = bf16[2,64,640]{2,1,0:T(8,128)(2,1)S(1)} collective-permute-done((bf16[2,64,640]{2,1,0:T(8,128)(2,1)S(1)}, bf16[2,64,640]{2,1,0:T(8,128)(2,1)S(1)}, u32[]{:S(2)}, u32[]{:S(2)}) %collective-permute-start.4) | collective-permute-done | bytes 163872 | tf_op jit(solution)/shard_map/ppermute | solution.py:85
  28.3 3.6 %collective-permute-done.5 = bf16[2,64,640]{2,1,0:T(8,128)(2,1)S(1)} collective-permute-done((bf16[2,64,640]{2,1,0:T(8,128)(2,1)S(1)}, bf16[2,64,640]{2,1,0:T(8,128)(2,1)S(1)}, u32[]{:S(2)}, u32[]{:S(2)}) %collective-permute-start.5) | collective-permute-done | bytes 163872 | tf_op jit(solution)/shard_map/ppermute | solution.py:85
  32.0 0.6 collective-permute-start.6
  32.6 1.2 %fusion.3.qt_ref = bf16[640,256]{1,0:T(8,128)(2,1)} fusion(bf16[640,640]{1,0:T(8,128)(2,1)S(1)} %copy-done.6, bf16[256,640]{1,0:T(8,128)(2,1)S(1)} %bitcast.51), kind=kOutput, calls=%fused_computation.12 | convolution fusion | flops 210042880 | bytes 1474560 | tf_op jit(solution)/shard_map/dot_general | solution.py:95
  33.8 0.5 collective-permute-done.6
  34.3 2.3 %fusion.vt_ref = bf16[640,1024]{1,0:T(8,128)(2,1)} fusion(bf16[512,640]{1,0:T(8,128)(2,1)S(1)} %collective-permute-done.6, bf16[512,640]{1,0:T(8,128)(2,1)S(1)} %bitcast.60, bf16[640,1280]{1,0:T(8,128)(2,1)S(1)} %copy-done.5), kind=kOutput, calls=%fused_computation.2 | convolution fusion | flops 842137600 | bytes 3440640 | tf_op jit(solution)/shard_map/dot_general | solution.py:99
  36.6 2.4 %convolution_convert_fusion.1.k_ref = bf16[1024,640]{1,0:T(8,128)(2,1)} fusion(bf16[512,640]{1,0:T(8,128)(2,1)S(1)} %collective-permute-done.6, bf16[512,640]{1,0:T(8,128)(2,1)S(1)} %bitcast.61, bf16[640,1280]{1,0:T(8,128)(2,1)S(1)} %copy-done.5), kind=kOutput, calls=%fused_computation.1 | convolution fusion | flops 842137600 | bytes 3440640 | tf_op jit(solution)/shard_map/dot_general | solution.py:98
  39.0 8.8 %shard_map.82 = bf16[640,256]{1,0:T(8,128)(2,1)} custom-call(bf16[1024,640]{1,0:T(8,128)(2,1)} %convolution_convert_fusion.1.k_ref, bf16[640,256]{1,0:T(8,128)(2,1)} %fusion.3.qt_ref, bf16[640,1024]{1,0:T(8,128)(2,1)} %fusion.vt_ref), custom_call_target="tpu_custom_call" | custom-call | tf_op jit(solution)/shard_map/pallas_call | solution.py:26
  47.8 1.6 %multiply_reduce_fusion = (f32[256]{0:T(256)S(1)}, f32[256,640]{1,0:T(8,128)S(1)}) fusion(bf16[640,256]{1,0:T(8,128)(2,1)} %shard_map.82, bf16[640,640]{1,0:T(8,128)(2,1)S(1)} %copy-done, bf16[256,640]{1,0:T(8,128)(2,1)S(1)} %bitcast.52), kind=kOutput, calls=%fused_computation.37 | convolution fusion | flops 210370304 | bytes 2130944 | tf_op jit(solution)/shard_map/dot_general | solution.py:103
  49.5 2.5 %collective-permute-start.7 = (bf16[2,128,640]{2,1,0:T(8,128)(2,1)S(1)}, bf16[2,128,640]{2,1,0:T(8,128)(2,1)S(1)}, u32[]{:S(2)}, u32[]{:S(2)}) collective-permute-start(bf16[2,128,640]{2,1,0:T(8,128)(2,1)S(1)} %bitcast.56), channel_id=1, source_target_pairs={{0,4},{4,8},{8,12},{1,5},{5,9},{9,13},{2,6},{6,10},{10,14},{3,7},{... | collective-permute-start | bytes 983048 | tf_op jit(solution)/shard_map/ppermute | solution.py:44
  52.0 1.9 %collective-permute-start.8 = (bf16[2,128,640]{2,1,0:T(8,128)(2,1)S(1)}, bf16[2,128,640]{2,1,0:T(8,128)(2,1)S(1)}, u32[]{:S(2)}, u32[]{:S(2)}) collective-permute-start(bf16[2,128,640]{2,1,0:T(8,128)(2,1)S(1)} %bitcast.57), channel_id=1, source_target_pairs={{4,0},{8,4},{12,8},{5,1},{9,5},{13,9},{6,2},{10,6},{14,10},{7,3},{... | collective-permute-start | bytes 983048 | tf_op jit(solution)/shard_map/ppermute | solution.py:45
  54.0 2.0 %collective-permute-done.7 = bf16[2,128,640]{2,1,0:T(8,128)(2,1)S(1)} collective-permute-done((bf16[2,128,640]{2,1,0:T(8,128)(2,1)S(1)}, bf16[2,128,640]{2,1,0:T(8,128)(2,1)S(1)}, u32[]{:S(2)}, u32[]{:S(2)}) %collective-permute-start.7) | collective-permute-done | bytes 327712 | tf_op jit(solution)/shard_map/ppermute | solution.py:44
  56.0 4.4 %collective-permute-done.8 = bf16[2,128,640]{2,1,0:T(8,128)(2,1)S(1)} collective-permute-done((bf16[2,128,640]{2,1,0:T(8,128)(2,1)S(1)}, bf16[2,128,640]{2,1,0:T(8,128)(2,1)S(1)}, u32[]{:S(2)}, u32[]{:S(2)}) %collective-permute-start.8) | collective-permute-done | bytes 327712 | tf_op jit(solution)/shard_map/ppermute | solution.py:45
  60.7 0.7 %fusion.11 = f32[512,640]{1,0:T(8,128)S(1)} fusion(bf16[512,640]{1,0:T(8,128)(2,1)S(1)} %bitcast.50, bf16[3,640,640]{2,1,0:T(8,128)(2,1)S(1)} %copy-done.3), kind=kOutput, calls=%fused_computation.20 | convolution fusion | flops 419430400 | bytes 2785280 | tf_op jit(solution)/shard_map/dot_general | solution.py:53
  61.4 0.7 %fusion.9 = f32[512,640]{1,0:T(8,128)S(1)} fusion(bf16[512,640]{1,0:T(8,128)(2,1)S(1)} %bitcast.49, bf16[3,640,640]{2,1,0:T(8,128)(2,1)S(1)} %copy-done.3), kind=kOutput, calls=%fused_computation.18 | convolution fusion | flops 419430400 | bytes 2785280 | tf_op jit(solution)/shard_map/dot_general | solution.py:53
  62.2 0.8 %multiply_convert_fusion = bf16[512,640]{1,0:T(8,128)(2,1)S(1)} fusion(f32[512,640]{1,0:T(8,128)S(1)} %fusion.9, f32[512,640]{1,0:T(8,128)S(1)} %fusion.11, bf16[512,640]{1,0:T(8,128)(2,1)S(1)} %bitcast.62, bf16[3,640,640]{2,1,0:T(8,128)(2,1)S(1)} %copy-done.3), kind=kOutput, calls=%fused_computation.6 | convolution fusion | flops 421724160 | bytes 4751360 | tf_op jit(solution)/shard_map/dot_general | solution.py:53
  63.2 1.5 %copy-done.1 = bf16[3,640,640]{2,1,0:T(8,128)(2,1)S(1)} copy-done((bf16[3,640,640]{2,1,0:T(8,128)(2,1)S(1)}, bf16[3,640,640]{2,1,0:T(8,128)(2,1)}, u32[]{:S(2)}) %copy-start.1) | copy-done | bytes 2457624
  64.7 0.5 fusion.7
  65.2 0.5 convolution_add_fusion.2
  65.6 1.2 %fusion.4 = bf16[256,640]{1,0:T(8,128)(2,1)} fusion(f32[256,640]{1,0:T(8,128)S(1)} %get-tuple-element.25, f32[256,640]{1,0:T(8,128)S(1)} %convolution_add_fusion.2, bf16[256,640]{1,0:T(8,128)(2,1)S(1)} %bitcast.55, bf16[3,640,640]{2,1,0:T(8,128)(2,1)S(1)} %copy-done.1), kind=kOutput, calls=%fused_computation.13 | convolution fusion | flops 210206720 | bytes 2785280 | tf_op jit(solution)/shard_map/dot_general | solution.py:53
  (26 shorter events, 1.3 us)
Async XLA Ops:
  0.0 47.8 %copy-start = (bf16[640,640]{1,0:T(8,128)(2,1)S(1)}, bf16[640,640]{1,0:T(8,128)(2,1)}, u32[]{:S(2)}) copy-start(bf16[640,640]{1,0:T(8,128)(2,1)} %param.12) | copy-start | bytes 2457604
  0.0 14.2 %copy-start.2 = (bf16[2,128,640]{2,1,0:T(8,128)(2,1)S(1)}, bf16[2,128,640]{2,1,0:T(8,128)(2,1)}, u32[]{:S(2)}) copy-start(bf16[2,128,640]{2,1,0:T(8,128)(2,1)} %param.8) | copy-start | bytes 983044
  4.8 6.4 %collective-permute-start = (bf16[2,64,640]{2,1,0:T(8,128)(2,1)S(1)}, bf16[2,64,640]{2,1,0:T(8,128)(2,1)S(1)}, u32[]{:S(2)}, u32[]{:S(2)}) collective-permute-start(bf16[2,64,640]{2,1,0:T(8,128)(2,1)S(1)} %pad_maximum_fusion.10), channel_id=1, source_target_pairs={{0,12},{4,0},{8,4},{12,8},{1,13},{5,1},{9,5},{13,9},{2,14},{6,2},{... | collective-permute-start | bytes 491528 | tf_op jit(solution)/shard_map/ppermute | solution.py:78
  5.5 27.1 %copy-start.6 = (bf16[640,640]{1,0:T(8,128)(2,1)S(1)}, bf16[640,640]{1,0:T(8,128)(2,1)}, u32[]{:S(2)}) copy-start(bf16[640,640]{1,0:T(8,128)(2,1)} %param.10) | copy-start | bytes 2457604
  5.6 6.3 %collective-permute-start.1 = (bf16[2,64,640]{2,1,0:T(8,128)(2,1)S(1)}, bf16[2,64,640]{2,1,0:T(8,128)(2,1)S(1)}, u32[]{:S(2)}, u32[]{:S(2)}) collective-permute-start(bf16[2,64,640]{2,1,0:T(8,128)(2,1)S(1)} %pad_maximum_fusion.11), channel_id=1, source_target_pairs={{0,8},{4,12},{8,0},{12,4},{1,9},{5,13},{9,1},{13,5},{2,10},{6,14},... | collective-permute-start | bytes 491528 | tf_op jit(solution)/shard_map/ppermute | solution.py:78
  6.9 7.3 %collective-permute-start.2 = (bf16[2,64,640]{2,1,0:T(8,128)(2,1)S(1)}, bf16[2,64,640]{2,1,0:T(8,128)(2,1)S(1)}, u32[]{:S(2)}, u32[]{:S(2)}) collective-permute-start(bf16[2,64,640]{2,1,0:T(8,128)(2,1)S(1)} %pad_maximum_fusion.12), channel_id=1, source_target_pairs={{0,4},{4,8},{8,12},{12,0},{1,5},{5,9},{9,13},{13,1},{2,6},{6,10},{... | collective-permute-start | bytes 491528 | tf_op jit(solution)/shard_map/ppermute | solution.py:78
  14.3 20.0 %copy-start.5 = (bf16[640,1280]{1,0:T(8,128)(2,1)S(1)}, bf16[640,1280]{1,0:T(8,128)(2,1)}, u32[]{:S(2)}) copy-start(bf16[640,1280]{1,0:T(8,128)(2,1)} %param.11) | copy-start | bytes 4915204
  14.4 4.2 %collective-permute-start.3 = (bf16[2,64,640]{2,1,0:T(8,128)(2,1)S(1)}, bf16[2,64,640]{2,1,0:T(8,128)(2,1)S(1)}, u32[]{:S(2)}, u32[]{:S(2)}) collective-permute-start(bf16[2,64,640]{2,1,0:T(8,128)(2,1)S(1)} %get-tuple-element.18), channel_id=1, source_target_pairs={{0,1},{1,2},{2,3},{3,0},{4,5},{5,6},{6,7},{7,4},{8,9},{9,10},{10,1... | collective-permute-start | bytes 491528 | tf_op jit(solution)/shard_map/ppermute | solution.py:85
  15.7 12.6 %collective-permute-start.4 = (bf16[2,64,640]{2,1,0:T(8,128)(2,1)S(1)}, bf16[2,64,640]{2,1,0:T(8,128)(2,1)S(1)}, u32[]{:S(2)}, u32[]{:S(2)}) collective-permute-start(bf16[2,64,640]{2,1,0:T(8,128)(2,1)S(1)} %get-tuple-element.18), channel_id=1, source_target_pairs={{0,2},{1,3},{2,0},{3,1},{4,6},{5,7},{6,4},{7,5},{8,10},{9,11},{10,... | collective-permute-start | bytes 491528 | tf_op jit(solution)/shard_map/ppermute | solution.py:85
  16.8 15.1 %collective-permute-start.5 = (bf16[2,64,640]{2,1,0:T(8,128)(2,1)S(1)}, bf16[2,64,640]{2,1,0:T(8,128)(2,1)S(1)}, u32[]{:S(2)}, u32[]{:S(2)}) collective-permute-start(bf16[2,64,640]{2,1,0:T(8,128)(2,1)S(1)} %get-tuple-element.18), channel_id=1, source_target_pairs={{0,3},{1,0},{2,1},{3,2},{4,7},{5,4},{6,5},{7,6},{8,11},{9,8},{10,9... | collective-permute-start | bytes 491528 | tf_op jit(solution)/shard_map/ppermute | solution.py:85
  32.0 2.3 %collective-permute-start.6 = (bf16[512,640]{1,0:T(8,128)(2,1)S(1)}, bf16[512,640]{1,0:T(8,128)(2,1)S(1)}, u32[]{:S(2)}, u32[]{:S(2)}) collective-permute-start(bf16[512,640]{1,0:T(8,128)(2,1)S(1)} %bitcast.59), channel_id=1, source_target_pairs={{0,4},{4,0},{8,12},{12,8},{1,5},{5,1},{9,13},{13,9},{2,6},{6,2},{1... | collective-permute-start | bytes 1966088 | tf_op jit(solution)/shard_map/ppermute | solution.py:87
  47.8 1.6 %copy-start.4 = (f32[640]{0:T(1024)S(1)}, f32[640]{0:T(1024)}, u32[]{:S(2)}) copy-start(f32[640]{0:T(1024)} %param.13) | copy-start | bytes 7684
  49.5 6.5 %collective-permute-start.7 = (bf16[2,128,640]{2,1,0:T(8,128)(2,1)S(1)}, bf16[2,128,640]{2,1,0:T(8,128)(2,1)S(1)}, u32[]{:S(2)}, u32[]{:S(2)}) collective-permute-start(bf16[2,128,640]{2,1,0:T(8,128)(2,1)S(1)} %bitcast.56), channel_id=1, source_target_pairs={{0,4},{4,8},{8,12},{1,5},{5,9},{9,13},{2,6},{6,10},{10,14},{3,7},{... | collective-permute-start | bytes 983048 | tf_op jit(solution)/shard_map/ppermute | solution.py:44
  52.0 8.4 %collective-permute-start.8 = (bf16[2,128,640]{2,1,0:T(8,128)(2,1)S(1)}, bf16[2,128,640]{2,1,0:T(8,128)(2,1)S(1)}, u32[]{:S(2)}, u32[]{:S(2)}) collective-permute-start(bf16[2,128,640]{2,1,0:T(8,128)(2,1)S(1)} %bitcast.57), channel_id=1, source_target_pairs={{4,0},{8,4},{12,8},{5,1},{9,5},{13,9},{6,2},{10,6},{14,10},{7,3},{... | collective-permute-start | bytes 983048 | tf_op jit(solution)/shard_map/ppermute | solution.py:45
  53.9 6.7 %copy-start.3 = (bf16[3,640,640]{2,1,0:T(8,128)(2,1)S(1)}, bf16[3,640,640]{2,1,0:T(8,128)(2,1)}, u32[]{:S(2)}) copy-start(bf16[3,640,640]{2,1,0:T(8,128)(2,1)} %param.14) | copy-start | bytes 7372804
  63.0 1.7 %copy-start.1 = (bf16[3,640,640]{2,1,0:T(8,128)(2,1)S(1)}, bf16[3,640,640]{2,1,0:T(8,128)(2,1)}, u32[]{:S(2)}) copy-start(bf16[3,640,640]{2,1,0:T(8,128)(2,1)} %param.15) | copy-start | bytes 7372804

commit v6 on v4

--- a/solution.py
+++ b/solution.py
@@ -58,7 +58,7 @@
     return result
 
 
-def gather_keyframes(frames, key_index):
+def gather_keyframes(frames, key_index, early):
     n_loc, rows, channels = frames.shape
     fsize = lax.axis_size("frame")
     rsize = lax.axis_size("row")
@@ -84,12 +84,13 @@
         got_a = jnp.where(source == owner_a, recv[0], got_a)
         got_b = jnp.where(source == owner_b, recv[1], got_b)
     piece = jnp.stack([got_a, got_b])
+    piece, early = lax.optimization_barrier((piece, early))
     pieces = [piece]
     for s in range(1, rsize):
         pieces.append(lax.ppermute(piece, "row", [(i, (i + s) % rsize) for i in range(rsize)]))
     mine = jnp.stack(pieces).reshape(-1, channels)
     sibling = lax.ppermute(mine, "frame", [(i, i ^ 1) for i in range(fsize)])
-    return jnp.concatenate([mine, sibling], axis=0)
+    return mine, sibling
 
 
 def shards(frames, key_index, w_query, w_keyval, w_out, norm_gain, w_first, w_second):
@@ -98,11 +99,19 @@
     flattened = frames.reshape(-1, channels)
     queries = jnp.dot(flattened, w_query, preferred_element_type=jnp.float32).astype(jnp.bfloat16)
     query_total = queries.shape[0]
-    key_tokens = gather_keyframes(frames, key_index)
-    keys_t = lax.dot_general(
-        w_keyval[:, :channels], key_tokens, (((0,), (1,)), ((), ())), preferred_element_type=jnp.float32
-    ).astype(jnp.bfloat16)
-    values = jnp.dot(key_tokens, w_keyval[:, channels:], preferred_element_type=jnp.float32).astype(jnp.bfloat16)
+    mine, sibling = gather_keyframes(frames, key_index, queries)
+
+    def project(tokens):
+        keys_t = lax.dot_general(
+            w_keyval[:, :channels], tokens, (((0,), (1,)), ((), ())), preferred_element_type=jnp.float32
+        ).astype(jnp.bfloat16)
+        values = jnp.dot(tokens, w_keyval[:, channels:], preferred_element_type=jnp.float32).astype(jnp.bfloat16)
+        return keys_t, values
+
+    keys_mine, values_mine = project(mine)
+    keys_sib, values_sib = project(sibling)
+    keys_t = jnp.concatenate([keys_mine, keys_sib], axis=1)
+    values = jnp.concatenate([values_mine, values_sib], axis=0)
     attended = attend(queries, keys_t, values)
     residual = flattened.astype(jnp.float32) + jnp.dot(
         attended, w_out, preferred_element_type=jnp.float32

time: 66.4 us -> 65.6 us (0.988)
  other arithmetic: 0.82 us -> 3.23 us
  matrix products: 11.9 us -> 10.1 us
  waiting for transfers between devices: 26.6 us -> 25.2 us
    concatenate x0 -> x2, other arithmetic: none -> 2.42 us  [the longest x1 1.24 us: shards(): keys_t = jnp.concatenate([keys_mine, keys_sib], axis=1)]
    dot_general x2 -> x4, matrix products: 4.7 us -> 2.93 us  [the longest x2 1.49 us: project(): jnp.dot(tokens, w_keyval[:, channels:], preferred_element_type=jnp.float32)]
    ppermute x3, waiting for transfers between devices: 5.91 us -> 4.76 us  [gather_keyframes(): lax.ppermute(sent, 'frame', [(i, (i + s) % fsize) for i in range(fsize)])]
  transfers between devices with their start and end apart: 9 -> 9, of which waited for: 9 -> 9; matrix products, arithmetic and copies ran while one was open for 2% -> 4% of each run, Pallas kernels for 0% -> 0%
where the time goes in v6:
time: 65.6 us; the launch traced here: 65.3 us
  waiting for transfers between devices  25.2 us (38%)
  starting transfers between devices  12.2 us (19%)
  matrix products  10.1 us (15%)
  Pallas kernels  8.05 us (12%)
  local copies, waits for them, and re-layouts  5.04 us (8%)
  other arithmetic  3.23 us (5%)
  between operations  1.5 us (2%)
    ppermute x3, waiting for transfers between devices, gather_keyframes(): lax.ppermute(piece, 'row', [(i, (i + s) % rsize) for i in range(rsize)])  13.7 us
    pallas_call x1, Pallas kernels, attend(): pl.pallas_call(attention_kernel, grid=(pairs, total // q_tile), in_specs=...  8.05 us
    ppermute x3, waiting for transfers between devices, gather_keyframes(): lax.ppermute(sent, 'frame', [(i, (i + s) % fsize) for i in range(fsize)])  4.76 us
    dot_general x6, matrix products, temporal_mix(): jnp.dot(window, weights[offset], preferred_element_type=jnp.float32)  4.43 us
    ppermute x1, waiting for transfers between devices, extended(): after = lax.ppermute(first, axis, down)  4.4 us
    ppermute x3, starting transfers between devices, gather_keyframes(): lax.ppermute(piece, 'row', [(i, (i + s) % rsize) for i in range(rsize)])  3.83 us
    ppermute x3, starting transfers between devices, gather_keyframes(): lax.ppermute(sent, 'frame', [(i, (i + s) % fsize) for i in range(fsize)])  3.4 us
    ppermute x1, starting transfers between devices, extended(): before = lax.ppermute(last, axis, up)  2.48 us
  transfers between devices with their start and end apart: 9, of which 9 were waited for; matrix products, arithmetic and copies ran while one was open for 4% of the time, Pallas kernels for 0%

profile of v6, /device:TPU:9, one launch (start us, length us, event | category | flops | bytes accessed | tf_op | source)
XLA Modules:
  0.0 65.3 jit_solution(15639149146401778937)
XLA Ops:
  0.0 1.4 %fusion.31 = (s32[1]{0:T(128)}, s32[1]{0:T(128)}) fusion(s32[2]{0:T(128)} %param.9), kind=kLoop, calls=%fused_computation.67 | loop fusion | bytes 16 | tf_op jit(solution)/shard_map/slice | solution.py:67
  2.7 0.9 %slice.84 = bf16[1,128,640]{2,1,0:T(8,128)(2,1)S(1)} slice(bf16[2,128,640]{2,1,0:T(8,128)(2,1)} %param.8), slice={[1:2], [0:128], [0:640]} | slice | bytes 327680 | tf_op jit(solution)/shard_map/slice | solution.py:70
  3.6 1.1 %constant_dynamic-slice_fusion.4 = (bf16[1,64,640]{2,1,0:T(8,128)(2,1)S(1)}, bf16[1,64,640]{2,1,0:T(8,128)(2,1)S(1)}, bf16[1,64,640]{2,1,0:T(8,128)(2,1)S(1)}, b...) fusion(bf16[1,128,640]{2,1,0:T(8,128)(2,1)S(1)} %slice.84, ...), kind=kLoop, calls=%fused_computation.63 | loop fusion | bytes 983068 | tf_op jit(solution)/shard_map/dynamic_slice | solution.py:75
  4.8 0.7 %collective-permute-start = (bf16[2,64,640]{2,1,0:T(8,128)(2,1)S(1)}, bf16[2,64,640]{2,1,0:T(8,128)(2,1)S(1)}, u32[]{:S(2)}, u32[]{:S(2)}) collective-permute-start(bf16[2,64,640]{2,1,0:T(8,128)(2,1)S(1)} %pad_maximum_fusion.9), channel_id=1, source_target_pairs={{0,12},{4,0},{8,4},{12,8},{1,13},{5,1},{9,5},{13,9},{2,14},{6,2},{... | collective-permute-start | bytes 491528 | tf_op jit(solution)/shard_map/ppermute | solution.py:82
  5.5 1.3 %collective-permute-start.1 = (bf16[2,64,640]{2,1,0:T(8,128)(2,1)S(1)}, bf16[2,64,640]{2,1,0:T(8,128)(2,1)S(1)}, u32[]{:S(2)}, u32[]{:S(2)}) collective-permute-start(bf16[2,64,640]{2,1,0:T(8,128)(2,1)S(1)} %pad_maximum_fusion.10), channel_id=1, source_target_pairs={{0,8},{4,12},{8,0},{12,4},{1,9},{5,13},{9,1},{13,5},{2,10},{6,14},... | collective-permute-start | bytes 491528 | tf_op jit(solution)/shard_map/ppermute | solution.py:82
  6.8 1.4 %collective-permute-start.2 = (bf16[2,64,640]{2,1,0:T(8,128)(2,1)S(1)}, bf16[2,64,640]{2,1,0:T(8,128)(2,1)S(1)}, u32[]{:S(2)}, u32[]{:S(2)}) collective-permute-start(bf16[2,64,640]{2,1,0:T(8,128)(2,1)S(1)} %pad_maximum_fusion.11), channel_id=1, source_target_pairs={{0,4},{4,8},{8,12},{12,0},{1,5},{5,9},{9,13},{13,1},{2,6},{6,10},{... | collective-permute-start | bytes 491528 | tf_op jit(solution)/shard_map/ppermute | solution.py:82
  8.3 1.2 %convolution_convert_fusion.4.q_ref = bf16[256,640]{1,0:T(8,128)(2,1)} fusion(bf16[256,640]{1,0:T(8,128)(2,1)S(1)} %bitcast.54, bf16[640,640]{1,0:T(8,128)(2,1)S(1)} %copy-done.4), kind=kOutput, calls=%fused_computation.16 | convolution fusion | flops 209879040 | bytes 1474560 | tf_op jit(solution)/shard_map/dot_general | solution.py:100
  9.4 1.8 %collective-permute-done = bf16[2,64,640]{2,1,0:T(8,128)(2,1)S(1)} collective-permute-done((bf16[2,64,640]{2,1,0:T(8,128)(2,1)S(1)}, bf16[2,64,640]{2,1,0:T(8,128)(2,1)S(1)}, u32[]{:S(2)}, u32[]{:S(2)}) %collective-permute-start) | collective-permute-done | bytes 163872 | tf_op jit(solution)/shard_map/ppermute | solution.py:82
  11.2 0.6 collective-permute-done.1
  11.8 2.4 %collective-permute-done.2 = bf16[2,64,640]{2,1,0:T(8,128)(2,1)S(1)} collective-permute-done((bf16[2,64,640]{2,1,0:T(8,128)(2,1)S(1)}, bf16[2,64,640]{2,1,0:T(8,128)(2,1)S(1)}, u32[]{:S(2)}, u32[]{:S(2)}) %collective-permute-start.2) | collective-permute-done | bytes 163872 | tf_op jit(solution)/shard_map/ppermute | solution.py:82
  14.4 1.4 %collective-permute-start.3 = (bf16[2,64,640]{2,1,0:T(8,128)(2,1)S(1)}, bf16[2,64,640]{2,1,0:T(8,128)(2,1)S(1)}, u32[]{:S(2)}, u32[]{:S(2)}) collective-permute-start(bf16[2,64,640]{2,1,0:T(8,128)(2,1)S(1)} %pad_maximum_fusion.12), channel_id=1, source_target_pairs={{0,1},{1,2},{2,3},{3,0},{4,5},{5,6},{6,7},{7,4},{8,9},{9,10},{10,1... | collective-permute-start | bytes 491528 | tf_op jit(solution)/shard_map/ppermute | solution.py:90
  15.7 1.1 %collective-permute-start.4 = (bf16[2,64,640]{2,1,0:T(8,128)(2,1)S(1)}, bf16[2,64,640]{2,1,0:T(8,128)(2,1)S(1)}, u32[]{:S(2)}, u32[]{:S(2)}) collective-permute-start(bf16[2,64,640]{2,1,0:T(8,128)(2,1)S(1)} %pad_maximum_fusion.12), channel_id=1, source_target_pairs={{0,2},{1,3},{2,0},{3,1},{4,6},{5,7},{6,4},{7,5},{8,10},{9,11},{10,... | collective-permute-start | bytes 491528 | tf_op jit(solution)/shard_map/ppermute | solution.py:90
  16.8 1.4 %collective-permute-start.5 = (bf16[2,64,640]{2,1,0:T(8,128)(2,1)S(1)}, bf16[2,64,640]{2,1,0:T(8,128)(2,1)S(1)}, u32[]{:S(2)}, u32[]{:S(2)}) collective-permute-start(bf16[2,64,640]{2,1,0:T(8,128)(2,1)S(1)} %pad_maximum_fusion.12), channel_id=1, source_target_pairs={{0,3},{1,0},{2,1},{3,2},{4,7},{5,4},{6,5},{7,6},{8,11},{9,8},{10,9... | collective-permute-start | bytes 491528 | tf_op jit(solution)/shard_map/ppermute | solution.py:90
  18.6 9.8 %collective-permute-done.4 = bf16[2,64,640]{2,1,0:T(8,128)(2,1)S(1)} collective-permute-done((bf16[2,64,640]{2,1,0:T(8,128)(2,1)S(1)}, bf16[2,64,640]{2,1,0:T(8,128)(2,1)S(1)}, u32[]{:S(2)}, u32[]{:S(2)}) %collective-permute-start.4) | collective-permute-done | bytes 163872 | tf_op jit(solution)/shard_map/ppermute | solution.py:90
  28.4 3.6 %collective-permute-done.5 = bf16[2,64,640]{2,1,0:T(8,128)(2,1)S(1)} collective-permute-done((bf16[2,64,640]{2,1,0:T(8,128)(2,1)S(1)}, bf16[2,64,640]{2,1,0:T(8,128)(2,1)S(1)}, u32[]{:S(2)}, u32[]{:S(2)}) %collective-permute-start.5) | collective-permute-done | bytes 163872 | tf_op jit(solution)/shard_map/ppermute | solution.py:90
  32.6 0.7 %convolution_convert_fusion.1 = bf16[512,640]{1,0:T(8,128)(2,1)S(1)} fusion(bf16[512,640]{1,0:T(8,128)(2,1)S(1)} %bitcast.66, bf16[640,1280]{1,0:T(8,128)(2,1)S(1)} %copy-done.6), kind=kOutput, calls=%fused_computation.3 | convolution fusion | flops 419758080 | bytes 2129920 | tf_op jit(solution)/shard_map/dot_general | solution.py:108
  33.4 0.7 %fusion.1 = bf16[640,512]{1,0:T(8,128)(2,1)S(1)} fusion(bf16[512,640]{1,0:T(8,128)(2,1)S(1)} %bitcast.67, bf16[640,1280]{1,0:T(8,128)(2,1)S(1)} %copy-done.6), kind=kOutput, calls=%fused_computation.9 | convolution fusion | flops 419758080 | bytes 2129920 | tf_op jit(solution)/shard_map/dot_general | solution.py:105
  34.3 0.7 %convolution_convert_fusion = bf16[512,640]{1,0:T(8,128)(2,1)S(1)} fusion(bf16[512,640]{1,0:T(8,128)(2,1)S(1)} %collective-permute-done.6, bf16[640,1280]{1,0:T(8,128)(2,1)S(1)} %copy-done.6), kind=kOutput, calls=%fused_computation.2 | convolution fusion | flops 419758080 | bytes 2129920 | tf_op jit(solution)/shard_map/dot_general | solution.py:108
  35.1 1.2 %pad_maximum_fusion.1.v_ref = bf16[1024,640]{1,0:T(8,128)(2,1)} fusion(bf16[512,640]{1,0:T(8,128)(2,1)S(1)} %convolution_convert_fusion, bf16[512,640]{1,0:T(8,128)(2,1)S(1)} %convolution_convert_fusion.1), kind=kLoop, calls=%fused_computation.7 | loop fusion | flops 2621440 | bytes 2621440 | tf_op jit(solution)/shard_map/concatenate | solution.py:114
  36.3 0.7 %fusion.2 = bf16[640,512]{1,0:T(8,128)(2,1)S(1)} fusion(bf16[512,640]{1,0:T(8,128)(2,1)S(1)} %collective-permute-done.6, bf16[640,1280]{1,0:T(8,128)(2,1)S(1)} %copy-done.6), kind=kOutput, calls=%fused_computation.10 | convolution fusion | flops 419758080 | bytes 2129920 | tf_op jit(solution)/shard_map/dot_general | solution.py:105
  37.0 1.2 %pad_maximum_fusion.kt_ref = bf16[640,1024]{1,0:T(8,128)(2,1)} fusion(bf16[640,512]{1,0:T(8,128)(2,1)S(1)} %fusion.2, bf16[640,512]{1,0:T(8,128)(2,1)S(1)} %fusion.1), kind=kLoop, calls=%fused_computation.6 | loop fusion | flops 2621440 | bytes 2621440 | tf_op jit(solution)/shard_map/concatenate | solution.py:113
  38.2 8.1 %shard_map.82 = bf16[256,640]{1,0:T(8,128)(2,1)} custom-call(bf16[256,640]{1,0:T(8,128)(2,1)} %convolution_convert_fusion.4.q_ref, bf16[640,1024]{1,0:T(8,128)(2,1)} %pad_maximum_fusion.kt_ref, bf16[1024,640]{1,0:T(8,128)(2,1)} %pad_maximum_fusion.1.v_ref), custom_call_target="tpu_custom_call" | custom-call | tf_op jit(solution)/shard_map/pallas_call | solution.py:30
  46.3 1.5 %multiply_reduce_fusion = (f32[256]{0:T(256)S(1)}, f32[256,640]{1,0:T(8,128)S(1)}) fusion(bf16[256,640]{1,0:T(8,128)(2,1)} %shard_map.82, bf16[640,640]{1,0:T(8,128)(2,1)S(1)} %copy-done, bf16[256,640]{1,0:T(8,128)(2,1)S(1)} %bitcast.55), kind=kOutput, calls=%fused_computation.42 | convolution fusion | flops 210370304 | bytes 2130944 | tf_op jit(solution)/shard_map/dot_general | solution.py:116
  48.0 2.5 %collective-permute-start.7 = (bf16[2,128,640]{2,1,0:T(8,128)(2,1)S(1)}, bf16[2,128,640]{2,1,0:T(8,128)(2,1)S(1)}, u32[]{:S(2)}, u32[]{:S(2)}) collective-permute-start(bf16[2,128,640]{2,1,0:T(8,128)(2,1)S(1)} %bitcast.61), channel_id=1, source_target_pairs={{0,4},{4,8},{8,12},{1,5},{5,9},{9,13},{2,6},{6,10},{10,14},{3,7},{... | collective-permute-start | bytes 983048 | tf_op jit(solution)/shard_map/ppermute | solution.py:48
  50.5 1.9 %collective-permute-start.8 = (bf16[2,128,640]{2,1,0:T(8,128)(2,1)S(1)}, bf16[2,128,640]{2,1,0:T(8,128)(2,1)S(1)}, u32[]{:S(2)}, u32[]{:S(2)}) collective-permute-start(bf16[2,128,640]{2,1,0:T(8,128)(2,1)S(1)} %bitcast.62), channel_id=1, source_target_pairs={{4,0},{8,4},{12,8},{5,1},{9,5},{13,9},{6,2},{10,6},{14,10},{7,3},{... | collective-permute-start | bytes 983048 | tf_op jit(solution)/shard_map/ppermute | solution.py:49
  52.4 2.0 %collective-permute-done.7 = bf16[2,128,640]{2,1,0:T(8,128)(2,1)S(1)} collective-permute-done((bf16[2,128,640]{2,1,0:T(8,128)(2,1)S(1)}, bf16[2,128,640]{2,1,0:T(8,128)(2,1)S(1)}, u32[]{:S(2)}, u32[]{:S(2)}) %collective-permute-start.7) | collective-permute-done | bytes 327712 | tf_op jit(solution)/shard_map/ppermute | solution.py:48
  54.5 4.4 %collective-permute-done.8 = bf16[2,128,640]{2,1,0:T(8,128)(2,1)S(1)} collective-permute-done((bf16[2,128,640]{2,1,0:T(8,128)(2,1)S(1)}, bf16[2,128,640]{2,1,0:T(8,128)(2,1)S(1)}, u32[]{:S(2)}, u32[]{:S(2)}) %collective-permute-start.8) | collective-permute-done | bytes 327712 | tf_op jit(solution)/shard_map/ppermute | solution.py:49
  59.1 0.7 %fusion.11 = f32[512,640]{1,0:T(8,128)S(1)} fusion(bf16[512,640]{1,0:T(8,128)(2,1)S(1)} %bitcast.57, bf16[3,640,640]{2,1,0:T(8,128)(2,1)S(1)} %copy-done.3), kind=kOutput, calls=%fused_computation.23 | convolution fusion | flops 419430400 | bytes 2785280 | tf_op jit(solution)/shard_map/dot_general | solution.py:57
  59.9 0.7 %fusion.9 = f32[512,640]{1,0:T(8,128)S(1)} fusion(bf16[512,640]{1,0:T(8,128)(2,1)S(1)} %bitcast.56, bf16[3,640,640]{2,1,0:T(8,128)(2,1)S(1)} %copy-done.3), kind=kOutput, calls=%fused_computation.21 | convolution fusion | flops 419430400 | bytes 2785280 | tf_op jit(solution)/shard_map/dot_general | solution.py:57
  60.6 0.8 %multiply_convert_fusion = bf16[512,640]{1,0:T(8,128)(2,1)S(1)} fusion(f32[512,640]{1,0:T(8,128)S(1)} %fusion.9, f32[512,640]{1,0:T(8,128)S(1)} %fusion.11, bf16[512,640]{1,0:T(8,128)(2,1)S(1)} %bitcast.68, bf16[3,640,640]{2,1,0:T(8,128)(2,1)S(1)} %copy-done.3), kind=kOutput, calls=%fused_computation.8 | convolution fusion | flops 421724160 | bytes 4751360 | tf_op jit(solution)/shard_map/dot_general | solution.py:57
  61.6 1.5 %copy-done.2 = bf16[3,640,640]{2,1,0:T(8,128)(2,1)S(1)} copy-done((bf16[3,640,640]{2,1,0:T(8,128)(2,1)S(1)}, bf16[3,640,640]{2,1,0:T(8,128)(2,1)}, u32[]{:S(2)}) %copy-start.2) | copy-done | bytes 2457624
  64.1 1.2 %fusion.4 = bf16[256,640]{1,0:T(8,128)(2,1)} fusion(f32[256,640]{1,0:T(8,128)S(1)} %get-tuple-element.25, f32[256,640]{1,0:T(8,128)S(1)} %convolution_add_fusion.2, bf16[256,640]{1,0:T(8,128)(2,1)S(1)} %bitcast.60, bf16[3,640,640]{2,1,0:T(8,128)(2,1)S(1)} %copy-done.2), kind=kOutput, calls=%fused_computation.15 | convolution fusion | flops 210206720 | bytes 2785280 | tf_op jit(solution)/shard_map/dot_general | solution.py:57
  (30 shorter events, 3.0 us)
Async XLA Ops:
  0.0 46.3 %copy-start = (bf16[640,640]{1,0:T(8,128)(2,1)S(1)}, bf16[640,640]{1,0:T(8,128)(2,1)}, u32[]{:S(2)}) copy-start(bf16[640,640]{1,0:T(8,128)(2,1)} %param.12) | copy-start | bytes 2457604
  0.0 8.2 %copy-start.1 = (bf16[2,128,640]{2,1,0:T(8,128)(2,1)S(1)}, bf16[2,128,640]{2,1,0:T(8,128)(2,1)}, u32[]{:S(2)}) copy-start(bf16[2,128,640]{2,1,0:T(8,128)(2,1)} %param.8) | copy-start | bytes 983044
  0.0 8.2 %copy-start.4 = (bf16[640,640]{1,0:T(8,128)(2,1)S(1)}, bf16[640,640]{1,0:T(8,128)(2,1)}, u32[]{:S(2)}) copy-start(bf16[640,640]{1,0:T(8,128)(2,1)} %param.10) | copy-start | bytes 2457604
  4.8 6.4 %collective-permute-start = (bf16[2,64,640]{2,1,0:T(8,128)(2,1)S(1)}, bf16[2,64,640]{2,1,0:T(8,128)(2,1)S(1)}, u32[]{:S(2)}, u32[]{:S(2)}) collective-permute-start(bf16[2,64,640]{2,1,0:T(8,128)(2,1)S(1)} %pad_maximum_fusion.9), channel_id=1, source_target_pairs={{0,12},{4,0},{8,4},{12,8},{1,13},{5,1},{9,5},{13,9},{2,14},{6,2},{... | collective-permute-start | bytes 491528 | tf_op jit(solution)/shard_map/ppermute | solution.py:82
  5.5 6.3 %collective-permute-start.1 = (bf16[2,64,640]{2,1,0:T(8,128)(2,1)S(1)}, bf16[2,64,640]{2,1,0:T(8,128)(2,1)S(1)}, u32[]{:S(2)}, u32[]{:S(2)}) collective-permute-start(bf16[2,64,640]{2,1,0:T(8,128)(2,1)S(1)} %pad_maximum_fusion.10), channel_id=1, source_target_pairs={{0,8},{4,12},{8,0},{12,4},{1,9},{5,13},{9,1},{13,5},{2,10},{6,14},... | collective-permute-start | bytes 491528 | tf_op jit(solution)/shard_map/ppermute | solution.py:82
  6.8 7.4 %collective-permute-start.2 = (bf16[2,64,640]{2,1,0:T(8,128)(2,1)S(1)}, bf16[2,64,640]{2,1,0:T(8,128)(2,1)S(1)}, u32[]{:S(2)}, u32[]{:S(2)}) collective-permute-start(bf16[2,64,640]{2,1,0:T(8,128)(2,1)S(1)} %pad_maximum_fusion.11), channel_id=1, source_target_pairs={{0,4},{4,8},{8,12},{12,0},{1,5},{5,9},{9,13},{13,1},{2,6},{6,10},{... | collective-permute-start | bytes 491528 | tf_op jit(solution)/shard_map/ppermute | solution.py:82
  8.3 24.3 %copy-start.6 = (bf16[640,1280]{1,0:T(8,128)(2,1)S(1)}, bf16[640,1280]{1,0:T(8,128)(2,1)}, u32[]{:S(2)}) copy-start(bf16[640,1280]{1,0:T(8,128)(2,1)} %param.11) | copy-start | bytes 4915204
  14.4 4.2 %collective-permute-start.3 = (bf16[2,64,640]{2,1,0:T(8,128)(2,1)S(1)}, bf16[2,64,640]{2,1,0:T(8,128)(2,1)S(1)}, u32[]{:S(2)}, u32[]{:S(2)}) collective-permute-start(bf16[2,64,640]{2,1,0:T(8,128)(2,1)S(1)} %pad_maximum_fusion.12), channel_id=1, source_target_pairs={{0,1},{1,2},{2,3},{3,0},{4,5},{5,6},{6,7},{7,4},{8,9},{9,10},{10,1... | collective-permute-start | bytes 491528 | tf_op jit(solution)/shard_map/ppermute | solution.py:90
  15.7 12.7 %collective-permute-start.4 = (bf16[2,64,640]{2,1,0:T(8,128)(2,1)S(1)}, bf16[2,64,640]{2,1,0:T(8,128)(2,1)S(1)}, u32[]{:S(2)}, u32[]{:S(2)}) collective-permute-start(bf16[2,64,640]{2,1,0:T(8,128)(2,1)S(1)} %pad_maximum_fusion.12), channel_id=1, source_target_pairs={{0,2},{1,3},{2,0},{3,1},{4,6},{5,7},{6,4},{7,5},{8,10},{9,11},{10,... | collective-permute-start | bytes 491528 | tf_op jit(solution)/shard_map/ppermute | solution.py:90
  16.8 15.1 %collective-permute-start.5 = (bf16[2,64,640]{2,1,0:T(8,128)(2,1)S(1)}, bf16[2,64,640]{2,1,0:T(8,128)(2,1)S(1)}, u32[]{:S(2)}, u32[]{:S(2)}) collective-permute-start(bf16[2,64,640]{2,1,0:T(8,128)(2,1)S(1)} %pad_maximum_fusion.12), channel_id=1, source_target_pairs={{0,3},{1,0},{2,1},{3,2},{4,7},{5,4},{6,5},{7,6},{8,11},{9,8},{10,9... | collective-permute-start | bytes 491528 | tf_op jit(solution)/shard_map/ppermute | solution.py:90
  32.0 2.3 %collective-permute-start.6 = (bf16[512,640]{1,0:T(8,128)(2,1)S(1)}, bf16[512,640]{1,0:T(8,128)(2,1)S(1)}, u32[]{:S(2)}, u32[]{:S(2)}) collective-permute-start(bf16[512,640]{1,0:T(8,128)(2,1)S(1)} %bitcast.65), channel_id=1, source_target_pairs={{0,4},{4,0},{8,12},{12,8},{1,5},{5,1},{9,13},{13,9},{2,6},{6,2},{1... | collective-permute-start | bytes 1966088 | tf_op jit(solution)/shard_map/ppermute | solution.py:92
  46.3 1.6 %copy-start.5 = (f32[640]{0:T(1024)S(1)}, f32[640]{0:T(1024)}, u32[]{:S(2)}) copy-start(f32[640]{0:T(1024)} %param.13) | copy-start | bytes 7684
  48.0 6.5 %collective-permute-start.7 = (bf16[2,128,640]{2,1,0:T(8,128)(2,1)S(1)}, bf16[2,128,640]{2,1,0:T(8,128)(2,1)S(1)}, u32[]{:S(2)}, u32[]{:S(2)}) collective-permute-start(bf16[2,128,640]{2,1,0:T(8,128)(2,1)S(1)} %bitcast.61), channel_id=1, source_target_pairs={{0,4},{4,8},{8,12},{1,5},{5,9},{9,13},{2,6},{6,10},{10,14},{3,7},{... | collective-permute-start | bytes 983048 | tf_op jit(solution)/shard_map/ppermute | solution.py:48
  50.5 8.4 %collective-permute-start.8 = (bf16[2,128,640]{2,1,0:T(8,128)(2,1)S(1)}, bf16[2,128,640]{2,1,0:T(8,128)(2,1)S(1)}, u32[]{:S(2)}, u32[]{:S(2)}) collective-permute-start(bf16[2,128,640]{2,1,0:T(8,128)(2,1)S(1)} %bitcast.62), channel_id=1, source_target_pairs={{4,0},{8,4},{12,8},{5,1},{9,5},{13,9},{6,2},{10,6},{14,10},{7,3},{... | collective-permute-start | bytes 983048 | tf_op jit(solution)/shard_map/ppermute | solution.py:49
  52.4 6.7 %copy-start.3 = (bf16[3,640,640]{2,1,0:T(8,128)(2,1)S(1)}, bf16[3,640,640]{2,1,0:T(8,128)(2,1)}, u32[]{:S(2)}) copy-start(bf16[3,640,640]{2,1,0:T(8,128)(2,1)} %param.14) | copy-start | bytes 7372804
  61.5 1.7 %copy-start.2 = (bf16[3,640,640]{2,1,0:T(8,128)(2,1)S(1)}, bf16[3,640,640]{2,1,0:T(8,128)(2,1)}, u32[]{:S(2)}) copy-start(bf16[3,640,640]{2,1,0:T(8,128)(2,1)} %param.15) | copy-start | bytes 7372804

commit v7 on v6

--- a/solution.py
+++ b/solution.py
@@ -66,23 +66,23 @@
     last = n_loc * fsize - 1
     other = key_index[0] + key_index[1] - last
     owner_a = other // n_loc
-    cand_a = lax.dynamic_index_in_dim(frames, other % n_loc, 0, keepdims=False)
-    cand_b = frames[n_loc - 1]
+    slot_a = other % n_loc
     owner_b = fsize - 1
     half = rows // 2
 
-    def half_of(x, h):
-        return lax.dynamic_slice_in_dim(x, h * half, half, 0)
+    def halves(h):
+        return lax.dynamic_slice_in_dim(frames, h * half, half, 1)
 
-    own = jnp.stack([half_of(cand_a, me % 2), half_of(cand_b, me % 2)])
-    got_a = jnp.where(me == owner_a, own[0], jnp.zeros((half, channels), frames.dtype))
-    got_b = own[1]
+    own = halves(me % 2)
+    got_a = jnp.where(
+        me == owner_a, lax.dynamic_index_in_dim(own, slot_a, 0, keepdims=False), jnp.zeros_like(own[0])
+    )
+    got_b = own[n_loc - 1]
     for s in range(1, fsize):
-        sent = jnp.stack([half_of(cand_a, (me + s) % 2), half_of(cand_b, (me + s) % 2)])
-        recv = lax.ppermute(sent, "frame", [(i, (i + s) % fsize) for i in range(fsize)])
+        recv = lax.ppermute(halves((me + s) % 2), "frame", [(i, (i + s) % fsize) for i in range(fsize)])
         source = (me - s) % fsize
-        got_a = jnp.where(source == owner_a, recv[0], got_a)
-        got_b = jnp.where(source == owner_b, recv[1], got_b)
+        got_a = jnp.where(source == owner_a, lax.dynamic_index_in_dim(recv, slot_a, 0, keepdims=False), got_a)
+        got_b = jnp.where(source == owner_b, recv[n_loc - 1], got_b)
     piece = jnp.stack([got_a, got_b])
     piece, early = lax.optimization_barrier((piece, early))
     pieces = [piece]

time: 65.6 us -> 62 us (0.945)
  waiting for transfers between devices: 25.2 us -> 21.2 us
  matrix products: 10.1 us -> 11.4 us
  local copies, waits for them, and re-layouts: 5.04 us -> 4.11 us
    ppermute x3, waiting for transfers between devices: 4.76 us -> 0.82 us  [gather_keyframes(): lax.ppermute(halves((me + s) % 2), 'frame', [(i, (i + s) % fsize) for i i...]
    dot_general x1, matrix products: 1.18 us -> 2.55 us  [shards(): jnp.dot(flattened, w_query, preferred_element_type=jnp.float32)]
    slice x1 -> x0, local copies, waits for them, and re-layouts: 0.93 us -> none  [gather_keyframes(): cand_b = frames[n_loc - 1]]
    unnamed x14 -> x12, local copies, waits for them, and re-layouts: 1.55 us -> 1.55 us
  transfers between devices with their start and end apart: 9 -> 9, of which waited for: 9 -> 7; matrix products, arithmetic and copies ran while one was open for 4% -> 9% of each run, Pallas kernels for 0% -> 0%
where the time goes in v7:
time: 62 us; the launch traced here: 61.7 us
  waiting for transfers between devices  21.2 us (34%)
  starting transfers between devices  12 us (19%)
  matrix products  11.4 us (18%)
  Pallas kernels  8.04 us (13%)
  local copies, waits for them, and re-layouts  4.11 us (7%)
  other arithmetic  3.16 us (5%)
  between operations  1.66 us (3%)
    ppermute x3, waiting for transfers between devices, gather_keyframes(): lax.ppermute(piece, 'row', [(i, (i + s) % rsize) for i in range(rsize)])  13.7 us
    pallas_call x1, Pallas kernels, attend(): pl.pallas_call(attention_kernel, grid=(pairs, total // q_tile), in_specs=...  8.04 us
    dot_general x6, matrix products, temporal_mix(): jnp.dot(window, weights[offset], preferred_element_type=jnp.float32)  4.43 us
    ppermute x1, waiting for transfers between devices, extended(): after = lax.ppermute(first, axis, down)  4.4 us
    ppermute x3, starting transfers between devices, gather_keyframes(): lax.ppermute(piece, 'row', [(i, (i + s) % rsize) for i in range(rsize)])  3.83 us
    ppermute x3, starting transfers between devices, gather_keyframes(): lax.ppermute(halves((me + s) % 2), 'frame', [(i, (i + s) % fsize) for i i...  3.29 us
    dot_general x1, matrix products, shards(): jnp.dot(flattened, w_query, preferred_element_type=jnp.float32)  2.55 us
    ppermute x1, starting transfers between devices, extended(): before = lax.ppermute(last, axis, up)  2.44 us
  transfers between devices with their start and end apart: 9, of which 7 were waited for; matrix products, arithmetic and copies ran while one was open for 9% of the time, Pallas kernels for 0%

profile of v7, /device:TPU:9, one launch (start us, length us, event | category | flops | bytes accessed | tf_op | source)
XLA Modules:
  0.0 61.7 jit_solution(3428042381810205030)
XLA Ops:
  0.0 1.2 %constant_dynamic-slice_fusion.2 = (bf16[2,64,640]{2,1,0:T(8,128)(2,1)S(1)}, bf16[2,64,640]{2,1,0:T(8,128)(2,1)S(1)}, bf16[2,64,640]{2,1,0:T(8,128)(2,1)S(1)}) fusion(bf16[2,128,640]{2,1,0:T(8,128)(2,1)} %param.8, s32[]{:T(128)S(6)} %select_n.137, s32[]{:T(128)S(6)} %select_n.147, s32[]{:T(128)S(6)} %select_n.143), kind=kLoop, calls=%fused_computation.56 | loop fusion | bytes 983052 | tf_op jit(solution)/shard_map/dynamic_slice | solution.py:74
  1.2 0.7 %collective-permute-start = (bf16[2,64,640]{2,1,0:T(8,128)(2,1)S(1)}, bf16[2,64,640]{2,1,0:T(8,128)(2,1)S(1)}, u32[]{:S(2)}, u32[]{:S(2)}) collective-permute-start(bf16[2,64,640]{2,1,0:T(8,128)(2,1)S(1)} %get-tuple-element.16), channel_id=1, source_target_pairs={{0,12},{4,0},{8,4},{12,8},{1,13},{5,1},{9,5},{13,9},{2,14},{6,2},{... | collective-permute-start | bytes 491528 | tf_op jit(solution)/shard_map/ppermute | solution.py:82
  1.9 1.2 %collective-permute-start.1 = (bf16[2,64,640]{2,1,0:T(8,128)(2,1)S(1)}, bf16[2,64,640]{2,1,0:T(8,128)(2,1)S(1)}, u32[]{:S(2)}, u32[]{:S(2)}) collective-permute-start(bf16[2,64,640]{2,1,0:T(8,128)(2,1)S(1)} %get-tuple-element.18), channel_id=1, source_target_pairs={{0,8},{4,12},{8,0},{12,4},{1,9},{5,13},{9,1},{13,5},{2,10},{6,14},... | collective-permute-start | bytes 491528 | tf_op jit(solution)/shard_map/ppermute | solution.py:82
  3.2 1.3 %collective-permute-start.2 = (bf16[2,64,640]{2,1,0:T(8,128)(2,1)S(1)}, bf16[2,64,640]{2,1,0:T(8,128)(2,1)S(1)}, u32[]{:S(2)}, u32[]{:S(2)}) collective-permute-start(bf16[2,64,640]{2,1,0:T(8,128)(2,1)S(1)} %get-tuple-element.17), channel_id=1, source_target_pairs={{0,4},{4,8},{8,12},{12,0},{1,5},{5,9},{9,13},{13,1},{2,6},{6,10},{... | collective-permute-start | bytes 491528 | tf_op jit(solution)/shard_map/ppermute | solution.py:82
  4.5 1.3 %fusion.29 = (s32[1]{0:T(128)}, s32[1]{0:T(128)}) fusion(s32[2]{0:T(128)} %param.9), kind=kLoop, calls=%fused_computation.59 | loop fusion | bytes 16 | tf_op jit(solution)/shard_map/slice | solution.py:67
  7.3 2.5 %convolution_convert_fusion.4.q_ref = bf16[256,640]{1,0:T(8,128)(2,1)} fusion(bf16[256,640]{1,0:T(8,128)(2,1)} %bitcast.54, bf16[640,640]{1,0:T(8,128)(2,1)} %param.10), kind=kOutput, calls=%fused_computation.16 | convolution fusion | flops 209879040 | bytes 1474560 | tf_op jit(solution)/shard_map/dot_general | solution.py:100
  9.9 0.8 %collective-permute-done.2 = bf16[2,64,640]{2,1,0:T(8,128)(2,1)S(1)} collective-permute-done((bf16[2,64,640]{2,1,0:T(8,128)(2,1)S(1)}, bf16[2,64,640]{2,1,0:T(8,128)(2,1)S(1)}, u32[]{:S(2)}, u32[]{:S(2)}) %collective-permute-start.2) | collective-permute-done | bytes 163872 | tf_op jit(solution)/shard_map/ppermute | solution.py:82
  10.8 1.4 %collective-permute-start.3 = (bf16[2,64,640]{2,1,0:T(8,128)(2,1)S(1)}, bf16[2,64,640]{2,1,0:T(8,128)(2,1)S(1)}, u32[]{:S(2)}, u32[]{:S(2)}) collective-permute-start(bf16[2,64,640]{2,1,0:T(8,128)(2,1)S(1)} %pad_maximum_fusion.9), channel_id=1, source_target_pairs={{0,1},{1,2},{2,3},{3,0},{4,5},{5,6},{6,7},{7,4},{8,9},{9,10},{10,1... | collective-permute-start | bytes 491528 | tf_op jit(solution)/shard_map/ppermute | solution.py:90
  12.2 1.1 %collective-permute-start.4 = (bf16[2,64,640]{2,1,0:T(8,128)(2,1)S(1)}, bf16[2,64,640]{2,1,0:T(8,128)(2,1)S(1)}, u32[]{:S(2)}, u32[]{:S(2)}) collective-permute-start(bf16[2,64,640]{2,1,0:T(8,128)(2,1)S(1)} %pad_maximum_fusion.9), channel_id=1, source_target_pairs={{0,2},{1,3},{2,0},{3,1},{4,6},{5,7},{6,4},{7,5},{8,10},{9,11},{10,... | collective-permute-start | bytes 491528 | tf_op jit(solution)/shard_map/ppermute | solution.py:90
  13.3 1.4 %collective-permute-start.5 = (bf16[2,64,640]{2,1,0:T(8,128)(2,1)S(1)}, bf16[2,64,640]{2,1,0:T(8,128)(2,1)S(1)}, u32[]{:S(2)}, u32[]{:S(2)}) collective-permute-start(bf16[2,64,640]{2,1,0:T(8,128)(2,1)S(1)} %pad_maximum_fusion.9), channel_id=1, source_target_pairs={{0,3},{1,0},{2,1},{3,2},{4,7},{5,4},{6,5},{7,6},{8,11},{9,8},{10,9... | collective-permute-start | bytes 491528 | tf_op jit(solution)/shard_map/ppermute | solution.py:90
  15.0 9.8 %collective-permute-done.4 = bf16[2,64,640]{2,1,0:T(8,128)(2,1)S(1)} collective-permute-done((bf16[2,64,640]{2,1,0:T(8,128)(2,1)S(1)}, bf16[2,64,640]{2,1,0:T(8,128)(2,1)S(1)}, u32[]{:S(2)}, u32[]{:S(2)}) %collective-permute-start.4) | collective-permute-done | bytes 163872 | tf_op jit(solution)/shard_map/ppermute | solution.py:90
  24.9 3.5 %collective-permute-done.5 = bf16[2,64,640]{2,1,0:T(8,128)(2,1)S(1)} collective-permute-done((bf16[2,64,640]{2,1,0:T(8,128)(2,1)S(1)}, bf16[2,64,640]{2,1,0:T(8,128)(2,1)S(1)}, u32[]{:S(2)}, u32[]{:S(2)}) %collective-permute-start.5) | collective-permute-done | bytes 163872 | tf_op jit(solution)/shard_map/ppermute | solution.py:90
  28.5 0.6 collective-permute-start.6
  29.0 0.7 %convolution_convert_fusion.1 = bf16[512,640]{1,0:T(8,128)(2,1)S(1)} fusion(bf16[512,640]{1,0:T(8,128)(2,1)S(1)} %bitcast.66, bf16[640,1280]{1,0:T(8,128)(2,1)S(1)} %copy-done.5), kind=kOutput, calls=%fused_computation.3 | convolution fusion | flops 419758080 | bytes 2129920 | tf_op jit(solution)/shard_map/dot_general | solution.py:108
  29.8 0.7 %fusion.1 = bf16[640,512]{1,0:T(8,128)(2,1)S(1)} fusion(bf16[512,640]{1,0:T(8,128)(2,1)S(1)} %bitcast.67, bf16[640,1280]{1,0:T(8,128)(2,1)S(1)} %copy-done.5), kind=kOutput, calls=%fused_computation.9 | convolution fusion | flops 419758080 | bytes 2129920 | tf_op jit(solution)/shard_map/dot_general | solution.py:105
  30.8 0.7 %convolution_convert_fusion = bf16[512,640]{1,0:T(8,128)(2,1)S(1)} fusion(bf16[512,640]{1,0:T(8,128)(2,1)S(1)} %collective-permute-done.6, bf16[640,1280]{1,0:T(8,128)(2,1)S(1)} %copy-done.5), kind=kOutput, calls=%fused_computation.2 | convolution fusion | flops 419758080 | bytes 2129920 | tf_op jit(solution)/shard_map/dot_general | solution.py:108
  31.5 1.2 %pad_maximum_fusion.1.v_ref = bf16[1024,640]{1,0:T(8,128)(2,1)} fusion(bf16[512,640]{1,0:T(8,128)(2,1)S(1)} %convolution_convert_fusion, bf16[512,640]{1,0:T(8,128)(2,1)S(1)} %convolution_convert_fusion.1), kind=kLoop, calls=%fused_computation.7 | loop fusion | flops 2621440 | bytes 2621440 | tf_op jit(solution)/shard_map/concatenate | solution.py:114
  32.7 0.7 %fusion.2 = bf16[640,512]{1,0:T(8,128)(2,1)S(1)} fusion(bf16[512,640]{1,0:T(8,128)(2,1)S(1)} %collective-permute-done.6, bf16[640,1280]{1,0:T(8,128)(2,1)S(1)} %copy-done.5), kind=kOutput, calls=%fused_computation.10 | convolution fusion | flops 419758080 | bytes 2129920 | tf_op jit(solution)/shard_map/dot_general | solution.py:105
  33.4 1.2 %pad_maximum_fusion.kt_ref = bf16[640,1024]{1,0:T(8,128)(2,1)} fusion(bf16[640,512]{1,0:T(8,128)(2,1)S(1)} %fusion.2, bf16[640,512]{1,0:T(8,128)(2,1)S(1)} %fusion.1), kind=kLoop, calls=%fused_computation.6 | loop fusion | flops 2621440 | bytes 2621440 | tf_op jit(solution)/shard_map/concatenate | solution.py:113
  34.7 8.0 %shard_map.82 = bf16[256,640]{1,0:T(8,128)(2,1)} custom-call(bf16[256,640]{1,0:T(8,128)(2,1)} %convolution_convert_fusion.4.q_ref, bf16[640,1024]{1,0:T(8,128)(2,1)} %pad_maximum_fusion.kt_ref, bf16[1024,640]{1,0:T(8,128)(2,1)} %pad_maximum_fusion.1.v_ref), custom_call_target="tpu_custom_call" | custom-call | tf_op jit(solution)/shard_map/pallas_call | solution.py:30
  42.7 1.5 %multiply_reduce_fusion = (f32[256]{0:T(256)S(1)}, f32[256,640]{1,0:T(8,128)S(1)}) fusion(bf16[256,640]{1,0:T(8,128)(2,1)} %shard_map.82, bf16[640,640]{1,0:T(8,128)(2,1)S(1)} %copy-done, bf16[256,640]{1,0:T(8,128)(2,1)S(1)} %bitcast.55), kind=kOutput, calls=%fused_computation.42 | convolution fusion | flops 210370304 | bytes 2130944 | tf_op jit(solution)/shard_map/dot_general | solution.py:116
  44.4 2.4 %collective-permute-start.7 = (bf16[2,128,640]{2,1,0:T(8,128)(2,1)S(1)}, bf16[2,128,640]{2,1,0:T(8,128)(2,1)S(1)}, u32[]{:S(2)}, u32[]{:S(2)}) collective-permute-start(bf16[2,128,640]{2,1,0:T(8,128)(2,1)S(1)} %bitcast.61), channel_id=1, source_target_pairs={{0,4},{4,8},{8,12},{1,5},{5,9},{9,13},{2,6},{6,10},{10,14},{3,7},{... | collective-permute-start | bytes 983048 | tf_op jit(solution)/shard_map/ppermute | solution.py:48
  46.9 1.9 %collective-permute-start.8 = (bf16[2,128,640]{2,1,0:T(8,128)(2,1)S(1)}, bf16[2,128,640]{2,1,0:T(8,128)(2,1)S(1)}, u32[]{:S(2)}, u32[]{:S(2)}) collective-permute-start(bf16[2,128,640]{2,1,0:T(8,128)(2,1)S(1)} %bitcast.62), channel_id=1, source_target_pairs={{4,0},{8,4},{12,8},{5,1},{9,5},{13,9},{6,2},{10,6},{14,10},{7,3},{... | collective-permute-start | bytes 983048 | tf_op jit(solution)/shard_map/ppermute | solution.py:49
  48.8 2.0 %collective-permute-done.7 = bf16[2,128,640]{2,1,0:T(8,128)(2,1)S(1)} collective-permute-done((bf16[2,128,640]{2,1,0:T(8,128)(2,1)S(1)}, bf16[2,128,640]{2,1,0:T(8,128)(2,1)S(1)}, u32[]{:S(2)}, u32[]{:S(2)}) %collective-permute-start.7) | collective-permute-done | bytes 327712 | tf_op jit(solution)/shard_map/ppermute | solution.py:48
  50.9 4.4 %collective-permute-done.8 = bf16[2,128,640]{2,1,0:T(8,128)(2,1)S(1)} collective-permute-done((bf16[2,128,640]{2,1,0:T(8,128)(2,1)S(1)}, bf16[2,128,640]{2,1,0:T(8,128)(2,1)S(1)}, u32[]{:S(2)}, u32[]{:S(2)}) %collective-permute-start.8) | collective-permute-done | bytes 327712 | tf_op jit(solution)/shard_map/ppermute | solution.py:49
  55.5 0.7 %fusion.11 = f32[512,640]{1,0:T(8,128)S(1)} fusion(bf16[512,640]{1,0:T(8,128)(2,1)S(1)} %bitcast.57, bf16[3,640,640]{2,1,0:T(8,128)(2,1)S(1)} %copy-done.3), kind=kOutput, calls=%fused_computation.23 | convolution fusion | flops 419430400 | bytes 2785280 | tf_op jit(solution)/shard_map/dot_general | solution.py:57
  56.3 0.7 %fusion.9 = f32[512,640]{1,0:T(8,128)S(1)} fusion(bf16[512,640]{1,0:T(8,128)(2,1)S(1)} %bitcast.56, bf16[3,640,640]{2,1,0:T(8,128)(2,1)S(1)} %copy-done.3), kind=kOutput, calls=%fused_computation.21 | convolution fusion | flops 419430400 | bytes 2785280 | tf_op jit(solution)/shard_map/dot_general | solution.py:57
  57.0 0.8 %multiply_convert_fusion = bf16[512,640]{1,0:T(8,128)(2,1)S(1)} fusion(f32[512,640]{1,0:T(8,128)S(1)} %fusion.9, f32[512,640]{1,0:T(8,128)S(1)} %fusion.11, bf16[512,640]{1,0:T(8,128)(2,1)S(1)} %bitcast.68, bf16[3,640,640]{2,1,0:T(8,128)(2,1)S(1)} %copy-done.3), kind=kOutput, calls=%fused_computation.8 | convolution fusion | flops 421724160 | bytes 4751360 | tf_op jit(solution)/shard_map/dot_general | solution.py:57
  58.0 1.5 %copy-done.2 = bf16[3,640,640]{2,1,0:T(8,128)(2,1)S(1)} copy-done((bf16[3,640,640]{2,1,0:T(8,128)(2,1)S(1)}, bf16[3,640,640]{2,1,0:T(8,128)(2,1)}, u32[]{:S(2)}) %copy-start.2) | copy-done | bytes 2457624
  59.6 0.5 fusion.7
  60.0 0.5 convolution_add_fusion.2
  60.5 1.2 %fusion.4 = bf16[256,640]{1,0:T(8,128)(2,1)} fusion(f32[256,640]{1,0:T(8,128)S(1)} %get-tuple-element.22, f32[256,640]{1,0:T(8,128)S(1)} %convolution_add_fusion.2, bf16[256,640]{1,0:T(8,128)(2,1)S(1)} %bitcast.60, bf16[3,640,640]{2,1,0:T(8,128)(2,1)S(1)} %copy-done.2), kind=kOutput, calls=%fused_computation.15 | convolution fusion | flops 210206720 | bytes 2785280 | tf_op jit(solution)/shard_map/dot_general | solution.py:57
  (24 shorter events, 1.4 us)
Async XLA Ops:
  0.0 42.7 %copy-start = (bf16[640,640]{1,0:T(8,128)(2,1)S(1)}, bf16[640,640]{1,0:T(8,128)(2,1)}, u32[]{:S(2)}) copy-start(bf16[640,640]{1,0:T(8,128)(2,1)} %param.12) | copy-start | bytes 2457604
  0.0 10.7 %copy-start.1 = (bf16[2,128,640]{2,1,0:T(8,128)(2,1)S(1)}, bf16[2,128,640]{2,1,0:T(8,128)(2,1)}, u32[]{:S(2)}) copy-start(bf16[2,128,640]{2,1,0:T(8,128)(2,1)} %param.8) | copy-start | bytes 983044
  1.2 8.6 %collective-permute-start = (bf16[2,64,640]{2,1,0:T(8,128)(2,1)S(1)}, bf16[2,64,640]{2,1,0:T(8,128)(2,1)S(1)}, u32[]{:S(2)}, u32[]{:S(2)}) collective-permute-start(bf16[2,64,640]{2,1,0:T(8,128)(2,1)S(1)} %get-tuple-element.16), channel_id=1, source_target_pairs={{0,12},{4,0},{8,4},{12,8},{1,13},{5,1},{9,5},{13,9},{2,14},{6,2},{... | collective-permute-start | bytes 491528 | tf_op jit(solution)/shard_map/ppermute | solution.py:82
  1.9 7.9 %collective-permute-start.1 = (bf16[2,64,640]{2,1,0:T(8,128)(2,1)S(1)}, bf16[2,64,640]{2,1,0:T(8,128)(2,1)S(1)}, u32[]{:S(2)}, u32[]{:S(2)}) collective-permute-start(bf16[2,64,640]{2,1,0:T(8,128)(2,1)S(1)} %get-tuple-element.18), channel_id=1, source_target_pairs={{0,8},{4,12},{8,0},{12,4},{1,9},{5,13},{9,1},{13,5},{2,10},{6,14},... | collective-permute-start | bytes 491528 | tf_op jit(solution)/shard_map/ppermute | solution.py:82
  3.2 7.5 %collective-permute-start.2 = (bf16[2,64,640]{2,1,0:T(8,128)(2,1)S(1)}, bf16[2,64,640]{2,1,0:T(8,128)(2,1)S(1)}, u32[]{:S(2)}, u32[]{:S(2)}) collective-permute-start(bf16[2,64,640]{2,1,0:T(8,128)(2,1)S(1)} %get-tuple-element.17), channel_id=1, source_target_pairs={{0,4},{4,8},{8,12},{12,0},{1,5},{5,9},{9,13},{13,1},{2,6},{6,10},{... | collective-permute-start | bytes 491528 | tf_op jit(solution)/shard_map/ppermute | solution.py:82
  7.3 21.8 %copy-start.5 = (bf16[640,1280]{1,0:T(8,128)(2,1)S(1)}, bf16[640,1280]{1,0:T(8,128)(2,1)}, u32[]{:S(2)}) copy-start(bf16[640,1280]{1,0:T(8,128)(2,1)} %param.11) | copy-start | bytes 4915204
  10.8 4.2 %collective-permute-start.3 = (bf16[2,64,640]{2,1,0:T(8,128)(2,1)S(1)}, bf16[2,64,640]{2,1,0:T(8,128)(2,1)S(1)}, u32[]{:S(2)}, u32[]{:S(2)}) collective-permute-start(bf16[2,64,640]{2,1,0:T(8,128)(2,1)S(1)} %pad_maximum_fusion.9), channel_id=1, source_target_pairs={{0,1},{1,2},{2,3},{3,0},{4,5},{5,6},{6,7},{7,4},{8,9},{9,10},{10,1... | collective-permute-start | bytes 491528 | tf_op jit(solution)/shard_map/ppermute | solution.py:90
  12.2 12.7 %collective-permute-start.4 = (bf16[2,64,640]{2,1,0:T(8,128)(2,1)S(1)}, bf16[2,64,640]{2,1,0:T(8,128)(2,1)S(1)}, u32[]{:S(2)}, u32[]{:S(2)}) collective-permute-start(bf16[2,64,640]{2,1,0:T(8,128)(2,1)S(1)} %pad_maximum_fusion.9), channel_id=1, source_target_pairs={{0,2},{1,3},{2,0},{3,1},{4,6},{5,7},{6,4},{7,5},{8,10},{9,11},{10,... | collective-permute-start | bytes 491528 | tf_op jit(solution)/shard_map/ppermute | solution.py:90
  13.3 15.1 %collective-permute-start.5 = (bf16[2,64,640]{2,1,0:T(8,128)(2,1)S(1)}, bf16[2,64,640]{2,1,0:T(8,128)(2,1)S(1)}, u32[]{:S(2)}, u32[]{:S(2)}) collective-permute-start(bf16[2,64,640]{2,1,0:T(8,128)(2,1)S(1)} %pad_maximum_fusion.9), channel_id=1, source_target_pairs={{0,3},{1,0},{2,1},{3,2},{4,7},{5,4},{6,5},{7,6},{8,11},{9,8},{10,9... | collective-permute-start | bytes 491528 | tf_op jit(solution)/shard_map/ppermute | solution.py:90
  28.5 2.3 %collective-permute-start.6 = (bf16[512,640]{1,0:T(8,128)(2,1)S(1)}, bf16[512,640]{1,0:T(8,128)(2,1)S(1)}, u32[]{:S(2)}, u32[]{:S(2)}) collective-permute-start(bf16[512,640]{1,0:T(8,128)(2,1)S(1)} %bitcast.65), channel_id=1, source_target_pairs={{0,4},{4,0},{8,12},{12,8},{1,5},{5,1},{9,13},{13,9},{2,6},{6,2},{1... | collective-permute-start | bytes 1966088 | tf_op jit(solution)/shard_map/ppermute | solution.py:92
  42.7 1.6 %copy-start.4 = (f32[640]{0:T(1024)S(1)}, f32[640]{0:T(1024)}, u32[]{:S(2)}) copy-start(f32[640]{0:T(1024)} %param.13) | copy-start | bytes 7684
  44.4 6.4 %collective-permute-start.7 = (bf16[2,128,640]{2,1,0:T(8,128)(2,1)S(1)}, bf16[2,128,640]{2,1,0:T(8,128)(2,1)S(1)}, u32[]{:S(2)}, u32[]{:S(2)}) collective-permute-start(bf16[2,128,640]{2,1,0:T(8,128)(2,1)S(1)} %bitcast.61), channel_id=1, source_target_pairs={{0,4},{4,8},{8,12},{1,5},{5,9},{9,13},{2,6},{6,10},{10,14},{3,7},{... | collective-permute-start | bytes 983048 | tf_op jit(solution)/shard_map/ppermute | solution.py:48
  46.9 8.4 %collective-permute-start.8 = (bf16[2,128,640]{2,1,0:T(8,128)(2,1)S(1)}, bf16[2,128,640]{2,1,0:T(8,128)(2,1)S(1)}, u32[]{:S(2)}, u32[]{:S(2)}) collective-permute-start(bf16[2,128,640]{2,1,0:T(8,128)(2,1)S(1)} %bitcast.62), channel_id=1, source_target_pairs={{4,0},{8,4},{12,8},{5,1},{9,5},{13,9},{6,2},{10,6},{14,10},{7,3},{... | collective-permute-start | bytes 983048 | tf_op jit(solution)/shard_map/ppermute | solution.py:49
  48.8 6.7 %copy-start.3 = (bf16[3,640,640]{2,1,0:T(8,128)(2,1)S(1)}, bf16[3,640,640]{2,1,0:T(8,128)(2,1)}, u32[]{:S(2)}) copy-start(bf16[3,640,640]{2,1,0:T(8,128)(2,1)} %param.14) | copy-start | bytes 7372804
  57.9 1.7 %copy-start.2 = (bf16[3,640,640]{2,1,0:T(8,128)(2,1)S(1)}, bf16[3,640,640]{2,1,0:T(8,128)(2,1)}, u32[]{:S(2)}) copy-start(bf16[3,640,640]{2,1,0:T(8,128)(2,1)} %param.15) | copy-start | bytes 7372804

commit v8 on v7

--- a/solution.py
+++ b/solution.py
@@ -69,20 +69,30 @@
     slot_a = other % n_loc
     owner_b = fsize - 1
     half = rows // 2
+    core = me % 2
+    chip = me // 2
+    chips = fsize // 2
 
     def halves(h):
         return lax.dynamic_slice_in_dim(frames, h * half, half, 1)
 
-    own = halves(me % 2)
-    got_a = jnp.where(
-        me == owner_a, lax.dynamic_index_in_dim(own, slot_a, 0, keepdims=False), jnp.zeros_like(own[0])
+    from_sibling = lax.ppermute(halves(1 - core), "frame", [(i, i ^ 1) for i in range(fsize)])
+    chip_frames = jnp.concatenate([halves(core), from_sibling], axis=0)
+    index_a = (owner_a % 2 != core).astype(jnp.int32) * n_loc + slot_a
+    index_b = (owner_b % 2 != core).astype(jnp.int32) * n_loc + n_loc - 1
+    cand = jnp.stack(
+        [
+            lax.dynamic_index_in_dim(chip_frames, index_a, 0, keepdims=False),
+            lax.dynamic_index_in_dim(chip_frames, index_b, 0, keepdims=False),
+        ]
     )
-    got_b = own[n_loc - 1]
-    for s in range(1, fsize):
-        recv = lax.ppermute(halves((me + s) % 2), "frame", [(i, (i + s) % fsize) for i in range(fsize)])
-        source = (me - s) % fsize
-        got_a = jnp.where(source == owner_a, lax.dynamic_index_in_dim(recv, slot_a, 0, keepdims=False), got_a)
-        got_b = jnp.where(source == owner_b, recv[n_loc - 1], got_b)
+    got_a = cand[0]
+    got_b = cand[1]
+    for s in range(1, chips):
+        recv = lax.ppermute(cand, "frame", [(i, (i + 2 * s) % fsize) for i in range(fsize)])
+        source = (chip - s) % chips
+        got_a = jnp.where(source == owner_a // 2, recv[0], got_a)
+        got_b = jnp.where(source == owner_b // 2, recv[1], got_b)
     piece = jnp.stack([got_a, got_b])
     piece, early = lax.optimization_barrier((piece, early))
     pieces = [piece]

time: 62 us -> 62.7 us (1.011)
  waiting for transfers between devices: 21.2 us -> 23.8 us
  matrix products: 11.4 us -> 10.1 us
    ppermute x3 -> x2, waiting for transfers between devices: 0.82 us -> 3.42 us  [the longest x1 3.42 us: gather_keyframes(): lax.ppermute(cand, 'frame', [(i, (i + 2 * s) % fsize) for i in range(fsiz...]
    dot_general x1, matrix products: 2.55 us -> 1.18 us  [shards(): jnp.dot(flattened, w_query, preferred_element_type=jnp.float32)]
    ppermute x3 -> x2, starting transfers between devices: 3.29 us -> 2.02 us  [the longest x1 1.28 us: gather_keyframes(): lax.ppermute(cand, 'frame', [(i, (i + 2 * s) % fsize) for i in range(fsiz...]
    ppermute x1, starting transfers between devices: 2.44 us -> 3.37 us  [extended(): before = lax.ppermute(last, axis, up)]
    unnamed x12 -> x14, local copies, waits for them, and re-layouts: 1.55 us -> 1.55 us
  transfers between devices with their start and end apart: 9 -> 8, of which waited for: 7 -> 7; matrix products, arithmetic and copies ran while one was open for 9% -> 6% of each run, Pallas kernels for 0% -> 0%
where the time goes in v8:
time: 62.7 us; the launch traced here: 62.4 us
  waiting for transfers between devices  23.8 us (38%)
  starting transfers between devices  11.7 us (19%)
  matrix products  10.1 us (16%)
  Pallas kernels  8.06 us (13%)
  local copies, waits for them, and re-layouts  4.06 us (6%)
  other arithmetic  3.17 us (5%)
  between operations  1.55 us (2%)
    ppermute x3, waiting for transfers between devices, gather_keyframes(): lax.ppermute(piece, 'row', [(i, (i + s) % rsize) for i in range(rsize)])  13.7 us
    pallas_call x1, Pallas kernels, attend(): pl.pallas_call(attention_kernel, grid=(pairs, total // q_tile), in_specs=...  8.06 us
    dot_general x6, matrix products, temporal_mix(): jnp.dot(window, weights[offset], preferred_element_type=jnp.float32)  4.43 us
    ppermute x1, waiting for transfers between devices, extended(): after = lax.ppermute(first, axis, down)  4.4 us
    ppermute x3, starting transfers between devices, gather_keyframes(): lax.ppermute(piece, 'row', [(i, (i + s) % rsize) for i in range(rsize)])  3.83 us
    ppermute x1, waiting for transfers between devices, gather_keyframes(): lax.ppermute(cand, 'frame', [(i, (i + 2 * s) % fsize) for i in range(fsiz...  3.42 us
    ppermute x1, starting transfers between devices, extended(): before = lax.ppermute(last, axis, up)  3.37 us
    ppermute x1, waiting for transfers between devices, extended(): before = lax.ppermute(last, axis, up)  2.05 us
  transfers between devices with their start and end apart: 8, of which 7 were waited for; matrix products, arithmetic and copies ran while one was open for 6% of the time, Pallas kernels for 0%

profile of v8, /device:TPU:9, one launch (start us, length us, event | category | flops | bytes accessed | tf_op | source)
XLA Modules:
  0.0 62.4 jit_solution(10594765484838582199)
XLA Ops:
  0.0 1.2 %constant_dynamic-slice_fusion = (bf16[2,64,640]{2,1,0:T(8,128)(2,1)S(1)}, bf16[2,64,640]{2,1,0:T(8,128)(2,1)S(1)}) fusion(bf16[2,128,640]{2,1,0:T(8,128)(2,1)} %param.8, s32[]{:T(128)S(6)} %select_n.85, s32[]{:T(128)S(6)} %select_n.84), kind=kLoop, calls=%fused_computation.59 | loop fusion | bytes 655368 | tf_op jit(solution)/shard_map/dynamic_slice | solution.py:77
  1.2 0.7 %collective-permute-start = (bf16[2,64,640]{2,1,0:T(8,128)(2,1)S(1)}, bf16[2,64,640]{2,1,0:T(8,128)(2,1)S(1)}, u32[]{:S(2)}, u32[]{:S(2)}) collective-permute-start(bf16[2,64,640]{2,1,0:T(8,128)(2,1)S(1)} %get-tuple-element.16), channel_id=1, source_target_pairs={{0,4},{4,0},{8,12},{12,8},{1,5},{5,1},{9,13},{13,9},{2,6},{6,2},{1... | collective-permute-start | bytes 491528 | tf_op jit(solution)/shard_map/ppermute | solution.py:79
  1.9 1.3 %fusion.29 = (s32[1]{0:T(128)}, s32[1]{0:T(128)}) fusion(s32[2]{0:T(128)} %param.9), kind=kLoop, calls=%fused_computation.63 | loop fusion | bytes 16 | tf_op jit(solution)/shard_map/slice | solution.py:67
  4.7 1.3 %collective-permute-start.1 = (bf16[2,64,640]{2,1,0:T(8,128)(2,1)S(1)}, bf16[2,64,640]{2,1,0:T(8,128)(2,1)S(1)}, u32[]{:S(2)}, u32[]{:S(2)}) collective-permute-start(bf16[2,64,640]{2,1,0:T(8,128)(2,1)S(1)} %pad_maximum_fusion.9), channel_id=1, source_target_pairs={{0,8},{4,12},{8,0},{12,4},{1,9},{5,13},{9,1},{13,5},{2,10},{6,14},... | collective-permute-start | bytes 491528 | tf_op jit(solution)/shard_map/ppermute | solution.py:92
  6.0 1.2 %convolution_convert_fusion.4.q_ref = bf16[256,640]{1,0:T(8,128)(2,1)} fusion(bf16[256,640]{1,0:T(8,128)(2,1)S(1)} %bitcast.54, bf16[640,640]{1,0:T(8,128)(2,1)S(1)} %copy-done.4), kind=kOutput, calls=%fused_computation.16 | convolution fusion | flops 209879040 | bytes 1474560 | tf_op jit(solution)/shard_map/dot_general | solution.py:110
  7.2 3.4 %collective-permute-done.1 = bf16[2,64,640]{2,1,0:T(8,128)(2,1)S(1)} collective-permute-done((bf16[2,64,640]{2,1,0:T(8,128)(2,1)S(1)}, bf16[2,64,640]{2,1,0:T(8,128)(2,1)S(1)}, u32[]{:S(2)}, u32[]{:S(2)}) %collective-permute-start.1) | collective-permute-done | bytes 163872 | tf_op jit(solution)/shard_map/ppermute | solution.py:92
  10.7 1.3 %collective-permute-start.2 = (bf16[2,64,640]{2,1,0:T(8,128)(2,1)S(1)}, bf16[2,64,640]{2,1,0:T(8,128)(2,1)S(1)}, u32[]{:S(2)}, u32[]{:S(2)}) collective-permute-start(bf16[2,64,640]{2,1,0:T(8,128)(2,1)S(1)} %pad_maximum_fusion.10), channel_id=1, source_target_pairs={{0,1},{1,2},{2,3},{3,0},{4,5},{5,6},{6,7},{7,4},{8,9},{9,10},{10,1... | collective-permute-start | bytes 491528 | tf_op jit(solution)/shard_map/ppermute | solution.py:100
  12.0 1.1 %collective-permute-start.3 = (bf16[2,64,640]{2,1,0:T(8,128)(2,1)S(1)}, bf16[2,64,640]{2,1,0:T(8,128)(2,1)S(1)}, u32[]{:S(2)}, u32[]{:S(2)}) collective-permute-start(bf16[2,64,640]{2,1,0:T(8,128)(2,1)S(1)} %pad_maximum_fusion.10), channel_id=1, source_target_pairs={{0,2},{1,3},{2,0},{3,1},{4,6},{5,7},{6,4},{7,5},{8,10},{9,11},{10,... | collective-permute-start | bytes 491528 | tf_op jit(solution)/shard_map/ppermute | solution.py:100
  13.1 1.4 %collective-permute-start.4 = (bf16[2,64,640]{2,1,0:T(8,128)(2,1)S(1)}, bf16[2,64,640]{2,1,0:T(8,128)(2,1)S(1)}, u32[]{:S(2)}, u32[]{:S(2)}) collective-permute-start(bf16[2,64,640]{2,1,0:T(8,128)(2,1)S(1)} %pad_maximum_fusion.10), channel_id=1, source_target_pairs={{0,3},{1,0},{2,1},{3,2},{4,7},{5,4},{6,5},{7,6},{8,11},{9,8},{10,9... | collective-permute-start | bytes 491528 | tf_op jit(solution)/shard_map/ppermute | solution.py:100
  14.5 1.2 %collective-permute-done.2 = bf16[2,64,640]{2,1,0:T(8,128)(2,1)S(1)} collective-permute-done((bf16[2,64,640]{2,1,0:T(8,128)(2,1)S(1)}, bf16[2,64,640]{2,1,0:T(8,128)(2,1)S(1)}, u32[]{:S(2)}, u32[]{:S(2)}) %collective-permute-start.2) | collective-permute-done | bytes 163872 | tf_op jit(solution)/shard_map/ppermute | solution.py:100
  15.6 9.6 %collective-permute-done.3 = bf16[2,64,640]{2,1,0:T(8,128)(2,1)S(1)} collective-permute-done((bf16[2,64,640]{2,1,0:T(8,128)(2,1)S(1)}, bf16[2,64,640]{2,1,0:T(8,128)(2,1)S(1)}, u32[]{:S(2)}, u32[]{:S(2)}) %collective-permute-start.3) | collective-permute-done | bytes 163872 | tf_op jit(solution)/shard_map/ppermute | solution.py:100
  25.3 2.9 %collective-permute-done.4 = bf16[2,64,640]{2,1,0:T(8,128)(2,1)S(1)} collective-permute-done((bf16[2,64,640]{2,1,0:T(8,128)(2,1)S(1)}, bf16[2,64,640]{2,1,0:T(8,128)(2,1)S(1)}, u32[]{:S(2)}, u32[]{:S(2)}) %collective-permute-start.4) | collective-permute-done | bytes 163872 | tf_op jit(solution)/shard_map/ppermute | solution.py:100
  28.3 0.6 collective-permute-start.5
  28.9 0.7 %convolution_convert_fusion.1 = bf16[512,640]{1,0:T(8,128)(2,1)S(1)} fusion(bf16[512,640]{1,0:T(8,128)(2,1)S(1)} %bitcast.66, bf16[640,1280]{1,0:T(8,128)(2,1)S(1)} %copy-done.6), kind=kOutput, calls=%fused_computation.3 | convolution fusion | flops 419758080 | bytes 2129920 | tf_op jit(solution)/shard_map/dot_general | solution.py:118
  29.6 0.7 %fusion.1 = bf16[640,512]{1,0:T(8,128)(2,1)S(1)} fusion(bf16[512,640]{1,0:T(8,128)(2,1)S(1)} %bitcast.67, bf16[640,1280]{1,0:T(8,128)(2,1)S(1)} %copy-done.6), kind=kOutput, calls=%fused_computation.9 | convolution fusion | flops 419758080 | bytes 2129920 | tf_op jit(solution)/shard_map/dot_general | solution.py:115
  30.6 0.7 %convolution_convert_fusion = bf16[512,640]{1,0:T(8,128)(2,1)S(1)} fusion(bf16[512,640]{1,0:T(8,128)(2,1)S(1)} %collective-permute-done.5, bf16[640,1280]{1,0:T(8,128)(2,1)S(1)} %copy-done.6), kind=kOutput, calls=%fused_computation.2 | convolution fusion | flops 419758080 | bytes 2129920 | tf_op jit(solution)/shard_map/dot_general | solution.py:118
  31.4 1.2 %pad_maximum_fusion.1.v_ref = bf16[1024,640]{1,0:T(8,128)(2,1)} fusion(bf16[512,640]{1,0:T(8,128)(2,1)S(1)} %convolution_convert_fusion, bf16[512,640]{1,0:T(8,128)(2,1)S(1)} %convolution_convert_fusion.1), kind=kLoop, calls=%fused_computation.7 | loop fusion | flops 2621440 | bytes 2621440 | tf_op jit(solution)/shard_map/concatenate | solution.py:124
  32.5 0.7 %fusion.2 = bf16[640,512]{1,0:T(8,128)(2,1)S(1)} fusion(bf16[512,640]{1,0:T(8,128)(2,1)S(1)} %collective-permute-done.5, bf16[640,1280]{1,0:T(8,128)(2,1)S(1)} %copy-done.6), kind=kOutput, calls=%fused_computation.10 | convolution fusion | flops 419758080 | bytes 2129920 | tf_op jit(solution)/shard_map/dot_general | solution.py:115
  33.3 1.2 %pad_maximum_fusion.kt_ref = bf16[640,1024]{1,0:T(8,128)(2,1)} fusion(bf16[640,512]{1,0:T(8,128)(2,1)S(1)} %fusion.2, bf16[640,512]{1,0:T(8,128)(2,1)S(1)} %fusion.1), kind=kLoop, calls=%fused_computation.6 | loop fusion | flops 2621440 | bytes 2621440 | tf_op jit(solution)/shard_map/concatenate | solution.py:123
  34.5 8.1 %shard_map.82 = bf16[256,640]{1,0:T(8,128)(2,1)} custom-call(bf16[256,640]{1,0:T(8,128)(2,1)} %convolution_convert_fusion.4.q_ref, bf16[640,1024]{1,0:T(8,128)(2,1)} %pad_maximum_fusion.kt_ref, bf16[1024,640]{1,0:T(8,128)(2,1)} %pad_maximum_fusion.1.v_ref), custom_call_target="tpu_custom_call" | custom-call | tf_op jit(solution)/shard_map/pallas_call | solution.py:30
  42.6 1.5 %multiply_reduce_fusion = (f32[256]{0:T(256)S(1)}, f32[256,640]{1,0:T(8,128)S(1)}) fusion(bf16[256,640]{1,0:T(8,128)(2,1)} %shard_map.82, bf16[640,640]{1,0:T(8,128)(2,1)S(1)} %copy-done, bf16[256,640]{1,0:T(8,128)(2,1)S(1)} %bitcast.55), kind=kOutput, calls=%fused_computation.42 | convolution fusion | flops 210370304 | bytes 2130944 | tf_op jit(solution)/shard_map/dot_general | solution.py:126
  44.3 3.4 %collective-permute-start.6 = (bf16[2,128,640]{2,1,0:T(8,128)(2,1)S(1)}, bf16[2,128,640]{2,1,0:T(8,128)(2,1)S(1)}, u32[]{:S(2)}, u32[]{:S(2)}) collective-permute-start(bf16[2,128,640]{2,1,0:T(8,128)(2,1)S(1)} %bitcast.61), channel_id=1, source_target_pairs={{0,4},{4,8},{8,12},{1,5},{5,9},{9,13},{2,6},{6,10},{10,14},{3,7},{... | collective-permute-start | bytes 983048 | tf_op jit(solution)/shard_map/ppermute | solution.py:48
  47.6 1.9 %collective-permute-start.7 = (bf16[2,128,640]{2,1,0:T(8,128)(2,1)S(1)}, bf16[2,128,640]{2,1,0:T(8,128)(2,1)S(1)}, u32[]{:S(2)}, u32[]{:S(2)}) collective-permute-start(bf16[2,128,640]{2,1,0:T(8,128)(2,1)S(1)} %bitcast.62), channel_id=1, source_target_pairs={{4,0},{8,4},{12,8},{5,1},{9,5},{13,9},{6,2},{10,6},{14,10},{7,3},{... | collective-permute-start | bytes 983048 | tf_op jit(solution)/shard_map/ppermute | solution.py:49
  49.6 2.0 %collective-permute-done.6 = bf16[2,128,640]{2,1,0:T(8,128)(2,1)S(1)} collective-permute-done((bf16[2,128,640]{2,1,0:T(8,128)(2,1)S(1)}, bf16[2,128,640]{2,1,0:T(8,128)(2,1)S(1)}, u32[]{:S(2)}, u32[]{:S(2)}) %collective-permute-start.6) | collective-permute-done | bytes 327712 | tf_op jit(solution)/shard_map/ppermute | solution.py:48
  51.6 4.4 %collective-permute-done.7 = bf16[2,128,640]{2,1,0:T(8,128)(2,1)S(1)} collective-permute-done((bf16[2,128,640]{2,1,0:T(8,128)(2,1)S(1)}, bf16[2,128,640]{2,1,0:T(8,128)(2,1)S(1)}, u32[]{:S(2)}, u32[]{:S(2)}) %collective-permute-start.7) | collective-permute-done | bytes 327712 | tf_op jit(solution)/shard_map/ppermute | solution.py:49
  56.3 0.7 %fusion.11 = f32[512,640]{1,0:T(8,128)S(1)} fusion(bf16[512,640]{1,0:T(8,128)(2,1)S(1)} %bitcast.57, bf16[3,640,640]{2,1,0:T(8,128)(2,1)S(1)} %copy-done.3), kind=kOutput, calls=%fused_computation.23 | convolution fusion | flops 419430400 | bytes 2785280 | tf_op jit(solution)/shard_map/dot_general | solution.py:57
  57.0 0.7 %fusion.9 = f32[512,640]{1,0:T(8,128)S(1)} fusion(bf16[512,640]{1,0:T(8,128)(2,1)S(1)} %bitcast.56, bf16[3,640,640]{2,1,0:T(8,128)(2,1)S(1)} %copy-done.3), kind=kOutput, calls=%fused_computation.21 | convolution fusion | flops 419430400 | bytes 2785280 | tf_op jit(solution)/shard_map/dot_general | solution.py:57
  57.8 0.8 %multiply_convert_fusion = bf16[512,640]{1,0:T(8,128)(2,1)S(1)} fusion(f32[512,640]{1,0:T(8,128)S(1)} %fusion.9, f32[512,640]{1,0:T(8,128)S(1)} %fusion.11, bf16[512,640]{1,0:T(8,128)(2,1)S(1)} %bitcast.68, bf16[3,640,640]{2,1,0:T(8,128)(2,1)S(1)} %copy-done.3), kind=kOutput, calls=%fused_computation.8 | convolution fusion | flops 421724160 | bytes 4751360 | tf_op jit(solution)/shard_map/dot_general | solution.py:57
  58.8 1.5 %copy-done.2 = bf16[3,640,640]{2,1,0:T(8,128)(2,1)S(1)} copy-done((bf16[3,640,640]{2,1,0:T(8,128)(2,1)S(1)}, bf16[3,640,640]{2,1,0:T(8,128)(2,1)}, u32[]{:S(2)}) %copy-start.2) | copy-done | bytes 2457624
  60.3 0.5 fusion.7
  60.8 0.5 convolution_add_fusion.2
  61.3 1.2 %fusion.4 = bf16[256,640]{1,0:T(8,128)(2,1)} fusion(f32[256,640]{1,0:T(8,128)S(1)} %get-tuple-element.23, f32[256,640]{1,0:T(8,128)S(1)} %convolution_add_fusion.2, bf16[256,640]{1,0:T(8,128)(2,1)S(1)} %bitcast.60, bf16[3,640,640]{2,1,0:T(8,128)(2,1)S(1)} %copy-done.2), kind=kOutput, calls=%fused_computation.15 | convolution fusion | flops 210206720 | bytes 2785280 | tf_op jit(solution)/shard_map/dot_general | solution.py:57
  (26 shorter events, 1.0 us)
Async XLA Ops:
  0.0 42.6 %copy-start = (bf16[640,640]{1,0:T(8,128)(2,1)S(1)}, bf16[640,640]{1,0:T(8,128)(2,1)}, u32[]{:S(2)}) copy-start(bf16[640,640]{1,0:T(8,128)(2,1)} %param.12) | copy-start | bytes 2457604
  0.0 6.0 %copy-start.1 = (bf16[2,128,640]{2,1,0:T(8,128)(2,1)S(1)}, bf16[2,128,640]{2,1,0:T(8,128)(2,1)}, u32[]{:S(2)}) copy-start(bf16[2,128,640]{2,1,0:T(8,128)(2,1)} %param.8) | copy-start | bytes 983044
  0.0 6.0 %copy-start.4 = (bf16[640,640]{1,0:T(8,128)(2,1)S(1)}, bf16[640,640]{1,0:T(8,128)(2,1)}, u32[]{:S(2)}) copy-start(bf16[640,640]{1,0:T(8,128)(2,1)} %param.10) | copy-start | bytes 2457604
  1.2 3.4 %collective-permute-start = (bf16[2,64,640]{2,1,0:T(8,128)(2,1)S(1)}, bf16[2,64,640]{2,1,0:T(8,128)(2,1)S(1)}, u32[]{:S(2)}, u32[]{:S(2)}) collective-permute-start(bf16[2,64,640]{2,1,0:T(8,128)(2,1)S(1)} %get-tuple-element.16), channel_id=1, source_target_pairs={{0,4},{4,0},{8,12},{12,8},{1,5},{5,1},{9,13},{13,9},{2,6},{6,2},{1... | collective-permute-start | bytes 491528 | tf_op jit(solution)/shard_map/ppermute | solution.py:79
  4.7 5.9 %collective-permute-start.1 = (bf16[2,64,640]{2,1,0:T(8,128)(2,1)S(1)}, bf16[2,64,640]{2,1,0:T(8,128)(2,1)S(1)}, u32[]{:S(2)}, u32[]{:S(2)}) collective-permute-start(bf16[2,64,640]{2,1,0:T(8,128)(2,1)S(1)} %pad_maximum_fusion.9), channel_id=1, source_target_pairs={{0,8},{4,12},{8,0},{12,4},{1,9},{5,13},{9,1},{13,5},{2,10},{6,14},... | collective-permute-start | bytes 491528 | tf_op jit(solution)/shard_map/ppermute | solution.py:92
  6.0 22.9 %copy-start.6 = (bf16[640,1280]{1,0:T(8,128)(2,1)S(1)}, bf16[640,1280]{1,0:T(8,128)(2,1)}, u32[]{:S(2)}) copy-start(bf16[640,1280]{1,0:T(8,128)(2,1)} %param.11) | copy-start | bytes 4915204
  10.7 5.0 %collective-permute-start.2 = (bf16[2,64,640]{2,1,0:T(8,128)(2,1)S(1)}, bf16[2,64,640]{2,1,0:T(8,128)(2,1)S(1)}, u32[]{:S(2)}, u32[]{:S(2)}) collective-permute-start(bf16[2,64,640]{2,1,0:T(8,128)(2,1)S(1)} %pad_maximum_fusion.10), channel_id=1, source_target_pairs={{0,1},{1,2},{2,3},{3,0},{4,5},{5,6},{6,7},{7,4},{8,9},{9,10},{10,1... | collective-permute-start | bytes 491528 | tf_op jit(solution)/shard_map/ppermute | solution.py:100
  12.0 13.3 %collective-permute-start.3 = (bf16[2,64,640]{2,1,0:T(8,128)(2,1)S(1)}, bf16[2,64,640]{2,1,0:T(8,128)(2,1)S(1)}, u32[]{:S(2)}, u32[]{:S(2)}) collective-permute-start(bf16[2,64,640]{2,1,0:T(8,128)(2,1)S(1)} %pad_maximum_fusion.10), channel_id=1, source_target_pairs={{0,2},{1,3},{2,0},{3,1},{4,6},{5,7},{6,4},{7,5},{8,10},{9,11},{10,... | collective-permute-start | bytes 491528 | tf_op jit(solution)/shard_map/ppermute | solution.py:100
  13.1 15.1 %collective-permute-start.4 = (bf16[2,64,640]{2,1,0:T(8,128)(2,1)S(1)}, bf16[2,64,640]{2,1,0:T(8,128)(2,1)S(1)}, u32[]{:S(2)}, u32[]{:S(2)}) collective-permute-start(bf16[2,64,640]{2,1,0:T(8,128)(2,1)S(1)} %pad_maximum_fusion.10), channel_id=1, source_target_pairs={{0,3},{1,0},{2,1},{3,2},{4,7},{5,4},{6,5},{7,6},{8,11},{9,8},{10,9... | collective-permute-start | bytes 491528 | tf_op jit(solution)/shard_map/ppermute | solution.py:100
  28.3 2.3 %collective-permute-start.5 = (bf16[512,640]{1,0:T(8,128)(2,1)S(1)}, bf16[512,640]{1,0:T(8,128)(2,1)S(1)}, u32[]{:S(2)}, u32[]{:S(2)}) collective-permute-start(bf16[512,640]{1,0:T(8,128)(2,1)S(1)} %bitcast.65), channel_id=1, source_target_pairs={{0,4},{4,0},{8,12},{12,8},{1,5},{5,1},{9,13},{13,9},{2,6},{6,2},{1... | collective-permute-start | bytes 1966088 | tf_op jit(solution)/shard_map/ppermute | solution.py:102
  42.6 1.6 %copy-start.5 = (f32[640]{0:T(1024)S(1)}, f32[640]{0:T(1024)}, u32[]{:S(2)}) copy-start(f32[640]{0:T(1024)} %param.13) | copy-start | bytes 7684
  44.3 7.4 %collective-permute-start.6 = (bf16[2,128,640]{2,1,0:T(8,128)(2,1)S(1)}, bf16[2,128,640]{2,1,0:T(8,128)(2,1)S(1)}, u32[]{:S(2)}, u32[]{:S(2)}) collective-permute-start(bf16[2,128,640]{2,1,0:T(8,128)(2,1)S(1)} %bitcast.61), channel_id=1, source_target_pairs={{0,4},{4,8},{8,12},{1,5},{5,9},{9,13},{2,6},{6,10},{10,14},{3,7},{... | collective-permute-start | bytes 983048 | tf_op jit(solution)/shard_map/ppermute | solution.py:48
  47.6 8.4 %collective-permute-start.7 = (bf16[2,128,640]{2,1,0:T(8,128)(2,1)S(1)}, bf16[2,128,640]{2,1,0:T(8,128)(2,1)S(1)}, u32[]{:S(2)}, u32[]{:S(2)}) collective-permute-start(bf16[2,128,640]{2,1,0:T(8,128)(2,1)S(1)} %bitcast.62), channel_id=1, source_target_pairs={{4,0},{8,4},{12,8},{5,1},{9,5},{13,9},{6,2},{10,6},{14,10},{7,3},{... | collective-permute-start | bytes 983048 | tf_op jit(solution)/shard_map/ppermute | solution.py:49
  49.6 6.7 %copy-start.3 = (bf16[3,640,640]{2,1,0:T(8,128)(2,1)S(1)}, bf16[3,640,640]{2,1,0:T(8,128)(2,1)}, u32[]{:S(2)}) copy-start(bf16[3,640,640]{2,1,0:T(8,128)(2,1)} %param.14) | copy-start | bytes 7372804
  58.6 1.7 %copy-start.2 = (bf16[3,640,640]{2,1,0:T(8,128)(2,1)S(1)}, bf16[3,640,640]{2,1,0:T(8,128)(2,1)}, u32[]{:S(2)}) copy-start(bf16[3,640,640]{2,1,0:T(8,128)(2,1)} %param.15) | copy-start | bytes 7372804

commit v9 on v7

--- a/solution.py
+++ b/solution.py
@@ -85,10 +85,8 @@
         got_b = jnp.where(source == owner_b, recv[n_loc - 1], got_b)
     piece = jnp.stack([got_a, got_b])
     piece, early = lax.optimization_barrier((piece, early))
-    pieces = [piece]
-    for s in range(1, rsize):
-        pieces.append(lax.ppermute(piece, "row", [(i, (i + s) % rsize) for i in range(rsize)]))
-    mine = jnp.stack(pieces).reshape(-1, channels)
+    copies = jnp.broadcast_to(piece[None], (rsize,) + piece.shape)
+    mine = lax.all_to_all(copies, "row", 0, 0, tiled=True).reshape(-1, channels)
     sibling = lax.ppermute(mine, "frame", [(i, i ^ 1) for i in range(fsize)])
     return mine, sibling
 

time: 62 us -> 67.3 us (1.085)
  the two profiles are of different devices: /device:TPU:9 before, /device:TPU:1 now
where the time goes in v9:
time: 67.3 us; the launch traced here: 67 us
  blocking collectives  20.8 us (31%)
  matrix products  11.3 us (17%)
  starting transfers between devices  10.4 us (15%)
  Pallas kernels  7.99 us (12%)
  waiting for transfers between devices  7.69 us (11%)
  local copies, waits for them, and re-layouts  4.15 us (6%)
  other arithmetic  3.05 us (5%)
  between operations  1.6 us (2%)
    all_to_all x1, blocking collectives, gather_keyframes(): mine = lax.all_to_all(copies, 'row', 0, 0, tiled=True).reshape(-1, channels)  20.8 us
    pallas_call x1, Pallas kernels, attend(): pl.pallas_call(attention_kernel, grid=(pairs, total // q_tile), in_specs=...  7.99 us
    dot_general x6, matrix products, temporal_mix(): jnp.dot(window, weights[offset], preferred_element_type=jnp.float32)  4.43 us
    ppermute x1, waiting for transfers between devices, extended(): after = lax.ppermute(first, axis, down)  4.4 us
    ppermute x3, starting transfers between devices, gather_keyframes(): lax.ppermute(halves((me + s) % 2), 'frame', [(i, (i + s) % fsize) for i i...  4.12 us
    ppermute x1, starting transfers between devices, extended(): before = lax.ppermute(last, axis, up)  2.48 us
    dot_general x1, matrix products, shards(): jnp.dot(flattened, w_query, preferred_element_type=jnp.float32)  2.44 us
    ppermute x1, waiting for transfers between devices, extended(): before = lax.ppermute(last, axis, up)  2.05 us
  transfers between devices with their start and end apart: 6, of which 4 were waited for; matrix products, arithmetic and copies ran while one was open for 8% of the time, Pallas kernels for 0%

profile of v9, /device:TPU:1, one launch (start us, length us, event | category | flops | bytes accessed | tf_op | source)
XLA Modules:
  0.0 67.0 jit_solution(9096236093844156759)
XLA Ops:
  0.0 1.2 %constant_dynamic-slice_fusion.2 = (bf16[2,64,640]{2,1,0:T(8,128)(2,1)S(1)}, bf16[2,64,640]{2,1,0:T(8,128)(2,1)S(1)}, bf16[2,64,640]{2,1,0:T(8,128)(2,1)S(1)}) fusion(bf16[2,128,640]{2,1,0:T(8,128)(2,1)} %param.8, s32[]{:T(128)S(6)} %select_n.137, s32[]{:T(128)S(6)} %select_n.147, s32[]{:T(128)S(6)} %select_n.143), kind=kLoop, calls=%fused_computation.55 | loop fusion | bytes 983052 | tf_op jit(solution)/shard_map/dynamic_slice | solution.py:74
  1.2 0.1 collective-permute-start
  1.3 2.7 %collective-permute-start.1 = (bf16[2,64,640]{2,1,0:T(8,128)(2,1)S(1)}, bf16[2,64,640]{2,1,0:T(8,128)(2,1)S(1)}, u32[]{:S(2)}, u32[]{:S(2)}) collective-permute-start(bf16[2,64,640]{2,1,0:T(8,128)(2,1)S(1)} %get-tuple-element.18), channel_id=1, source_target_pairs={{0,8},{4,12},{8,0},{12,4},{1,9},{5,13},{9,1},{13,5},{2,10},{6,14},... | collective-permute-start | bytes 491528 | tf_op jit(solution)/shard_map/ppermute | solution.py:82
  4.0 1.3 %collective-permute-start.2 = (bf16[2,64,640]{2,1,0:T(8,128)(2,1)S(1)}, bf16[2,64,640]{2,1,0:T(8,128)(2,1)S(1)}, u32[]{:S(2)}, u32[]{:S(2)}) collective-permute-start(bf16[2,64,640]{2,1,0:T(8,128)(2,1)S(1)} %get-tuple-element.17), channel_id=1, source_target_pairs={{0,4},{4,8},{8,12},{12,0},{1,5},{5,9},{9,13},{13,1},{2,6},{6,10},{... | collective-permute-start | bytes 491528 | tf_op jit(solution)/shard_map/ppermute | solution.py:82
  5.3 1.3 %fusion.29 = (s32[1]{0:T(128)}, s32[1]{0:T(128)}) fusion(s32[2]{0:T(128)} %param.9), kind=kLoop, calls=%fused_computation.58 | loop fusion | bytes 16 | tf_op jit(solution)/shard_map/slice | solution.py:67
  8.1 2.4 %convolution_convert_fusion.4.q_ref = bf16[256,640]{1,0:T(8,128)(2,1)} fusion(bf16[256,640]{1,0:T(8,128)(2,1)} %bitcast.50, bf16[640,640]{1,0:T(8,128)(2,1)} %param.10), kind=kOutput, calls=%fused_computation.16 | convolution fusion | flops 209879040 | bytes 1474560 | tf_op jit(solution)/shard_map/dot_general | solution.py:98
  10.5 1.0 %collective-permute-done.2 = bf16[2,64,640]{2,1,0:T(8,128)(2,1)S(1)} collective-permute-done((bf16[2,64,640]{2,1,0:T(8,128)(2,1)S(1)}, bf16[2,64,640]{2,1,0:T(8,128)(2,1)S(1)}, u32[]{:S(2)}, u32[]{:S(2)}) %collective-permute-start.2) | collective-permute-done | bytes 163872 | tf_op jit(solution)/shard_map/ppermute | solution.py:82
  11.5 0.1 select_select_fusion
  11.7 20.8 %all_to_all.5 = bf16[4,2,64,640]{3,2,1,0:T(8,128)(2,1)S(1)} all-to-all(bf16[4,2,64,640]{3,2,1,0:T(8,128)(2,1)S(1)} %broadcast_in_dim.7), channel_id=1, replica_groups=mesh['clips'=2,'frame'=4,'row'=4] {'row'}, dimensions={0} | all-to-all | bytes 1310720 | tf_op jit(solution)/shard_map/all_to_all | solution.py:89
  32.5 1.9 %collective-permute-start.3 = (bf16[512,640]{1,0:T(8,128)(2,1)S(1)}, bf16[512,640]{1,0:T(8,128)(2,1)S(1)}, u32[]{:S(2)}, u32[]{:S(2)}) collective-permute-start(bf16[512,640]{1,0:T(8,128)(2,1)S(1)} %bitcast.60), channel_id=1, source_target_pairs={{0,4},{4,0},{8,12},{12,8},{1,5},{5,1},{9,13},{13,9},{2,6},{6,2},{1... | collective-permute-start | bytes 1966088 | tf_op jit(solution)/shard_map/ppermute | solution.py:90
  34.4 0.7 %convolution_convert_fusion.1 = bf16[512,640]{1,0:T(8,128)(2,1)S(1)} fusion(bf16[512,640]{1,0:T(8,128)(2,1)S(1)} %bitcast.61, bf16[640,1280]{1,0:T(8,128)(2,1)S(1)} %copy-done.5), kind=kOutput, calls=%fused_computation.3 | convolution fusion | flops 419758080 | bytes 2129920 | tf_op jit(solution)/shard_map/dot_general | solution.py:106
  35.1 0.7 %fusion.1 = bf16[640,512]{1,0:T(8,128)(2,1)S(1)} fusion(bf16[512,640]{1,0:T(8,128)(2,1)S(1)} %bitcast.62, bf16[640,1280]{1,0:T(8,128)(2,1)S(1)} %copy-done.5), kind=kOutput, calls=%fused_computation.9 | convolution fusion | flops 419758080 | bytes 2129920 | tf_op jit(solution)/shard_map/dot_general | solution.py:103
  35.8 0.2 collective-permute-done.3
  36.1 0.7 %convolution_convert_fusion = bf16[512,640]{1,0:T(8,128)(2,1)S(1)} fusion(bf16[512,640]{1,0:T(8,128)(2,1)S(1)} %collective-permute-done.3, bf16[640,1280]{1,0:T(8,128)(2,1)S(1)} %copy-done.5), kind=kOutput, calls=%fused_computation.2 | convolution fusion | flops 419758080 | bytes 2129920 | tf_op jit(solution)/shard_map/dot_general | solution.py:106
  36.8 1.2 %pad_maximum_fusion.1.v_ref = bf16[1024,640]{1,0:T(8,128)(2,1)} fusion(bf16[512,640]{1,0:T(8,128)(2,1)S(1)} %convolution_convert_fusion, bf16[512,640]{1,0:T(8,128)(2,1)S(1)} %convolution_convert_fusion.1), kind=kLoop, calls=%fused_computation.7 | loop fusion | flops 2621440 | bytes 2621440 | tf_op jit(solution)/shard_map/concatenate | solution.py:112
  38.0 0.7 %fusion.2 = bf16[640,512]{1,0:T(8,128)(2,1)S(1)} fusion(bf16[512,640]{1,0:T(8,128)(2,1)S(1)} %collective-permute-done.3, bf16[640,1280]{1,0:T(8,128)(2,1)S(1)} %copy-done.5), kind=kOutput, calls=%fused_computation.10 | convolution fusion | flops 419758080 | bytes 2129920 | tf_op jit(solution)/shard_map/dot_general | solution.py:103
  38.8 1.2 %pad_maximum_fusion.kt_ref = bf16[640,1024]{1,0:T(8,128)(2,1)} fusion(bf16[640,512]{1,0:T(8,128)(2,1)S(1)} %fusion.2, bf16[640,512]{1,0:T(8,128)(2,1)S(1)} %fusion.1), kind=kLoop, calls=%fused_computation.6 | loop fusion | flops 2621440 | bytes 2621440 | tf_op jit(solution)/shard_map/concatenate | solution.py:111
  40.0 8.0 %shard_map.82 = bf16[256,640]{1,0:T(8,128)(2,1)} custom-call(bf16[256,640]{1,0:T(8,128)(2,1)} %convolution_convert_fusion.4.q_ref, bf16[640,1024]{1,0:T(8,128)(2,1)} %pad_maximum_fusion.kt_ref, bf16[1024,640]{1,0:T(8,128)(2,1)} %pad_maximum_fusion.1.v_ref), custom_call_target="tpu_custom_call" | custom-call | tf_op jit(solution)/shard_map/pallas_call | solution.py:30
  48.0 1.5 %multiply_reduce_fusion = (f32[256]{0:T(256)S(1)}, f32[256,640]{1,0:T(8,128)S(1)}) fusion(bf16[256,640]{1,0:T(8,128)(2,1)} %shard_map.82, bf16[640,640]{1,0:T(8,128)(2,1)S(1)} %copy-done, bf16[256,640]{1,0:T(8,128)(2,1)S(1)} %bitcast.51), kind=kOutput, calls=%fused_computation.41 | convolution fusion | flops 210370304 | bytes 2130944 | tf_op jit(solution)/shard_map/dot_general | solution.py:114
  49.6 0.1 multiply_convert_fusion.1
  49.7 2.5 %collective-permute-start.4 = (bf16[2,128,640]{2,1,0:T(8,128)(2,1)S(1)}, bf16[2,128,640]{2,1,0:T(8,128)(2,1)S(1)}, u32[]{:S(2)}, u32[]{:S(2)}) collective-permute-start(bf16[2,128,640]{2,1,0:T(8,128)(2,1)S(1)} %bitcast.57), channel_id=1, source_target_pairs={{0,4},{4,8},{8,12},{1,5},{5,9},{9,13},{2,6},{6,10},{10,14},{3,7},{... | collective-permute-start | bytes 983048 | tf_op jit(solution)/shard_map/ppermute | solution.py:48
  52.2 1.9 %collective-permute-start.5 = (bf16[2,128,640]{2,1,0:T(8,128)(2,1)S(1)}, bf16[2,128,640]{2,1,0:T(8,128)(2,1)S(1)}, u32[]{:S(2)}, u32[]{:S(2)}) collective-permute-start(bf16[2,128,640]{2,1,0:T(8,128)(2,1)S(1)} %bitcast.58), channel_id=1, source_target_pairs={{4,0},{8,4},{12,8},{5,1},{9,5},{13,9},{6,2},{10,6},{14,10},{7,3},{... | collective-permute-start | bytes 983048 | tf_op jit(solution)/shard_map/ppermute | solution.py:49
  54.1 2.0 %collective-permute-done.4 = bf16[2,128,640]{2,1,0:T(8,128)(2,1)S(1)} collective-permute-done((bf16[2,128,640]{2,1,0:T(8,128)(2,1)S(1)}, bf16[2,128,640]{2,1,0:T(8,128)(2,1)S(1)}, u32[]{:S(2)}, u32[]{:S(2)}) %collective-permute-start.4) | collective-permute-done | bytes 327712 | tf_op jit(solution)/shard_map/ppermute | solution.py:48
  56.2 4.4 %collective-permute-done.5 = bf16[2,128,640]{2,1,0:T(8,128)(2,1)S(1)} collective-permute-done((bf16[2,128,640]{2,1,0:T(8,128)(2,1)S(1)}, bf16[2,128,640]{2,1,0:T(8,128)(2,1)S(1)}, u32[]{:S(2)}, u32[]{:S(2)}) %collective-permute-start.5) | collective-permute-done | bytes 327712 | tf_op jit(solution)/shard_map/ppermute | solution.py:49
  60.6 0.2 pad_maximum_fusion.4
  60.8 0.7 %fusion.11 = f32[512,640]{1,0:T(8,128)S(1)} fusion(bf16[512,640]{1,0:T(8,128)(2,1)S(1)} %bitcast.53, bf16[3,640,640]{2,1,0:T(8,128)(2,1)S(1)} %copy-done.3), kind=kOutput, calls=%fused_computation.23 | convolution fusion | flops 419430400 | bytes 2785280 | tf_op jit(solution)/shard_map/dot_general | solution.py:57
  61.6 0.7 %fusion.9 = f32[512,640]{1,0:T(8,128)S(1)} fusion(bf16[512,640]{1,0:T(8,128)(2,1)S(1)} %bitcast.52, bf16[3,640,640]{2,1,0:T(8,128)(2,1)S(1)} %copy-done.3), kind=kOutput, calls=%fused_computation.21 | convolution fusion | flops 419430400 | bytes 2785280 | tf_op jit(solution)/shard_map/dot_general | solution.py:57
  62.3 0.8 %multiply_convert_fusion = bf16[512,640]{1,0:T(8,128)(2,1)S(1)} fusion(f32[512,640]{1,0:T(8,128)S(1)} %fusion.9, f32[512,640]{1,0:T(8,128)S(1)} %fusion.11, bf16[512,640]{1,0:T(8,128)(2,1)S(1)} %bitcast.63, bf16[3,640,640]{2,1,0:T(8,128)(2,1)S(1)} %copy-done.3), kind=kOutput, calls=%fused_computation.8 | convolution fusion | flops 421724160 | bytes 4751360 | tf_op jit(solution)/shard_map/dot_general | solution.py:57
  63.4 1.5 %copy-done.2 = bf16[3,640,640]{2,1,0:T(8,128)(2,1)S(1)} copy-done((bf16[3,640,640]{2,1,0:T(8,128)(2,1)S(1)}, bf16[3,640,640]{2,1,0:T(8,128)(2,1)}, u32[]{:S(2)}) %copy-start.2) | copy-done | bytes 2457624
  64.9 0.5 fusion.7
  65.3 0.5 convolution_add_fusion.2
  65.8 1.2 %fusion.4 = bf16[256,640]{1,0:T(8,128)(2,1)} fusion(f32[256,640]{1,0:T(8,128)S(1)} %get-tuple-element.22, f32[256,640]{1,0:T(8,128)S(1)} %convolution_add_fusion.2, bf16[256,640]{1,0:T(8,128)(2,1)S(1)} %bitcast.56, bf16[3,640,640]{2,1,0:T(8,128)(2,1)S(1)} %copy-done.2), kind=kOutput, calls=%fused_computation.15 | convolution fusion | flops 210206720 | bytes 2785280 | tf_op jit(solution)/shard_map/dot_general | solution.py:57
  (19 shorter events, 0.3 us)
Async XLA Ops:
  0.0 48.0 %copy-start = (bf16[640,640]{1,0:T(8,128)(2,1)S(1)}, bf16[640,640]{1,0:T(8,128)(2,1)}, u32[]{:S(2)}) copy-start(bf16[640,640]{1,0:T(8,128)(2,1)} %param.12) | copy-start | bytes 2457604
  0.0 11.5 %copy-start.1 = (bf16[2,128,640]{2,1,0:T(8,128)(2,1)S(1)}, bf16[2,128,640]{2,1,0:T(8,128)(2,1)}, u32[]{:S(2)}) copy-start(bf16[2,128,640]{2,1,0:T(8,128)(2,1)} %param.8) | copy-start | bytes 983044
  1.2 9.3 %collective-permute-start = (bf16[2,64,640]{2,1,0:T(8,128)(2,1)S(1)}, bf16[2,64,640]{2,1,0:T(8,128)(2,1)S(1)}, u32[]{:S(2)}, u32[]{:S(2)}) collective-permute-start(bf16[2,64,640]{2,1,0:T(8,128)(2,1)S(1)} %get-tuple-element.16), channel_id=1, source_target_pairs={{0,12},{4,0},{8,4},{12,8},{1,13},{5,1},{9,5},{13,9},{2,14},{6,2},{... | collective-permute-start | bytes 491528 | tf_op jit(solution)/shard_map/ppermute | solution.py:82
  1.3 9.2 %collective-permute-start.1 = (bf16[2,64,640]{2,1,0:T(8,128)(2,1)S(1)}, bf16[2,64,640]{2,1,0:T(8,128)(2,1)S(1)}, u32[]{:S(2)}, u32[]{:S(2)}) collective-permute-start(bf16[2,64,640]{2,1,0:T(8,128)(2,1)S(1)} %get-tuple-element.18), channel_id=1, source_target_pairs={{0,8},{4,12},{8,0},{12,4},{1,9},{5,13},{9,1},{13,5},{2,10},{6,14},... | collective-permute-start | bytes 491528 | tf_op jit(solution)/shard_map/ppermute | solution.py:82
  4.0 7.5 %collective-permute-start.2 = (bf16[2,64,640]{2,1,0:T(8,128)(2,1)S(1)}, bf16[2,64,640]{2,1,0:T(8,128)(2,1)S(1)}, u32[]{:S(2)}, u32[]{:S(2)}) collective-permute-start(bf16[2,64,640]{2,1,0:T(8,128)(2,1)S(1)} %get-tuple-element.17), channel_id=1, source_target_pairs={{0,4},{4,8},{8,12},{12,0},{1,5},{5,9},{9,13},{13,1},{2,6},{6,10},{... | collective-permute-start | bytes 491528 | tf_op jit(solution)/shard_map/ppermute | solution.py:82
  10.5 23.9 %copy-start.5 = (bf16[640,1280]{1,0:T(8,128)(2,1)S(1)}, bf16[640,1280]{1,0:T(8,128)(2,1)}, u32[]{:S(2)}) copy-start(bf16[640,1280]{1,0:T(8,128)(2,1)} %param.11) | copy-start | bytes 4915204
  32.5 3.6 %collective-permute-start.3 = (bf16[512,640]{1,0:T(8,128)(2,1)S(1)}, bf16[512,640]{1,0:T(8,128)(2,1)S(1)}, u32[]{:S(2)}, u32[]{:S(2)}) collective-permute-start(bf16[512,640]{1,0:T(8,128)(2,1)S(1)} %bitcast.60), channel_id=1, source_target_pairs={{0,4},{4,0},{8,12},{12,8},{1,5},{5,1},{9,13},{13,9},{2,6},{6,2},{1... | collective-permute-start | bytes 1966088 | tf_op jit(solution)/shard_map/ppermute | solution.py:90
  48.0 1.6 %copy-start.4 = (f32[640]{0:T(1024)S(1)}, f32[640]{0:T(1024)}, u32[]{:S(2)}) copy-start(f32[640]{0:T(1024)} %param.13) | copy-start | bytes 7684
  49.7 6.5 %collective-permute-start.4 = (bf16[2,128,640]{2,1,0:T(8,128)(2,1)S(1)}, bf16[2,128,640]{2,1,0:T(8,128)(2,1)S(1)}, u32[]{:S(2)}, u32[]{:S(2)}) collective-permute-start(bf16[2,128,640]{2,1,0:T(8,128)(2,1)S(1)} %bitcast.57), channel_id=1, source_target_pairs={{0,4},{4,8},{8,12},{1,5},{5,9},{9,13},{2,6},{6,10},{10,14},{3,7},{... | collective-permute-start | bytes 983048 | tf_op jit(solution)/shard_map/ppermute | solution.py:48
  52.2 8.4 %collective-permute-start.5 = (bf16[2,128,640]{2,1,0:T(8,128)(2,1)S(1)}, bf16[2,128,640]{2,1,0:T(8,128)(2,1)S(1)}, u32[]{:S(2)}, u32[]{:S(2)}) collective-permute-start(bf16[2,128,640]{2,1,0:T(8,128)(2,1)S(1)} %bitcast.58), channel_id=1, source_target_pairs={{4,0},{8,4},{12,8},{5,1},{9,5},{13,9},{6,2},{10,6},{14,10},{7,3},{... | collective-permute-start | bytes 983048 | tf_op jit(solution)/shard_map/ppermute | solution.py:49
  54.1 6.7 %copy-start.3 = (bf16[3,640,640]{2,1,0:T(8,128)(2,1)S(1)}, bf16[3,640,640]{2,1,0:T(8,128)(2,1)}, u32[]{:S(2)}) copy-start(bf16[3,640,640]{2,1,0:T(8,128)(2,1)} %param.14) | copy-start | bytes 7372804
  63.2 1.7 %copy-start.2 = (bf16[3,640,640]{2,1,0:T(8,128)(2,1)S(1)}, bf16[3,640,640]{2,1,0:T(8,128)(2,1)}, u32[]{:S(2)}) copy-start(bf16[3,640,640]{2,1,0:T(8,128)(2,1)} %param.15) | copy-start | bytes 7372804

commit v10 on v7

--- a/solution.py
+++ b/solution.py
@@ -8,36 +8,41 @@
 HEAD_DIM = 64
 
 
-def attention_kernel(q_ref, kt_ref, v_ref, o_ref):
+def attention_kernel(q_ref, kt_a_ref, kt_b_ref, v_a_ref, v_b_ref, o_ref):
     outs = []
     for hh in range(2):
         cols = slice(hh * HEAD_DIM, (hh + 1) * HEAD_DIM)
-        scores = jnp.dot(q_ref[:, cols], kt_ref[cols, :], preferred_element_type=jnp.float32)
-        scores = scores * HEAD_DIM ** (-0.5)
-        highest = jnp.max(scores, axis=1, keepdims=True)
-        exponent = jnp.exp(scores - highest)
-        denominator = jnp.sum(exponent, axis=1, keepdims=True)
-        mixed = jnp.dot(exponent.astype(jnp.bfloat16), v_ref[:, cols], preferred_element_type=jnp.float32)
+        query = q_ref[:, cols]
+        scores_a = jnp.dot(query, kt_a_ref[cols, :], preferred_element_type=jnp.float32) * HEAD_DIM ** (-0.5)
+        scores_b = jnp.dot(query, kt_b_ref[cols, :], preferred_element_type=jnp.float32) * HEAD_DIM ** (-0.5)
+        highest = jnp.maximum(
+            jnp.max(scores_a, axis=1, keepdims=True), jnp.max(scores_b, axis=1, keepdims=True)
+        )
+        exponent_a = jnp.exp(scores_a - highest)
+        exponent_b = jnp.exp(scores_b - highest)
+        denominator = jnp.sum(exponent_a, axis=1, keepdims=True) + jnp.sum(exponent_b, axis=1, keepdims=True)
+        mixed = jnp.dot(
+            exponent_a.astype(jnp.bfloat16), v_a_ref[:, cols], preferred_element_type=jnp.float32
+        ) + jnp.dot(exponent_b.astype(jnp.bfloat16), v_b_ref[:, cols], preferred_element_type=jnp.float32)
         outs.append(mixed / denominator)
     o_ref[...] = jnp.concatenate(outs, axis=1).astype(o_ref.dtype)
 
 
-def attend(queries, keys_t, values, q_tile=256):
+def attend(queries, keys_a, keys_b, values_a, values_b):
     total, channels = queries.shape
-    count = values.shape[0]
+    count = values_a.shape[0]
     pairs = channels // (2 * HEAD_DIM)
     width = 2 * HEAD_DIM
+    key_spec = pl.BlockSpec((width, count), lambda j: (j, 0))
+    value_spec = pl.BlockSpec((count, width), lambda j: (0, j))
     return pl.pallas_call(
         attention_kernel,
-        grid=(pairs, total // q_tile),
-        in_specs=[
-            pl.BlockSpec((q_tile, width), lambda j, i: (i, j)),
-            pl.BlockSpec((width, count), lambda j, i: (j, 0)),
-            pl.BlockSpec((count, width), lambda j, i: (0, j)),
-        ],
-        out_specs=pl.BlockSpec((q_tile, width), lambda j, i: (i, j)),
+        grid=(pairs,),
+        in_specs=[pl.BlockSpec((total, width), lambda j: (0, j)), key_spec, key_spec, value_spec, value_spec],
+        out_specs=pl.BlockSpec((total, width), lambda j: (0, j)),
         out_shape=jax.ShapeDtypeStruct((total, channels), jnp.bfloat16),
-    )(queries, keys_t, values)
+    )(queries, keys_a, keys_b, values_a, values_b)
+
 
 def extended(array, axis, width):
     size, length = (lax.axis_size(axis), array.shape[0])
@@ -110,9 +115,7 @@
 
     keys_mine, values_mine = project(mine)
     keys_sib, values_sib = project(sibling)
-    keys_t = jnp.concatenate([keys_mine, keys_sib], axis=1)
-    values = jnp.concatenate([values_mine, values_sib], axis=0)
-    attended = attend(queries, keys_t, values)
+    attended = attend(queries, keys_mine, keys_sib, values_mine, values_sib)
     residual = flattened.astype(jnp.float32) + jnp.dot(
         attended, w_out, preferred_element_type=jnp.float32
     )

time: 62 us -> 62.3 us (level)
  matrix products: 11.4 us -> 14.9 us
  other arithmetic: 3.16 us -> 0.73 us
    concatenate x2 -> x0, other arithmetic: 2.43 us -> none  [the longest x1 1.25 us: shards(): keys_t = jnp.concatenate([keys_mine, keys_sib], axis=1)]
    dot_general x2, matrix products: 1.44 us -> 3.15 us  [project(): lax.dot_general(w_keyval[:, :channels], tokens, (((0,), (1,)), ((), ())),...]
    dot_general x2, matrix products: 1.49 us -> 3.19 us  [project(): jnp.dot(tokens, w_keyval[:, channels:], preferred_element_type=jnp.float32)]
  transfers between devices with their start and end apart: 9 -> 9, of which waited for: 7 -> 6; matrix products, arithmetic and copies ran while one was open for 9% -> 11% of each run, Pallas kernels for 0% -> 0%
where the time goes in v10:
time: 62.3 us; the launch traced here: 62 us
  waiting for transfers between devices  20.7 us (33%)
  matrix products  14.9 us (24%)
  starting transfers between devices  12 us (19%)
  Pallas kernels  7.99 us (13%)
  local copies, waits for them, and re-layouts  4.11 us (7%)
  between operations  1.63 us (3%)
  other arithmetic  0.73 us (1%)
    ppermute x3, waiting for transfers between devices, gather_keyframes(): lax.ppermute(piece, 'row', [(i, (i + s) % rsize) for i in range(rsize)])  13.7 us
    pallas_call x1, Pallas kernels, attend(): pl.pallas_call(attention_kernel, grid=(pairs,), in_specs=[pl.BlockSpec((t...  7.99 us
    dot_general x6, matrix products, temporal_mix(): jnp.dot(window, weights[offset], preferred_element_type=jnp.float32)  4.43 us
    ppermute x1, waiting for transfers between devices, extended(): after = lax.ppermute(first, axis, down)  4.4 us
    ppermute x3, starting transfers between devices, gather_keyframes(): lax.ppermute(piece, 'row', [(i, (i + s) % rsize) for i in range(rsize)])  3.83 us
    ppermute x3, starting transfers between devices, gather_keyframes(): lax.ppermute(halves((me + s) % 2), 'frame', [(i, (i + s) % fsize) for i i...  3.29 us
    dot_general x2, matrix products, project(): jnp.dot(tokens, w_keyval[:, channels:], preferred_element_type=jnp.float32)  3.19 us
    dot_general x2, matrix products, project(): lax.dot_general(w_keyval[:, :channels], tokens, (((0,), (1,)), ((), ())),...  3.15 us
  transfers between devices with their start and end apart: 9, of which 6 were waited for; matrix products, arithmetic and copies ran while one was open for 11% of the time, Pallas kernels for 0%

profile of v10, /device:TPU:9, one launch (start us, length us, event | category | flops | bytes accessed | tf_op | source)
XLA Modules:
  0.0 62.0 jit_solution(10710920314001678242)
XLA Ops:
  0.0 1.2 %constant_dynamic-slice_fusion.2 = (bf16[2,64,640]{2,1,0:T(8,128)(2,1)S(1)}, bf16[2,64,640]{2,1,0:T(8,128)(2,1)S(1)}, bf16[2,64,640]{2,1,0:T(8,128)(2,1)S(1)}) fusion(bf16[2,128,640]{2,1,0:T(8,128)(2,1)} %param.8, s32[]{:T(128)S(6)} %select_n.137, s32[]{:T(128)S(6)} %select_n.147, s32[]{:T(128)S(6)} %select_n.143), kind=kLoop, calls=%fused_computation.54 | loop fusion | bytes 983052 | tf_op jit(solution)/shard_map/dynamic_slice | solution.py:79
  1.2 0.7 %collective-permute-start = (bf16[2,64,640]{2,1,0:T(8,128)(2,1)S(1)}, bf16[2,64,640]{2,1,0:T(8,128)(2,1)S(1)}, u32[]{:S(2)}, u32[]{:S(2)}) collective-permute-start(bf16[2,64,640]{2,1,0:T(8,128)(2,1)S(1)} %get-tuple-element.16), channel_id=1, source_target_pairs={{0,12},{4,0},{8,4},{12,8},{1,13},{5,1},{9,5},{13,9},{2,14},{6,2},{... | collective-permute-start | bytes 491528 | tf_op jit(solution)/shard_map/ppermute | solution.py:87
  1.9 1.2 %collective-permute-start.1 = (bf16[2,64,640]{2,1,0:T(8,128)(2,1)S(1)}, bf16[2,64,640]{2,1,0:T(8,128)(2,1)S(1)}, u32[]{:S(2)}, u32[]{:S(2)}) collective-permute-start(bf16[2,64,640]{2,1,0:T(8,128)(2,1)S(1)} %get-tuple-element.18), channel_id=1, source_target_pairs={{0,8},{4,12},{8,0},{12,4},{1,9},{5,13},{9,1},{13,5},{2,10},{6,14},... | collective-permute-start | bytes 491528 | tf_op jit(solution)/shard_map/ppermute | solution.py:87
  3.2 1.3 %collective-permute-start.2 = (bf16[2,64,640]{2,1,0:T(8,128)(2,1)S(1)}, bf16[2,64,640]{2,1,0:T(8,128)(2,1)S(1)}, u32[]{:S(2)}, u32[]{:S(2)}) collective-permute-start(bf16[2,64,640]{2,1,0:T(8,128)(2,1)S(1)} %get-tuple-element.17), channel_id=1, source_target_pairs={{0,4},{4,8},{8,12},{12,0},{1,5},{5,9},{9,13},{13,1},{2,6},{6,10},{... | collective-permute-start | bytes 491528 | tf_op jit(solution)/shard_map/ppermute | solution.py:87
  4.5 1.3 %fusion.29 = (s32[1]{0:T(128)}, s32[1]{0:T(128)}) fusion(s32[2]{0:T(128)} %param.9), kind=kLoop, calls=%fused_computation.57 | loop fusion | bytes 16 | tf_op jit(solution)/shard_map/slice | solution.py:72
  7.3 2.5 %convolution_convert_fusion.4.q_ref = bf16[256,640]{1,0:T(8,128)(2,1)} fusion(bf16[256,640]{1,0:T(8,128)(2,1)} %bitcast.54, bf16[640,640]{1,0:T(8,128)(2,1)} %param.10), kind=kOutput, calls=%fused_computation.14 | convolution fusion | flops 209879040 | bytes 1474560 | tf_op jit(solution)/shard_map/dot_general | solution.py:105
  9.9 0.8 %collective-permute-done.2 = bf16[2,64,640]{2,1,0:T(8,128)(2,1)S(1)} collective-permute-done((bf16[2,64,640]{2,1,0:T(8,128)(2,1)S(1)}, bf16[2,64,640]{2,1,0:T(8,128)(2,1)S(1)}, u32[]{:S(2)}, u32[]{:S(2)}) %collective-permute-start.2) | collective-permute-done | bytes 163872 | tf_op jit(solution)/shard_map/ppermute | solution.py:87
  10.8 1.4 %collective-permute-start.3 = (bf16[2,64,640]{2,1,0:T(8,128)(2,1)S(1)}, bf16[2,64,640]{2,1,0:T(8,128)(2,1)S(1)}, u32[]{:S(2)}, u32[]{:S(2)}) collective-permute-start(bf16[2,64,640]{2,1,0:T(8,128)(2,1)S(1)} %pad_maximum_fusion.7), channel_id=1, source_target_pairs={{0,1},{1,2},{2,3},{3,0},{4,5},{5,6},{6,7},{7,4},{8,9},{9,10},{10,1... | collective-permute-start | bytes 491528 | tf_op jit(solution)/shard_map/ppermute | solution.py:95
  12.2 1.1 %collective-permute-start.4 = (bf16[2,64,640]{2,1,0:T(8,128)(2,1)S(1)}, bf16[2,64,640]{2,1,0:T(8,128)(2,1)S(1)}, u32[]{:S(2)}, u32[]{:S(2)}) collective-permute-start(bf16[2,64,640]{2,1,0:T(8,128)(2,1)S(1)} %pad_maximum_fusion.7), channel_id=1, source_target_pairs={{0,2},{1,3},{2,0},{3,1},{4,6},{5,7},{6,4},{7,5},{8,10},{9,11},{10,... | collective-permute-start | bytes 491528 | tf_op jit(solution)/shard_map/ppermute | solution.py:95
  13.3 1.4 %collective-permute-start.5 = (bf16[2,64,640]{2,1,0:T(8,128)(2,1)S(1)}, bf16[2,64,640]{2,1,0:T(8,128)(2,1)S(1)}, u32[]{:S(2)}, u32[]{:S(2)}) collective-permute-start(bf16[2,64,640]{2,1,0:T(8,128)(2,1)S(1)} %pad_maximum_fusion.7), channel_id=1, source_target_pairs={{0,3},{1,0},{2,1},{3,2},{4,7},{5,4},{6,5},{7,6},{8,11},{9,8},{10,9... | collective-permute-start | bytes 491528 | tf_op jit(solution)/shard_map/ppermute | solution.py:95
  14.7 0.4 collective-permute-done.3
  15.0 9.8 %collective-permute-done.4 = bf16[2,64,640]{2,1,0:T(8,128)(2,1)S(1)} collective-permute-done((bf16[2,64,640]{2,1,0:T(8,128)(2,1)S(1)}, bf16[2,64,640]{2,1,0:T(8,128)(2,1)S(1)}, u32[]{:S(2)}, u32[]{:S(2)}) %collective-permute-start.4) | collective-permute-done | bytes 163872 | tf_op jit(solution)/shard_map/ppermute | solution.py:95
  24.9 3.5 %collective-permute-done.5 = bf16[2,64,640]{2,1,0:T(8,128)(2,1)S(1)} collective-permute-done((bf16[2,64,640]{2,1,0:T(8,128)(2,1)S(1)}, bf16[2,64,640]{2,1,0:T(8,128)(2,1)S(1)}, u32[]{:S(2)}, u32[]{:S(2)}) %collective-permute-start.5) | collective-permute-done | bytes 163872 | tf_op jit(solution)/shard_map/ppermute | solution.py:95
  28.5 0.6 collective-permute-start.6
  29.0 1.6 %convolution_convert_fusion.1.v_a_ref = bf16[512,640]{1,0:T(8,128)(2,1)} fusion(bf16[512,640]{1,0:T(8,128)(2,1)S(1)} %bitcast.66, bf16[640,1280]{1,0:T(8,128)(2,1)S(1)} %copy-done.5), kind=kOutput, calls=%fused_computation.3 | convolution fusion | flops 419758080 | bytes 2129920 | tf_op jit(solution)/shard_map/dot_general | solution.py:113
  30.6 1.6 %fusion.1.kt_a_ref = bf16[640,512]{1,0:T(8,128)(2,1)} fusion(bf16[512,640]{1,0:T(8,128)(2,1)S(1)} %bitcast.67, bf16[640,1280]{1,0:T(8,128)(2,1)S(1)} %copy-done.5), kind=kOutput, calls=%fused_computation.7 | convolution fusion | flops 419758080 | bytes 2129920 | tf_op jit(solution)/shard_map/dot_general | solution.py:110
  32.2 1.6 %convolution_convert_fusion.v_b_ref = bf16[512,640]{1,0:T(8,128)(2,1)} fusion(bf16[512,640]{1,0:T(8,128)(2,1)S(1)} %collective-permute-done.6, bf16[640,1280]{1,0:T(8,128)(2,1)S(1)} %copy-done.5), kind=kOutput, calls=%fused_computation.2 | convolution fusion | flops 419758080 | bytes 2129920 | tf_op jit(solution)/shard_map/dot_general | solution.py:113
  33.8 1.6 %fusion.2.kt_b_ref = bf16[640,512]{1,0:T(8,128)(2,1)} fusion(bf16[512,640]{1,0:T(8,128)(2,1)S(1)} %collective-permute-done.6, bf16[640,1280]{1,0:T(8,128)(2,1)S(1)} %copy-done.5), kind=kOutput, calls=%fused_computation.8 | convolution fusion | flops 419758080 | bytes 2129920 | tf_op jit(solution)/shard_map/dot_general | solution.py:110
  35.4 8.0 %shard_map.82 = bf16[256,640]{1,0:T(8,128)(2,1)} custom-call(bf16[256,640]{1,0:T(8,128)(2,1)} %convolution_convert_fusion.4.q_ref, bf16[640,512]{1,0:T(8,128)(2,1)} %fusion.1.kt_a_ref, bf16[640,512]{1,0:T(8,128)(2,1)} %fusion.2.kt_b_ref, bf16[512,640]{1,0:T(8,128)(2,1)} %convolution_convert_fusion.1.v_a_ref, bf16[512,640]{1,0:T(8,128)(2,1)} %convolution_convert_fusion.v_b_ref), custom_call_target="tpu_custom_call" | custom-call | tf_op jit(solution)/shard_map/pallas_call | solution.py:38
  43.4 1.5 %multiply_reduce_fusion = (f32[256]{0:T(256)S(1)}, f32[256,640]{1,0:T(8,128)S(1)}) fusion(bf16[256,640]{1,0:T(8,128)(2,1)} %shard_map.82, bf16[640,640]{1,0:T(8,128)(2,1)S(1)} %copy-done, bf16[256,640]{1,0:T(8,128)(2,1)S(1)} %bitcast.55), kind=kOutput, calls=%fused_computation.40 | convolution fusion | flops 210370304 | bytes 2130944 | tf_op jit(solution)/shard_map/dot_general | solution.py:119
  45.1 2.1 %collective-permute-start.7 = (bf16[2,128,640]{2,1,0:T(8,128)(2,1)S(1)}, bf16[2,128,640]{2,1,0:T(8,128)(2,1)S(1)}, u32[]{:S(2)}, u32[]{:S(2)}) collective-permute-start(bf16[2,128,640]{2,1,0:T(8,128)(2,1)S(1)} %bitcast.61), channel_id=1, source_target_pairs={{0,4},{4,8},{8,12},{1,5},{5,9},{9,13},{2,6},{6,10},{10,14},{3,7},{... | collective-permute-start | bytes 983048 | tf_op jit(solution)/shard_map/ppermute | solution.py:53
  47.2 2.3 %collective-permute-start.8 = (bf16[2,128,640]{2,1,0:T(8,128)(2,1)S(1)}, bf16[2,128,640]{2,1,0:T(8,128)(2,1)S(1)}, u32[]{:S(2)}, u32[]{:S(2)}) collective-permute-start(bf16[2,128,640]{2,1,0:T(8,128)(2,1)S(1)} %bitcast.62), channel_id=1, source_target_pairs={{4,0},{8,4},{12,8},{5,1},{9,5},{13,9},{6,2},{10,6},{14,10},{7,3},{... | collective-permute-start | bytes 983048 | tf_op jit(solution)/shard_map/ppermute | solution.py:54
  49.5 1.7 %collective-permute-done.7 = bf16[2,128,640]{2,1,0:T(8,128)(2,1)S(1)} collective-permute-done((bf16[2,128,640]{2,1,0:T(8,128)(2,1)S(1)}, bf16[2,128,640]{2,1,0:T(8,128)(2,1)S(1)}, u32[]{:S(2)}, u32[]{:S(2)}) %collective-permute-start.7) | collective-permute-done | bytes 327712 | tf_op jit(solution)/shard_map/ppermute | solution.py:53
  51.2 4.4 %collective-permute-done.8 = bf16[2,128,640]{2,1,0:T(8,128)(2,1)S(1)} collective-permute-done((bf16[2,128,640]{2,1,0:T(8,128)(2,1)S(1)}, bf16[2,128,640]{2,1,0:T(8,128)(2,1)S(1)}, u32[]{:S(2)}, u32[]{:S(2)}) %collective-permute-start.8) | collective-permute-done | bytes 327712 | tf_op jit(solution)/shard_map/ppermute | solution.py:54
  55.6 0.2 pad_maximum_fusion.3
  55.8 0.7 %fusion.11 = f32[512,640]{1,0:T(8,128)S(1)} fusion(bf16[512,640]{1,0:T(8,128)(2,1)S(1)} %bitcast.57, bf16[3,640,640]{2,1,0:T(8,128)(2,1)S(1)} %copy-done.3), kind=kOutput, calls=%fused_computation.21 | convolution fusion | flops 419430400 | bytes 2785280 | tf_op jit(solution)/shard_map/dot_general | solution.py:62
  56.6 0.7 %fusion.9 = f32[512,640]{1,0:T(8,128)S(1)} fusion(bf16[512,640]{1,0:T(8,128)(2,1)S(1)} %bitcast.56, bf16[3,640,640]{2,1,0:T(8,128)(2,1)S(1)} %copy-done.3), kind=kOutput, calls=%fused_computation.19 | convolution fusion | flops 419430400 | bytes 2785280 | tf_op jit(solution)/shard_map/dot_general | solution.py:62
  57.3 0.8 %multiply_convert_fusion = bf16[512,640]{1,0:T(8,128)(2,1)S(1)} fusion(f32[512,640]{1,0:T(8,128)S(1)} %fusion.9, f32[512,640]{1,0:T(8,128)S(1)} %fusion.11, bf16[512,640]{1,0:T(8,128)(2,1)S(1)} %bitcast.68, bf16[3,640,640]{2,1,0:T(8,128)(2,1)S(1)} %copy-done.3), kind=kOutput, calls=%fused_computation.6 | convolution fusion | flops 421724160 | bytes 4751360 | tf_op jit(solution)/shard_map/dot_general | solution.py:62
  58.3 1.5 %copy-done.2 = bf16[3,640,640]{2,1,0:T(8,128)(2,1)S(1)} copy-done((bf16[3,640,640]{2,1,0:T(8,128)(2,1)S(1)}, bf16[3,640,640]{2,1,0:T(8,128)(2,1)}, u32[]{:S(2)}) %copy-start.2) | copy-done | bytes 2457624
  59.9 0.5 fusion.7
  60.3 0.5 convolution_add_fusion.2
  60.8 1.2 %fusion.4 = bf16[256,640]{1,0:T(8,128)(2,1)} fusion(f32[256,640]{1,0:T(8,128)S(1)} %get-tuple-element.22, f32[256,640]{1,0:T(8,128)S(1)} %convolution_add_fusion.2, bf16[256,640]{1,0:T(8,128)(2,1)S(1)} %bitcast.60, bf16[3,640,640]{2,1,0:T(8,128)(2,1)S(1)} %copy-done.2), kind=kOutput, calls=%fused_computation.13 | convolution fusion | flops 210206720 | bytes 2785280 | tf_op jit(solution)/shard_map/dot_general | solution.py:62
  (22 shorter events, 0.6 us)
Async XLA Ops:
  0.0 43.4 %copy-start = (bf16[640,640]{1,0:T(8,128)(2,1)S(1)}, bf16[640,640]{1,0:T(8,128)(2,1)}, u32[]{:S(2)}) copy-start(bf16[640,640]{1,0:T(8,128)(2,1)} %param.12) | copy-start | bytes 2457604
  0.0 10.7 %copy-start.1 = (bf16[2,128,640]{2,1,0:T(8,128)(2,1)S(1)}, bf16[2,128,640]{2,1,0:T(8,128)(2,1)}, u32[]{:S(2)}) copy-start(bf16[2,128,640]{2,1,0:T(8,128)(2,1)} %param.8) | copy-start | bytes 983044
  1.2 8.6 %collective-permute-start = (bf16[2,64,640]{2,1,0:T(8,128)(2,1)S(1)}, bf16[2,64,640]{2,1,0:T(8,128)(2,1)S(1)}, u32[]{:S(2)}, u32[]{:S(2)}) collective-permute-start(bf16[2,64,640]{2,1,0:T(8,128)(2,1)S(1)} %get-tuple-element.16), channel_id=1, source_target_pairs={{0,12},{4,0},{8,4},{12,8},{1,13},{5,1},{9,5},{13,9},{2,14},{6,2},{... | collective-permute-start | bytes 491528 | tf_op jit(solution)/shard_map/ppermute | solution.py:87
  1.9 7.9 %collective-permute-start.1 = (bf16[2,64,640]{2,1,0:T(8,128)(2,1)S(1)}, bf16[2,64,640]{2,1,0:T(8,128)(2,1)S(1)}, u32[]{:S(2)}, u32[]{:S(2)}) collective-permute-start(bf16[2,64,640]{2,1,0:T(8,128)(2,1)S(1)} %get-tuple-element.18), channel_id=1, source_target_pairs={{0,8},{4,12},{8,0},{12,4},{1,9},{5,13},{9,1},{13,5},{2,10},{6,14},... | collective-permute-start | bytes 491528 | tf_op jit(solution)/shard_map/ppermute | solution.py:87
  3.2 7.5 %collective-permute-start.2 = (bf16[2,64,640]{2,1,0:T(8,128)(2,1)S(1)}, bf16[2,64,640]{2,1,0:T(8,128)(2,1)S(1)}, u32[]{:S(2)}, u32[]{:S(2)}) collective-permute-start(bf16[2,64,640]{2,1,0:T(8,128)(2,1)S(1)} %get-tuple-element.17), channel_id=1, source_target_pairs={{0,4},{4,8},{8,12},{12,0},{1,5},{5,9},{9,13},{13,1},{2,6},{6,10},{... | collective-permute-start | bytes 491528 | tf_op jit(solution)/shard_map/ppermute | solution.py:87
  7.3 21.8 %copy-start.5 = (bf16[640,1280]{1,0:T(8,128)(2,1)S(1)}, bf16[640,1280]{1,0:T(8,128)(2,1)}, u32[]{:S(2)}) copy-start(bf16[640,1280]{1,0:T(8,128)(2,1)} %param.11) | copy-start | bytes 4915204
  10.8 4.2 %collective-permute-start.3 = (bf16[2,64,640]{2,1,0:T(8,128)(2,1)S(1)}, bf16[2,64,640]{2,1,0:T(8,128)(2,1)S(1)}, u32[]{:S(2)}, u32[]{:S(2)}) collective-permute-start(bf16[2,64,640]{2,1,0:T(8,128)(2,1)S(1)} %pad_maximum_fusion.7), channel_id=1, source_target_pairs={{0,1},{1,2},{2,3},{3,0},{4,5},{5,6},{6,7},{7,4},{8,9},{9,10},{10,1... | collective-permute-start | bytes 491528 | tf_op jit(solution)/shard_map/ppermute | solution.py:95
  12.2 12.7 %collective-permute-start.4 = (bf16[2,64,640]{2,1,0:T(8,128)(2,1)S(1)}, bf16[2,64,640]{2,1,0:T(8,128)(2,1)S(1)}, u32[]{:S(2)}, u32[]{:S(2)}) collective-permute-start(bf16[2,64,640]{2,1,0:T(8,128)(2,1)S(1)} %pad_maximum_fusion.7), channel_id=1, source_target_pairs={{0,2},{1,3},{2,0},{3,1},{4,6},{5,7},{6,4},{7,5},{8,10},{9,11},{10,... | collective-permute-start | bytes 491528 | tf_op jit(solution)/shard_map/ppermute | solution.py:95
  13.3 15.1 %collective-permute-start.5 = (bf16[2,64,640]{2,1,0:T(8,128)(2,1)S(1)}, bf16[2,64,640]{2,1,0:T(8,128)(2,1)S(1)}, u32[]{:S(2)}, u32[]{:S(2)}) collective-permute-start(bf16[2,64,640]{2,1,0:T(8,128)(2,1)S(1)} %pad_maximum_fusion.7), channel_id=1, source_target_pairs={{0,3},{1,0},{2,1},{3,2},{4,7},{5,4},{6,5},{7,6},{8,11},{9,8},{10,9... | collective-permute-start | bytes 491528 | tf_op jit(solution)/shard_map/ppermute | solution.py:95
  28.5 3.7 %collective-permute-start.6 = (bf16[512,640]{1,0:T(8,128)(2,1)S(1)}, bf16[512,640]{1,0:T(8,128)(2,1)S(1)}, u32[]{:S(2)}, u32[]{:S(2)}) collective-permute-start(bf16[512,640]{1,0:T(8,128)(2,1)S(1)} %bitcast.65), channel_id=1, source_target_pairs={{0,4},{4,0},{8,12},{12,8},{1,5},{5,1},{9,13},{13,9},{2,6},{6,2},{1... | collective-permute-start | bytes 1966088 | tf_op jit(solution)/shard_map/ppermute | solution.py:97
  43.4 1.6 %copy-start.4 = (f32[640]{0:T(1024)S(1)}, f32[640]{0:T(1024)}, u32[]{:S(2)}) copy-start(f32[640]{0:T(1024)} %param.13) | copy-start | bytes 7684
  45.1 6.1 %collective-permute-start.7 = (bf16[2,128,640]{2,1,0:T(8,128)(2,1)S(1)}, bf16[2,128,640]{2,1,0:T(8,128)(2,1)S(1)}, u32[]{:S(2)}, u32[]{:S(2)}) collective-permute-start(bf16[2,128,640]{2,1,0:T(8,128)(2,1)S(1)} %bitcast.61), channel_id=1, source_target_pairs={{0,4},{4,8},{8,12},{1,5},{5,9},{9,13},{2,6},{6,10},{10,14},{3,7},{... | collective-permute-start | bytes 983048 | tf_op jit(solution)/shard_map/ppermute | solution.py:53
  47.2 8.4 %collective-permute-start.8 = (bf16[2,128,640]{2,1,0:T(8,128)(2,1)S(1)}, bf16[2,128,640]{2,1,0:T(8,128)(2,1)S(1)}, u32[]{:S(2)}, u32[]{:S(2)}) collective-permute-start(bf16[2,128,640]{2,1,0:T(8,128)(2,1)S(1)} %bitcast.62), channel_id=1, source_target_pairs={{4,0},{8,4},{12,8},{5,1},{9,5},{13,9},{6,2},{10,6},{14,10},{7,3},{... | collective-permute-start | bytes 983048 | tf_op jit(solution)/shard_map/ppermute | solution.py:54
  49.5 6.4 %copy-start.3 = (bf16[3,640,640]{2,1,0:T(8,128)(2,1)S(1)}, bf16[3,640,640]{2,1,0:T(8,128)(2,1)}, u32[]{:S(2)}) copy-start(bf16[3,640,640]{2,1,0:T(8,128)(2,1)} %param.14) | copy-start | bytes 7372804
  58.2 1.7 %copy-start.2 = (bf16[3,640,640]{2,1,0:T(8,128)(2,1)S(1)}, bf16[3,640,640]{2,1,0:T(8,128)(2,1)}, u32[]{:S(2)}) copy-start(bf16[3,640,640]{2,1,0:T(8,128)(2,1)} %param.15) | copy-start | bytes 7372804

commit v11 on v7

--- a/solution.py
+++ b/solution.py
@@ -8,36 +8,64 @@
 HEAD_DIM = 64
 
 
-def attention_kernel(q_ref, kt_ref, v_ref, o_ref):
+def first_chunk_kernel(q_ref, kt_ref, v_ref, m_ref, l_ref, acc_ref):
+    for hh in range(2):
+        cols = slice(hh * HEAD_DIM, (hh + 1) * HEAD_DIM)
+        scores = jnp.dot(q_ref[:, cols], kt_ref[cols, :], preferred_element_type=jnp.float32) * HEAD_DIM ** (-0.5)
+        highest = jnp.max(scores, axis=1, keepdims=True)
+        exponent = jnp.exp(scores - highest)
+        total = jnp.sum(exponent, axis=1, keepdims=True)
+        mixed = jnp.dot(exponent.astype(jnp.bfloat16), v_ref[:, cols], preferred_element_type=jnp.float32)
+        m_ref[:, cols] = jnp.broadcast_to(highest, mixed.shape)
+        l_ref[:, cols] = jnp.broadcast_to(total, mixed.shape)
+        acc_ref[:, cols] = mixed
+
+
+def last_chunk_kernel(q_ref, kt_ref, v_ref, m_ref, l_ref, acc_ref, o_ref):
     outs = []
     for hh in range(2):
         cols = slice(hh * HEAD_DIM, (hh + 1) * HEAD_DIM)
-        scores = jnp.dot(q_ref[:, cols], kt_ref[cols, :], preferred_element_type=jnp.float32)
-        scores = scores * HEAD_DIM ** (-0.5)
-        highest = jnp.max(scores, axis=1, keepdims=True)
+        scores = jnp.dot(q_ref[:, cols], kt_ref[cols, :], preferred_element_type=jnp.float32) * HEAD_DIM ** (-0.5)
+        before = jnp.max(m_ref[:, cols], axis=1, keepdims=True)
+        highest = jnp.maximum(before, jnp.max(scores, axis=1, keepdims=True))
+        kept = jnp.exp(before - highest)
         exponent = jnp.exp(scores - highest)
-        denominator = jnp.sum(exponent, axis=1, keepdims=True)
-        mixed = jnp.dot(exponent.astype(jnp.bfloat16), v_ref[:, cols], preferred_element_type=jnp.float32)
-        outs.append(mixed / denominator)
+        total = jnp.max(l_ref[:, cols], axis=1, keepdims=True) * kept + jnp.sum(exponent, axis=1, keepdims=True)
+        mixed = acc_ref[:, cols] * kept + jnp.dot(
+            exponent.astype(jnp.bfloat16), v_ref[:, cols], preferred_element_type=jnp.float32
+        )
+        outs.append(mixed / total)
     o_ref[...] = jnp.concatenate(outs, axis=1).astype(o_ref.dtype)
 
 
-def attend(queries, keys_t, values, q_tile=256):
+def attend_first(queries, keys_t, values):
     total, channels = queries.shape
     count = values.shape[0]
-    pairs = channels // (2 * HEAD_DIM)
     width = 2 * HEAD_DIM
+    row_spec = pl.BlockSpec((total, width), lambda j: (0, j))
+    state = jax.ShapeDtypeStruct((total, channels), jnp.float32)
     return pl.pallas_call(
-        attention_kernel,
-        grid=(pairs, total // q_tile),
-        in_specs=[
-            pl.BlockSpec((q_tile, width), lambda j, i: (i, j)),
-            pl.BlockSpec((width, count), lambda j, i: (j, 0)),
-            pl.BlockSpec((count, width), lambda j, i: (0, j)),
-        ],
-        out_specs=pl.BlockSpec((q_tile, width), lambda j, i: (i, j)),
+        first_chunk_kernel,
+        grid=(channels // width,),
+        in_specs=[row_spec, pl.BlockSpec((width, count), lambda j: (j, 0)), pl.BlockSpec((count, width), lambda j: (0, j))],
+        out_specs=[row_spec, row_spec, row_spec],
+        out_shape=[state, state, state],
+    )(queries, keys_t, values)
+
+
+def attend_last(queries, keys_t, values, state):
+    total, channels = queries.shape
+    count = values.shape[0]
+    width = 2 * HEAD_DIM
+    row_spec = pl.BlockSpec((total, width), lambda j: (0, j))
+    return pl.pallas_call(
+        last_chunk_kernel,
+        grid=(channels // width,),
+        in_specs=[row_spec, pl.BlockSpec((width, count), lambda j: (j, 0)), pl.BlockSpec((count, width), lambda j: (0, j))]
+        + [row_spec] * 3,
+        out_specs=row_spec,
         out_shape=jax.ShapeDtypeStruct((total, channels), jnp.bfloat16),
-    )(queries, keys_t, values)
+    )(queries, keys_t, values, *state)
 
 def extended(array, axis, width):
     size, length = (lax.axis_size(axis), array.shape[0])
@@ -85,12 +113,12 @@
         got_b = jnp.where(source == owner_b, recv[n_loc - 1], got_b)
     piece = jnp.stack([got_a, got_b])
     piece, early = lax.optimization_barrier((piece, early))
-    pieces = [piece]
+    swap = [(i, i ^ 1) for i in range(fsize)]
+    own_row = jnp.concatenate([piece, lax.ppermute(piece, "frame", swap)], axis=0).reshape(-1, channels)
+    pieces = []
     for s in range(1, rsize):
         pieces.append(lax.ppermute(piece, "row", [(i, (i + s) % rsize) for i in range(rsize)]))
-    mine = jnp.stack(pieces).reshape(-1, channels)
-    sibling = lax.ppermute(mine, "frame", [(i, i ^ 1) for i in range(fsize)])
-    return mine, sibling
+    return own_row, pieces
 
 
 def shards(frames, key_index, w_query, w_keyval, w_out, norm_gain, w_first, w_second):
@@ -99,7 +127,7 @@
     flattened = frames.reshape(-1, channels)
     queries = jnp.dot(flattened, w_query, preferred_element_type=jnp.float32).astype(jnp.bfloat16)
     query_total = queries.shape[0]
-    mine, sibling = gather_keyframes(frames, key_index, queries)
+    own_row, pieces = gather_keyframes(frames, key_index, queries)
 
     def project(tokens):
         keys_t = lax.dot_general(
@@ -108,11 +136,15 @@
         values = jnp.dot(tokens, w_keyval[:, channels:], preferred_element_type=jnp.float32).astype(jnp.bfloat16)
         return keys_t, values
 
+    state = attend_first(queries, *project(own_row))
+    pieces, state = lax.optimization_barrier((pieces, state))
+    mine = jnp.stack(pieces).reshape(-1, channels)
+    sibling = lax.ppermute(mine, "frame", [(i, i ^ 1) for i in range(lax.axis_size("frame"))])
     keys_mine, values_mine = project(mine)
     keys_sib, values_sib = project(sibling)
     keys_t = jnp.concatenate([keys_mine, keys_sib], axis=1)
     values = jnp.concatenate([values_mine, values_sib], axis=0)
-    attended = attend(queries, keys_t, values)
+    attended = attend_last(queries, keys_t, values, state)
     residual = flattened.astype(jnp.float32) + jnp.dot(
         attended, w_out, preferred_element_type=jnp.float32
     )

time: 62 us -> 63.3 us (1.021)
  waiting for transfers between devices: 21.2 us -> 13.5 us
  Pallas kernels: 8.04 us -> 12.9 us
  starting transfers between devices: 12 us -> 14.2 us
  matrix products: 11.4 us -> 13.5 us
    ppermute x3, waiting for transfers between devices: 13.7 us -> 6.03 us  [gather_keyframes(): lax.ppermute(piece, 'row', [(i, (i + s) % rsize) for i in range(rsize)])]
    pallas_call x1 -> x2, Pallas kernels: 8.04 us -> 12.9 us  [the longest x1 7.6 us: attend_last(): pl.pallas_call(last_chunk_kernel, grid=(channels // width,), in_specs=[ro...]
    ppermute x1 -> x2, starting transfers between devices: 0.56 us -> 1.94 us  [the longest x1 1.4 us: gather_keyframes(): lax.ppermute(piece, 'frame', swap)]
    dot_general x2 -> x3, matrix products: 1.44 us -> 2.61 us  [project(): lax.dot_general(w_keyval[:, :channels], tokens, (((0,), (1,)), ((), ())),...]
    dot_general x2 -> x3, matrix products: 1.49 us -> 2.41 us  [project(): jnp.dot(tokens, w_keyval[:, channels:], preferred_element_type=jnp.float32)]
    ppermute x1, starting transfers between devices: 2.44 us -> 3.32 us  [extended(): before = lax.ppermute(last, axis, up)]
    unnamed x12 -> x14, local copies, waits for them, and re-layouts: 1.55 us -> 1.55 us
  transfers between devices with their start and end apart: 9 -> 10, of which waited for: 7 -> 6; matrix products, arithmetic and copies ran while one was open for 9% -> 12% of each run, Pallas kernels for 0% -> 8%
where the time goes in v11:
time: 63.3 us; the launch traced here: 62.7 us
  starting transfers between devices  14.2 us (22%)
  matrix products  13.5 us (21%)
  waiting for transfers between devices  13.5 us (21%)
  Pallas kernels  12.9 us (20%)
  local copies, waits for them, and re-layouts  4.11 us (6%)
  other arithmetic  2.84 us (4%)
  between operations  1.62 us (3%)
    pallas_call x1, Pallas kernels, attend_last(): pl.pallas_call(last_chunk_kernel, grid=(channels // width,), in_specs=[ro...  7.6 us
    ppermute x3, waiting for transfers between devices, gather_keyframes(): lax.ppermute(piece, 'row', [(i, (i + s) % rsize) for i in range(rsize)])  6.03 us
    pallas_call x1, Pallas kernels, attend_first(): pl.pallas_call(first_chunk_kernel, grid=(channels // width,), in_specs=[r...  5.25 us
    dot_general x6, matrix products, temporal_mix(): jnp.dot(window, weights[offset], preferred_element_type=jnp.float32)  4.44 us
    ppermute x1, waiting for transfers between devices, extended(): after = lax.ppermute(first, axis, down)  4.4 us
    ppermute x3, starting transfers between devices, gather_keyframes(): lax.ppermute(piece, 'row', [(i, (i + s) % rsize) for i in range(rsize)])  3.78 us
    ppermute x1, starting transfers between devices, extended(): before = lax.ppermute(last, axis, up)  3.32 us
    ppermute x3, starting transfers between devices, gather_keyframes(): lax.ppermute(halves((me + s) % 2), 'frame', [(i, (i + s) % fsize) for i i...  3.29 us
  transfers between devices with their start and end apart: 10, of which 6 were waited for; matrix products, arithmetic and copies ran while one was open for 12% of the time, Pallas kernels for 8%

profile of v11, /device:TPU:9, one launch (start us, length us, event | category | flops | bytes accessed | tf_op | source)
XLA Modules:
  0.0 62.7 jit_solution(9992677050465401993)
XLA Ops:
  0.0 1.2 %constant_dynamic-slice_fusion.2 = (bf16[2,64,640]{2,1,0:T(8,128)(2,1)S(1)}, bf16[2,64,640]{2,1,0:T(8,128)(2,1)S(1)}, bf16[2,64,640]{2,1,0:T(8,128)(2,1)S(1)}) fusion(bf16[2,128,640]{2,1,0:T(8,128)(2,1)} %param.8, s32[]{:T(128)S(6)} %select_n.137, s32[]{:T(128)S(6)} %select_n.147, s32[]{:T(128)S(6)} %select_n.143), kind=kLoop, calls=%fused_computation.62 | loop fusion | bytes 983052 | tf_op jit(solution)/shard_map/dynamic_slice | solution.py:102
  1.2 0.7 %collective-permute-start = (bf16[2,64,640]{2,1,0:T(8,128)(2,1)S(1)}, bf16[2,64,640]{2,1,0:T(8,128)(2,1)S(1)}, u32[]{:S(2)}, u32[]{:S(2)}) collective-permute-start(bf16[2,64,640]{2,1,0:T(8,128)(2,1)S(1)} %get-tuple-element.34), channel_id=1, source_target_pairs={{0,12},{4,0},{8,4},{12,8},{1,13},{5,1},{9,5},{13,9},{2,14},{6,2},{... | collective-permute-start | bytes 491528 | tf_op jit(solution)/shard_map/ppermute | solution.py:110
  1.9 1.2 %collective-permute-start.1 = (bf16[2,64,640]{2,1,0:T(8,128)(2,1)S(1)}, bf16[2,64,640]{2,1,0:T(8,128)(2,1)S(1)}, u32[]{:S(2)}, u32[]{:S(2)}) collective-permute-start(bf16[2,64,640]{2,1,0:T(8,128)(2,1)S(1)} %get-tuple-element.36), channel_id=1, source_target_pairs={{0,8},{4,12},{8,0},{12,4},{1,9},{5,13},{9,1},{13,5},{2,10},{6,14},... | collective-permute-start | bytes 491528 | tf_op jit(solution)/shard_map/ppermute | solution.py:110
  3.2 1.3 %collective-permute-start.2 = (bf16[2,64,640]{2,1,0:T(8,128)(2,1)S(1)}, bf16[2,64,640]{2,1,0:T(8,128)(2,1)S(1)}, u32[]{:S(2)}, u32[]{:S(2)}) collective-permute-start(bf16[2,64,640]{2,1,0:T(8,128)(2,1)S(1)} %get-tuple-element.35), channel_id=1, source_target_pairs={{0,4},{4,8},{8,12},{12,0},{1,5},{5,9},{9,13},{13,1},{2,6},{6,10},{... | collective-permute-start | bytes 491528 | tf_op jit(solution)/shard_map/ppermute | solution.py:110
  4.5 1.3 %fusion.32 = (s32[1]{0:T(128)}, s32[1]{0:T(128)}) fusion(s32[2]{0:T(128)} %param.9), kind=kLoop, calls=%fused_computation.65 | loop fusion | bytes 16 | tf_op jit(solution)/shard_map/slice | solution.py:95
  7.2 2.5 %convolution_convert_fusion.6.q_ref = bf16[256,640]{1,0:T(8,128)(2,1)} fusion(bf16[256,640]{1,0:T(8,128)(2,1)} %bitcast.58, bf16[640,640]{1,0:T(8,128)(2,1)} %param.10), kind=kOutput, calls=%fused_computation.16 | convolution fusion | flops 209879040 | bytes 1474560 | tf_op jit(solution)/shard_map/dot_general | solution.py:128
  9.8 0.9 %collective-permute-done.2 = bf16[2,64,640]{2,1,0:T(8,128)(2,1)S(1)} collective-permute-done((bf16[2,64,640]{2,1,0:T(8,128)(2,1)S(1)}, bf16[2,64,640]{2,1,0:T(8,128)(2,1)S(1)}, u32[]{:S(2)}, u32[]{:S(2)}) %collective-permute-start.2) | collective-permute-done | bytes 163872 | tf_op jit(solution)/shard_map/ppermute | solution.py:110
  10.8 1.4 %collective-permute-start.6 = (bf16[2,64,640]{2,1,0:T(8,128)(2,1)S(1)}, bf16[2,64,640]{2,1,0:T(8,128)(2,1)S(1)}, u32[]{:S(2)}, u32[]{:S(2)}) collective-permute-start(bf16[2,64,640]{2,1,0:T(8,128)(2,1)S(1)} %pad_maximum_fusion.10), channel_id=1, source_target_pairs={{0,4},{4,0},{8,12},{12,8},{1,5},{5,1},{9,13},{13,9},{2,6},{6,2},{1... | collective-permute-start | bytes 491528 | tf_op jit(solution)/shard_map/ppermute | solution.py:117
  12.2 1.3 %collective-permute-start.3 = (bf16[2,64,640]{2,1,0:T(8,128)(2,1)S(1)}, bf16[2,64,640]{2,1,0:T(8,128)(2,1)S(1)}, u32[]{:S(2)}, u32[]{:S(2)}) collective-permute-start(bf16[2,64,640]{2,1,0:T(8,128)(2,1)S(1)} %pad_maximum_fusion.10), channel_id=1, source_target_pairs={{0,1},{1,2},{2,3},{3,0},{4,5},{5,6},{6,7},{7,4},{8,9},{9,10},{10,1... | collective-permute-start | bytes 491528 | tf_op jit(solution)/shard_map/ppermute | solution.py:120
  13.5 1.0 %collective-permute-start.4 = (bf16[2,64,640]{2,1,0:T(8,128)(2,1)S(1)}, bf16[2,64,640]{2,1,0:T(8,128)(2,1)S(1)}, u32[]{:S(2)}, u32[]{:S(2)}) collective-permute-start(bf16[2,64,640]{2,1,0:T(8,128)(2,1)S(1)} %pad_maximum_fusion.10), channel_id=1, source_target_pairs={{0,2},{1,3},{2,0},{3,1},{4,6},{5,7},{6,4},{7,5},{8,10},{9,11},{10,... | collective-permute-start | bytes 491528 | tf_op jit(solution)/shard_map/ppermute | solution.py:120
  14.5 1.5 %collective-permute-start.5 = (bf16[2,64,640]{2,1,0:T(8,128)(2,1)S(1)}, bf16[2,64,640]{2,1,0:T(8,128)(2,1)S(1)}, u32[]{:S(2)}, u32[]{:S(2)}) collective-permute-start(bf16[2,64,640]{2,1,0:T(8,128)(2,1)S(1)} %pad_maximum_fusion.10), channel_id=1, source_target_pairs={{0,3},{1,0},{2,1},{3,2},{4,7},{5,4},{6,5},{7,6},{8,11},{9,8},{10,9... | collective-permute-start | bytes 491528 | tf_op jit(solution)/shard_map/ppermute | solution.py:120
  16.1 1.2 %convolution_convert_fusion.4.v_ref = bf16[256,640]{1,0:T(8,128)(2,1)} fusion(bf16[256,640]{1,0:T(8,128)(2,1)S(1)} %bitcast.72, bf16[640,1280]{1,0:T(8,128)(2,1)S(1)} %copy-done.5), kind=kOutput, calls=%fused_computation.14 | convolution fusion | flops 209879040 | bytes 1474560 | tf_op jit(solution)/shard_map/dot_general | solution.py:136
  17.3 1.2 %fusion.5.kt_ref = bf16[640,256]{1,0:T(8,128)(2,1)} fusion(bf16[256,640]{1,0:T(8,128)(2,1)S(1)} %bitcast.73, bf16[640,1280]{1,0:T(8,128)(2,1)S(1)} %copy-done.5), kind=kOutput, calls=%fused_computation.17 | convolution fusion | flops 209879040 | bytes 1474560 | tf_op jit(solution)/shard_map/dot_general | solution.py:133
  18.5 5.3 %shard_map.82 = (f32[256,640]{1,0:T(8,128)}, f32[256,640]{1,0:T(8,128)}, f32[256,640]{1,0:T(8,128)}) custom-call(bf16[256,640]{1,0:T(8,128)(2,1)} %convolution_convert_fusion.6.q_ref, bf16[640,256]{1,0:T(8,128)(2,1)} %fusion.5.kt_ref, bf16[256,640]{1,0:T(8,128)(2,1)} %convolution_convert_fusion.4.v_ref), custom_call_target="tpu_custom_call" | custom-call | tf_op jit(solution)/shard_map/pallas_call | solution.py:47
  23.7 3.9 %collective-permute-done.4 = bf16[2,64,640]{2,1,0:T(8,128)(2,1)S(1)} collective-permute-done((bf16[2,64,640]{2,1,0:T(8,128)(2,1)S(1)}, bf16[2,64,640]{2,1,0:T(8,128)(2,1)S(1)}, u32[]{:S(2)}, u32[]{:S(2)}) %collective-permute-start.4) | collective-permute-done | bytes 163872 | tf_op jit(solution)/shard_map/ppermute | solution.py:120
  27.6 2.1 %collective-permute-done.5 = bf16[2,64,640]{2,1,0:T(8,128)(2,1)S(1)} collective-permute-done((bf16[2,64,640]{2,1,0:T(8,128)(2,1)S(1)}, bf16[2,64,640]{2,1,0:T(8,128)(2,1)S(1)}, u32[]{:S(2)}, u32[]{:S(2)}) %collective-permute-start.5) | collective-permute-done | bytes 163872 | tf_op jit(solution)/shard_map/ppermute | solution.py:120
  31.0 0.7 %fusion.3 = bf16[640,384]{1,0:T(8,128)(2,1)S(1)} fusion(bf16[384,640]{1,0:T(8,128)(2,1)S(1)} %bitcast.71, bf16[640,1280]{1,0:T(8,128)(2,1)S(1)} %copy-done.6), kind=kOutput, calls=%fused_computation.12 | convolution fusion | flops 314818560 | bytes 1802240 | tf_op jit(solution)/shard_map/dot_general | solution.py:133
  31.9 0.6 convolution_convert_fusion
  32.5 1.1 %pad_maximum_fusion.1.v_ref = bf16[768,640]{1,0:T(8,128)(2,1)} fusion(bf16[384,640]{1,0:T(8,128)(2,1)S(1)} %convolution_convert_fusion, bf16[384,640]{1,0:T(8,128)(2,1)S(1)} %convolution_convert_fusion.1), kind=kLoop, calls=%fused_computation.19 | loop fusion | flops 1966080 | bytes 1966080 | tf_op jit(solution)/shard_map/concatenate | solution.py:146
  33.5 0.7 %fusion.4 = bf16[640,384]{1,0:T(8,128)(2,1)S(1)} fusion(bf16[384,640]{1,0:T(8,128)(2,1)S(1)} %collective-permute-done.7, bf16[640,1280]{1,0:T(8,128)(2,1)S(1)} %copy-done.6), kind=kOutput, calls=%fused_computation.13 | convolution fusion | flops 314818560 | bytes 1802240 | tf_op jit(solution)/shard_map/dot_general | solution.py:133
  34.3 1.0 %pad_maximum_fusion.kt_ref = bf16[640,768]{1,0:T(8,128)(2,1)} fusion(bf16[640,384]{1,0:T(8,128)(2,1)S(1)} %fusion.4, bf16[640,384]{1,0:T(8,128)(2,1)S(1)} %fusion.3), kind=kLoop, calls=%fused_computation.18 | loop fusion | flops 1966080 | bytes 1966080 | tf_op jit(solution)/shard_map/concatenate | solution.py:145
  35.3 7.6 %shard_map.83 = bf16[256,640]{1,0:T(8,128)(2,1)} custom-call(bf16[256,640]{1,0:T(8,128)(2,1)} %convolution_convert_fusion.6.q_ref, bf16[640,768]{1,0:T(8,128)(2,1)} %pad_maximum_fusion.kt_ref, bf16[768,640]{1,0:T(8,128)(2,1)} %pad_maximum_fusion.1.v_ref, f32[256,640]{1,0:T(8,128)} %get-tuple-element.22.m_ref, f32[256,640]{1,0:T(8,128)} %get-tuple-element.23.l_ref, ...), custom_call_target="tpu_custom_call" | custom-call | tf_op jit(solution)/shard_map/pallas_call | solution.py:61
  42.9 1.5 %multiply_reduce_fusion = (f32[256]{0:T(256)S(1)}, f32[256,640]{1,0:T(8,128)S(1)}) fusion(bf16[256,640]{1,0:T(8,128)(2,1)} %shard_map.83, bf16[640,640]{1,0:T(8,128)(2,1)S(1)} %copy-done, bf16[256,640]{1,0:T(8,128)(2,1)S(1)} %bitcast.59), kind=kOutput, calls=%fused_computation.40 | convolution fusion | flops 210370304 | bytes 2130944 | tf_op jit(solution)/shard_map/dot_general | solution.py:148
  44.6 3.3 %collective-permute-start.8 = (bf16[2,128,640]{2,1,0:T(8,128)(2,1)S(1)}, bf16[2,128,640]{2,1,0:T(8,128)(2,1)S(1)}, u32[]{:S(2)}, u32[]{:S(2)}) collective-permute-start(bf16[2,128,640]{2,1,0:T(8,128)(2,1)S(1)} %bitcast.65), channel_id=1, source_target_pairs={{0,4},{4,8},{8,12},{1,5},{5,9},{9,13},{2,6},{6,10},{10,14},{3,7},{... | collective-permute-start | bytes 983048 | tf_op jit(solution)/shard_map/ppermute | solution.py:76
  47.9 1.9 %collective-permute-start.9 = (bf16[2,128,640]{2,1,0:T(8,128)(2,1)S(1)}, bf16[2,128,640]{2,1,0:T(8,128)(2,1)S(1)}, u32[]{:S(2)}, u32[]{:S(2)}) collective-permute-start(bf16[2,128,640]{2,1,0:T(8,128)(2,1)S(1)} %bitcast.66), channel_id=1, source_target_pairs={{4,0},{8,4},{12,8},{5,1},{9,5},{13,9},{6,2},{10,6},{14,10},{7,3},{... | collective-permute-start | bytes 983048 | tf_op jit(solution)/shard_map/ppermute | solution.py:77
  49.9 2.0 %collective-permute-done.8 = bf16[2,128,640]{2,1,0:T(8,128)(2,1)S(1)} collective-permute-done((bf16[2,128,640]{2,1,0:T(8,128)(2,1)S(1)}, bf16[2,128,640]{2,1,0:T(8,128)(2,1)S(1)}, u32[]{:S(2)}, u32[]{:S(2)}) %collective-permute-start.8) | collective-permute-done | bytes 327712 | tf_op jit(solution)/shard_map/ppermute | solution.py:76
  51.9 4.4 %collective-permute-done.9 = bf16[2,128,640]{2,1,0:T(8,128)(2,1)S(1)} collective-permute-done((bf16[2,128,640]{2,1,0:T(8,128)(2,1)S(1)}, bf16[2,128,640]{2,1,0:T(8,128)(2,1)S(1)}, u32[]{:S(2)}, u32[]{:S(2)}) %collective-permute-start.9) | collective-permute-done | bytes 327712 | tf_op jit(solution)/shard_map/ppermute | solution.py:77
  56.6 0.7 %fusion.10 = f32[512,640]{1,0:T(8,128)S(1)} fusion(bf16[512,640]{1,0:T(8,128)(2,1)S(1)} %bitcast.61, bf16[3,640,640]{2,1,0:T(8,128)(2,1)S(1)} %copy-done.3), kind=kOutput, calls=%fused_computation.24 | convolution fusion | flops 419430400 | bytes 2785280 | tf_op jit(solution)/shard_map/dot_general | solution.py:85
  57.3 0.7 %fusion.12 = f32[512,640]{1,0:T(8,128)S(1)} fusion(bf16[512,640]{1,0:T(8,128)(2,1)S(1)} %bitcast.60, bf16[3,640,640]{2,1,0:T(8,128)(2,1)S(1)} %copy-done.3), kind=kOutput, calls=%fused_computation.26 | convolution fusion | flops 419430400 | bytes 2785280 | tf_op jit(solution)/shard_map/dot_general | solution.py:85
  58.1 0.8 %multiply_convert_fusion = bf16[512,640]{1,0:T(8,128)(2,1)S(1)} fusion(f32[512,640]{1,0:T(8,128)S(1)} %fusion.10, f32[512,640]{1,0:T(8,128)S(1)} %fusion.12, bf16[512,640]{1,0:T(8,128)(2,1)S(1)} %bitcast.68, bf16[3,640,640]{2,1,0:T(8,128)(2,1)S(1)} %copy-done.3), kind=kOutput, calls=%fused_computation.2 | convolution fusion | flops 421724160 | bytes 4751360 | tf_op jit(solution)/shard_map/dot_general | solution.py:85
  59.1 1.5 %copy-done.2 = bf16[3,640,640]{2,1,0:T(8,128)(2,1)S(1)} copy-done((bf16[3,640,640]{2,1,0:T(8,128)(2,1)S(1)}, bf16[3,640,640]{2,1,0:T(8,128)(2,1)}, u32[]{:S(2)}) %copy-start.2) | copy-done | bytes 2457624
  61.5 1.2 %fusion.2 = bf16[256,640]{1,0:T(8,128)(2,1)} fusion(f32[256,640]{1,0:T(8,128)S(1)} %get-tuple-element.40, f32[256,640]{1,0:T(8,128)S(1)} %convolution_add_fusion.2, bf16[256,640]{1,0:T(8,128)(2,1)S(1)} %bitcast.64, bf16[3,640,640]{2,1,0:T(8,128)(2,1)S(1)} %copy-done.2), kind=kOutput, calls=%fused_computation.11 | convolution fusion | flops 210206720 | bytes 2785280 | tf_op jit(solution)/shard_map/dot_general | solution.py:85
  (32 shorter events, 3.0 us)
Async XLA Ops:
  0.0 42.9 %copy-start = (bf16[640,640]{1,0:T(8,128)(2,1)S(1)}, bf16[640,640]{1,0:T(8,128)(2,1)}, u32[]{:S(2)}) copy-start(bf16[640,640]{1,0:T(8,128)(2,1)} %param.12) | copy-start | bytes 2457604
  0.0 10.7 %copy-start.1 = (bf16[2,128,640]{2,1,0:T(8,128)(2,1)S(1)}, bf16[2,128,640]{2,1,0:T(8,128)(2,1)}, u32[]{:S(2)}) copy-start(bf16[2,128,640]{2,1,0:T(8,128)(2,1)} %param.8) | copy-start | bytes 983044
  1.2 8.6 %collective-permute-start = (bf16[2,64,640]{2,1,0:T(8,128)(2,1)S(1)}, bf16[2,64,640]{2,1,0:T(8,128)(2,1)S(1)}, u32[]{:S(2)}, u32[]{:S(2)}) collective-permute-start(bf16[2,64,640]{2,1,0:T(8,128)(2,1)S(1)} %get-tuple-element.34), channel_id=1, source_target_pairs={{0,12},{4,0},{8,4},{12,8},{1,13},{5,1},{9,5},{13,9},{2,14},{6,2},{... | collective-permute-start | bytes 491528 | tf_op jit(solution)/shard_map/ppermute | solution.py:110
  1.9 7.8 %collective-permute-start.1 = (bf16[2,64,640]{2,1,0:T(8,128)(2,1)S(1)}, bf16[2,64,640]{2,1,0:T(8,128)(2,1)S(1)}, u32[]{:S(2)}, u32[]{:S(2)}) collective-permute-start(bf16[2,64,640]{2,1,0:T(8,128)(2,1)S(1)} %get-tuple-element.36), channel_id=1, source_target_pairs={{0,8},{4,12},{8,0},{12,4},{1,9},{5,13},{9,1},{13,5},{2,10},{6,14},... | collective-permute-start | bytes 491528 | tf_op jit(solution)/shard_map/ppermute | solution.py:110
  3.2 7.5 %collective-permute-start.2 = (bf16[2,64,640]{2,1,0:T(8,128)(2,1)S(1)}, bf16[2,64,640]{2,1,0:T(8,128)(2,1)S(1)}, u32[]{:S(2)}, u32[]{:S(2)}) collective-permute-start(bf16[2,64,640]{2,1,0:T(8,128)(2,1)S(1)} %get-tuple-element.35), channel_id=1, source_target_pairs={{0,4},{4,8},{8,12},{12,0},{1,5},{5,9},{9,13},{13,1},{2,6},{6,10},{... | collective-permute-start | bytes 491528 | tf_op jit(solution)/shard_map/ppermute | solution.py:110
  7.2 8.8 %copy-start.5 = (bf16[640,1280]{1,0:T(8,128)(2,1)S(1)}, bf16[640,1280]{1,0:T(8,128)(2,1)}, u32[]{:S(2)}) copy-start(bf16[640,1280]{1,0:T(8,128)(2,1)} %param.11) | copy-start | bytes 4915204
  10.8 5.2 %collective-permute-start.6 = (bf16[2,64,640]{2,1,0:T(8,128)(2,1)S(1)}, bf16[2,64,640]{2,1,0:T(8,128)(2,1)S(1)}, u32[]{:S(2)}, u32[]{:S(2)}) collective-permute-start(bf16[2,64,640]{2,1,0:T(8,128)(2,1)S(1)} %pad_maximum_fusion.10), channel_id=1, source_target_pairs={{0,4},{4,0},{8,12},{12,8},{1,5},{5,1},{9,13},{13,9},{2,6},{6,2},{1... | collective-permute-start | bytes 491528 | tf_op jit(solution)/shard_map/ppermute | solution.py:117
  12.2 11.5 %collective-permute-start.3 = (bf16[2,64,640]{2,1,0:T(8,128)(2,1)S(1)}, bf16[2,64,640]{2,1,0:T(8,128)(2,1)S(1)}, u32[]{:S(2)}, u32[]{:S(2)}) collective-permute-start(bf16[2,64,640]{2,1,0:T(8,128)(2,1)S(1)} %pad_maximum_fusion.10), channel_id=1, source_target_pairs={{0,1},{1,2},{2,3},{3,0},{4,5},{5,6},{6,7},{7,4},{8,9},{9,10},{10,1... | collective-permute-start | bytes 491528 | tf_op jit(solution)/shard_map/ppermute | solution.py:120
  13.5 14.1 %collective-permute-start.4 = (bf16[2,64,640]{2,1,0:T(8,128)(2,1)S(1)}, bf16[2,64,640]{2,1,0:T(8,128)(2,1)S(1)}, u32[]{:S(2)}, u32[]{:S(2)}) collective-permute-start(bf16[2,64,640]{2,1,0:T(8,128)(2,1)S(1)} %pad_maximum_fusion.10), channel_id=1, source_target_pairs={{0,2},{1,3},{2,0},{3,1},{4,6},{5,7},{6,4},{7,5},{8,10},{9,11},{10,... | collective-permute-start | bytes 491528 | tf_op jit(solution)/shard_map/ppermute | solution.py:120
  14.5 15.2 %collective-permute-start.5 = (bf16[2,64,640]{2,1,0:T(8,128)(2,1)S(1)}, bf16[2,64,640]{2,1,0:T(8,128)(2,1)S(1)}, u32[]{:S(2)}, u32[]{:S(2)}) collective-permute-start(bf16[2,64,640]{2,1,0:T(8,128)(2,1)S(1)} %pad_maximum_fusion.10), channel_id=1, source_target_pairs={{0,3},{1,0},{2,1},{3,2},{4,7},{5,4},{6,5},{7,6},{8,11},{9,8},{10,9... | collective-permute-start | bytes 491528 | tf_op jit(solution)/shard_map/ppermute | solution.py:120
  17.3 13.1 %copy-start.6 = (bf16[640,1280]{1,0:T(8,128)(2,1)S(1)}, bf16[640,1280]{1,0:T(8,128)(2,1)}, u32[]{:S(2)}) copy-start(bf16[640,1280]{1,0:T(8,128)(2,1)} %param.11) | copy-start | bytes 4915204
  29.8 2.0 %collective-permute-start.7 = (bf16[384,640]{1,0:T(8,128)(2,1)S(1)}, bf16[384,640]{1,0:T(8,128)(2,1)S(1)}, u32[]{:S(2)}, u32[]{:S(2)}) collective-permute-start(bf16[384,640]{1,0:T(8,128)(2,1)S(1)} %bitcast.69), channel_id=1, source_target_pairs={{0,4},{4,0},{8,12},{12,8},{1,5},{5,1},{9,13},{13,9},{2,6},{6,2},{1... | collective-permute-start | bytes 1474568 | tf_op jit(solution)/shard_map/ppermute | solution.py:142
  42.9 1.6 %copy-start.4 = (f32[640]{0:T(1024)S(1)}, f32[640]{0:T(1024)}, u32[]{:S(2)}) copy-start(f32[640]{0:T(1024)} %param.13) | copy-start | bytes 7684
  44.6 7.3 %collective-permute-start.8 = (bf16[2,128,640]{2,1,0:T(8,128)(2,1)S(1)}, bf16[2,128,640]{2,1,0:T(8,128)(2,1)S(1)}, u32[]{:S(2)}, u32[]{:S(2)}) collective-permute-start(bf16[2,128,640]{2,1,0:T(8,128)(2,1)S(1)} %bitcast.65), channel_id=1, source_target_pairs={{0,4},{4,8},{8,12},{1,5},{5,9},{9,13},{2,6},{6,10},{10,14},{3,7},{... | collective-permute-start | bytes 983048 | tf_op jit(solution)/shard_map/ppermute | solution.py:76
  47.9 8.4 %collective-permute-start.9 = (bf16[2,128,640]{2,1,0:T(8,128)(2,1)S(1)}, bf16[2,128,640]{2,1,0:T(8,128)(2,1)S(1)}, u32[]{:S(2)}, u32[]{:S(2)}) collective-permute-start(bf16[2,128,640]{2,1,0:T(8,128)(2,1)S(1)} %bitcast.66), channel_id=1, source_target_pairs={{4,0},{8,4},{12,8},{5,1},{9,5},{13,9},{6,2},{10,6},{14,10},{7,3},{... | collective-permute-start | bytes 983048 | tf_op jit(solution)/shard_map/ppermute | solution.py:77
  49.9 6.7 %copy-start.3 = (bf16[3,640,640]{2,1,0:T(8,128)(2,1)S(1)}, bf16[3,640,640]{2,1,0:T(8,128)(2,1)}, u32[]{:S(2)}) copy-start(bf16[3,640,640]{2,1,0:T(8,128)(2,1)} %param.14) | copy-start | bytes 7372804
  58.9 1.7 %copy-start.2 = (bf16[3,640,640]{2,1,0:T(8,128)(2,1)S(1)}, bf16[3,640,640]{2,1,0:T(8,128)(2,1)}, u32[]{:S(2)}) copy-start(bf16[3,640,640]{2,1,0:T(8,128)(2,1)} %param.15) | copy-start | bytes 7372804

commit v12 on v7

--- a/solution.py
+++ b/solution.py
@@ -9,35 +9,36 @@
 
 
 def attention_kernel(q_ref, kt_ref, v_ref, o_ref):
-    outs = []
-    for hh in range(2):
-        cols = slice(hh * HEAD_DIM, (hh + 1) * HEAD_DIM)
-        scores = jnp.dot(q_ref[:, cols], kt_ref[cols, :], preferred_element_type=jnp.float32)
-        scores = scores * HEAD_DIM ** (-0.5)
-        highest = jnp.max(scores, axis=1, keepdims=True)
-        exponent = jnp.exp(scores - highest)
-        denominator = jnp.sum(exponent, axis=1, keepdims=True)
-        mixed = jnp.dot(exponent.astype(jnp.bfloat16), v_ref[:, cols], preferred_element_type=jnp.float32)
-        outs.append(mixed / denominator)
-    o_ref[...] = jnp.concatenate(outs, axis=1).astype(o_ref.dtype)
+    heads = [slice(h * HEAD_DIM, (h + 1) * HEAD_DIM) for h in range(q_ref.shape[1] // HEAD_DIM)]
+    scores = [
+        jnp.dot(q_ref[:, c], kt_ref[c, :], preferred_element_type=jnp.float32) * HEAD_DIM ** (-0.5) for c in heads
+    ]
+    highest = [jnp.max(s, axis=1, keepdims=True) for s in scores]
+    exponent = [jnp.exp(s - m) for s, m in zip(scores, highest)]
+    denominator = [jnp.sum(e, axis=1, keepdims=True) for e in exponent]
+    mixed = [
+        jnp.dot(e.astype(jnp.bfloat16), v_ref[:, c], preferred_element_type=jnp.float32)
+        for e, c in zip(exponent, heads)
+    ]
+    o_ref[...] = jnp.concatenate([m / d for m, d in zip(mixed, denominator)], axis=1).astype(o_ref.dtype)
 
 
-def attend(queries, keys_t, values, q_tile=256):
+def attend(queries, keys_t, values):
     total, channels = queries.shape
     count = values.shape[0]
-    pairs = channels // (2 * HEAD_DIM)
-    width = 2 * HEAD_DIM
+    width = channels if total * count * channels <= 256 * 1024 * 640 else 2 * HEAD_DIM
     return pl.pallas_call(
         attention_kernel,
-        grid=(pairs, total // q_tile),
+        grid=(channels // width,),
         in_specs=[
-            pl.BlockSpec((q_tile, width), lambda j, i: (i, j)),
-            pl.BlockSpec((width, count), lambda j, i: (j, 0)),
-            pl.BlockSpec((count, width), lambda j, i: (0, j)),
+            pl.BlockSpec((total, width), lambda j: (0, j)),
+            pl.BlockSpec((width, count), lambda j: (j, 0)),
+            pl.BlockSpec((count, width), lambda j: (0, j)),
         ],
-        out_specs=pl.BlockSpec((q_tile, width), lambda j, i: (i, j)),
+        out_specs=pl.BlockSpec((total, width), lambda j: (0, j)),
         out_shape=jax.ShapeDtypeStruct((total, channels), jnp.bfloat16),
     )(queries, keys_t, values)
+
 
 def extended(array, axis, width):
     size, length = (lax.axis_size(axis), array.shape[0])

time: 62 us -> 60.8 us (0.981)
  Pallas kernels: 8.04 us -> 6.86 us
    pallas_call x1, Pallas kernels: 8.04 us -> 6.86 us  [attend(): pl.pallas_call(attention_kernel, grid=(channels // width,), in_specs=[pl....]
where the time goes in v12:
time: 60.8 us; the launch traced here: 60.5 us
  waiting for transfers between devices  21.1 us (35%)
  starting transfers between devices  12.2 us (20%)
  matrix products  11.5 us (19%)
  Pallas kernels  6.86 us (11%)
  local copies, waits for them, and re-layouts  4.11 us (7%)
  other arithmetic  3.16 us (5%)
  between operations  1.66 us (3%)
    ppermute x3, waiting for transfers between devices, gather_keyframes(): lax.ppermute(piece, 'row', [(i, (i + s) % rsize) for i in range(rsize)])  13.7 us
    pallas_call x1, Pallas kernels, attend(): pl.pallas_call(attention_kernel, grid=(channels // width,), in_specs=[pl....  6.86 us
    dot_general x6, matrix products, temporal_mix(): jnp.dot(window, weights[offset], preferred_element_type=jnp.float32)  4.44 us
    ppermute x1, waiting for transfers between devices, extended(): after = lax.ppermute(first, axis, down)  4.4 us
    ppermute x3, starting transfers between devices, gather_keyframes(): lax.ppermute(piece, 'row', [(i, (i + s) % rsize) for i in range(rsize)])  3.83 us
    ppermute x3, starting transfers between devices, gather_keyframes(): lax.ppermute(halves((me + s) % 2), 'frame', [(i, (i + s) % fsize) for i i...  3.29 us
    dot_general x1, matrix products, shards(): jnp.dot(flattened, w_query, preferred_element_type=jnp.float32)  2.55 us
    ppermute x1, starting transfers between devices, extended(): before = lax.ppermute(last, axis, up)  2.44 us
  transfers between devices with their start and end apart: 9, of which 7 were waited for; matrix products, arithmetic and copies ran while one was open for 9% of the time, Pallas kernels for 0%

profile of v12, /device:TPU:9, one launch (start us, length us, event | category | flops | bytes accessed | tf_op | source)
XLA Modules:
  0.0 60.5 jit_solution(13147425709018492076)
XLA Ops:
  0.0 1.2 %constant_dynamic-slice_fusion.2 = (bf16[2,64,640]{2,1,0:T(8,128)(2,1)S(1)}, bf16[2,64,640]{2,1,0:T(8,128)(2,1)S(1)}, bf16[2,64,640]{2,1,0:T(8,128)(2,1)S(1)}) fusion(bf16[2,128,640]{2,1,0:T(8,128)(2,1)} %param.8, s32[]{:T(128)S(6)} %select_n.137, s32[]{:T(128)S(6)} %select_n.147, s32[]{:T(128)S(6)} %select_n.143), kind=kLoop, calls=%fused_computation.56 | loop fusion | bytes 983052 | tf_op jit(solution)/shard_map/dynamic_slice | solution.py:75
  1.2 0.7 %collective-permute-start = (bf16[2,64,640]{2,1,0:T(8,128)(2,1)S(1)}, bf16[2,64,640]{2,1,0:T(8,128)(2,1)S(1)}, u32[]{:S(2)}, u32[]{:S(2)}) collective-permute-start(bf16[2,64,640]{2,1,0:T(8,128)(2,1)S(1)} %get-tuple-element.16), channel_id=1, source_target_pairs={{0,12},{4,0},{8,4},{12,8},{1,13},{5,1},{9,5},{13,9},{2,14},{6,2},{... | collective-permute-start | bytes 491528 | tf_op jit(solution)/shard_map/ppermute | solution.py:83
  1.9 1.2 %collective-permute-start.1 = (bf16[2,64,640]{2,1,0:T(8,128)(2,1)S(1)}, bf16[2,64,640]{2,1,0:T(8,128)(2,1)S(1)}, u32[]{:S(2)}, u32[]{:S(2)}) collective-permute-start(bf16[2,64,640]{2,1,0:T(8,128)(2,1)S(1)} %get-tuple-element.18), channel_id=1, source_target_pairs={{0,8},{4,12},{8,0},{12,4},{1,9},{5,13},{9,1},{13,5},{2,10},{6,14},... | collective-permute-start | bytes 491528 | tf_op jit(solution)/shard_map/ppermute | solution.py:83
  3.2 1.3 %collective-permute-start.2 = (bf16[2,64,640]{2,1,0:T(8,128)(2,1)S(1)}, bf16[2,64,640]{2,1,0:T(8,128)(2,1)S(1)}, u32[]{:S(2)}, u32[]{:S(2)}) collective-permute-start(bf16[2,64,640]{2,1,0:T(8,128)(2,1)S(1)} %get-tuple-element.17), channel_id=1, source_target_pairs={{0,4},{4,8},{8,12},{12,0},{1,5},{5,9},{9,13},{13,1},{2,6},{6,10},{... | collective-permute-start | bytes 491528 | tf_op jit(solution)/shard_map/ppermute | solution.py:83
  4.5 1.3 %fusion.29 = (s32[1]{0:T(128)}, s32[1]{0:T(128)}) fusion(s32[2]{0:T(128)} %param.9), kind=kLoop, calls=%fused_computation.59 | loop fusion | bytes 16 | tf_op jit(solution)/shard_map/slice | solution.py:68
  7.3 2.5 %convolution_convert_fusion.4.q_ref = bf16[256,640]{1,0:T(8,128)(2,1)} fusion(bf16[256,640]{1,0:T(8,128)(2,1)} %bitcast.54, bf16[640,640]{1,0:T(8,128)(2,1)} %param.10), kind=kOutput, calls=%fused_computation.16 | convolution fusion | flops 209879040 | bytes 1474560 | tf_op jit(solution)/shard_map/dot_general | solution.py:101
  9.9 0.8 %collective-permute-done.2 = bf16[2,64,640]{2,1,0:T(8,128)(2,1)S(1)} collective-permute-done((bf16[2,64,640]{2,1,0:T(8,128)(2,1)S(1)}, bf16[2,64,640]{2,1,0:T(8,128)(2,1)S(1)}, u32[]{:S(2)}, u32[]{:S(2)}) %collective-permute-start.2) | collective-permute-done | bytes 163872 | tf_op jit(solution)/shard_map/ppermute | solution.py:83
  10.8 1.4 %collective-permute-start.3 = (bf16[2,64,640]{2,1,0:T(8,128)(2,1)S(1)}, bf16[2,64,640]{2,1,0:T(8,128)(2,1)S(1)}, u32[]{:S(2)}, u32[]{:S(2)}) collective-permute-start(bf16[2,64,640]{2,1,0:T(8,128)(2,1)S(1)} %pad_maximum_fusion.9), channel_id=1, source_target_pairs={{0,1},{1,2},{2,3},{3,0},{4,5},{5,6},{6,7},{7,4},{8,9},{9,10},{10,1... | collective-permute-start | bytes 491528 | tf_op jit(solution)/shard_map/ppermute | solution.py:91
  12.2 1.1 %collective-permute-start.4 = (bf16[2,64,640]{2,1,0:T(8,128)(2,1)S(1)}, bf16[2,64,640]{2,1,0:T(8,128)(2,1)S(1)}, u32[]{:S(2)}, u32[]{:S(2)}) collective-permute-start(bf16[2,64,640]{2,1,0:T(8,128)(2,1)S(1)} %pad_maximum_fusion.9), channel_id=1, source_target_pairs={{0,2},{1,3},{2,0},{3,1},{4,6},{5,7},{6,4},{7,5},{8,10},{9,11},{10,... | collective-permute-start | bytes 491528 | tf_op jit(solution)/shard_map/ppermute | solution.py:91
  13.3 1.4 %collective-permute-start.5 = (bf16[2,64,640]{2,1,0:T(8,128)(2,1)S(1)}, bf16[2,64,640]{2,1,0:T(8,128)(2,1)S(1)}, u32[]{:S(2)}, u32[]{:S(2)}) collective-permute-start(bf16[2,64,640]{2,1,0:T(8,128)(2,1)S(1)} %pad_maximum_fusion.9), channel_id=1, source_target_pairs={{0,3},{1,0},{2,1},{3,2},{4,7},{5,4},{6,5},{7,6},{8,11},{9,8},{10,9... | collective-permute-start | bytes 491528 | tf_op jit(solution)/shard_map/ppermute | solution.py:91
  15.0 9.8 %collective-permute-done.4 = bf16[2,64,640]{2,1,0:T(8,128)(2,1)S(1)} collective-permute-done((bf16[2,64,640]{2,1,0:T(8,128)(2,1)S(1)}, bf16[2,64,640]{2,1,0:T(8,128)(2,1)S(1)}, u32[]{:S(2)}, u32[]{:S(2)}) %collective-permute-start.4) | collective-permute-done | bytes 163872 | tf_op jit(solution)/shard_map/ppermute | solution.py:91
  24.9 3.5 %collective-permute-done.5 = bf16[2,64,640]{2,1,0:T(8,128)(2,1)S(1)} collective-permute-done((bf16[2,64,640]{2,1,0:T(8,128)(2,1)S(1)}, bf16[2,64,640]{2,1,0:T(8,128)(2,1)S(1)}, u32[]{:S(2)}, u32[]{:S(2)}) %collective-permute-start.5) | collective-permute-done | bytes 163872 | tf_op jit(solution)/shard_map/ppermute | solution.py:91
  28.5 0.6 collective-permute-start.6
  29.0 0.7 %convolution_convert_fusion.1 = bf16[512,640]{1,0:T(8,128)(2,1)S(1)} fusion(bf16[512,640]{1,0:T(8,128)(2,1)S(1)} %bitcast.66, bf16[640,1280]{1,0:T(8,128)(2,1)S(1)} %copy-done.5), kind=kOutput, calls=%fused_computation.3 | convolution fusion | flops 419758080 | bytes 2129920 | tf_op jit(solution)/shard_map/dot_general | solution.py:109
  29.8 0.7 %fusion.1 = bf16[640,512]{1,0:T(8,128)(2,1)S(1)} fusion(bf16[512,640]{1,0:T(8,128)(2,1)S(1)} %bitcast.67, bf16[640,1280]{1,0:T(8,128)(2,1)S(1)} %copy-done.5), kind=kOutput, calls=%fused_computation.9 | convolution fusion | flops 419758080 | bytes 2129920 | tf_op jit(solution)/shard_map/dot_general | solution.py:106
  30.8 0.7 %convolution_convert_fusion = bf16[512,640]{1,0:T(8,128)(2,1)S(1)} fusion(bf16[512,640]{1,0:T(8,128)(2,1)S(1)} %collective-permute-done.6, bf16[640,1280]{1,0:T(8,128)(2,1)S(1)} %copy-done.5), kind=kOutput, calls=%fused_computation.2 | convolution fusion | flops 419758080 | bytes 2129920 | tf_op jit(solution)/shard_map/dot_general | solution.py:109
  31.5 1.2 %pad_maximum_fusion.1.v_ref = bf16[1024,640]{1,0:T(8,128)(2,1)} fusion(bf16[512,640]{1,0:T(8,128)(2,1)S(1)} %convolution_convert_fusion, bf16[512,640]{1,0:T(8,128)(2,1)S(1)} %convolution_convert_fusion.1), kind=kLoop, calls=%fused_computation.7 | loop fusion | flops 2621440 | bytes 2621440 | tf_op jit(solution)/shard_map/concatenate | solution.py:115
  32.7 0.7 %fusion.2 = bf16[640,512]{1,0:T(8,128)(2,1)S(1)} fusion(bf16[512,640]{1,0:T(8,128)(2,1)S(1)} %collective-permute-done.6, bf16[640,1280]{1,0:T(8,128)(2,1)S(1)} %copy-done.5), kind=kOutput, calls=%fused_computation.10 | convolution fusion | flops 419758080 | bytes 2129920 | tf_op jit(solution)/shard_map/dot_general | solution.py:106
  33.4 1.2 %pad_maximum_fusion.kt_ref = bf16[640,1024]{1,0:T(8,128)(2,1)} fusion(bf16[640,512]{1,0:T(8,128)(2,1)S(1)} %fusion.2, bf16[640,512]{1,0:T(8,128)(2,1)S(1)} %fusion.1), kind=kLoop, calls=%fused_computation.6 | loop fusion | flops 2621440 | bytes 2621440 | tf_op jit(solution)/shard_map/concatenate | solution.py:114
  34.7 6.9 %shard_map.82 = bf16[256,640]{1,0:T(8,128)(2,1)} custom-call(bf16[256,640]{1,0:T(8,128)(2,1)} %convolution_convert_fusion.4.q_ref, bf16[640,1024]{1,0:T(8,128)(2,1)} %pad_maximum_fusion.kt_ref, bf16[1024,640]{1,0:T(8,128)(2,1)} %pad_maximum_fusion.1.v_ref), custom_call_target="tpu_custom_call" | custom-call | tf_op jit(solution)/shard_map/pallas_call | solution.py:30
  41.5 1.5 %multiply_reduce_fusion = (f32[256]{0:T(256)S(1)}, f32[256,640]{1,0:T(8,128)S(1)}) fusion(bf16[256,640]{1,0:T(8,128)(2,1)} %shard_map.82, bf16[640,640]{1,0:T(8,128)(2,1)S(1)} %copy-done, bf16[256,640]{1,0:T(8,128)(2,1)S(1)} %bitcast.55), kind=kOutput, calls=%fused_computation.42 | convolution fusion | flops 210370304 | bytes 2130944 | tf_op jit(solution)/shard_map/dot_general | solution.py:117
  43.2 2.4 %collective-permute-start.7 = (bf16[2,128,640]{2,1,0:T(8,128)(2,1)S(1)}, bf16[2,128,640]{2,1,0:T(8,128)(2,1)S(1)}, u32[]{:S(2)}, u32[]{:S(2)}) collective-permute-start(bf16[2,128,640]{2,1,0:T(8,128)(2,1)S(1)} %bitcast.61), channel_id=1, source_target_pairs={{0,4},{4,8},{8,12},{1,5},{5,9},{9,13},{2,6},{6,10},{10,14},{3,7},{... | collective-permute-start | bytes 983048 | tf_op jit(solution)/shard_map/ppermute | solution.py:49
  45.7 2.1 %collective-permute-start.8 = (bf16[2,128,640]{2,1,0:T(8,128)(2,1)S(1)}, bf16[2,128,640]{2,1,0:T(8,128)(2,1)S(1)}, u32[]{:S(2)}, u32[]{:S(2)}) collective-permute-start(bf16[2,128,640]{2,1,0:T(8,128)(2,1)S(1)} %bitcast.62), channel_id=1, source_target_pairs={{4,0},{8,4},{12,8},{5,1},{9,5},{13,9},{6,2},{10,6},{14,10},{7,3},{... | collective-permute-start | bytes 983048 | tf_op jit(solution)/shard_map/ppermute | solution.py:50
  47.8 1.9 %collective-permute-done.7 = bf16[2,128,640]{2,1,0:T(8,128)(2,1)S(1)} collective-permute-done((bf16[2,128,640]{2,1,0:T(8,128)(2,1)S(1)}, bf16[2,128,640]{2,1,0:T(8,128)(2,1)S(1)}, u32[]{:S(2)}, u32[]{:S(2)}) %collective-permute-start.7) | collective-permute-done | bytes 327712 | tf_op jit(solution)/shard_map/ppermute | solution.py:49
  49.7 4.4 %collective-permute-done.8 = bf16[2,128,640]{2,1,0:T(8,128)(2,1)S(1)} collective-permute-done((bf16[2,128,640]{2,1,0:T(8,128)(2,1)S(1)}, bf16[2,128,640]{2,1,0:T(8,128)(2,1)S(1)}, u32[]{:S(2)}, u32[]{:S(2)}) %collective-permute-start.8) | collective-permute-done | bytes 327712 | tf_op jit(solution)/shard_map/ppermute | solution.py:50
  54.3 0.7 %fusion.11 = f32[512,640]{1,0:T(8,128)S(1)} fusion(bf16[512,640]{1,0:T(8,128)(2,1)S(1)} %bitcast.57, bf16[3,640,640]{2,1,0:T(8,128)(2,1)S(1)} %copy-done.3), kind=kOutput, calls=%fused_computation.23 | convolution fusion | flops 419430400 | bytes 2785280 | tf_op jit(solution)/shard_map/dot_general | solution.py:58
  55.1 0.7 %fusion.9 = f32[512,640]{1,0:T(8,128)S(1)} fusion(bf16[512,640]{1,0:T(8,128)(2,1)S(1)} %bitcast.56, bf16[3,640,640]{2,1,0:T(8,128)(2,1)S(1)} %copy-done.3), kind=kOutput, calls=%fused_computation.21 | convolution fusion | flops 419430400 | bytes 2785280 | tf_op jit(solution)/shard_map/dot_general | solution.py:58
  55.8 0.8 %multiply_convert_fusion = bf16[512,640]{1,0:T(8,128)(2,1)S(1)} fusion(f32[512,640]{1,0:T(8,128)S(1)} %fusion.9, f32[512,640]{1,0:T(8,128)S(1)} %fusion.11, bf16[512,640]{1,0:T(8,128)(2,1)S(1)} %bitcast.68, bf16[3,640,640]{2,1,0:T(8,128)(2,1)S(1)} %copy-done.3), kind=kOutput, calls=%fused_computation.8 | convolution fusion | flops 421724160 | bytes 4751360 | tf_op jit(solution)/shard_map/dot_general | solution.py:58
  56.9 1.5 %copy-done.2 = bf16[3,640,640]{2,1,0:T(8,128)(2,1)S(1)} copy-done((bf16[3,640,640]{2,1,0:T(8,128)(2,1)S(1)}, bf16[3,640,640]{2,1,0:T(8,128)(2,1)}, u32[]{:S(2)}) %copy-start.2) | copy-done | bytes 2457624
  58.4 0.5 fusion.7
  58.8 0.5 convolution_add_fusion.2
  59.3 1.2 %fusion.4 = bf16[256,640]{1,0:T(8,128)(2,1)} fusion(f32[256,640]{1,0:T(8,128)S(1)} %get-tuple-element.22, f32[256,640]{1,0:T(8,128)S(1)} %convolution_add_fusion.2, bf16[256,640]{1,0:T(8,128)(2,1)S(1)} %bitcast.60, bf16[3,640,640]{2,1,0:T(8,128)(2,1)S(1)} %copy-done.2), kind=kOutput, calls=%fused_computation.15 | convolution fusion | flops 210206720 | bytes 2785280 | tf_op jit(solution)/shard_map/dot_general | solution.py:58
  (24 shorter events, 1.4 us)
Async XLA Ops:
  0.0 41.5 %copy-start = (bf16[640,640]{1,0:T(8,128)(2,1)S(1)}, bf16[640,640]{1,0:T(8,128)(2,1)}, u32[]{:S(2)}) copy-start(bf16[640,640]{1,0:T(8,128)(2,1)} %param.12) | copy-start | bytes 2457604
  0.0 10.7 %copy-start.1 = (bf16[2,128,640]{2,1,0:T(8,128)(2,1)S(1)}, bf16[2,128,640]{2,1,0:T(8,128)(2,1)}, u32[]{:S(2)}) copy-start(bf16[2,128,640]{2,1,0:T(8,128)(2,1)} %param.8) | copy-start | bytes 983044
  1.2 8.6 %collective-permute-start = (bf16[2,64,640]{2,1,0:T(8,128)(2,1)S(1)}, bf16[2,64,640]{2,1,0:T(8,128)(2,1)S(1)}, u32[]{:S(2)}, u32[]{:S(2)}) collective-permute-start(bf16[2,64,640]{2,1,0:T(8,128)(2,1)S(1)} %get-tuple-element.16), channel_id=1, source_target_pairs={{0,12},{4,0},{8,4},{12,8},{1,13},{5,1},{9,5},{13,9},{2,14},{6,2},{... | collective-permute-start | bytes 491528 | tf_op jit(solution)/shard_map/ppermute | solution.py:83
  1.9 7.9 %collective-permute-start.1 = (bf16[2,64,640]{2,1,0:T(8,128)(2,1)S(1)}, bf16[2,64,640]{2,1,0:T(8,128)(2,1)S(1)}, u32[]{:S(2)}, u32[]{:S(2)}) collective-permute-start(bf16[2,64,640]{2,1,0:T(8,128)(2,1)S(1)} %get-tuple-element.18), channel_id=1, source_target_pairs={{0,8},{4,12},{8,0},{12,4},{1,9},{5,13},{9,1},{13,5},{2,10},{6,14},... | collective-permute-start | bytes 491528 | tf_op jit(solution)/shard_map/ppermute | solution.py:83
  3.2 7.5 %collective-permute-start.2 = (bf16[2,64,640]{2,1,0:T(8,128)(2,1)S(1)}, bf16[2,64,640]{2,1,0:T(8,128)(2,1)S(1)}, u32[]{:S(2)}, u32[]{:S(2)}) collective-permute-start(bf16[2,64,640]{2,1,0:T(8,128)(2,1)S(1)} %get-tuple-element.17), channel_id=1, source_target_pairs={{0,4},{4,8},{8,12},{12,0},{1,5},{5,9},{9,13},{13,1},{2,6},{6,10},{... | collective-permute-start | bytes 491528 | tf_op jit(solution)/shard_map/ppermute | solution.py:83
  7.3 21.8 %copy-start.5 = (bf16[640,1280]{1,0:T(8,128)(2,1)S(1)}, bf16[640,1280]{1,0:T(8,128)(2,1)}, u32[]{:S(2)}) copy-start(bf16[640,1280]{1,0:T(8,128)(2,1)} %param.11) | copy-start | bytes 4915204
  10.8 4.2 %collective-permute-start.3 = (bf16[2,64,640]{2,1,0:T(8,128)(2,1)S(1)}, bf16[2,64,640]{2,1,0:T(8,128)(2,1)S(1)}, u32[]{:S(2)}, u32[]{:S(2)}) collective-permute-start(bf16[2,64,640]{2,1,0:T(8,128)(2,1)S(1)} %pad_maximum_fusion.9), channel_id=1, source_target_pairs={{0,1},{1,2},{2,3},{3,0},{4,5},{5,6},{6,7},{7,4},{8,9},{9,10},{10,1... | collective-permute-start | bytes 491528 | tf_op jit(solution)/shard_map/ppermute | solution.py:91
  12.2 12.7 %collective-permute-start.4 = (bf16[2,64,640]{2,1,0:T(8,128)(2,1)S(1)}, bf16[2,64,640]{2,1,0:T(8,128)(2,1)S(1)}, u32[]{:S(2)}, u32[]{:S(2)}) collective-permute-start(bf16[2,64,640]{2,1,0:T(8,128)(2,1)S(1)} %pad_maximum_fusion.9), channel_id=1, source_target_pairs={{0,2},{1,3},{2,0},{3,1},{4,6},{5,7},{6,4},{7,5},{8,10},{9,11},{10,... | collective-permute-start | bytes 491528 | tf_op jit(solution)/shard_map/ppermute | solution.py:91
  13.3 15.1 %collective-permute-start.5 = (bf16[2,64,640]{2,1,0:T(8,128)(2,1)S(1)}, bf16[2,64,640]{2,1,0:T(8,128)(2,1)S(1)}, u32[]{:S(2)}, u32[]{:S(2)}) collective-permute-start(bf16[2,64,640]{2,1,0:T(8,128)(2,1)S(1)} %pad_maximum_fusion.9), channel_id=1, source_target_pairs={{0,3},{1,0},{2,1},{3,2},{4,7},{5,4},{6,5},{7,6},{8,11},{9,8},{10,9... | collective-permute-start | bytes 491528 | tf_op jit(solution)/shard_map/ppermute | solution.py:91
  28.5 2.3 %collective-permute-start.6 = (bf16[512,640]{1,0:T(8,128)(2,1)S(1)}, bf16[512,640]{1,0:T(8,128)(2,1)S(1)}, u32[]{:S(2)}, u32[]{:S(2)}) collective-permute-start(bf16[512,640]{1,0:T(8,128)(2,1)S(1)} %bitcast.65), channel_id=1, source_target_pairs={{0,4},{4,0},{8,12},{12,8},{1,5},{5,1},{9,13},{13,9},{2,6},{6,2},{1... | collective-permute-start | bytes 1966088 | tf_op jit(solution)/shard_map/ppermute | solution.py:93
  41.5 1.6 %copy-start.4 = (f32[640]{0:T(1024)S(1)}, f32[640]{0:T(1024)}, u32[]{:S(2)}) copy-start(f32[640]{0:T(1024)} %param.13) | copy-start | bytes 7684
  43.2 6.4 %collective-permute-start.7 = (bf16[2,128,640]{2,1,0:T(8,128)(2,1)S(1)}, bf16[2,128,640]{2,1,0:T(8,128)(2,1)S(1)}, u32[]{:S(2)}, u32[]{:S(2)}) collective-permute-start(bf16[2,128,640]{2,1,0:T(8,128)(2,1)S(1)} %bitcast.61), channel_id=1, source_target_pairs={{0,4},{4,8},{8,12},{1,5},{5,9},{9,13},{2,6},{6,10},{10,14},{3,7},{... | collective-permute-start | bytes 983048 | tf_op jit(solution)/shard_map/ppermute | solution.py:49
  45.7 8.4 %collective-permute-start.8 = (bf16[2,128,640]{2,1,0:T(8,128)(2,1)S(1)}, bf16[2,128,640]{2,1,0:T(8,128)(2,1)S(1)}, u32[]{:S(2)}, u32[]{:S(2)}) collective-permute-start(bf16[2,128,640]{2,1,0:T(8,128)(2,1)S(1)} %bitcast.62), channel_id=1, source_target_pairs={{4,0},{8,4},{12,8},{5,1},{9,5},{13,9},{6,2},{10,6},{14,10},{7,3},{... | collective-permute-start | bytes 983048 | tf_op jit(solution)/shard_map/ppermute | solution.py:50
  47.8 6.5 %copy-start.3 = (bf16[3,640,640]{2,1,0:T(8,128)(2,1)S(1)}, bf16[3,640,640]{2,1,0:T(8,128)(2,1)}, u32[]{:S(2)}) copy-start(bf16[3,640,640]{2,1,0:T(8,128)(2,1)} %param.14) | copy-start | bytes 7372804
  56.7 1.7 %copy-start.2 = (bf16[3,640,640]{2,1,0:T(8,128)(2,1)S(1)}, bf16[3,640,640]{2,1,0:T(8,128)(2,1)}, u32[]{:S(2)}) copy-start(bf16[3,640,640]{2,1,0:T(8,128)(2,1)} %param.15) | copy-start | bytes 7372804

commit v13 on v12

--- a/solution.py
+++ b/solution.py
@@ -52,11 +52,9 @@
 
 
 def temporal_mix(padded, weights, count):
-    result = jnp.zeros((count * padded.shape[1], padded.shape[2]), jnp.float32)
-    for offset in range(3):
-        window = padded[offset : offset + count].reshape(-1, padded.shape[2])
-        result = result + jnp.dot(window, weights[offset], preferred_element_type=jnp.float32)
-    return result
+    windows = jnp.concatenate([padded[offset : offset + count] for offset in range(3)], axis=-1)
+    stacked = weights.reshape(-1, weights.shape[-1])
+    return jnp.dot(windows.reshape(-1, stacked.shape[0]), stacked, preferred_element_type=jnp.float32)
 
 
 def gather_keyframes(frames, key_index, early):

time: 60.8 us -> 62.9 us (1.035)
  other arithmetic: 3.16 us -> 5.25 us
  local copies, waits for them, and re-layouts: 4.11 us -> 4.83 us
  matrix products: 11.5 us -> 10.8 us
    concatenate x1, other arithmetic: 0.24 us -> 1.39 us  [temporal_mix(): jnp.concatenate([padded[offset:offset + count] for offset in range(3)], a...]
    select_n x1, other arithmetic: 0.12 us -> 1.07 us  [gather_keyframes(): jnp.where(source == owner_a, lax.dynamic_index_in_dim(recv, slot_a, 0, ke...]
    dot_general x6 -> x2, matrix products: 4.44 us -> 3.5 us  [temporal_mix(): jnp.dot(windows.reshape(-1, stacked.shape[0]), stacked, preferred_element...]
    dynamic_slice x1, local copies, waits for them, and re-layouts: 1.21 us -> 1.94 us  [halves(): return lax.dynamic_slice_in_dim(frames, h * half, half, 1)]
    unnamed x12 -> x10, local copies, waits for them, and re-layouts: 1.55 us -> 1.54 us
where the time goes in v13:
time: 62.9 us; the launch traced here: 62.6 us
  waiting for transfers between devices  20.6 us (33%)
  starting transfers between devices  12.7 us (20%)
  matrix products  10.8 us (17%)
  Pallas kernels  6.89 us (11%)
  other arithmetic  5.25 us (8%)
  local copies, waits for them, and re-layouts  4.83 us (8%)
  between operations  1.61 us (3%)
    ppermute x3, waiting for transfers between devices, gather_keyframes(): lax.ppermute(piece, 'row', [(i, (i + s) % rsize) for i in range(rsize)])  13.7 us
    pallas_call x1, Pallas kernels, attend(): pl.pallas_call(attention_kernel, grid=(channels // width,), in_specs=[pl....  6.89 us
    ppermute x1, waiting for transfers between devices, extended(): after = lax.ppermute(first, axis, down)  4.5 us
    ppermute x3, starting transfers between devices, gather_keyframes(): lax.ppermute(piece, 'row', [(i, (i + s) % rsize) for i in range(rsize)])  3.83 us
    dot_general x2, matrix products, temporal_mix(): jnp.dot(windows.reshape(-1, stacked.shape[0]), stacked, preferred_element...  3.5 us
    ppermute x3, starting transfers between devices, gather_keyframes(): lax.ppermute(halves((me + s) % 2), 'frame', [(i, (i + s) % fsize) for i i...  3.24 us
    ppermute x1, starting transfers between devices, extended(): after = lax.ppermute(first, axis, down)  2.65 us
    dot_general x1, matrix products, shards(): jnp.dot(flattened, w_query, preferred_element_type=jnp.float32)  2.55 us
  transfers between devices with their start and end apart: 9, of which 7 were waited for; matrix products, arithmetic and copies ran while one was open for 9% of the time, Pallas kernels for 0%

profile of v13, /device:TPU:9, one launch (start us, length us, event | category | flops | bytes accessed | tf_op | source)
XLA Modules:
  0.0 62.6 jit_solution(6768964987071117355)
XLA Ops:
  0.0 1.9 %constant_dynamic-slice_fusion.2 = (bf16[2,64,640]{2,1,0:T(8,128)(2,1)}, bf16[2,64,640]{2,1,0:T(8,128)(2,1)S(1)}, bf16[2,64,640]{2,1,0:T(8,128)(2,1)S(1)}) fusion(bf16[2,128,640]{2,1,0:T(8,128)(2,1)} %param.8, s32[]{:T(128)S(6)} %select_n.137, s32[]{:T(128)S(6)} %select_n.147, s32[]{:T(128)S(6)} %select_n.143), kind=kLoop, calls=%fused_computation.42 | loop fusion | bytes 983052 | tf_op jit(solution)/shard_map/dynamic_slice | solution.py:73
  1.9 0.7 %collective-permute-start = (bf16[2,64,640]{2,1,0:T(8,128)(2,1)}, bf16[2,64,640]{2,1,0:T(8,128)(2,1)S(1)}, u32[]{:S(2)}, u32[]{:S(2)}) collective-permute-start(bf16[2,64,640]{2,1,0:T(8,128)(2,1)} %get-tuple-element.13), channel_id=1, source_target_pairs={{0,12},{4,0},{8,4},{12,8},{1,13},{5,1},{9,5},{13,9},{2,14},{6,2},{... | collective-permute-start | bytes 491528 | tf_op jit(solution)/shard_map/ppermute | solution.py:81
  2.6 1.2 %collective-permute-start.1 = (bf16[2,64,640]{2,1,0:T(8,128)(2,1)S(1)}, bf16[2,64,640]{2,1,0:T(8,128)(2,1)S(1)}, u32[]{:S(2)}, u32[]{:S(2)}) collective-permute-start(bf16[2,64,640]{2,1,0:T(8,128)(2,1)S(1)} %get-tuple-element.15), channel_id=1, source_target_pairs={{0,8},{4,12},{8,0},{12,4},{1,9},{5,13},{9,1},{13,5},{2,10},{6,14},... | collective-permute-start | bytes 491528 | tf_op jit(solution)/shard_map/ppermute | solution.py:81
  3.8 1.4 %collective-permute-start.2 = (bf16[2,64,640]{2,1,0:T(8,128)(2,1)S(1)}, bf16[2,64,640]{2,1,0:T(8,128)(2,1)}, u32[]{:S(2)}, u32[]{:S(2)}) collective-permute-start(bf16[2,64,640]{2,1,0:T(8,128)(2,1)S(1)} %get-tuple-element.14), channel_id=1, source_target_pairs={{0,4},{4,8},{8,12},{12,0},{1,5},{5,9},{9,13},{13,1},{2,6},{6,10},{... | collective-permute-start | bytes 491528 | tf_op jit(solution)/shard_map/ppermute | solution.py:81
  5.2 1.3 %fusion.19 = (s32[1]{0:T(128)}, s32[1]{0:T(128)}) fusion(s32[2]{0:T(128)} %param.9), kind=kLoop, calls=%fused_computation.45 | loop fusion | bytes 16 | tf_op jit(solution)/shard_map/slice | solution.py:66
  8.0 2.5 %convolution_convert_fusion.4.q_ref = bf16[256,640]{1,0:T(8,128)(2,1)} fusion(bf16[256,640]{1,0:T(8,128)(2,1)} %bitcast.35, bf16[640,640]{1,0:T(8,128)(2,1)} %param.10), kind=kOutput, calls=%fused_computation.16 | convolution fusion | flops 209879040 | bytes 1474560 | tf_op jit(solution)/shard_map/dot_general | solution.py:99
  10.5 0.7 %collective-permute-done.2 = bf16[2,64,640]{2,1,0:T(8,128)(2,1)} collective-permute-done((bf16[2,64,640]{2,1,0:T(8,128)(2,1)S(1)}, bf16[2,64,640]{2,1,0:T(8,128)(2,1)}, u32[]{:S(2)}, u32[]{:S(2)}) %collective-permute-start.2) | collective-permute-done | bytes 163872 | tf_op jit(solution)/shard_map/ppermute | solution.py:81
  11.3 1.1 %select_select_fusion = (bf16[1,64,640]{2,1,0:T(8,128)(2,1)S(1)}, bf16[1,64,640]{2,1,0:T(8,128)(2,1)S(1)}) fusion(bf16[2,128,640]{2,1,0:T(8,128)(2,1)S(1)} %copy-done.1, s32[]{:T(128)S(6)} %select_n.149, s32[]{:T(128)S(6)} %select_n.152, bf16[2,64,640]{2,1,0:T(8,128)(2,1)} %collective-permute-done.2, s32[]{:T(128)S(6)} %select_n.139, ...), kind=kLoop, calls=%fused_computation.39 | loop fusion | flops 286720 | bytes 819227 | tf_op jit(solution)/shard_map/jit(_where)/select_n | solution.py:83
  12.4 1.3 %collective-permute-start.3 = (bf16[2,64,640]{2,1,0:T(8,128)(2,1)S(1)}, bf16[2,64,640]{2,1,0:T(8,128)(2,1)S(1)}, u32[]{:S(2)}, u32[]{:S(2)}) collective-permute-start(bf16[2,64,640]{2,1,0:T(8,128)(2,1)S(1)} %pad_maximum_fusion.7), channel_id=1, source_target_pairs={{0,1},{1,2},{2,3},{3,0},{4,5},{5,6},{6,7},{7,4},{8,9},{9,10},{10,1... | collective-permute-start | bytes 491528 | tf_op jit(solution)/shard_map/ppermute | solution.py:89
  13.7 1.1 %collective-permute-start.4 = (bf16[2,64,640]{2,1,0:T(8,128)(2,1)S(1)}, bf16[2,64,640]{2,1,0:T(8,128)(2,1)S(1)}, u32[]{:S(2)}, u32[]{:S(2)}) collective-permute-start(bf16[2,64,640]{2,1,0:T(8,128)(2,1)S(1)} %pad_maximum_fusion.7), channel_id=1, source_target_pairs={{0,2},{1,3},{2,0},{3,1},{4,6},{5,7},{6,4},{7,5},{8,10},{9,11},{10,... | collective-permute-start | bytes 491528 | tf_op jit(solution)/shard_map/ppermute | solution.py:89
  14.8 1.4 %collective-permute-start.5 = (bf16[2,64,640]{2,1,0:T(8,128)(2,1)S(1)}, bf16[2,64,640]{2,1,0:T(8,128)(2,1)S(1)}, u32[]{:S(2)}, u32[]{:S(2)}) collective-permute-start(bf16[2,64,640]{2,1,0:T(8,128)(2,1)S(1)} %pad_maximum_fusion.7), channel_id=1, source_target_pairs={{0,3},{1,0},{2,1},{3,2},{4,7},{5,4},{6,5},{7,6},{8,11},{9,8},{10,9... | collective-permute-start | bytes 491528 | tf_op jit(solution)/shard_map/ppermute | solution.py:89
  16.2 0.4 collective-permute-done.3
  16.6 9.7 %collective-permute-done.4 = bf16[2,64,640]{2,1,0:T(8,128)(2,1)S(1)} collective-permute-done((bf16[2,64,640]{2,1,0:T(8,128)(2,1)S(1)}, bf16[2,64,640]{2,1,0:T(8,128)(2,1)S(1)}, u32[]{:S(2)}, u32[]{:S(2)}) %collective-permute-start.4) | collective-permute-done | bytes 163872 | tf_op jit(solution)/shard_map/ppermute | solution.py:89
  26.2 3.7 %collective-permute-done.5 = bf16[2,64,640]{2,1,0:T(8,128)(2,1)S(1)} collective-permute-done((bf16[2,64,640]{2,1,0:T(8,128)(2,1)S(1)}, bf16[2,64,640]{2,1,0:T(8,128)(2,1)S(1)}, u32[]{:S(2)}, u32[]{:S(2)}) %collective-permute-start.5) | collective-permute-done | bytes 163872 | tf_op jit(solution)/shard_map/ppermute | solution.py:89
  30.0 0.6 collective-permute-start.6
  30.6 0.7 %convolution_convert_fusion.1 = bf16[512,640]{1,0:T(8,128)(2,1)S(1)} fusion(bf16[512,640]{1,0:T(8,128)(2,1)S(1)} %bitcast.44, bf16[640,1280]{1,0:T(8,128)(2,1)S(1)} %copy-done.4), kind=kOutput, calls=%fused_computation.5 | convolution fusion | flops 419758080 | bytes 2129920 | tf_op jit(solution)/shard_map/dot_general | solution.py:107
  31.3 0.7 %fusion.2 = bf16[640,512]{1,0:T(8,128)(2,1)S(1)} fusion(bf16[512,640]{1,0:T(8,128)(2,1)S(1)} %bitcast.45, bf16[640,1280]{1,0:T(8,128)(2,1)S(1)} %copy-done.4), kind=kOutput, calls=%fused_computation.11 | convolution fusion | flops 419758080 | bytes 2129920 | tf_op jit(solution)/shard_map/dot_general | solution.py:104
  32.1 0.2 collective-permute-done.6
  32.3 0.7 %convolution_convert_fusion = bf16[512,640]{1,0:T(8,128)(2,1)S(1)} fusion(bf16[512,640]{1,0:T(8,128)(2,1)S(1)} %collective-permute-done.6, bf16[640,1280]{1,0:T(8,128)(2,1)S(1)} %copy-done.4), kind=kOutput, calls=%fused_computation.4 | convolution fusion | flops 419758080 | bytes 2129920 | tf_op jit(solution)/shard_map/dot_general | solution.py:107
  33.1 1.2 %pad_maximum_fusion.3.v_ref = bf16[1024,640]{1,0:T(8,128)(2,1)} fusion(bf16[512,640]{1,0:T(8,128)(2,1)S(1)} %convolution_convert_fusion, bf16[512,640]{1,0:T(8,128)(2,1)S(1)} %convolution_convert_fusion.1), kind=kLoop, calls=%fused_computation.9 | loop fusion | flops 2621440 | bytes 2621440 | tf_op jit(solution)/shard_map/concatenate | solution.py:113
  34.2 0.7 %fusion.3 = bf16[640,512]{1,0:T(8,128)(2,1)S(1)} fusion(bf16[512,640]{1,0:T(8,128)(2,1)S(1)} %collective-permute-done.6, bf16[640,1280]{1,0:T(8,128)(2,1)S(1)} %copy-done.4), kind=kOutput, calls=%fused_computation.12 | convolution fusion | flops 419758080 | bytes 2129920 | tf_op jit(solution)/shard_map/dot_general | solution.py:104
  35.0 1.2 %pad_maximum_fusion.2.kt_ref = bf16[640,1024]{1,0:T(8,128)(2,1)} fusion(bf16[640,512]{1,0:T(8,128)(2,1)S(1)} %fusion.3, bf16[640,512]{1,0:T(8,128)(2,1)S(1)} %fusion.2), kind=kLoop, calls=%fused_computation.8 | loop fusion | flops 2621440 | bytes 2621440 | tf_op jit(solution)/shard_map/concatenate | solution.py:112
  36.2 6.9 %shard_map.82 = bf16[256,640]{1,0:T(8,128)(2,1)} custom-call(bf16[256,640]{1,0:T(8,128)(2,1)} %convolution_convert_fusion.4.q_ref, bf16[640,1024]{1,0:T(8,128)(2,1)} %pad_maximum_fusion.2.kt_ref, bf16[1024,640]{1,0:T(8,128)(2,1)} %pad_maximum_fusion.3.v_ref), custom_call_target="tpu_custom_call" | custom-call | tf_op jit(solution)/shard_map/pallas_call | solution.py:30
  43.1 1.8 %multiply_reduce_fusion = (f32[256]{0:T(256)S(1)}, f32[256,640]{1,0:T(8,128)S(1)}) fusion(bf16[256,640]{1,0:T(8,128)(2,1)} %shard_map.82, bf16[640,640]{1,0:T(8,128)(2,1)} %param.12, bf16[256,640]{1,0:T(8,128)(2,1)S(1)} %bitcast.36), kind=kOutput, calls=%fused_computation.28 | convolution fusion | flops 210370304 | bytes 2130944 | tf_op jit(solution)/shard_map/dot_general | solution.py:115
  45.1 2.4 %collective-permute-start.7 = (bf16[2,128,640]{2,1,0:T(8,128)(2,1)S(1)}, bf16[2,128,640]{2,1,0:T(8,128)(2,1)}, u32[]{:S(2)}, u32[]{:S(2)}) collective-permute-start(bf16[2,128,640]{2,1,0:T(8,128)(2,1)S(1)} %bitcast.39), channel_id=1, source_target_pairs={{0,4},{4,8},{8,12},{1,5},{5,9},{9,13},{2,6},{6,10},{10,14},{3,7},{... | collective-permute-start | bytes 983048 | tf_op jit(solution)/shard_map/ppermute | solution.py:49
  47.5 2.6 %collective-permute-start.8 = (bf16[2,128,640]{2,1,0:T(8,128)(2,1)S(1)}, bf16[2,128,640]{2,1,0:T(8,128)(2,1)}, u32[]{:S(2)}, u32[]{:S(2)}) collective-permute-start(bf16[2,128,640]{2,1,0:T(8,128)(2,1)S(1)} %bitcast.40), channel_id=1, source_target_pairs={{4,0},{8,4},{12,8},{5,1},{9,5},{13,9},{6,2},{10,6},{14,10},{7,3},{... | collective-permute-start | bytes 983048 | tf_op jit(solution)/shard_map/ppermute | solution.py:50
  50.1 1.3 %collective-permute-done.7 = bf16[2,128,640]{2,1,0:T(8,128)(2,1)} collective-permute-done((bf16[2,128,640]{2,1,0:T(8,128)(2,1)S(1)}, bf16[2,128,640]{2,1,0:T(8,128)(2,1)}, u32[]{:S(2)}, u32[]{:S(2)}) %collective-permute-start.7) | collective-permute-done | bytes 327712 | tf_op jit(solution)/shard_map/ppermute | solution.py:49
  51.5 4.5 %collective-permute-done.8 = bf16[2,128,640]{2,1,0:T(8,128)(2,1)} collective-permute-done((bf16[2,128,640]{2,1,0:T(8,128)(2,1)S(1)}, bf16[2,128,640]{2,1,0:T(8,128)(2,1)}, u32[]{:S(2)}, u32[]{:S(2)}) %collective-permute-start.8) | collective-permute-done | bytes 327712 | tf_op jit(solution)/shard_map/ppermute | solution.py:50
  56.0 1.4 %fusion.1 = bf16[4,128,1920]{2,1,0:T(8,128)(2,1)S(1)} fusion(bf16[2,128,640]{2,1,0:T(8,128)(2,1)} %collective-permute-done.8, bf16[2,128,640]{2,1,0:T(8,128)(2,1)S(1)} %bitcast.41, bf16[2,128,640]{2,1,0:T(8,128)(2,1)} %collective-permute-done.7), kind=kLoop, calls=%fused_computation.2 | loop fusion | flops 13762560 | bytes 2949120 | tf_op jit(solution)/shard_map/concatenate | solution.py:55
  57.4 1.8 %multiply_convert_fusion = bf16[512,640]{1,0:T(8,128)(2,1)S(1)} fusion(bf16[512,1920]{1,0:T(8,128)(2,1)S(1)} %bitcast.37, bf16[1920,640]{1,0:T(8,128)(2,1)S(1)} %bitcast.34), kind=kOutput, calls=%fused_computation.10 | convolution fusion | flops 1259929600 | bytes 5079040 | tf_op jit(solution)/shard_map/dot_general | solution.py:57
  59.3 1.5 %copy-done.3 = bf16[3,640,640]{2,1,0:T(8,128)(2,1)S(1)} copy-done((bf16[3,640,640]{2,1,0:T(8,128)(2,1)S(1)}, bf16[3,640,640]{2,1,0:T(8,128)(2,1)}, u32[]{:S(2)}) %copy-start.3) | copy-done | bytes 2457624
  60.9 1.7 %fusion.4 = bf16[256,640]{1,0:T(8,128)(2,1)} fusion(f32[256,640]{1,0:T(8,128)S(1)} %get-tuple-element.19, bf16[1920,640]{1,0:T(8,128)(2,1)S(1)} %bitcast.51, bf16[256,640]{1,0:T(8,128)(2,1)S(1)} %bitcast.47, bf16[256,640]{1,0:T(8,128)(2,1)S(1)} %slice.74, bf16[256,640]{1,0:T(8,128)(2,1)S(1)} %bitcast.46), kind=kOutput, calls=%fused_computation.15 | convolution fusion | flops 632422400 | bytes 4423680 | tf_op jit(solution)/shard_map/dot_general | solution.py:57
  (18 shorter events, 0.4 us)
Async XLA Ops:
  0.0 57.4 %copy-start = (bf16[3,640,640]{2,1,0:T(8,128)(2,1)S(1)}, bf16[3,640,640]{2,1,0:T(8,128)(2,1)}, u32[]{:S(2)}) copy-start(bf16[3,640,640]{2,1,0:T(8,128)(2,1)} %param.14) | copy-start | bytes 7372804
  0.0 11.3 %copy-start.1 = (bf16[2,128,640]{2,1,0:T(8,128)(2,1)S(1)}, bf16[2,128,640]{2,1,0:T(8,128)(2,1)}, u32[]{:S(2)}) copy-start(bf16[2,128,640]{2,1,0:T(8,128)(2,1)} %param.8) | copy-start | bytes 983044
  1.9 8.6 %collective-permute-start = (bf16[2,64,640]{2,1,0:T(8,128)(2,1)}, bf16[2,64,640]{2,1,0:T(8,128)(2,1)S(1)}, u32[]{:S(2)}, u32[]{:S(2)}) collective-permute-start(bf16[2,64,640]{2,1,0:T(8,128)(2,1)} %get-tuple-element.13), channel_id=1, source_target_pairs={{0,12},{4,0},{8,4},{12,8},{1,13},{5,1},{9,5},{13,9},{2,14},{6,2},{... | collective-permute-start | bytes 491528 | tf_op jit(solution)/shard_map/ppermute | solution.py:81
  2.6 7.9 %collective-permute-start.1 = (bf16[2,64,640]{2,1,0:T(8,128)(2,1)S(1)}, bf16[2,64,640]{2,1,0:T(8,128)(2,1)S(1)}, u32[]{:S(2)}, u32[]{:S(2)}) collective-permute-start(bf16[2,64,640]{2,1,0:T(8,128)(2,1)S(1)} %get-tuple-element.15), channel_id=1, source_target_pairs={{0,8},{4,12},{8,0},{12,4},{1,9},{5,13},{9,1},{13,5},{2,10},{6,14},... | collective-permute-start | bytes 491528 | tf_op jit(solution)/shard_map/ppermute | solution.py:81
  3.8 7.4 %collective-permute-start.2 = (bf16[2,64,640]{2,1,0:T(8,128)(2,1)S(1)}, bf16[2,64,640]{2,1,0:T(8,128)(2,1)}, u32[]{:S(2)}, u32[]{:S(2)}) collective-permute-start(bf16[2,64,640]{2,1,0:T(8,128)(2,1)S(1)} %get-tuple-element.14), channel_id=1, source_target_pairs={{0,4},{4,8},{8,12},{12,0},{1,5},{5,9},{9,13},{13,1},{2,6},{6,10},{... | collective-permute-start | bytes 491528 | tf_op jit(solution)/shard_map/ppermute | solution.py:81
  7.9 22.6 %copy-start.4 = (bf16[640,1280]{1,0:T(8,128)(2,1)S(1)}, bf16[640,1280]{1,0:T(8,128)(2,1)}, u32[]{:S(2)}) copy-start(bf16[640,1280]{1,0:T(8,128)(2,1)} %param.11) | copy-start | bytes 4915204
  12.4 4.2 %collective-permute-start.3 = (bf16[2,64,640]{2,1,0:T(8,128)(2,1)S(1)}, bf16[2,64,640]{2,1,0:T(8,128)(2,1)S(1)}, u32[]{:S(2)}, u32[]{:S(2)}) collective-permute-start(bf16[2,64,640]{2,1,0:T(8,128)(2,1)S(1)} %pad_maximum_fusion.7), channel_id=1, source_target_pairs={{0,1},{1,2},{2,3},{3,0},{4,5},{5,6},{6,7},{7,4},{8,9},{9,10},{10,1... | collective-permute-start | bytes 491528 | tf_op jit(solution)/shard_map/ppermute | solution.py:89
  13.7 12.5 %collective-permute-start.4 = (bf16[2,64,640]{2,1,0:T(8,128)(2,1)S(1)}, bf16[2,64,640]{2,1,0:T(8,128)(2,1)S(1)}, u32[]{:S(2)}, u32[]{:S(2)}) collective-permute-start(bf16[2,64,640]{2,1,0:T(8,128)(2,1)S(1)} %pad_maximum_fusion.7), channel_id=1, source_target_pairs={{0,2},{1,3},{2,0},{3,1},{4,6},{5,7},{6,4},{7,5},{8,10},{9,11},{10,... | collective-permute-start | bytes 491528 | tf_op jit(solution)/shard_map/ppermute | solution.py:89
  14.8 15.1 %collective-permute-start.5 = (bf16[2,64,640]{2,1,0:T(8,128)(2,1)S(1)}, bf16[2,64,640]{2,1,0:T(8,128)(2,1)S(1)}, u32[]{:S(2)}, u32[]{:S(2)}) collective-permute-start(bf16[2,64,640]{2,1,0:T(8,128)(2,1)S(1)} %pad_maximum_fusion.7), channel_id=1, source_target_pairs={{0,3},{1,0},{2,1},{3,2},{4,7},{5,4},{6,5},{7,6},{8,11},{9,8},{10,9... | collective-permute-start | bytes 491528 | tf_op jit(solution)/shard_map/ppermute | solution.py:89
  30.0 2.3 %collective-permute-start.6 = (bf16[512,640]{1,0:T(8,128)(2,1)S(1)}, bf16[512,640]{1,0:T(8,128)(2,1)S(1)}, u32[]{:S(2)}, u32[]{:S(2)}) collective-permute-start(bf16[512,640]{1,0:T(8,128)(2,1)S(1)} %bitcast.43), channel_id=1, source_target_pairs={{0,4},{4,0},{8,12},{12,8},{1,5},{5,1},{9,13},{13,9},{2,6},{6,2},{1... | collective-permute-start | bytes 1966088 | tf_op jit(solution)/shard_map/ppermute | solution.py:91
  36.2 8.7 %copy-start.2 = (f32[640]{0:T(1024)S(1)}, f32[640]{0:T(1024)}, u32[]{:S(2)}) copy-start(f32[640]{0:T(1024)} %param.13) | copy-start | bytes 7684
  45.1 6.4 %collective-permute-start.7 = (bf16[2,128,640]{2,1,0:T(8,128)(2,1)S(1)}, bf16[2,128,640]{2,1,0:T(8,128)(2,1)}, u32[]{:S(2)}, u32[]{:S(2)}) collective-permute-start(bf16[2,128,640]{2,1,0:T(8,128)(2,1)S(1)} %bitcast.39), channel_id=1, source_target_pairs={{0,4},{4,8},{8,12},{1,5},{5,9},{9,13},{2,6},{6,10},{10,14},{3,7},{... | collective-permute-start | bytes 983048 | tf_op jit(solution)/shard_map/ppermute | solution.py:49
  47.5 8.5 %collective-permute-start.8 = (bf16[2,128,640]{2,1,0:T(8,128)(2,1)S(1)}, bf16[2,128,640]{2,1,0:T(8,128)(2,1)}, u32[]{:S(2)}, u32[]{:S(2)}) collective-permute-start(bf16[2,128,640]{2,1,0:T(8,128)(2,1)S(1)} %bitcast.40), channel_id=1, source_target_pairs={{4,0},{8,4},{12,8},{5,1},{9,5},{13,9},{6,2},{10,6},{14,10},{7,3},{... | collective-permute-start | bytes 983048 | tf_op jit(solution)/shard_map/ppermute | solution.py:50
  59.2 1.7 %copy-start.3 = (bf16[3,640,640]{2,1,0:T(8,128)(2,1)S(1)}, bf16[3,640,640]{2,1,0:T(8,128)(2,1)}, u32[]{:S(2)}) copy-start(bf16[3,640,640]{2,1,0:T(8,128)(2,1)} %param.15) | copy-start | bytes 7372804

commit v14 on v12

--- a/solution.py
+++ b/solution.py
@@ -8,36 +8,34 @@
 HEAD_DIM = 64
 
 
-def attention_kernel(q_ref, kt_ref, v_ref, o_ref):
-    heads = [slice(h * HEAD_DIM, (h + 1) * HEAD_DIM) for h in range(q_ref.shape[1] // HEAD_DIM)]
-    scores = [
-        jnp.dot(q_ref[:, c], kt_ref[c, :], preferred_element_type=jnp.float32) * HEAD_DIM ** (-0.5) for c in heads
-    ]
-    highest = [jnp.max(s, axis=1, keepdims=True) for s in scores]
+def attention_kernel(k_ref, qt_ref, vt_ref, o_ref):
+    heads = [slice(h * HEAD_DIM, (h + 1) * HEAD_DIM) for h in range(qt_ref.shape[0] // HEAD_DIM)]
+    scores = [jnp.dot(k_ref[:, c], qt_ref[c, :], preferred_element_type=jnp.float32) for c in heads]
+    highest = [jnp.max(s, axis=0, keepdims=True) for s in scores]
     exponent = [jnp.exp(s - m) for s, m in zip(scores, highest)]
-    denominator = [jnp.sum(e, axis=1, keepdims=True) for e in exponent]
+    denominator = [jnp.sum(e, axis=0, keepdims=True) for e in exponent]
     mixed = [
-        jnp.dot(e.astype(jnp.bfloat16), v_ref[:, c], preferred_element_type=jnp.float32)
+        jnp.dot(vt_ref[c, :], e.astype(jnp.bfloat16), preferred_element_type=jnp.float32)
         for e, c in zip(exponent, heads)
     ]
-    o_ref[...] = jnp.concatenate([m / d for m, d in zip(mixed, denominator)], axis=1).astype(o_ref.dtype)
+    o_ref[...] = jnp.concatenate([m / d for m, d in zip(mixed, denominator)], axis=0).astype(o_ref.dtype)
 
 
-def attend(queries, keys_t, values):
-    total, channels = queries.shape
-    count = values.shape[0]
+def attend(keys, queries_t, values_t):
+    channels, total = queries_t.shape
+    count = keys.shape[0]
     width = channels if total * count * channels <= 256 * 1024 * 640 else 2 * HEAD_DIM
     return pl.pallas_call(
         attention_kernel,
         grid=(channels // width,),
         in_specs=[
-            pl.BlockSpec((total, width), lambda j: (0, j)),
+            pl.BlockSpec((count, width), lambda j: (0, j)),
+            pl.BlockSpec((width, total), lambda j: (j, 0)),
             pl.BlockSpec((width, count), lambda j: (j, 0)),
-            pl.BlockSpec((count, width), lambda j: (0, j)),
         ],
-        out_specs=pl.BlockSpec((total, width), lambda j: (0, j)),
-        out_shape=jax.ShapeDtypeStruct((total, channels), jnp.bfloat16),
-    )(queries, keys_t, values)
+        out_specs=pl.BlockSpec((width, total), lambda j: (j, 0)),
+        out_shape=jax.ShapeDtypeStruct((channels, total), jnp.bfloat16),
+    )(keys, queries_t, values_t)
 
 
 def extended(array, axis, width):
@@ -98,24 +96,24 @@
     frame_count, row_count, channels = frames.shape
     assert frame_count >= 2
     flattened = frames.reshape(-1, channels)
-    queries = jnp.dot(flattened, w_query, preferred_element_type=jnp.float32).astype(jnp.bfloat16)
-    query_total = queries.shape[0]
-    mine, sibling = gather_keyframes(frames, key_index, queries)
+    queries_t = lax.dot_general(w_query, flattened, (((0,), (1,)), ((), ())), preferred_element_type=jnp.float32)
+    queries_t = (queries_t * HEAD_DIM ** (-0.5)).astype(jnp.bfloat16)
+    mine, sibling = gather_keyframes(frames, key_index, queries_t)
 
     def project(tokens):
-        keys_t = lax.dot_general(
-            w_keyval[:, :channels], tokens, (((0,), (1,)), ((), ())), preferred_element_type=jnp.float32
+        keys = jnp.dot(tokens, w_keyval[:, :channels], preferred_element_type=jnp.float32).astype(jnp.bfloat16)
+        values_t = lax.dot_general(
+            w_keyval[:, channels:], tokens, (((0,), (1,)), ((), ())), preferred_element_type=jnp.float32
         ).astype(jnp.bfloat16)
-        values = jnp.dot(tokens, w_keyval[:, channels:], preferred_element_type=jnp.float32).astype(jnp.bfloat16)
-        return keys_t, values
+        return keys, values_t
 
     keys_mine, values_mine = project(mine)
     keys_sib, values_sib = project(sibling)
-    keys_t = jnp.concatenate([keys_mine, keys_sib], axis=1)
-    values = jnp.concatenate([values_mine, values_sib], axis=0)
-    attended = attend(queries, keys_t, values)
-    residual = flattened.astype(jnp.float32) + jnp.dot(
-        attended, w_out, preferred_element_type=jnp.float32
+    keys = jnp.concatenate([keys_mine, keys_sib], axis=0)
+    values_t = jnp.concatenate([values_mine, values_sib], axis=1)
+    attended_t = attend(keys, queries_t, values_t)
+    residual = flattened.astype(jnp.float32) + lax.dot_general(
+        attended_t, w_out, (((0,), (0,)), ((), ())), preferred_element_type=jnp.float32
     )
     mean_square = jnp.mean(residual * residual, axis=-1, keepdims=True)
     normed = (residual * lax.rsqrt(mean_square + 1e-06) * norm_gain).astype(jnp.bfloat16)

time: 60.8 us -> 59.8 us (0.984)
  Pallas kernels: 6.86 us -> 5.85 us
    pallas_call x1, Pallas kernels: 6.86 us -> 5.85 us  [attend(): pl.pallas_call(attention_kernel, grid=(channels // width,), in_specs=[pl....]
where the time goes in v14:
time: 59.8 us; the launch traced here: 59.5 us
  waiting for transfers between devices  21.2 us (35%)
  starting transfers between devices  12 us (20%)
  matrix products  11.5 us (19%)
  Pallas kernels  5.85 us (10%)
  local copies, waits for them, and re-layouts  4.11 us (7%)
  other arithmetic  3.16 us (5%)
  between operations  1.65 us (3%)
    ppermute x3, waiting for transfers between devices, gather_keyframes(): lax.ppermute(piece, 'row', [(i, (i + s) % rsize) for i in range(rsize)])  13.7 us
    pallas_call x1, Pallas kernels, attend(): pl.pallas_call(attention_kernel, grid=(channels // width,), in_specs=[pl....  5.85 us
    dot_general x6, matrix products, temporal_mix(): jnp.dot(window, weights[offset], preferred_element_type=jnp.float32)  4.43 us
    ppermute x1, waiting for transfers between devices, extended(): after = lax.ppermute(first, axis, down)  4.4 us
    ppermute x3, starting transfers between devices, gather_keyframes(): lax.ppermute(piece, 'row', [(i, (i + s) % rsize) for i in range(rsize)])  3.83 us
    ppermute x3, starting transfers between devices, gather_keyframes(): lax.ppermute(halves((me + s) % 2), 'frame', [(i, (i + s) % fsize) for i i...  3.29 us
    dot_general x1, matrix products, shards(): lax.dot_general(w_query, flattened, (((0,), (1,)), ((), ())), preferred_e...  2.54 us
    ppermute x1, starting transfers between devices, extended(): before = lax.ppermute(last, axis, up)  2.44 us
  transfers between devices with their start and end apart: 9, of which 7 were waited for; matrix products, arithmetic and copies ran while one was open for 9% of the time, Pallas kernels for 0%

profile of v14, /device:TPU:9, one launch (start us, length us, event | category | flops | bytes accessed | tf_op | source)
XLA Modules:
  0.0 59.5 jit_solution(7208642390850679492)
XLA Ops:
  0.0 1.2 %constant_dynamic-slice_fusion.2 = (bf16[2,64,640]{2,1,0:T(8,128)(2,1)S(1)}, bf16[2,64,640]{2,1,0:T(8,128)(2,1)S(1)}, bf16[2,64,640]{2,1,0:T(8,128)(2,1)S(1)}) fusion(bf16[2,128,640]{2,1,0:T(8,128)(2,1)} %param.8, s32[]{:T(128)S(6)} %select_n.137, s32[]{:T(128)S(6)} %select_n.147, s32[]{:T(128)S(6)} %select_n.143), kind=kLoop, calls=%fused_computation.57 | loop fusion | bytes 983052 | tf_op jit(solution)/shard_map/dynamic_slice | solution.py:73
  1.2 0.7 %collective-permute-start = (bf16[2,64,640]{2,1,0:T(8,128)(2,1)S(1)}, bf16[2,64,640]{2,1,0:T(8,128)(2,1)S(1)}, u32[]{:S(2)}, u32[]{:S(2)}) collective-permute-start(bf16[2,64,640]{2,1,0:T(8,128)(2,1)S(1)} %get-tuple-element.16), channel_id=1, source_target_pairs={{0,12},{4,0},{8,4},{12,8},{1,13},{5,1},{9,5},{13,9},{2,14},{6,2},{... | collective-permute-start | bytes 491528 | tf_op jit(solution)/shard_map/ppermute | solution.py:81
  1.9 1.2 %collective-permute-start.1 = (bf16[2,64,640]{2,1,0:T(8,128)(2,1)S(1)}, bf16[2,64,640]{2,1,0:T(8,128)(2,1)S(1)}, u32[]{:S(2)}, u32[]{:S(2)}) collective-permute-start(bf16[2,64,640]{2,1,0:T(8,128)(2,1)S(1)} %get-tuple-element.18), channel_id=1, source_target_pairs={{0,8},{4,12},{8,0},{12,4},{1,9},{5,13},{9,1},{13,5},{2,10},{6,14},... | collective-permute-start | bytes 491528 | tf_op jit(solution)/shard_map/ppermute | solution.py:81
  3.2 1.3 %collective-permute-start.2 = (bf16[2,64,640]{2,1,0:T(8,128)(2,1)S(1)}, bf16[2,64,640]{2,1,0:T(8,128)(2,1)S(1)}, u32[]{:S(2)}, u32[]{:S(2)}) collective-permute-start(bf16[2,64,640]{2,1,0:T(8,128)(2,1)S(1)} %get-tuple-element.17), channel_id=1, source_target_pairs={{0,4},{4,8},{8,12},{12,0},{1,5},{5,9},{9,13},{13,1},{2,6},{6,10},{... | collective-permute-start | bytes 491528 | tf_op jit(solution)/shard_map/ppermute | solution.py:81
  4.5 1.3 %fusion.30 = (s32[1]{0:T(128)}, s32[1]{0:T(128)}) fusion(s32[2]{0:T(128)} %param.9), kind=kLoop, calls=%fused_computation.60 | loop fusion | bytes 16 | tf_op jit(solution)/shard_map/slice | solution.py:66
  7.3 2.5 %fusion.4.qt_ref = bf16[640,256]{1,0:T(8,128)(2,1)} fusion(bf16[640,640]{1,0:T(8,128)(2,1)} %param.10, bf16[256,640]{1,0:T(8,128)(2,1)} %bitcast.54), kind=kOutput, calls=%fused_computation.16 | convolution fusion | flops 210042880 | bytes 1474560 | tf_op jit(solution)/shard_map/dot_general | solution.py:99
  9.8 0.8 %collective-permute-done.2 = bf16[2,64,640]{2,1,0:T(8,128)(2,1)S(1)} collective-permute-done((bf16[2,64,640]{2,1,0:T(8,128)(2,1)S(1)}, bf16[2,64,640]{2,1,0:T(8,128)(2,1)S(1)}, u32[]{:S(2)}, u32[]{:S(2)}) %collective-permute-start.2) | collective-permute-done | bytes 163872 | tf_op jit(solution)/shard_map/ppermute | solution.py:81
  10.8 1.4 %collective-permute-start.3 = (bf16[2,64,640]{2,1,0:T(8,128)(2,1)S(1)}, bf16[2,64,640]{2,1,0:T(8,128)(2,1)S(1)}, u32[]{:S(2)}, u32[]{:S(2)}) collective-permute-start(bf16[2,64,640]{2,1,0:T(8,128)(2,1)S(1)} %pad_maximum_fusion.9), channel_id=1, source_target_pairs={{0,1},{1,2},{2,3},{3,0},{4,5},{5,6},{6,7},{7,4},{8,9},{9,10},{10,1... | collective-permute-start | bytes 491528 | tf_op jit(solution)/shard_map/ppermute | solution.py:89
  12.2 1.1 %collective-permute-start.4 = (bf16[2,64,640]{2,1,0:T(8,128)(2,1)S(1)}, bf16[2,64,640]{2,1,0:T(8,128)(2,1)S(1)}, u32[]{:S(2)}, u32[]{:S(2)}) collective-permute-start(bf16[2,64,640]{2,1,0:T(8,128)(2,1)S(1)} %pad_maximum_fusion.9), channel_id=1, source_target_pairs={{0,2},{1,3},{2,0},{3,1},{4,6},{5,7},{6,4},{7,5},{8,10},{9,11},{10,... | collective-permute-start | bytes 491528 | tf_op jit(solution)/shard_map/ppermute | solution.py:89
  13.3 1.4 %collective-permute-start.5 = (bf16[2,64,640]{2,1,0:T(8,128)(2,1)S(1)}, bf16[2,64,640]{2,1,0:T(8,128)(2,1)S(1)}, u32[]{:S(2)}, u32[]{:S(2)}) collective-permute-start(bf16[2,64,640]{2,1,0:T(8,128)(2,1)S(1)} %pad_maximum_fusion.9), channel_id=1, source_target_pairs={{0,3},{1,0},{2,1},{3,2},{4,7},{5,4},{6,5},{7,6},{8,11},{9,8},{10,9... | collective-permute-start | bytes 491528 | tf_op jit(solution)/shard_map/ppermute | solution.py:89
  15.0 9.8 %collective-permute-done.4 = bf16[2,64,640]{2,1,0:T(8,128)(2,1)S(1)} collective-permute-done((bf16[2,64,640]{2,1,0:T(8,128)(2,1)S(1)}, bf16[2,64,640]{2,1,0:T(8,128)(2,1)S(1)}, u32[]{:S(2)}, u32[]{:S(2)}) %collective-permute-start.4) | collective-permute-done | bytes 163872 | tf_op jit(solution)/shard_map/ppermute | solution.py:89
  24.9 3.5 %collective-permute-done.5 = bf16[2,64,640]{2,1,0:T(8,128)(2,1)S(1)} collective-permute-done((bf16[2,64,640]{2,1,0:T(8,128)(2,1)S(1)}, bf16[2,64,640]{2,1,0:T(8,128)(2,1)S(1)}, u32[]{:S(2)}, u32[]{:S(2)}) %collective-permute-start.5) | collective-permute-done | bytes 163872 | tf_op jit(solution)/shard_map/ppermute | solution.py:89
  28.5 0.6 collective-permute-start.6
  29.0 0.7 %fusion.1 = bf16[640,512]{1,0:T(8,128)(2,1)S(1)} fusion(bf16[512,640]{1,0:T(8,128)(2,1)S(1)} %bitcast.66, bf16[640,1280]{1,0:T(8,128)(2,1)S(1)} %copy-done.5), kind=kOutput, calls=%fused_computation.9 | convolution fusion | flops 419758080 | bytes 2129920 | tf_op jit(solution)/shard_map/dot_general | solution.py:105
  29.8 0.7 %convolution_convert_fusion.3 = bf16[512,640]{1,0:T(8,128)(2,1)S(1)} fusion(bf16[512,640]{1,0:T(8,128)(2,1)S(1)} %bitcast.67, bf16[640,1280]{1,0:T(8,128)(2,1)S(1)} %copy-done.5), kind=kOutput, calls=%fused_computation.5 | convolution fusion | flops 419758080 | bytes 2129920 | tf_op jit(solution)/shard_map/dot_general | solution.py:104
  30.8 0.7 %fusion.2 = bf16[640,512]{1,0:T(8,128)(2,1)S(1)} fusion(bf16[512,640]{1,0:T(8,128)(2,1)S(1)} %collective-permute-done.6, bf16[640,1280]{1,0:T(8,128)(2,1)S(1)} %copy-done.5), kind=kOutput, calls=%fused_computation.10 | convolution fusion | flops 419758080 | bytes 2129920 | tf_op jit(solution)/shard_map/dot_general | solution.py:105
  31.5 1.2 %pad_maximum_fusion.1.vt_ref = bf16[640,1024]{1,0:T(8,128)(2,1)} fusion(bf16[640,512]{1,0:T(8,128)(2,1)S(1)} %fusion.2, bf16[640,512]{1,0:T(8,128)(2,1)S(1)} %fusion.1), kind=kLoop, calls=%fused_computation.7 | loop fusion | flops 2621440 | bytes 2621440 | tf_op jit(solution)/shard_map/concatenate | solution.py:113
  32.7 0.7 %convolution_convert_fusion.2 = bf16[512,640]{1,0:T(8,128)(2,1)S(1)} fusion(bf16[512,640]{1,0:T(8,128)(2,1)S(1)} %collective-permute-done.6, bf16[640,1280]{1,0:T(8,128)(2,1)S(1)} %copy-done.5), kind=kOutput, calls=%fused_computation.4 | convolution fusion | flops 419758080 | bytes 2129920 | tf_op jit(solution)/shard_map/dot_general | solution.py:104
  33.5 1.2 %pad_maximum_fusion.k_ref = bf16[1024,640]{1,0:T(8,128)(2,1)} fusion(bf16[512,640]{1,0:T(8,128)(2,1)S(1)} %convolution_convert_fusion.2, bf16[512,640]{1,0:T(8,128)(2,1)S(1)} %convolution_convert_fusion.3), kind=kLoop, calls=%fused_computation.6 | loop fusion | flops 2621440 | bytes 2621440 | tf_op jit(solution)/shard_map/concatenate | solution.py:112
  34.7 5.8 %shard_map.82 = bf16[640,256]{1,0:T(8,128)(2,1)} custom-call(bf16[1024,640]{1,0:T(8,128)(2,1)} %pad_maximum_fusion.k_ref, bf16[640,256]{1,0:T(8,128)(2,1)} %fusion.4.qt_ref, bf16[640,1024]{1,0:T(8,128)(2,1)} %pad_maximum_fusion.1.vt_ref), custom_call_target="tpu_custom_call" | custom-call | tf_op jit(solution)/shard_map/pallas_call | solution.py:28
  40.5 1.6 %multiply_reduce_fusion = (f32[256]{0:T(256)S(1)}, f32[256,640]{1,0:T(8,128)S(1)}) fusion(bf16[640,256]{1,0:T(8,128)(2,1)} %shard_map.82, bf16[640,640]{1,0:T(8,128)(2,1)S(1)} %copy-done, bf16[256,640]{1,0:T(8,128)(2,1)S(1)} %bitcast.55), kind=kOutput, calls=%fused_computation.43 | convolution fusion | flops 210370304 | bytes 2130944 | tf_op jit(solution)/shard_map/dot_general | solution.py:115
  42.3 2.4 %collective-permute-start.7 = (bf16[2,128,640]{2,1,0:T(8,128)(2,1)S(1)}, bf16[2,128,640]{2,1,0:T(8,128)(2,1)S(1)}, u32[]{:S(2)}, u32[]{:S(2)}) collective-permute-start(bf16[2,128,640]{2,1,0:T(8,128)(2,1)S(1)} %bitcast.61), channel_id=1, source_target_pairs={{0,4},{4,8},{8,12},{1,5},{5,9},{9,13},{2,6},{6,10},{10,14},{3,7},{... | collective-permute-start | bytes 983048 | tf_op jit(solution)/shard_map/ppermute | solution.py:47
  44.7 1.9 %collective-permute-start.8 = (bf16[2,128,640]{2,1,0:T(8,128)(2,1)S(1)}, bf16[2,128,640]{2,1,0:T(8,128)(2,1)S(1)}, u32[]{:S(2)}, u32[]{:S(2)}) collective-permute-start(bf16[2,128,640]{2,1,0:T(8,128)(2,1)S(1)} %bitcast.62), channel_id=1, source_target_pairs={{4,0},{8,4},{12,8},{5,1},{9,5},{13,9},{6,2},{10,6},{14,10},{7,3},{... | collective-permute-start | bytes 983048 | tf_op jit(solution)/shard_map/ppermute | solution.py:48
  46.6 2.0 %collective-permute-done.7 = bf16[2,128,640]{2,1,0:T(8,128)(2,1)S(1)} collective-permute-done((bf16[2,128,640]{2,1,0:T(8,128)(2,1)S(1)}, bf16[2,128,640]{2,1,0:T(8,128)(2,1)S(1)}, u32[]{:S(2)}, u32[]{:S(2)}) %collective-permute-start.7) | collective-permute-done | bytes 327712 | tf_op jit(solution)/shard_map/ppermute | solution.py:47
  48.7 4.4 %collective-permute-done.8 = bf16[2,128,640]{2,1,0:T(8,128)(2,1)S(1)} collective-permute-done((bf16[2,128,640]{2,1,0:T(8,128)(2,1)S(1)}, bf16[2,128,640]{2,1,0:T(8,128)(2,1)S(1)}, u32[]{:S(2)}, u32[]{:S(2)}) %collective-permute-start.8) | collective-permute-done | bytes 327712 | tf_op jit(solution)/shard_map/ppermute | solution.py:48
  53.3 0.7 %fusion.10 = f32[512,640]{1,0:T(8,128)S(1)} fusion(bf16[512,640]{1,0:T(8,128)(2,1)S(1)} %bitcast.57, bf16[3,640,640]{2,1,0:T(8,128)(2,1)S(1)} %copy-done.3), kind=kOutput, calls=%fused_computation.22 | convolution fusion | flops 419430400 | bytes 2785280 | tf_op jit(solution)/shard_map/dot_general | solution.py:56
  54.1 0.7 %fusion.12 = f32[512,640]{1,0:T(8,128)S(1)} fusion(bf16[512,640]{1,0:T(8,128)(2,1)S(1)} %bitcast.56, bf16[3,640,640]{2,1,0:T(8,128)(2,1)S(1)} %copy-done.3), kind=kOutput, calls=%fused_computation.24 | convolution fusion | flops 419430400 | bytes 2785280 | tf_op jit(solution)/shard_map/dot_general | solution.py:56
  54.9 0.8 %multiply_convert_fusion = bf16[512,640]{1,0:T(8,128)(2,1)S(1)} fusion(f32[512,640]{1,0:T(8,128)S(1)} %fusion.10, f32[512,640]{1,0:T(8,128)S(1)} %fusion.12, bf16[512,640]{1,0:T(8,128)(2,1)S(1)} %bitcast.68, bf16[3,640,640]{2,1,0:T(8,128)(2,1)S(1)} %copy-done.3), kind=kOutput, calls=%fused_computation.8 | convolution fusion | flops 421724160 | bytes 4751360 | tf_op jit(solution)/shard_map/dot_general | solution.py:56
  55.9 1.5 %copy-done.2 = bf16[3,640,640]{2,1,0:T(8,128)(2,1)S(1)} copy-done((bf16[3,640,640]{2,1,0:T(8,128)(2,1)S(1)}, bf16[3,640,640]{2,1,0:T(8,128)(2,1)}, u32[]{:S(2)}) %copy-start.2) | copy-done | bytes 2457624
  57.4 0.5 fusion.8
  57.9 0.5 convolution_add_fusion.2
  58.3 1.2 %fusion.5 = bf16[256,640]{1,0:T(8,128)(2,1)} fusion(f32[256,640]{1,0:T(8,128)S(1)} %get-tuple-element.22, f32[256,640]{1,0:T(8,128)S(1)} %convolution_add_fusion.2, bf16[256,640]{1,0:T(8,128)(2,1)S(1)} %bitcast.60, bf16[3,640,640]{2,1,0:T(8,128)(2,1)S(1)} %copy-done.2), kind=kOutput, calls=%fused_computation.17 | convolution fusion | flops 210206720 | bytes 2785280 | tf_op jit(solution)/shard_map/dot_general | solution.py:56
  (24 shorter events, 1.4 us)
Async XLA Ops:
  0.0 40.5 %copy-start = (bf16[640,640]{1,0:T(8,128)(2,1)S(1)}, bf16[640,640]{1,0:T(8,128)(2,1)}, u32[]{:S(2)}) copy-start(bf16[640,640]{1,0:T(8,128)(2,1)} %param.12) | copy-start | bytes 2457604
  0.0 10.7 %copy-start.1 = (bf16[2,128,640]{2,1,0:T(8,128)(2,1)S(1)}, bf16[2,128,640]{2,1,0:T(8,128)(2,1)}, u32[]{:S(2)}) copy-start(bf16[2,128,640]{2,1,0:T(8,128)(2,1)} %param.8) | copy-start | bytes 983044
  1.2 8.6 %collective-permute-start = (bf16[2,64,640]{2,1,0:T(8,128)(2,1)S(1)}, bf16[2,64,640]{2,1,0:T(8,128)(2,1)S(1)}, u32[]{:S(2)}, u32[]{:S(2)}) collective-permute-start(bf16[2,64,640]{2,1,0:T(8,128)(2,1)S(1)} %get-tuple-element.16), channel_id=1, source_target_pairs={{0,12},{4,0},{8,4},{12,8},{1,13},{5,1},{9,5},{13,9},{2,14},{6,2},{... | collective-permute-start | bytes 491528 | tf_op jit(solution)/shard_map/ppermute | solution.py:81
  1.9 7.9 %collective-permute-start.1 = (bf16[2,64,640]{2,1,0:T(8,128)(2,1)S(1)}, bf16[2,64,640]{2,1,0:T(8,128)(2,1)S(1)}, u32[]{:S(2)}, u32[]{:S(2)}) collective-permute-start(bf16[2,64,640]{2,1,0:T(8,128)(2,1)S(1)} %get-tuple-element.18), channel_id=1, source_target_pairs={{0,8},{4,12},{8,0},{12,4},{1,9},{5,13},{9,1},{13,5},{2,10},{6,14},... | collective-permute-start | bytes 491528 | tf_op jit(solution)/shard_map/ppermute | solution.py:81
  3.2 7.5 %collective-permute-start.2 = (bf16[2,64,640]{2,1,0:T(8,128)(2,1)S(1)}, bf16[2,64,640]{2,1,0:T(8,128)(2,1)S(1)}, u32[]{:S(2)}, u32[]{:S(2)}) collective-permute-start(bf16[2,64,640]{2,1,0:T(8,128)(2,1)S(1)} %get-tuple-element.17), channel_id=1, source_target_pairs={{0,4},{4,8},{8,12},{12,0},{1,5},{5,9},{9,13},{13,1},{2,6},{6,10},{... | collective-permute-start | bytes 491528 | tf_op jit(solution)/shard_map/ppermute | solution.py:81
  7.3 21.8 %copy-start.5 = (bf16[640,1280]{1,0:T(8,128)(2,1)S(1)}, bf16[640,1280]{1,0:T(8,128)(2,1)}, u32[]{:S(2)}) copy-start(bf16[640,1280]{1,0:T(8,128)(2,1)} %param.11) | copy-start | bytes 4915204
  10.8 4.2 %collective-permute-start.3 = (bf16[2,64,640]{2,1,0:T(8,128)(2,1)S(1)}, bf16[2,64,640]{2,1,0:T(8,128)(2,1)S(1)}, u32[]{:S(2)}, u32[]{:S(2)}) collective-permute-start(bf16[2,64,640]{2,1,0:T(8,128)(2,1)S(1)} %pad_maximum_fusion.9), channel_id=1, source_target_pairs={{0,1},{1,2},{2,3},{3,0},{4,5},{5,6},{6,7},{7,4},{8,9},{9,10},{10,1... | collective-permute-start | bytes 491528 | tf_op jit(solution)/shard_map/ppermute | solution.py:89
  12.2 12.7 %collective-permute-start.4 = (bf16[2,64,640]{2,1,0:T(8,128)(2,1)S(1)}, bf16[2,64,640]{2,1,0:T(8,128)(2,1)S(1)}, u32[]{:S(2)}, u32[]{:S(2)}) collective-permute-start(bf16[2,64,640]{2,1,0:T(8,128)(2,1)S(1)} %pad_maximum_fusion.9), channel_id=1, source_target_pairs={{0,2},{1,3},{2,0},{3,1},{4,6},{5,7},{6,4},{7,5},{8,10},{9,11},{10,... | collective-permute-start | bytes 491528 | tf_op jit(solution)/shard_map/ppermute | solution.py:89
  13.3 15.1 %collective-permute-start.5 = (bf16[2,64,640]{2,1,0:T(8,128)(2,1)S(1)}, bf16[2,64,640]{2,1,0:T(8,128)(2,1)S(1)}, u32[]{:S(2)}, u32[]{:S(2)}) collective-permute-start(bf16[2,64,640]{2,1,0:T(8,128)(2,1)S(1)} %pad_maximum_fusion.9), channel_id=1, source_target_pairs={{0,3},{1,0},{2,1},{3,2},{4,7},{5,4},{6,5},{7,6},{8,11},{9,8},{10,9... | collective-permute-start | bytes 491528 | tf_op jit(solution)/shard_map/ppermute | solution.py:89
  28.5 2.3 %collective-permute-start.6 = (bf16[512,640]{1,0:T(8,128)(2,1)S(1)}, bf16[512,640]{1,0:T(8,128)(2,1)S(1)}, u32[]{:S(2)}, u32[]{:S(2)}) collective-permute-start(bf16[512,640]{1,0:T(8,128)(2,1)S(1)} %bitcast.65), channel_id=1, source_target_pairs={{0,4},{4,0},{8,12},{12,8},{1,5},{5,1},{9,13},{13,9},{2,6},{6,2},{1... | collective-permute-start | bytes 1966088 | tf_op jit(solution)/shard_map/ppermute | solution.py:91
  40.5 1.6 %copy-start.4 = (f32[640]{0:T(1024)S(1)}, f32[640]{0:T(1024)}, u32[]{:S(2)}) copy-start(f32[640]{0:T(1024)} %param.13) | copy-start | bytes 7684
  42.3 6.4 %collective-permute-start.7 = (bf16[2,128,640]{2,1,0:T(8,128)(2,1)S(1)}, bf16[2,128,640]{2,1,0:T(8,128)(2,1)S(1)}, u32[]{:S(2)}, u32[]{:S(2)}) collective-permute-start(bf16[2,128,640]{2,1,0:T(8,128)(2,1)S(1)} %bitcast.61), channel_id=1, source_target_pairs={{0,4},{4,8},{8,12},{1,5},{5,9},{9,13},{2,6},{6,10},{10,14},{3,7},{... | collective-permute-start | bytes 983048 | tf_op jit(solution)/shard_map/ppermute | solution.py:47
  44.7 8.4 %collective-permute-start.8 = (bf16[2,128,640]{2,1,0:T(8,128)(2,1)S(1)}, bf16[2,128,640]{2,1,0:T(8,128)(2,1)S(1)}, u32[]{:S(2)}, u32[]{:S(2)}) collective-permute-start(bf16[2,128,640]{2,1,0:T(8,128)(2,1)S(1)} %bitcast.62), channel_id=1, source_target_pairs={{4,0},{8,4},{12,8},{5,1},{9,5},{13,9},{6,2},{10,6},{14,10},{7,3},{... | collective-permute-start | bytes 983048 | tf_op jit(solution)/shard_map/ppermute | solution.py:48
  46.6 6.7 %copy-start.3 = (bf16[3,640,640]{2,1,0:T(8,128)(2,1)S(1)}, bf16[3,640,640]{2,1,0:T(8,128)(2,1)}, u32[]{:S(2)}) copy-start(bf16[3,640,640]{2,1,0:T(8,128)(2,1)} %param.14) | copy-start | bytes 7372804
  55.7 1.7 %copy-start.2 = (bf16[3,640,640]{2,1,0:T(8,128)(2,1)S(1)}, bf16[3,640,640]{2,1,0:T(8,128)(2,1)}, u32[]{:S(2)}) copy-start(bf16[3,640,640]{2,1,0:T(8,128)(2,1)} %param.15) | copy-start | bytes 7372804

commit v15 on v14

--- a/solution.py
+++ b/solution.py
@@ -8,34 +8,40 @@
 HEAD_DIM = 64
 
 
-def attention_kernel(k_ref, qt_ref, vt_ref, o_ref):
+def attention_kernel(k_a_ref, k_b_ref, qt_ref, vt_a_ref, vt_b_ref, o_ref):
     heads = [slice(h * HEAD_DIM, (h + 1) * HEAD_DIM) for h in range(qt_ref.shape[0] // HEAD_DIM)]
-    scores = [jnp.dot(k_ref[:, c], qt_ref[c, :], preferred_element_type=jnp.float32) for c in heads]
-    highest = [jnp.max(s, axis=0, keepdims=True) for s in scores]
-    exponent = [jnp.exp(s - m) for s, m in zip(scores, highest)]
-    denominator = [jnp.sum(e, axis=0, keepdims=True) for e in exponent]
+    scores_a = [jnp.dot(k_a_ref[:, c], qt_ref[c, :], preferred_element_type=jnp.float32) for c in heads]
+    scores_b = [jnp.dot(k_b_ref[:, c], qt_ref[c, :], preferred_element_type=jnp.float32) for c in heads]
+    highest = [
+        jnp.maximum(jnp.max(a, axis=0, keepdims=True), jnp.max(b, axis=0, keepdims=True))
+        for a, b in zip(scores_a, scores_b)
+    ]
+    exp_a = [jnp.exp(a - m) for a, m in zip(scores_a, highest)]
+    exp_b = [jnp.exp(b - m) for b, m in zip(scores_b, highest)]
+    denominator = [
+        jnp.sum(a, axis=0, keepdims=True) + jnp.sum(b, axis=0, keepdims=True) for a, b in zip(exp_a, exp_b)
+    ]
     mixed = [
-        jnp.dot(vt_ref[c, :], e.astype(jnp.bfloat16), preferred_element_type=jnp.float32)
-        for e, c in zip(exponent, heads)
+        jnp.dot(vt_a_ref[c, :], a.astype(jnp.bfloat16), preferred_element_type=jnp.float32)
+        + jnp.dot(vt_b_ref[c, :], b.astype(jnp.bfloat16), preferred_element_type=jnp.float32)
+        for a, b, c in zip(exp_a, exp_b, heads)
     ]
     o_ref[...] = jnp.concatenate([m / d for m, d in zip(mixed, denominator)], axis=0).astype(o_ref.dtype)
 
 
-def attend(keys, queries_t, values_t):
+def attend(keys_a, keys_b, queries_t, values_a, values_b):
     channels, total = queries_t.shape
-    count = keys.shape[0]
-    width = channels if total * count * channels <= 256 * 1024 * 640 else 2 * HEAD_DIM
+    count = keys_a.shape[0]
+    width = channels if total * count * channels <= 256 * 512 * 640 else 2 * HEAD_DIM
+    key_spec = pl.BlockSpec((count, width), lambda j: (0, j))
+    value_spec = pl.BlockSpec((width, count), lambda j: (j, 0))
     return pl.pallas_call(
         attention_kernel,
         grid=(channels // width,),
-        in_specs=[
-            pl.BlockSpec((count, width), lambda j: (0, j)),
-            pl.BlockSpec((width, total), lambda j: (j, 0)),
-            pl.BlockSpec((width, count), lambda j: (j, 0)),
-        ],
+        in_specs=[key_spec, key_spec, pl.BlockSpec((width, total), lambda j: (j, 0)), value_spec, value_spec],
         out_specs=pl.BlockSpec((width, total), lambda j: (j, 0)),
         out_shape=jax.ShapeDtypeStruct((channels, total), jnp.bfloat16),
-    )(keys, queries_t, values_t)
+    )(keys_a, keys_b, queries_t, values_a, values_b)
 
 
 def extended(array, axis, width):
@@ -109,9 +115,7 @@
 
     keys_mine, values_mine = project(mine)
     keys_sib, values_sib = project(sibling)
-    keys = jnp.concatenate([keys_mine, keys_sib], axis=0)
-    values_t = jnp.concatenate([values_mine, values_sib], axis=1)
-    attended_t = attend(keys, queries_t, values_t)
+    attended_t = attend(keys_mine, keys_sib, queries_t, values_mine, values_sib)
     residual = flattened.astype(jnp.float32) + lax.dot_general(
         attended_t, w_out, (((0,), (0,)), ((), ())), preferred_element_type=jnp.float32
     )

time: 59.8 us -> 60.4 us (1.010)
  matrix products: 11.5 us -> 14.9 us
  other arithmetic: 3.16 us -> 0.73 us
    concatenate x2 -> x0, other arithmetic: 2.43 us -> none  [the longest x1 1.23 us: shards(): values_t = jnp.concatenate([values_mine, values_sib], axis=1)]
    dot_general x2, matrix products: 1.5 us -> 3.2 us  [project(): jnp.dot(tokens, w_keyval[:, :channels], preferred_element_type=jnp.float32)]
    dot_general x2, matrix products: 1.44 us -> 3.14 us  [project(): lax.dot_general(w_keyval[:, channels:], tokens, (((0,), (1,)), ((), ())),...]
  transfers between devices with their start and end apart: 9 -> 9, of which waited for: 7 -> 6; matrix products, arithmetic and copies ran while one was open for 9% -> 12% of each run, Pallas kernels for 0% -> 0%
where the time goes in v15:
time: 60.4 us; the launch traced here: 60.1 us
  waiting for transfers between devices  20.7 us (34%)
  matrix products  14.9 us (25%)
  starting transfers between devices  12 us (20%)
  Pallas kernels  6.03 us (10%)
  local copies, waits for them, and re-layouts  4.11 us (7%)
  between operations  1.62 us (3%)
  other arithmetic  0.73 us (1%)
    ppermute x3, waiting for transfers between devices, gather_keyframes(): lax.ppermute(piece, 'row', [(i, (i + s) % rsize) for i in range(rsize)])  13.7 us
    pallas_call x1, Pallas kernels, attend(): pl.pallas_call(attention_kernel, grid=(channels // width,), in_specs=[key...  6.03 us
    dot_general x6, matrix products, temporal_mix(): jnp.dot(window, weights[offset], preferred_element_type=jnp.float32)  4.44 us
    ppermute x1, waiting for transfers between devices, extended(): after = lax.ppermute(first, axis, down)  4.4 us
    ppermute x3, starting transfers between devices, gather_keyframes(): lax.ppermute(piece, 'row', [(i, (i + s) % rsize) for i in range(rsize)])  3.83 us
    ppermute x3, starting transfers between devices, gather_keyframes(): lax.ppermute(halves((me + s) % 2), 'frame', [(i, (i + s) % fsize) for i i...  3.29 us
    dot_general x2, matrix products, project(): jnp.dot(tokens, w_keyval[:, :channels], preferred_element_type=jnp.float32)  3.2 us
    dot_general x2, matrix products, project(): lax.dot_general(w_keyval[:, channels:], tokens, (((0,), (1,)), ((), ())),...  3.14 us
  transfers between devices with their start and end apart: 9, of which 6 were waited for; matrix products, arithmetic and copies ran while one was open for 12% of the time, Pallas kernels for 0%

profile of v15, /device:TPU:9, one launch (start us, length us, event | category | flops | bytes accessed | tf_op | source)
XLA Modules:
  0.0 60.1 jit_solution(9047029275094584186)
XLA Ops:
  0.0 1.2 %constant_dynamic-slice_fusion.2 = (bf16[2,64,640]{2,1,0:T(8,128)(2,1)S(1)}, bf16[2,64,640]{2,1,0:T(8,128)(2,1)S(1)}, bf16[2,64,640]{2,1,0:T(8,128)(2,1)S(1)}) fusion(bf16[2,128,640]{2,1,0:T(8,128)(2,1)} %param.8, s32[]{:T(128)S(6)} %select_n.137, s32[]{:T(128)S(6)} %select_n.147, s32[]{:T(128)S(6)} %select_n.143), kind=kLoop, calls=%fused_computation.55 | loop fusion | bytes 983052 | tf_op jit(solution)/shard_map/dynamic_slice | solution.py:79
  1.2 0.7 %collective-permute-start = (bf16[2,64,640]{2,1,0:T(8,128)(2,1)S(1)}, bf16[2,64,640]{2,1,0:T(8,128)(2,1)S(1)}, u32[]{:S(2)}, u32[]{:S(2)}) collective-permute-start(bf16[2,64,640]{2,1,0:T(8,128)(2,1)S(1)} %get-tuple-element.16), channel_id=1, source_target_pairs={{0,12},{4,0},{8,4},{12,8},{1,13},{5,1},{9,5},{13,9},{2,14},{6,2},{... | collective-permute-start | bytes 491528 | tf_op jit(solution)/shard_map/ppermute | solution.py:87
  1.9 1.2 %collective-permute-start.1 = (bf16[2,64,640]{2,1,0:T(8,128)(2,1)S(1)}, bf16[2,64,640]{2,1,0:T(8,128)(2,1)S(1)}, u32[]{:S(2)}, u32[]{:S(2)}) collective-permute-start(bf16[2,64,640]{2,1,0:T(8,128)(2,1)S(1)} %get-tuple-element.18), channel_id=1, source_target_pairs={{0,8},{4,12},{8,0},{12,4},{1,9},{5,13},{9,1},{13,5},{2,10},{6,14},... | collective-permute-start | bytes 491528 | tf_op jit(solution)/shard_map/ppermute | solution.py:87
  3.2 1.3 %collective-permute-start.2 = (bf16[2,64,640]{2,1,0:T(8,128)(2,1)S(1)}, bf16[2,64,640]{2,1,0:T(8,128)(2,1)S(1)}, u32[]{:S(2)}, u32[]{:S(2)}) collective-permute-start(bf16[2,64,640]{2,1,0:T(8,128)(2,1)S(1)} %get-tuple-element.17), channel_id=1, source_target_pairs={{0,4},{4,8},{8,12},{12,0},{1,5},{5,9},{9,13},{13,1},{2,6},{6,10},{... | collective-permute-start | bytes 491528 | tf_op jit(solution)/shard_map/ppermute | solution.py:87
  4.5 1.3 %fusion.30 = (s32[1]{0:T(128)}, s32[1]{0:T(128)}) fusion(s32[2]{0:T(128)} %param.9), kind=kLoop, calls=%fused_computation.58 | loop fusion | bytes 16 | tf_op jit(solution)/shard_map/slice | solution.py:72
  7.3 2.5 %fusion.4.qt_ref = bf16[640,256]{1,0:T(8,128)(2,1)} fusion(bf16[640,640]{1,0:T(8,128)(2,1)} %param.10, bf16[256,640]{1,0:T(8,128)(2,1)} %bitcast.54), kind=kOutput, calls=%fused_computation.14 | convolution fusion | flops 210042880 | bytes 1474560 | tf_op jit(solution)/shard_map/dot_general | solution.py:105
  9.8 0.8 %collective-permute-done.2 = bf16[2,64,640]{2,1,0:T(8,128)(2,1)S(1)} collective-permute-done((bf16[2,64,640]{2,1,0:T(8,128)(2,1)S(1)}, bf16[2,64,640]{2,1,0:T(8,128)(2,1)S(1)}, u32[]{:S(2)}, u32[]{:S(2)}) %collective-permute-start.2) | collective-permute-done | bytes 163872 | tf_op jit(solution)/shard_map/ppermute | solution.py:87
  10.8 1.4 %collective-permute-start.3 = (bf16[2,64,640]{2,1,0:T(8,128)(2,1)S(1)}, bf16[2,64,640]{2,1,0:T(8,128)(2,1)S(1)}, u32[]{:S(2)}, u32[]{:S(2)}) collective-permute-start(bf16[2,64,640]{2,1,0:T(8,128)(2,1)S(1)} %pad_maximum_fusion.7), channel_id=1, source_target_pairs={{0,1},{1,2},{2,3},{3,0},{4,5},{5,6},{6,7},{7,4},{8,9},{9,10},{10,1... | collective-permute-start | bytes 491528 | tf_op jit(solution)/shard_map/ppermute | solution.py:95
  12.2 1.1 %collective-permute-start.4 = (bf16[2,64,640]{2,1,0:T(8,128)(2,1)S(1)}, bf16[2,64,640]{2,1,0:T(8,128)(2,1)S(1)}, u32[]{:S(2)}, u32[]{:S(2)}) collective-permute-start(bf16[2,64,640]{2,1,0:T(8,128)(2,1)S(1)} %pad_maximum_fusion.7), channel_id=1, source_target_pairs={{0,2},{1,3},{2,0},{3,1},{4,6},{5,7},{6,4},{7,5},{8,10},{9,11},{10,... | collective-permute-start | bytes 491528 | tf_op jit(solution)/shard_map/ppermute | solution.py:95
  13.3 1.4 %collective-permute-start.5 = (bf16[2,64,640]{2,1,0:T(8,128)(2,1)S(1)}, bf16[2,64,640]{2,1,0:T(8,128)(2,1)S(1)}, u32[]{:S(2)}, u32[]{:S(2)}) collective-permute-start(bf16[2,64,640]{2,1,0:T(8,128)(2,1)S(1)} %pad_maximum_fusion.7), channel_id=1, source_target_pairs={{0,3},{1,0},{2,1},{3,2},{4,7},{5,4},{6,5},{7,6},{8,11},{9,8},{10,9... | collective-permute-start | bytes 491528 | tf_op jit(solution)/shard_map/ppermute | solution.py:95
  14.7 0.4 collective-permute-done.3
  15.0 9.8 %collective-permute-done.4 = bf16[2,64,640]{2,1,0:T(8,128)(2,1)S(1)} collective-permute-done((bf16[2,64,640]{2,1,0:T(8,128)(2,1)S(1)}, bf16[2,64,640]{2,1,0:T(8,128)(2,1)S(1)}, u32[]{:S(2)}, u32[]{:S(2)}) %collective-permute-start.4) | collective-permute-done | bytes 163872 | tf_op jit(solution)/shard_map/ppermute | solution.py:95
  24.9 3.5 %collective-permute-done.5 = bf16[2,64,640]{2,1,0:T(8,128)(2,1)S(1)} collective-permute-done((bf16[2,64,640]{2,1,0:T(8,128)(2,1)S(1)}, bf16[2,64,640]{2,1,0:T(8,128)(2,1)S(1)}, u32[]{:S(2)}, u32[]{:S(2)}) %collective-permute-start.5) | collective-permute-done | bytes 163872 | tf_op jit(solution)/shard_map/ppermute | solution.py:95
  28.5 0.6 collective-permute-start.6
  29.0 1.6 %convolution_convert_fusion.3.k_a_ref = bf16[512,640]{1,0:T(8,128)(2,1)} fusion(bf16[512,640]{1,0:T(8,128)(2,1)S(1)} %bitcast.66, bf16[640,1280]{1,0:T(8,128)(2,1)S(1)} %copy-done.5), kind=kOutput, calls=%fused_computation.5 | convolution fusion | flops 419758080 | bytes 2129920 | tf_op jit(solution)/shard_map/dot_general | solution.py:110
  30.7 1.6 %fusion.1.vt_a_ref = bf16[640,512]{1,0:T(8,128)(2,1)} fusion(bf16[512,640]{1,0:T(8,128)(2,1)S(1)} %bitcast.67, bf16[640,1280]{1,0:T(8,128)(2,1)S(1)} %copy-done.5), kind=kOutput, calls=%fused_computation.7 | convolution fusion | flops 419758080 | bytes 2129920 | tf_op jit(solution)/shard_map/dot_general | solution.py:111
  32.2 1.6 %convolution_convert_fusion.2.k_b_ref = bf16[512,640]{1,0:T(8,128)(2,1)} fusion(bf16[512,640]{1,0:T(8,128)(2,1)S(1)} %collective-permute-done.6, bf16[640,1280]{1,0:T(8,128)(2,1)S(1)} %copy-done.5), kind=kOutput, calls=%fused_computation.4 | convolution fusion | flops 419758080 | bytes 2129920 | tf_op jit(solution)/shard_map/dot_general | solution.py:110
  33.8 1.6 %fusion.2.vt_b_ref = bf16[640,512]{1,0:T(8,128)(2,1)} fusion(bf16[512,640]{1,0:T(8,128)(2,1)S(1)} %collective-permute-done.6, bf16[640,1280]{1,0:T(8,128)(2,1)S(1)} %copy-done.5), kind=kOutput, calls=%fused_computation.8 | convolution fusion | flops 419758080 | bytes 2129920 | tf_op jit(solution)/shard_map/dot_general | solution.py:111
  35.4 6.0 %shard_map.82 = bf16[640,256]{1,0:T(8,128)(2,1)} custom-call(bf16[512,640]{1,0:T(8,128)(2,1)} %convolution_convert_fusion.3.k_a_ref, bf16[512,640]{1,0:T(8,128)(2,1)} %convolution_convert_fusion.2.k_b_ref, bf16[640,256]{1,0:T(8,128)(2,1)} %fusion.4.qt_ref, bf16[640,512]{1,0:T(8,128)(2,1)} %fusion.1.vt_a_ref, bf16[640,512]{1,0:T(8,128)(2,1)} %fusion.2.vt_b_ref), custom_call_target="tpu_custom_call" | custom-call | tf_op jit(solution)/shard_map/pallas_call | solution.py:38
  41.4 1.6 %multiply_reduce_fusion = (f32[256]{0:T(256)S(1)}, f32[256,640]{1,0:T(8,128)S(1)}) fusion(bf16[640,256]{1,0:T(8,128)(2,1)} %shard_map.82, bf16[640,640]{1,0:T(8,128)(2,1)S(1)} %copy-done, bf16[256,640]{1,0:T(8,128)(2,1)S(1)} %bitcast.55), kind=kOutput, calls=%fused_computation.41 | convolution fusion | flops 210370304 | bytes 2130944 | tf_op jit(solution)/shard_map/dot_general | solution.py:119
  43.2 2.1 %collective-permute-start.7 = (bf16[2,128,640]{2,1,0:T(8,128)(2,1)S(1)}, bf16[2,128,640]{2,1,0:T(8,128)(2,1)S(1)}, u32[]{:S(2)}, u32[]{:S(2)}) collective-permute-start(bf16[2,128,640]{2,1,0:T(8,128)(2,1)S(1)} %bitcast.61), channel_id=1, source_target_pairs={{0,4},{4,8},{8,12},{1,5},{5,9},{9,13},{2,6},{6,10},{10,14},{3,7},{... | collective-permute-start | bytes 983048 | tf_op jit(solution)/shard_map/ppermute | solution.py:53
  45.2 2.3 %collective-permute-start.8 = (bf16[2,128,640]{2,1,0:T(8,128)(2,1)S(1)}, bf16[2,128,640]{2,1,0:T(8,128)(2,1)S(1)}, u32[]{:S(2)}, u32[]{:S(2)}) collective-permute-start(bf16[2,128,640]{2,1,0:T(8,128)(2,1)S(1)} %bitcast.62), channel_id=1, source_target_pairs={{4,0},{8,4},{12,8},{5,1},{9,5},{13,9},{6,2},{10,6},{14,10},{7,3},{... | collective-permute-start | bytes 983048 | tf_op jit(solution)/shard_map/ppermute | solution.py:54
  47.5 1.7 %collective-permute-done.7 = bf16[2,128,640]{2,1,0:T(8,128)(2,1)S(1)} collective-permute-done((bf16[2,128,640]{2,1,0:T(8,128)(2,1)S(1)}, bf16[2,128,640]{2,1,0:T(8,128)(2,1)S(1)}, u32[]{:S(2)}, u32[]{:S(2)}) %collective-permute-start.7) | collective-permute-done | bytes 327712 | tf_op jit(solution)/shard_map/ppermute | solution.py:53
  49.2 4.4 %collective-permute-done.8 = bf16[2,128,640]{2,1,0:T(8,128)(2,1)S(1)} collective-permute-done((bf16[2,128,640]{2,1,0:T(8,128)(2,1)S(1)}, bf16[2,128,640]{2,1,0:T(8,128)(2,1)S(1)}, u32[]{:S(2)}, u32[]{:S(2)}) %collective-permute-start.8) | collective-permute-done | bytes 327712 | tf_op jit(solution)/shard_map/ppermute | solution.py:54
  53.6 0.2 pad_maximum_fusion.3
  53.9 0.7 %fusion.10 = f32[512,640]{1,0:T(8,128)S(1)} fusion(bf16[512,640]{1,0:T(8,128)(2,1)S(1)} %bitcast.57, bf16[3,640,640]{2,1,0:T(8,128)(2,1)S(1)} %copy-done.3), kind=kOutput, calls=%fused_computation.20 | convolution fusion | flops 419430400 | bytes 2785280 | tf_op jit(solution)/shard_map/dot_general | solution.py:62
  54.6 0.7 %fusion.12 = f32[512,640]{1,0:T(8,128)S(1)} fusion(bf16[512,640]{1,0:T(8,128)(2,1)S(1)} %bitcast.56, bf16[3,640,640]{2,1,0:T(8,128)(2,1)S(1)} %copy-done.3), kind=kOutput, calls=%fused_computation.22 | convolution fusion | flops 419430400 | bytes 2785280 | tf_op jit(solution)/shard_map/dot_general | solution.py:62
  55.4 0.8 %multiply_convert_fusion = bf16[512,640]{1,0:T(8,128)(2,1)S(1)} fusion(f32[512,640]{1,0:T(8,128)S(1)} %fusion.10, f32[512,640]{1,0:T(8,128)S(1)} %fusion.12, bf16[512,640]{1,0:T(8,128)(2,1)S(1)} %bitcast.68, bf16[3,640,640]{2,1,0:T(8,128)(2,1)S(1)} %copy-done.3), kind=kOutput, calls=%fused_computation.6 | convolution fusion | flops 421724160 | bytes 4751360 | tf_op jit(solution)/shard_map/dot_general | solution.py:62
  56.4 1.5 %copy-done.2 = bf16[3,640,640]{2,1,0:T(8,128)(2,1)S(1)} copy-done((bf16[3,640,640]{2,1,0:T(8,128)(2,1)S(1)}, bf16[3,640,640]{2,1,0:T(8,128)(2,1)}, u32[]{:S(2)}) %copy-start.2) | copy-done | bytes 2457624
  57.9 0.5 fusion.8
  58.4 0.5 convolution_add_fusion.2
  58.9 1.2 %fusion.5 = bf16[256,640]{1,0:T(8,128)(2,1)} fusion(f32[256,640]{1,0:T(8,128)S(1)} %get-tuple-element.22, f32[256,640]{1,0:T(8,128)S(1)} %convolution_add_fusion.2, bf16[256,640]{1,0:T(8,128)(2,1)S(1)} %bitcast.60, bf16[3,640,640]{2,1,0:T(8,128)(2,1)S(1)} %copy-done.2), kind=kOutput, calls=%fused_computation.15 | convolution fusion | flops 210206720 | bytes 2785280 | tf_op jit(solution)/shard_map/dot_general | solution.py:62
  (22 shorter events, 0.6 us)
Async XLA Ops:
  0.0 41.4 %copy-start = (bf16[640,640]{1,0:T(8,128)(2,1)S(1)}, bf16[640,640]{1,0:T(8,128)(2,1)}, u32[]{:S(2)}) copy-start(bf16[640,640]{1,0:T(8,128)(2,1)} %param.12) | copy-start | bytes 2457604
  0.0 10.7 %copy-start.1 = (bf16[2,128,640]{2,1,0:T(8,128)(2,1)S(1)}, bf16[2,128,640]{2,1,0:T(8,128)(2,1)}, u32[]{:S(2)}) copy-start(bf16[2,128,640]{2,1,0:T(8,128)(2,1)} %param.8) | copy-start | bytes 983044
  1.2 8.6 %collective-permute-start = (bf16[2,64,640]{2,1,0:T(8,128)(2,1)S(1)}, bf16[2,64,640]{2,1,0:T(8,128)(2,1)S(1)}, u32[]{:S(2)}, u32[]{:S(2)}) collective-permute-start(bf16[2,64,640]{2,1,0:T(8,128)(2,1)S(1)} %get-tuple-element.16), channel_id=1, source_target_pairs={{0,12},{4,0},{8,4},{12,8},{1,13},{5,1},{9,5},{13,9},{2,14},{6,2},{... | collective-permute-start | bytes 491528 | tf_op jit(solution)/shard_map/ppermute | solution.py:87
  1.9 7.9 %collective-permute-start.1 = (bf16[2,64,640]{2,1,0:T(8,128)(2,1)S(1)}, bf16[2,64,640]{2,1,0:T(8,128)(2,1)S(1)}, u32[]{:S(2)}, u32[]{:S(2)}) collective-permute-start(bf16[2,64,640]{2,1,0:T(8,128)(2,1)S(1)} %get-tuple-element.18), channel_id=1, source_target_pairs={{0,8},{4,12},{8,0},{12,4},{1,9},{5,13},{9,1},{13,5},{2,10},{6,14},... | collective-permute-start | bytes 491528 | tf_op jit(solution)/shard_map/ppermute | solution.py:87
  3.2 7.5 %collective-permute-start.2 = (bf16[2,64,640]{2,1,0:T(8,128)(2,1)S(1)}, bf16[2,64,640]{2,1,0:T(8,128)(2,1)S(1)}, u32[]{:S(2)}, u32[]{:S(2)}) collective-permute-start(bf16[2,64,640]{2,1,0:T(8,128)(2,1)S(1)} %get-tuple-element.17), channel_id=1, source_target_pairs={{0,4},{4,8},{8,12},{12,0},{1,5},{5,9},{9,13},{13,1},{2,6},{6,10},{... | collective-permute-start | bytes 491528 | tf_op jit(solution)/shard_map/ppermute | solution.py:87
  7.3 21.8 %copy-start.5 = (bf16[640,1280]{1,0:T(8,128)(2,1)S(1)}, bf16[640,1280]{1,0:T(8,128)(2,1)}, u32[]{:S(2)}) copy-start(bf16[640,1280]{1,0:T(8,128)(2,1)} %param.11) | copy-start | bytes 4915204
  10.8 4.2 %collective-permute-start.3 = (bf16[2,64,640]{2,1,0:T(8,128)(2,1)S(1)}, bf16[2,64,640]{2,1,0:T(8,128)(2,1)S(1)}, u32[]{:S(2)}, u32[]{:S(2)}) collective-permute-start(bf16[2,64,640]{2,1,0:T(8,128)(2,1)S(1)} %pad_maximum_fusion.7), channel_id=1, source_target_pairs={{0,1},{1,2},{2,3},{3,0},{4,5},{5,6},{6,7},{7,4},{8,9},{9,10},{10,1... | collective-permute-start | bytes 491528 | tf_op jit(solution)/shard_map/ppermute | solution.py:95
  12.2 12.7 %collective-permute-start.4 = (bf16[2,64,640]{2,1,0:T(8,128)(2,1)S(1)}, bf16[2,64,640]{2,1,0:T(8,128)(2,1)S(1)}, u32[]{:S(2)}, u32[]{:S(2)}) collective-permute-start(bf16[2,64,640]{2,1,0:T(8,128)(2,1)S(1)} %pad_maximum_fusion.7), channel_id=1, source_target_pairs={{0,2},{1,3},{2,0},{3,1},{4,6},{5,7},{6,4},{7,5},{8,10},{9,11},{10,... | collective-permute-start | bytes 491528 | tf_op jit(solution)/shard_map/ppermute | solution.py:95
  13.3 15.1 %collective-permute-start.5 = (bf16[2,64,640]{2,1,0:T(8,128)(2,1)S(1)}, bf16[2,64,640]{2,1,0:T(8,128)(2,1)S(1)}, u32[]{:S(2)}, u32[]{:S(2)}) collective-permute-start(bf16[2,64,640]{2,1,0:T(8,128)(2,1)S(1)} %pad_maximum_fusion.7), channel_id=1, source_target_pairs={{0,3},{1,0},{2,1},{3,2},{4,7},{5,4},{6,5},{7,6},{8,11},{9,8},{10,9... | collective-permute-start | bytes 491528 | tf_op jit(solution)/shard_map/ppermute | solution.py:95
  28.5 3.7 %collective-permute-start.6 = (bf16[512,640]{1,0:T(8,128)(2,1)S(1)}, bf16[512,640]{1,0:T(8,128)(2,1)S(1)}, u32[]{:S(2)}, u32[]{:S(2)}) collective-permute-start(bf16[512,640]{1,0:T(8,128)(2,1)S(1)} %bitcast.65), channel_id=1, source_target_pairs={{0,4},{4,0},{8,12},{12,8},{1,5},{5,1},{9,13},{13,9},{2,6},{6,2},{1... | collective-permute-start | bytes 1966088 | tf_op jit(solution)/shard_map/ppermute | solution.py:97
  41.4 1.6 %copy-start.4 = (f32[640]{0:T(1024)S(1)}, f32[640]{0:T(1024)}, u32[]{:S(2)}) copy-start(f32[640]{0:T(1024)} %param.13) | copy-start | bytes 7684
  43.2 6.1 %collective-permute-start.7 = (bf16[2,128,640]{2,1,0:T(8,128)(2,1)S(1)}, bf16[2,128,640]{2,1,0:T(8,128)(2,1)S(1)}, u32[]{:S(2)}, u32[]{:S(2)}) collective-permute-start(bf16[2,128,640]{2,1,0:T(8,128)(2,1)S(1)} %bitcast.61), channel_id=1, source_target_pairs={{0,4},{4,8},{8,12},{1,5},{5,9},{9,13},{2,6},{6,10},{10,14},{3,7},{... | collective-permute-start | bytes 983048 | tf_op jit(solution)/shard_map/ppermute | solution.py:53
  45.2 8.4 %collective-permute-start.8 = (bf16[2,128,640]{2,1,0:T(8,128)(2,1)S(1)}, bf16[2,128,640]{2,1,0:T(8,128)(2,1)S(1)}, u32[]{:S(2)}, u32[]{:S(2)}) collective-permute-start(bf16[2,128,640]{2,1,0:T(8,128)(2,1)S(1)} %bitcast.62), channel_id=1, source_target_pairs={{4,0},{8,4},{12,8},{5,1},{9,5},{13,9},{6,2},{10,6},{14,10},{7,3},{... | collective-permute-start | bytes 983048 | tf_op jit(solution)/shard_map/ppermute | solution.py:54
  47.5 6.4 %copy-start.3 = (bf16[3,640,640]{2,1,0:T(8,128)(2,1)S(1)}, bf16[3,640,640]{2,1,0:T(8,128)(2,1)}, u32[]{:S(2)}) copy-start(bf16[3,640,640]{2,1,0:T(8,128)(2,1)} %param.14) | copy-start | bytes 7372804
  56.2 1.7 %copy-start.2 = (bf16[3,640,640]{2,1,0:T(8,128)(2,1)S(1)}, bf16[3,640,640]{2,1,0:T(8,128)(2,1)}, u32[]{:S(2)}) copy-start(bf16[3,640,640]{2,1,0:T(8,128)(2,1)} %param.15) | copy-start | bytes 7372804

commit v16 on v14

--- a/solution.py
+++ b/solution.py
@@ -118,8 +118,27 @@
     mean_square = jnp.mean(residual * residual, axis=-1, keepdims=True)
     normed = (residual * lax.rsqrt(mean_square + 1e-06) * norm_gain).astype(jnp.bfloat16)
     normed = normed.reshape(frame_count, row_count, channels)
-    padded = extended(normed, "frame", 2)
-    hidden = jax.nn.silu(temporal_mix(padded, w_first, frame_count + 2)).astype(jnp.bfloat16)
+    halo = extended(normed, "frame", 2)
+    before, after = halo[:2], halo[-2:]
+    flat_normed = normed.reshape(-1, channels)
+    local = 0.0
+    for tap in range(3):
+        part = jnp.dot(flat_normed, w_first[tap], preferred_element_type=jnp.float32)
+        part = part.reshape(frame_count, row_count, channels)
+        local = local + jnp.pad(part, ((2 - tap, tap), (0, 0), (0, 0)))
+    first_out = jnp.einsum("frc,fcd->rd", before, w_first[0:2], preferred_element_type=jnp.float32)
+    second_out = jnp.dot(before[1], w_first[0], preferred_element_type=jnp.float32)
+    last_but_one = jnp.dot(after[0], w_first[2], preferred_element_type=jnp.float32)
+    last_out = jnp.einsum("frc,fcd->rd", after, w_first[1:3], preferred_element_type=jnp.float32)
+    halo_part = jnp.concatenate(
+        [
+            jnp.stack([first_out, second_out]),
+            jnp.zeros((frame_count - 2, row_count, channels), jnp.float32),
+            jnp.stack([last_but_one, last_out]),
+        ],
+        axis=0,
+    )
+    hidden = jax.nn.silu(local + halo_part).astype(jnp.bfloat16)
     hidden = hidden.reshape(frame_count + 2, row_count, channels)
     me = lax.axis_index("frame")
     outside = jnp.zeros((1, row_count, channels), hidden.dtype)

time: 59.8 us -> 62.4 us (1.043); the launches traced: 59.5 us -> 61.2 us
  matrix products: 11.5 us -> 16 us
  waiting for transfers between devices: 21.2 us -> 17.5 us
  starting transfers between devices: 12 us -> 13.2 us
    ppermute x1, waiting for transfers between devices: 4.4 us -> 0.01 us  [extended(): after = lax.ppermute(first, axis, down)]
    dot_general x6 -> x3, matrix products: 4.43 us -> 2.1 us  [temporal_mix(): jnp.dot(window, weights[offset], preferred_element_type=jnp.float32)]
    dot_general x2, matrix products: 1.44 us -> 3.67 us  [project(): lax.dot_general(w_keyval[:, channels:], tokens, (((0,), (1,)), ((), ())),...]
    dot_general x0 -> x5, matrix products: none -> 1.94 us  [the longest x1 0.46 us: shards(): jnp.dot(flat_normed, w_first[tap], preferred_element_type=jnp.float32)]
    pad x0 -> x2, matrix products: none -> 1.57 us  [shards(): local = local + jnp.pad(part, ((2 - tap, tap), (0, 0), (0, 0)))]
    ppermute x1, starting transfers between devices: 2.44 us -> 3.53 us  [extended(): before = lax.ppermute(last, axis, up)]
    dot_general x2, matrix products: 1.5 us -> 2.58 us  [project(): jnp.dot(tokens, w_keyval[:, :channels], preferred_element_type=jnp.float32)]
    ppermute x1, waiting for transfers between devices: 2.05 us -> 2.76 us  [extended(): before = lax.ppermute(last, axis, up)]
  transfers between devices with their start and end apart: 9 -> 9, of which waited for: 7 -> 5; matrix products, arithmetic and copies ran while one was open for 9% -> 14% of each run, Pallas kernels for 0% -> 0%
where the time goes in v16:
time: 62.4 us; the launch traced here: 61.2 us
  waiting for transfers between devices  17.5 us (28%)
  matrix products  16 us (26%)
  starting transfers between devices  13.2 us (21%)
  Pallas kernels  5.86 us (9%)
  local copies, waits for them, and re-layouts  4.1 us (7%)
  other arithmetic  2.93 us (5%)
  between operations  1.67 us (3%)
    ppermute x3, waiting for transfers between devices, gather_keyframes(): lax.ppermute(piece, 'row', [(i, (i + s) % rsize) for i in range(rsize)])  13.7 us
    pallas_call x1, Pallas kernels, attend(): pl.pallas_call(attention_kernel, grid=(channels // width,), in_specs=[pl....  5.86 us
    ppermute x3, starting transfers between devices, gather_keyframes(): lax.ppermute(piece, 'row', [(i, (i + s) % rsize) for i in range(rsize)])  3.83 us
    dot_general x2, matrix products, project(): lax.dot_general(w_keyval[:, channels:], tokens, (((0,), (1,)), ((), ())),...  3.67 us
    ppermute x1, starting transfers between devices, extended(): before = lax.ppermute(last, axis, up)  3.53 us
    ppermute x3, starting transfers between devices, gather_keyframes(): lax.ppermute(halves((me + s) % 2), 'frame', [(i, (i + s) % fsize) for i i...  3.29 us
    ppermute x1, waiting for transfers between devices, extended(): before = lax.ppermute(last, axis, up)  2.76 us
    dot_general x2, matrix products, project(): jnp.dot(tokens, w_keyval[:, :channels], preferred_element_type=jnp.float32)  2.58 us
  transfers between devices with their start and end apart: 9, of which 5 were waited for; matrix products, arithmetic and copies ran while one was open for 14% of the time, Pallas kernels for 0%

profile of v16, /device:TPU:9, one launch (start us, length us, event | category | flops | bytes accessed | tf_op | source)
XLA Modules:
  0.0 61.2 jit_solution(17138784924968072945)
XLA Ops:
  0.0 1.2 %constant_dynamic-slice_fusion.2 = (bf16[2,64,640]{2,1,0:T(8,128)(2,1)S(1)}, bf16[2,64,640]{2,1,0:T(8,128)(2,1)S(1)}, bf16[2,64,640]{2,1,0:T(8,128)(2,1)S(1)}) fusion(bf16[2,128,640]{2,1,0:T(8,128)(2,1)} %param.8, s32[]{:T(128)S(6)} %select_n.131, s32[]{:T(128)S(6)} %select_n.141, s32[]{:T(128)S(6)} %select_n.137), kind=kLoop, calls=%fused_computation.66 | loop fusion | bytes 983052 | tf_op jit(solution)/shard_map/dynamic_slice | solution.py:73
  1.2 0.7 %collective-permute-start = (bf16[2,64,640]{2,1,0:T(8,128)(2,1)S(1)}, bf16[2,64,640]{2,1,0:T(8,128)(2,1)S(1)}, u32[]{:S(2)}, u32[]{:S(2)}) collective-permute-start(bf16[2,64,640]{2,1,0:T(8,128)(2,1)S(1)} %get-tuple-element.13), channel_id=1, source_target_pairs={{0,12},{4,0},{8,4},{12,8},{1,13},{5,1},{9,5},{13,9},{2,14},{6,2},{... | collective-permute-start | bytes 491528 | tf_op jit(solution)/shard_map/ppermute | solution.py:81
  1.9 1.2 %collective-permute-start.1 = (bf16[2,64,640]{2,1,0:T(8,128)(2,1)S(1)}, bf16[2,64,640]{2,1,0:T(8,128)(2,1)S(1)}, u32[]{:S(2)}, u32[]{:S(2)}) collective-permute-start(bf16[2,64,640]{2,1,0:T(8,128)(2,1)S(1)} %get-tuple-element.15), channel_id=1, source_target_pairs={{0,8},{4,12},{8,0},{12,4},{1,9},{5,13},{9,1},{13,5},{2,10},{6,14},... | collective-permute-start | bytes 491528 | tf_op jit(solution)/shard_map/ppermute | solution.py:81
  3.2 1.3 %collective-permute-start.2 = (bf16[2,64,640]{2,1,0:T(8,128)(2,1)S(1)}, bf16[2,64,640]{2,1,0:T(8,128)(2,1)S(1)}, u32[]{:S(2)}, u32[]{:S(2)}) collective-permute-start(bf16[2,64,640]{2,1,0:T(8,128)(2,1)S(1)} %get-tuple-element.14), channel_id=1, source_target_pairs={{0,4},{4,8},{8,12},{12,0},{1,5},{5,9},{9,13},{13,1},{2,6},{6,10},{... | collective-permute-start | bytes 491528 | tf_op jit(solution)/shard_map/ppermute | solution.py:81
  4.5 1.3 %fusion.41 = (s32[1]{0:T(128)}, s32[1]{0:T(128)}) fusion(s32[2]{0:T(128)} %param.9), kind=kLoop, calls=%fused_computation.68 | loop fusion | bytes 16 | tf_op jit(solution)/shard_map/slice | solution.py:66
  7.3 2.4 %fusion.8.qt_ref = bf16[640,256]{1,0:T(8,128)(2,1)} fusion(bf16[640,640]{1,0:T(8,128)(2,1)} %param.10, bf16[256,640]{1,0:T(8,128)(2,1)} %bitcast.79), kind=kOutput, calls=%fused_computation.21 | convolution fusion | flops 210042880 | bytes 1474560 | tf_op jit(solution)/shard_map/dot_general | solution.py:99
  9.7 1.0 %collective-permute-done.2 = bf16[2,64,640]{2,1,0:T(8,128)(2,1)S(1)} collective-permute-done((bf16[2,64,640]{2,1,0:T(8,128)(2,1)S(1)}, bf16[2,64,640]{2,1,0:T(8,128)(2,1)S(1)}, u32[]{:S(2)}, u32[]{:S(2)}) %collective-permute-start.2) | collective-permute-done | bytes 163872 | tf_op jit(solution)/shard_map/ppermute | solution.py:81
  10.8 1.4 %collective-permute-start.3 = (bf16[2,64,640]{2,1,0:T(8,128)(2,1)S(1)}, bf16[2,64,640]{2,1,0:T(8,128)(2,1)S(1)}, u32[]{:S(2)}, u32[]{:S(2)}) collective-permute-start(bf16[2,64,640]{2,1,0:T(8,128)(2,1)S(1)} %pad_maximum_fusion.5), channel_id=1, source_target_pairs={{0,1},{1,2},{2,3},{3,0},{4,5},{5,6},{6,7},{7,4},{8,9},{9,10},{10,1... | collective-permute-start | bytes 491528 | tf_op jit(solution)/shard_map/ppermute | solution.py:89
  12.2 1.1 %collective-permute-start.4 = (bf16[2,64,640]{2,1,0:T(8,128)(2,1)S(1)}, bf16[2,64,640]{2,1,0:T(8,128)(2,1)S(1)}, u32[]{:S(2)}, u32[]{:S(2)}) collective-permute-start(bf16[2,64,640]{2,1,0:T(8,128)(2,1)S(1)} %pad_maximum_fusion.5), channel_id=1, source_target_pairs={{0,2},{1,3},{2,0},{3,1},{4,6},{5,7},{6,4},{7,5},{8,10},{9,11},{10,... | collective-permute-start | bytes 491528 | tf_op jit(solution)/shard_map/ppermute | solution.py:89
  13.3 1.4 %collective-permute-start.5 = (bf16[2,64,640]{2,1,0:T(8,128)(2,1)S(1)}, bf16[2,64,640]{2,1,0:T(8,128)(2,1)S(1)}, u32[]{:S(2)}, u32[]{:S(2)}) collective-permute-start(bf16[2,64,640]{2,1,0:T(8,128)(2,1)S(1)} %pad_maximum_fusion.5), channel_id=1, source_target_pairs={{0,3},{1,0},{2,1},{3,2},{4,7},{5,4},{6,5},{7,6},{8,11},{9,8},{10,9... | collective-permute-start | bytes 491528 | tf_op jit(solution)/shard_map/ppermute | solution.py:89
  15.0 9.8 %collective-permute-done.4 = bf16[2,64,640]{2,1,0:T(8,128)(2,1)S(1)} collective-permute-done((bf16[2,64,640]{2,1,0:T(8,128)(2,1)S(1)}, bf16[2,64,640]{2,1,0:T(8,128)(2,1)S(1)}, u32[]{:S(2)}, u32[]{:S(2)}) %collective-permute-start.4) | collective-permute-done | bytes 163872 | tf_op jit(solution)/shard_map/ppermute | solution.py:89
  24.9 3.5 %collective-permute-done.5 = bf16[2,64,640]{2,1,0:T(8,128)(2,1)S(1)} collective-permute-done((bf16[2,64,640]{2,1,0:T(8,128)(2,1)S(1)}, bf16[2,64,640]{2,1,0:T(8,128)(2,1)S(1)}, u32[]{:S(2)}, u32[]{:S(2)}) %collective-permute-start.5) | collective-permute-done | bytes 163872 | tf_op jit(solution)/shard_map/ppermute | solution.py:89
  28.5 0.6 collective-permute-start.6
  29.0 1.9 %fusion.5 = bf16[640,512]{1,0:T(8,128)(2,1)S(1)} fusion(bf16[512,640]{1,0:T(8,128)(2,1)S(1)} %bitcast.85, bf16[640,1280]{1,0:T(8,128)(2,1)} %param.11), kind=kOutput, calls=%fused_computation.14 | convolution fusion | flops 419758080 | bytes 2129920 | tf_op jit(solution)/shard_map/dot_general | solution.py:105
  30.9 0.7 %convolution_convert_fusion.3 = bf16[512,640]{1,0:T(8,128)(2,1)S(1)} fusion(bf16[512,640]{1,0:T(8,128)(2,1)S(1)} %bitcast.86, bf16[640,1280]{1,0:T(8,128)(2,1)S(1)} %copy-done.5), kind=kOutput, calls=%fused_computation.9 | convolution fusion | flops 419758080 | bytes 2129920 | tf_op jit(solution)/shard_map/dot_general | solution.py:104
  31.7 1.8 %fusion.6 = bf16[640,512]{1,0:T(8,128)(2,1)S(1)} fusion(bf16[512,640]{1,0:T(8,128)(2,1)} %collective-permute-done.6, bf16[640,1280]{1,0:T(8,128)(2,1)S(1)} %copy-done.5), kind=kOutput, calls=%fused_computation.15 | convolution fusion | flops 419758080 | bytes 2129920 | tf_op jit(solution)/shard_map/dot_general | solution.py:105
  33.5 1.3 %pad_maximum_fusion.1.vt_ref = bf16[640,1024]{1,0:T(8,128)(2,1)} fusion(bf16[640,512]{1,0:T(8,128)(2,1)S(1)} %fusion.6, bf16[640,512]{1,0:T(8,128)(2,1)S(1)} %fusion.5), kind=kLoop, calls=%fused_computation.11 | loop fusion | flops 2621440 | bytes 2621440 | tf_op jit(solution)/shard_map/concatenate | solution.py:113
  34.8 1.8 %convolution_convert_fusion.2 = bf16[512,640]{1,0:T(8,128)(2,1)S(1)} fusion(bf16[512,640]{1,0:T(8,128)(2,1)} %collective-permute-done.6, bf16[640,1280]{1,0:T(8,128)(2,1)S(1)} %copy-done.5), kind=kOutput, calls=%fused_computation.8 | convolution fusion | flops 419758080 | bytes 2129920 | tf_op jit(solution)/shard_map/dot_general | solution.py:104
  36.6 1.2 %pad_maximum_fusion.k_ref = bf16[1024,640]{1,0:T(8,128)(2,1)} fusion(bf16[512,640]{1,0:T(8,128)(2,1)S(1)} %convolution_convert_fusion.2, bf16[512,640]{1,0:T(8,128)(2,1)S(1)} %convolution_convert_fusion.3), kind=kLoop, calls=%fused_computation.10 | loop fusion | flops 2621440 | bytes 2621440 | tf_op jit(solution)/shard_map/concatenate | solution.py:112
  37.8 5.9 %shard_map.82 = bf16[640,256]{1,0:T(8,128)(2,1)} custom-call(bf16[1024,640]{1,0:T(8,128)(2,1)} %pad_maximum_fusion.k_ref, bf16[640,256]{1,0:T(8,128)(2,1)} %fusion.8.qt_ref, bf16[640,1024]{1,0:T(8,128)(2,1)} %pad_maximum_fusion.1.vt_ref), custom_call_target="tpu_custom_call" | custom-call | tf_op jit(solution)/shard_map/pallas_call | solution.py:28
  43.6 1.7 %multiply_reduce_fusion = (f32[256]{0:T(256)S(1)}, f32[256,640]{1,0:T(8,128)S(1)}) fusion(bf16[640,256]{1,0:T(8,128)(2,1)} %shard_map.82, bf16[640,640]{1,0:T(8,128)(2,1)S(1)} %copy-done, bf16[256,640]{1,0:T(8,128)(2,1)S(1)} %bitcast.80), kind=kOutput, calls=%fused_computation.52 | convolution fusion | flops 210370304 | bytes 2130944 | tf_op jit(solution)/shard_map/dot_general | solution.py:115
  45.5 2.0 %collective-permute-start.8 = (bf16[2,128,640]{2,1,0:T(8,128)(2,1)S(1)}, bf16[2,128,640]{2,1,0:T(8,128)(2,1)S(1)}, u32[]{:S(2)}, u32[]{:S(2)}) collective-permute-start(bf16[2,128,640]{2,1,0:T(8,128)(2,1)S(1)} %bitcast.73), channel_id=1, source_target_pairs={{4,0},{8,4},{12,8},{5,1},{9,5},{13,9},{6,2},{10,6},{14,10},{7,3},{... | collective-permute-start | bytes 983048 | tf_op jit(solution)/shard_map/ppermute | solution.py:48
  47.6 3.5 %collective-permute-start.7 = (bf16[2,128,640]{2,1,0:T(8,128)(2,1)S(1)}, bf16[2,128,640]{2,1,0:T(8,128)(2,1)S(1)}, u32[]{:S(2)}, u32[]{:S(2)}) collective-permute-start(bf16[2,128,640]{2,1,0:T(8,128)(2,1)S(1)} %bitcast.74), channel_id=1, source_target_pairs={{0,4},{4,8},{8,12},{1,5},{5,9},{9,13},{2,6},{6,10},{10,14},{3,7},{... | collective-permute-start | bytes 983048 | tf_op jit(solution)/shard_map/ppermute | solution.py:47
  51.1 0.5 fusion.20
  51.6 0.7 %fusion.24 = f32[4,128,640]{2,1,0:T(8,128)S(1)} fusion(bf16[2,128,640]{2,1,0:T(8,128)(2,1)S(1)} %bitcast.76, bf16[3,640,640]{2,1,0:T(8,128)(2,1)S(1)} %copy-done.1), kind=kOutput, calls=%fused_computation.35 | convolution fusion | flops 209715200 | bytes 2457600 | tf_op jit(solution)/shard_map/jit(_pad)/pad | solution.py:128
  52.3 2.8 %collective-permute-done.7 = bf16[2,128,640]{2,1,0:T(8,128)(2,1)S(1)} collective-permute-done((bf16[2,128,640]{2,1,0:T(8,128)(2,1)S(1)}, bf16[2,128,640]{2,1,0:T(8,128)(2,1)S(1)}, u32[]{:S(2)}, u32[]{:S(2)}) %collective-permute-start.7) | collective-permute-done | bytes 327712 | tf_op jit(solution)/shard_map/ppermute | solution.py:47
  55.4 0.4 fusion.10
  56.6 0.8 %multiply_convert_fusion = bf16[4,128,640]{2,1,0:T(8,128)(2,1)S(1)} fusion(f32[1,128,640]{2,1,0:T(8,128)S(1)} %fusion.13, f32[1,128,640]{2,1,0:T(8,128)S(1)} %convolution_bitcast_fusion, f32[1,128,640]{2,1,0:T(8,128)S(1)} %convolution_bitcast_fusion.1, f32[1,128,640]{2,1,0:T(8,128)S(1)} %fusion.10, f32[2,128,640]{2,1,0:T(8,128)S(1)} %fusion.20, ...), kind=kOutput, calls=%fused_computation.13 | convolution fusion | flops 213319680 | bytes 5079040 | tf_op jit(solution)/shard_map/jit(_pad)/pad | solution.py:128
  57.6 1.5 %copy-done.3 = bf16[3,640,640]{2,1,0:T(8,128)(2,1)S(1)} copy-done((bf16[3,640,640]{2,1,0:T(8,128)(2,1)S(1)}, bf16[3,640,640]{2,1,0:T(8,128)(2,1)}, u32[]{:S(2)}) %copy-start.3) | copy-done | bytes 2457624
  59.1 0.5 fusion.18
  59.6 0.5 convolution_add_fusion.2
  60.1 1.2 %fusion.9 = bf16[256,640]{1,0:T(8,128)(2,1)} fusion(f32[256,640]{1,0:T(8,128)S(1)} %get-tuple-element.19, f32[256,640]{1,0:T(8,128)S(1)} %convolution_add_fusion.2, bf16[256,640]{1,0:T(8,128)(2,1)S(1)} %bitcast.82, bf16[3,640,640]{2,1,0:T(8,128)(2,1)S(1)} %copy-done.3), kind=kOutput, calls=%fused_computation.22 | convolution fusion | flops 210206720 | bytes 2785280 | tf_op jit(solution)/shard_map/dot_general | solution.py:56
  (27 shorter events, 2.0 us)
Async XLA Ops:
  0.0 43.6 %copy-start = (bf16[640,640]{1,0:T(8,128)(2,1)S(1)}, bf16[640,640]{1,0:T(8,128)(2,1)}, u32[]{:S(2)}) copy-start(bf16[640,640]{1,0:T(8,128)(2,1)} %param.12) | copy-start | bytes 2457604
  0.0 10.7 %copy-start.2 = (bf16[2,128,640]{2,1,0:T(8,128)(2,1)S(1)}, bf16[2,128,640]{2,1,0:T(8,128)(2,1)}, u32[]{:S(2)}) copy-start(bf16[2,128,640]{2,1,0:T(8,128)(2,1)} %param.8) | copy-start | bytes 983044
  1.2 8.5 %collective-permute-start = (bf16[2,64,640]{2,1,0:T(8,128)(2,1)S(1)}, bf16[2,64,640]{2,1,0:T(8,128)(2,1)S(1)}, u32[]{:S(2)}, u32[]{:S(2)}) collective-permute-start(bf16[2,64,640]{2,1,0:T(8,128)(2,1)S(1)} %get-tuple-element.13), channel_id=1, source_target_pairs={{0,12},{4,0},{8,4},{12,8},{1,13},{5,1},{9,5},{13,9},{2,14},{6,2},{... | collective-permute-start | bytes 491528 | tf_op jit(solution)/shard_map/ppermute | solution.py:81
  1.9 7.8 %collective-permute-start.1 = (bf16[2,64,640]{2,1,0:T(8,128)(2,1)S(1)}, bf16[2,64,640]{2,1,0:T(8,128)(2,1)S(1)}, u32[]{:S(2)}, u32[]{:S(2)}) collective-permute-start(bf16[2,64,640]{2,1,0:T(8,128)(2,1)S(1)} %get-tuple-element.15), channel_id=1, source_target_pairs={{0,8},{4,12},{8,0},{12,4},{1,9},{5,13},{9,1},{13,5},{2,10},{6,14},... | collective-permute-start | bytes 491528 | tf_op jit(solution)/shard_map/ppermute | solution.py:81
  3.2 7.5 %collective-permute-start.2 = (bf16[2,64,640]{2,1,0:T(8,128)(2,1)S(1)}, bf16[2,64,640]{2,1,0:T(8,128)(2,1)S(1)}, u32[]{:S(2)}, u32[]{:S(2)}) collective-permute-start(bf16[2,64,640]{2,1,0:T(8,128)(2,1)S(1)} %get-tuple-element.14), channel_id=1, source_target_pairs={{0,4},{4,8},{8,12},{12,0},{1,5},{5,9},{9,13},{13,1},{2,6},{6,10},{... | collective-permute-start | bytes 491528 | tf_op jit(solution)/shard_map/ppermute | solution.py:81
  10.8 4.2 %collective-permute-start.3 = (bf16[2,64,640]{2,1,0:T(8,128)(2,1)S(1)}, bf16[2,64,640]{2,1,0:T(8,128)(2,1)S(1)}, u32[]{:S(2)}, u32[]{:S(2)}) collective-permute-start(bf16[2,64,640]{2,1,0:T(8,128)(2,1)S(1)} %pad_maximum_fusion.5), channel_id=1, source_target_pairs={{0,1},{1,2},{2,3},{3,0},{4,5},{5,6},{6,7},{7,4},{8,9},{9,10},{10,1... | collective-permute-start | bytes 491528 | tf_op jit(solution)/shard_map/ppermute | solution.py:89
  12.2 12.7 %collective-permute-start.4 = (bf16[2,64,640]{2,1,0:T(8,128)(2,1)S(1)}, bf16[2,64,640]{2,1,0:T(8,128)(2,1)S(1)}, u32[]{:S(2)}, u32[]{:S(2)}) collective-permute-start(bf16[2,64,640]{2,1,0:T(8,128)(2,1)S(1)} %pad_maximum_fusion.5), channel_id=1, source_target_pairs={{0,2},{1,3},{2,0},{3,1},{4,6},{5,7},{6,4},{7,5},{8,10},{9,11},{10,... | collective-permute-start | bytes 491528 | tf_op jit(solution)/shard_map/ppermute | solution.py:89
  13.3 15.1 %collective-permute-start.5 = (bf16[2,64,640]{2,1,0:T(8,128)(2,1)S(1)}, bf16[2,64,640]{2,1,0:T(8,128)(2,1)S(1)}, u32[]{:S(2)}, u32[]{:S(2)}) collective-permute-start(bf16[2,64,640]{2,1,0:T(8,128)(2,1)S(1)} %pad_maximum_fusion.5), channel_id=1, source_target_pairs={{0,3},{1,0},{2,1},{3,2},{4,7},{5,4},{6,5},{7,6},{8,11},{9,8},{10,9... | collective-permute-start | bytes 491528 | tf_op jit(solution)/shard_map/ppermute | solution.py:89
  28.4 2.5 %copy-start.5 = (bf16[640,1280]{1,0:T(8,128)(2,1)S(1)}, bf16[640,1280]{1,0:T(8,128)(2,1)}, u32[]{:S(2)}) copy-start(bf16[640,1280]{1,0:T(8,128)(2,1)} %param.11) | copy-start | bytes 4915204
  28.5 3.2 %collective-permute-start.6 = (bf16[512,640]{1,0:T(8,128)(2,1)S(1)}, bf16[512,640]{1,0:T(8,128)(2,1)}, u32[]{:S(2)}, u32[]{:S(2)}) collective-permute-start(bf16[512,640]{1,0:T(8,128)(2,1)S(1)} %bitcast.84), channel_id=1, source_target_pairs={{0,4},{4,0},{8,12},{12,8},{1,5},{5,1},{9,13},{13,9},{2,6},{6,2},{1... | collective-permute-start | bytes 1966088 | tf_op jit(solution)/shard_map/ppermute | solution.py:91
  37.8 7.6 %copy-start.4 = (f32[640]{0:T(1024)S(1)}, f32[640]{0:T(1024)}, u32[]{:S(2)}) copy-start(f32[640]{0:T(1024)} %param.13) | copy-start | bytes 7684
  43.6 7.4 %copy-start.1 = (bf16[3,640,640]{2,1,0:T(8,128)(2,1)S(1)}, bf16[3,640,640]{2,1,0:T(8,128)(2,1)}, u32[]{:S(2)}) copy-start(bf16[3,640,640]{2,1,0:T(8,128)(2,1)} %param.14) | copy-start | bytes 7372804
  45.5 10.3 %collective-permute-start.8 = (bf16[2,128,640]{2,1,0:T(8,128)(2,1)S(1)}, bf16[2,128,640]{2,1,0:T(8,128)(2,1)S(1)}, u32[]{:S(2)}, u32[]{:S(2)}) collective-permute-start(bf16[2,128,640]{2,1,0:T(8,128)(2,1)S(1)} %bitcast.73), channel_id=1, source_target_pairs={{4,0},{8,4},{12,8},{5,1},{9,5},{13,9},{6,2},{10,6},{14,10},{7,3},{... | collective-permute-start | bytes 983048 | tf_op jit(solution)/shard_map/ppermute | solution.py:48
  47.6 7.5 %collective-permute-start.7 = (bf16[2,128,640]{2,1,0:T(8,128)(2,1)S(1)}, bf16[2,128,640]{2,1,0:T(8,128)(2,1)S(1)}, u32[]{:S(2)}, u32[]{:S(2)}) collective-permute-start(bf16[2,128,640]{2,1,0:T(8,128)(2,1)S(1)} %bitcast.74), channel_id=1, source_target_pairs={{0,4},{4,8},{8,12},{1,5},{5,9},{9,13},{2,6},{6,10},{10,14},{3,7},{... | collective-permute-start | bytes 983048 | tf_op jit(solution)/shard_map/ppermute | solution.py:47
  57.4 1.7 %copy-start.3 = (bf16[3,640,640]{2,1,0:T(8,128)(2,1)S(1)}, bf16[3,640,640]{2,1,0:T(8,128)(2,1)}, u32[]{:S(2)}) copy-start(bf16[3,640,640]{2,1,0:T(8,128)(2,1)} %param.15) | copy-start | bytes 7372804

commit v17 on v14

--- a/solution.py
+++ b/solution.py
@@ -8,34 +8,68 @@
 HEAD_DIM = 64
 
 
-def attention_kernel(k_ref, qt_ref, vt_ref, o_ref):
-    heads = [slice(h * HEAD_DIM, (h + 1) * HEAD_DIM) for h in range(qt_ref.shape[0] // HEAD_DIM)]
+def _heads(ref):
+    return [slice(h * HEAD_DIM, (h + 1) * HEAD_DIM) for h in range(ref.shape[0] // HEAD_DIM)]
+
+
+def first_chunk_kernel(k_ref, qt_ref, vt_ref, m_ref, l_ref, acc_ref):
+    heads = _heads(qt_ref)
     scores = [jnp.dot(k_ref[:, c], qt_ref[c, :], preferred_element_type=jnp.float32) for c in heads]
     highest = [jnp.max(s, axis=0, keepdims=True) for s in scores]
     exponent = [jnp.exp(s - m) for s, m in zip(scores, highest)]
-    denominator = [jnp.sum(e, axis=0, keepdims=True) for e in exponent]
-    mixed = [
-        jnp.dot(vt_ref[c, :], e.astype(jnp.bfloat16), preferred_element_type=jnp.float32)
-        for e, c in zip(exponent, heads)
-    ]
-    o_ref[...] = jnp.concatenate([m / d for m, d in zip(mixed, denominator)], axis=0).astype(o_ref.dtype)
+    for c, m, e in zip(heads, highest, exponent):
+        mixed = jnp.dot(vt_ref[c, :], e.astype(jnp.bfloat16), preferred_element_type=jnp.float32)
+        m_ref[c, :] = jnp.broadcast_to(m, mixed.shape)
+        l_ref[c, :] = jnp.broadcast_to(jnp.sum(e, axis=0, keepdims=True), mixed.shape)
+        acc_ref[c, :] = mixed
 
 
-def attend(keys, queries_t, values_t):
+def last_chunk_kernel(k_ref, qt_ref, vt_ref, m_ref, l_ref, acc_ref, o_ref):
+    heads = _heads(qt_ref)
+    scores = [jnp.dot(k_ref[:, c], qt_ref[c, :], preferred_element_type=jnp.float32) for c in heads]
+    before = [jnp.max(m_ref[c, :], axis=0, keepdims=True) for c in heads]
+    highest = [jnp.maximum(b, jnp.max(s, axis=0, keepdims=True)) for b, s in zip(before, scores)]
+    kept = [jnp.exp(b - m) for b, m in zip(before, highest)]
+    exponent = [jnp.exp(s - m) for s, m in zip(scores, highest)]
+    outs = []
+    for c, k, e in zip(heads, kept, exponent):
+        total = jnp.max(l_ref[c, :], axis=0, keepdims=True) * k + jnp.sum(e, axis=0, keepdims=True)
+        mixed = acc_ref[c, :] * k + jnp.dot(vt_ref[c, :], e.astype(jnp.bfloat16), preferred_element_type=jnp.float32)
+        outs.append(mixed / total)
+    o_ref[...] = jnp.concatenate(outs, axis=0).astype(o_ref.dtype)
+
+
+def _attention_specs(channels, total, count):
+    width = channels if total * count * channels <= 256 * 1024 * 640 else 2 * HEAD_DIM
+    rows = pl.BlockSpec((width, total), lambda j: (j, 0))
+    keys = pl.BlockSpec((count, width), lambda j: (0, j))
+    values = pl.BlockSpec((width, count), lambda j: (j, 0))
+    return channels // width, rows, keys, values
+
+
+def attend_first(keys, queries_t, values_t):
     channels, total = queries_t.shape
-    count = keys.shape[0]
-    width = channels if total * count * channels <= 256 * 1024 * 640 else 2 * HEAD_DIM
+    steps, rows, key_spec, value_spec = _attention_specs(channels, total, keys.shape[0])
+    state = jax.ShapeDtypeStruct((channels, total), jnp.float32)
     return pl.pallas_call(
-        attention_kernel,
-        grid=(channels // width,),
-        in_specs=[
-            pl.BlockSpec((count, width), lambda j: (0, j)),
-            pl.BlockSpec((width, total), lambda j: (j, 0)),
-            pl.BlockSpec((width, count), lambda j: (j, 0)),
-        ],
-        out_specs=pl.BlockSpec((width, total), lambda j: (j, 0)),
+        first_chunk_kernel,
+        grid=(steps,),
+        in_specs=[key_spec, rows, value_spec],
+        out_specs=[rows, rows, rows],
+        out_shape=[state, state, state],
+    )(keys, queries_t, values_t)
+
+
+def attend_last(keys, queries_t, values_t, state):
+    channels, total = queries_t.shape
+    steps, rows, key_spec, value_spec = _attention_specs(channels, total, keys.shape[0])
+    return pl.pallas_call(
+        last_chunk_kernel,
+        grid=(steps,),
+        in_specs=[key_spec, rows, value_spec, rows, rows, rows],
+        out_specs=rows,
         out_shape=jax.ShapeDtypeStruct((channels, total), jnp.bfloat16),
-    )(keys, queries_t, values_t)
+    )(keys, queries_t, values_t, *state)
 
 
 def extended(array, axis, width):
@@ -84,12 +118,12 @@
         got_b = jnp.where(source == owner_b, recv[n_loc - 1], got_b)
     piece = jnp.stack([got_a, got_b])
     piece, early = lax.optimization_barrier((piece, early))
-    pieces = [piece]
+    swap = [(i, i ^ 1) for i in range(fsize)]
+    own_row = jnp.concatenate([piece, lax.ppermute(piece, "frame", swap)], axis=0).reshape(-1, channels)
+    pieces = []
     for s in range(1, rsize):
         pieces.append(lax.ppermute(piece, "row", [(i, (i + s) % rsize) for i in range(rsize)]))
-    mine = jnp.stack(pieces).reshape(-1, channels)
-    sibling = lax.ppermute(mine, "frame", [(i, i ^ 1) for i in range(fsize)])
-    return mine, sibling
+    return own_row, pieces
 
 
 def shards(frames, key_index, w_query, w_keyval, w_out, norm_gain, w_first, w_second):
@@ -98,7 +132,7 @@
     flattened = frames.reshape(-1, channels)
     queries_t = lax.dot_general(w_query, flattened, (((0,), (1,)), ((), ())), preferred_element_type=jnp.float32)
     queries_t = (queries_t * HEAD_DIM ** (-0.5)).astype(jnp.bfloat16)
-    mine, sibling = gather_keyframes(frames, key_index, queries_t)
+    own_row, pieces = gather_keyframes(frames, key_index, queries_t)
 
     def project(tokens):
         keys = jnp.dot(tokens, w_keyval[:, :channels], preferred_element_type=jnp.float32).astype(jnp.bfloat16)
@@ -107,11 +141,15 @@
         ).astype(jnp.bfloat16)
         return keys, values_t
 
+    state = attend_first(project(own_row)[0], queries_t, project(own_row)[1])
+    pieces, state = lax.optimization_barrier((pieces, state))
+    mine = jnp.stack(pieces).reshape(-1, channels)
+    sibling = lax.ppermute(mine, "frame", [(i, i ^ 1) for i in range(lax.axis_size("frame"))])
     keys_mine, values_mine = project(mine)
     keys_sib, values_sib = project(sibling)
     keys = jnp.concatenate([keys_mine, keys_sib], axis=0)
     values_t = jnp.concatenate([values_mine, values_sib], axis=1)
-    attended_t = attend(keys, queries_t, values_t)
+    attended_t = attend_last(keys, queries_t, values_t, state)
     residual = flattened.astype(jnp.float32) + lax.dot_general(
         attended_t, w_out, (((0,), (0,)), ((), ())), preferred_element_type=jnp.float32
     )

time: 59.8 us -> 61.1 us (1.022)
  waiting for transfers between devices: 21.2 us -> 15.4 us
  Pallas kernels: 5.85 us -> 8.92 us
  starting transfers between devices: 12 us -> 14.4 us
  matrix products: 11.5 us -> 13.6 us
    ppermute x3, waiting for transfers between devices: 13.7 us -> 8.02 us  [gather_keyframes(): lax.ppermute(piece, 'row', [(i, (i + s) % rsize) for i in range(rsize)])]
    pallas_call x1 -> x2, Pallas kernels: 5.85 us -> 8.92 us  [the longest x1 5.65 us: attend_last(): pl.pallas_call(last_chunk_kernel, grid=(steps,), in_specs=[key_spec, rows...]
    ppermute x1 -> x2, starting transfers between devices: 0.56 us -> 1.94 us  [the longest x1 1.4 us: gather_keyframes(): lax.ppermute(piece, 'frame', swap)]
    dot_general x2 -> x3, matrix products: 1.44 us -> 2.63 us  [project(): lax.dot_general(w_keyval[:, channels:], tokens, (((0,), (1,)), ((), ())),...]
    ppermute x1, starting transfers between devices: 2.44 us -> 3.34 us  [extended(): before = lax.ppermute(last, axis, up)]
    dot_general x2 -> x3, matrix products: 1.5 us -> 2.39 us  [project(): jnp.dot(tokens, w_keyval[:, :channels], preferred_element_type=jnp.float32)]
    unnamed x12 -> x14, local copies, waits for them, and re-layouts: 1.55 us -> 1.55 us
  transfers between devices with their start and end apart: 9 -> 10, of which waited for: 7 -> 6; matrix products, arithmetic and copies ran while one was open for 9% -> 12% of each run, Pallas kernels for 0% -> 5%
where the time goes in v17:
time: 61.1 us; the launch traced here: 60.8 us
  waiting for transfers between devices  15.4 us (25%)
  starting transfers between devices  14.4 us (24%)
  matrix products  13.6 us (22%)
  Pallas kernels  8.92 us (15%)
  local copies, waits for them, and re-layouts  4.11 us (7%)
  other arithmetic  2.84 us (5%)
  between operations  1.61 us (3%)
    ppermute x3, waiting for transfers between devices, gather_keyframes(): lax.ppermute(piece, 'row', [(i, (i + s) % rsize) for i in range(rsize)])  8.02 us
    pallas_call x1, Pallas kernels, attend_last(): pl.pallas_call(last_chunk_kernel, grid=(steps,), in_specs=[key_spec, rows...  5.65 us
    dot_general x6, matrix products, temporal_mix(): jnp.dot(window, weights[offset], preferred_element_type=jnp.float32)  4.45 us
    ppermute x1, waiting for transfers between devices, extended(): after = lax.ppermute(first, axis, down)  4.4 us
    ppermute x3, starting transfers between devices, gather_keyframes(): lax.ppermute(piece, 'row', [(i, (i + s) % rsize) for i in range(rsize)])  3.78 us
    ppermute x1, starting transfers between devices, extended(): before = lax.ppermute(last, axis, up)  3.34 us
    ppermute x3, starting transfers between devices, gather_keyframes(): lax.ppermute(halves((me + s) % 2), 'frame', [(i, (i + s) % fsize) for i i...  3.29 us
    pallas_call x1, Pallas kernels, attend_first(): pl.pallas_call(first_chunk_kernel, grid=(steps,), in_specs=[key_spec, row...  3.27 us
  transfers between devices with their start and end apart: 10, of which 6 were waited for; matrix products, arithmetic and copies ran while one was open for 12% of the time, Pallas kernels for 5%

profile of v17, /device:TPU:9, one launch (start us, length us, event | category | flops | bytes accessed | tf_op | source)
XLA Modules:
  0.0 60.8 jit_solution(8742575718837553137)
XLA Ops:
  0.0 1.2 %constant_dynamic-slice_fusion.2 = (bf16[2,64,640]{2,1,0:T(8,128)(2,1)S(1)}, bf16[2,64,640]{2,1,0:T(8,128)(2,1)S(1)}, bf16[2,64,640]{2,1,0:T(8,128)(2,1)S(1)}) fusion(bf16[2,128,640]{2,1,0:T(8,128)(2,1)} %param.8, s32[]{:T(128)S(6)} %select_n.137, s32[]{:T(128)S(6)} %select_n.147, s32[]{:T(128)S(6)} %select_n.143), kind=kLoop, calls=%fused_computation.63 | loop fusion | bytes 983052 | tf_op jit(solution)/shard_map/dynamic_slice | solution.py:107
  1.2 0.7 %collective-permute-start = (bf16[2,64,640]{2,1,0:T(8,128)(2,1)S(1)}, bf16[2,64,640]{2,1,0:T(8,128)(2,1)S(1)}, u32[]{:S(2)}, u32[]{:S(2)}) collective-permute-start(bf16[2,64,640]{2,1,0:T(8,128)(2,1)S(1)} %get-tuple-element.34), channel_id=1, source_target_pairs={{0,12},{4,0},{8,4},{12,8},{1,13},{5,1},{9,5},{13,9},{2,14},{6,2},{... | collective-permute-start | bytes 491528 | tf_op jit(solution)/shard_map/ppermute | solution.py:115
  1.9 1.2 %collective-permute-start.1 = (bf16[2,64,640]{2,1,0:T(8,128)(2,1)S(1)}, bf16[2,64,640]{2,1,0:T(8,128)(2,1)S(1)}, u32[]{:S(2)}, u32[]{:S(2)}) collective-permute-start(bf16[2,64,640]{2,1,0:T(8,128)(2,1)S(1)} %get-tuple-element.36), channel_id=1, source_target_pairs={{0,8},{4,12},{8,0},{12,4},{1,9},{5,13},{9,1},{13,5},{2,10},{6,14},... | collective-permute-start | bytes 491528 | tf_op jit(solution)/shard_map/ppermute | solution.py:115
  3.2 1.3 %collective-permute-start.2 = (bf16[2,64,640]{2,1,0:T(8,128)(2,1)S(1)}, bf16[2,64,640]{2,1,0:T(8,128)(2,1)S(1)}, u32[]{:S(2)}, u32[]{:S(2)}) collective-permute-start(bf16[2,64,640]{2,1,0:T(8,128)(2,1)S(1)} %get-tuple-element.35), channel_id=1, source_target_pairs={{0,4},{4,8},{8,12},{12,0},{1,5},{5,9},{9,13},{13,1},{2,6},{6,10},{... | collective-permute-start | bytes 491528 | tf_op jit(solution)/shard_map/ppermute | solution.py:115
  4.5 1.3 %fusion.33 = (s32[1]{0:T(128)}, s32[1]{0:T(128)}) fusion(s32[2]{0:T(128)} %param.9), kind=kLoop, calls=%fused_computation.66 | loop fusion | bytes 16 | tf_op jit(solution)/shard_map/slice | solution.py:100
  7.2 2.5 %fusion.2.qt_ref = bf16[640,256]{1,0:T(8,128)(2,1)} fusion(bf16[640,640]{1,0:T(8,128)(2,1)} %param.10, bf16[256,640]{1,0:T(8,128)(2,1)} %bitcast.58), kind=kOutput, calls=%fused_computation.12 | convolution fusion | flops 210042880 | bytes 1474560 | tf_op jit(solution)/shard_map/dot_general | solution.py:133
  9.8 0.9 %collective-permute-done.2 = bf16[2,64,640]{2,1,0:T(8,128)(2,1)S(1)} collective-permute-done((bf16[2,64,640]{2,1,0:T(8,128)(2,1)S(1)}, bf16[2,64,640]{2,1,0:T(8,128)(2,1)S(1)}, u32[]{:S(2)}, u32[]{:S(2)}) %collective-permute-start.2) | collective-permute-done | bytes 163872 | tf_op jit(solution)/shard_map/ppermute | solution.py:115
  10.8 1.4 %collective-permute-start.6 = (bf16[2,64,640]{2,1,0:T(8,128)(2,1)S(1)}, bf16[2,64,640]{2,1,0:T(8,128)(2,1)S(1)}, u32[]{:S(2)}, u32[]{:S(2)}) collective-permute-start(bf16[2,64,640]{2,1,0:T(8,128)(2,1)S(1)} %pad_maximum_fusion.10), channel_id=1, source_target_pairs={{0,4},{4,0},{8,12},{12,8},{1,5},{5,1},{9,13},{13,9},{2,6},{6,2},{1... | collective-permute-start | bytes 491528 | tf_op jit(solution)/shard_map/ppermute | solution.py:122
  12.2 1.3 %collective-permute-start.3 = (bf16[2,64,640]{2,1,0:T(8,128)(2,1)S(1)}, bf16[2,64,640]{2,1,0:T(8,128)(2,1)S(1)}, u32[]{:S(2)}, u32[]{:S(2)}) collective-permute-start(bf16[2,64,640]{2,1,0:T(8,128)(2,1)S(1)} %pad_maximum_fusion.10), channel_id=1, source_target_pairs={{0,1},{1,2},{2,3},{3,0},{4,5},{5,6},{6,7},{7,4},{8,9},{9,10},{10,1... | collective-permute-start | bytes 491528 | tf_op jit(solution)/shard_map/ppermute | solution.py:125
  13.5 1.0 %collective-permute-start.4 = (bf16[2,64,640]{2,1,0:T(8,128)(2,1)S(1)}, bf16[2,64,640]{2,1,0:T(8,128)(2,1)S(1)}, u32[]{:S(2)}, u32[]{:S(2)}) collective-permute-start(bf16[2,64,640]{2,1,0:T(8,128)(2,1)S(1)} %pad_maximum_fusion.10), channel_id=1, source_target_pairs={{0,2},{1,3},{2,0},{3,1},{4,6},{5,7},{6,4},{7,5},{8,10},{9,11},{10,... | collective-permute-start | bytes 491528 | tf_op jit(solution)/shard_map/ppermute | solution.py:125
  14.5 1.5 %collective-permute-start.5 = (bf16[2,64,640]{2,1,0:T(8,128)(2,1)S(1)}, bf16[2,64,640]{2,1,0:T(8,128)(2,1)S(1)}, u32[]{:S(2)}, u32[]{:S(2)}) collective-permute-start(bf16[2,64,640]{2,1,0:T(8,128)(2,1)S(1)} %pad_maximum_fusion.10), channel_id=1, source_target_pairs={{0,3},{1,0},{2,1},{3,2},{4,7},{5,4},{6,5},{7,6},{8,11},{9,8},{10,9... | collective-permute-start | bytes 491528 | tf_op jit(solution)/shard_map/ppermute | solution.py:125
  16.1 1.2 %convolution_convert_fusion.5.k_ref = bf16[256,640]{1,0:T(8,128)(2,1)} fusion(bf16[256,640]{1,0:T(8,128)(2,1)S(1)} %bitcast.72, bf16[640,1280]{1,0:T(8,128)(2,1)S(1)} %copy-done.5), kind=kOutput, calls=%fused_computation.17 | convolution fusion | flops 209879040 | bytes 1474560 | tf_op jit(solution)/shard_map/dot_general | solution.py:138
  17.2 1.2 %fusion.6.vt_ref = bf16[640,256]{1,0:T(8,128)(2,1)} fusion(bf16[256,640]{1,0:T(8,128)(2,1)S(1)} %bitcast.73, bf16[640,1280]{1,0:T(8,128)(2,1)S(1)} %copy-done.5), kind=kOutput, calls=%fused_computation.18 | convolution fusion | flops 209879040 | bytes 1474560 | tf_op jit(solution)/shard_map/dot_general | solution.py:139
  18.5 3.3 %shard_map.82 = (f32[640,256]{1,0:T(8,128)}, f32[640,256]{1,0:T(8,128)}, f32[640,256]{1,0:T(8,128)}) custom-call(bf16[256,640]{1,0:T(8,128)(2,1)} %convolution_convert_fusion.5.k_ref, bf16[640,256]{1,0:T(8,128)(2,1)} %fusion.2.qt_ref, bf16[640,256]{1,0:T(8,128)(2,1)} %fusion.6.vt_ref), custom_call_target="tpu_custom_call" | custom-call | tf_op jit(solution)/shard_map/pallas_call | solution.py:54
  21.7 5.9 %collective-permute-done.4 = bf16[2,64,640]{2,1,0:T(8,128)(2,1)S(1)} collective-permute-done((bf16[2,64,640]{2,1,0:T(8,128)(2,1)S(1)}, bf16[2,64,640]{2,1,0:T(8,128)(2,1)S(1)}, u32[]{:S(2)}, u32[]{:S(2)}) %collective-permute-start.4) | collective-permute-done | bytes 163872 | tf_op jit(solution)/shard_map/ppermute | solution.py:125
  27.6 2.1 %collective-permute-done.5 = bf16[2,64,640]{2,1,0:T(8,128)(2,1)S(1)} collective-permute-done((bf16[2,64,640]{2,1,0:T(8,128)(2,1)S(1)}, bf16[2,64,640]{2,1,0:T(8,128)(2,1)S(1)}, u32[]{:S(2)}, u32[]{:S(2)}) %collective-permute-start.5) | collective-permute-done | bytes 163872 | tf_op jit(solution)/shard_map/ppermute | solution.py:125
  30.4 0.7 %fusion.4 = bf16[640,384]{1,0:T(8,128)(2,1)S(1)} fusion(bf16[384,640]{1,0:T(8,128)(2,1)S(1)} %bitcast.70, bf16[640,1280]{1,0:T(8,128)(2,1)S(1)} %copy-done.6), kind=kOutput, calls=%fused_computation.14 | convolution fusion | flops 314818560 | bytes 1802240 | tf_op jit(solution)/shard_map/dot_general | solution.py:139
  31.9 0.7 %fusion.5 = bf16[640,384]{1,0:T(8,128)(2,1)S(1)} fusion(bf16[384,640]{1,0:T(8,128)(2,1)S(1)} %collective-permute-done.7, bf16[640,1280]{1,0:T(8,128)(2,1)S(1)} %copy-done.6), kind=kOutput, calls=%fused_computation.15 | convolution fusion | flops 314818560 | bytes 1802240 | tf_op jit(solution)/shard_map/dot_general | solution.py:139
  32.6 1.1 %pad_maximum_fusion.1.vt_ref = bf16[640,768]{1,0:T(8,128)(2,1)} fusion(bf16[640,384]{1,0:T(8,128)(2,1)S(1)} %fusion.5, bf16[640,384]{1,0:T(8,128)(2,1)S(1)} %fusion.4), kind=kLoop, calls=%fused_computation.20 | loop fusion | flops 1966080 | bytes 1966080 | tf_op jit(solution)/shard_map/concatenate | solution.py:151
  33.6 0.6 convolution_convert_fusion.2
  34.2 1.0 %pad_maximum_fusion.k_ref = bf16[768,640]{1,0:T(8,128)(2,1)} fusion(bf16[384,640]{1,0:T(8,128)(2,1)S(1)} %convolution_convert_fusion.2, bf16[384,640]{1,0:T(8,128)(2,1)S(1)} %convolution_convert_fusion.3), kind=kLoop, calls=%fused_computation.19 | loop fusion | flops 1966080 | bytes 1966080 | tf_op jit(solution)/shard_map/concatenate | solution.py:150
  35.3 5.7 %shard_map.83 = bf16[640,256]{1,0:T(8,128)(2,1)} custom-call(bf16[768,640]{1,0:T(8,128)(2,1)} %pad_maximum_fusion.k_ref, bf16[640,256]{1,0:T(8,128)(2,1)} %fusion.2.qt_ref, bf16[640,768]{1,0:T(8,128)(2,1)} %pad_maximum_fusion.1.vt_ref, f32[640,256]{1,0:T(8,128)} %get-tuple-element.22.m_ref, f32[640,256]{1,0:T(8,128)} %get-tuple-element.23.l_ref, ...), custom_call_target="tpu_custom_call" | custom-call | tf_op jit(solution)/shard_map/pallas_call | solution.py:66
  40.9 1.6 %multiply_reduce_fusion = (f32[256]{0:T(256)S(1)}, f32[256,640]{1,0:T(8,128)S(1)}) fusion(bf16[640,256]{1,0:T(8,128)(2,1)} %shard_map.83, bf16[640,640]{1,0:T(8,128)(2,1)S(1)} %copy-done, bf16[256,640]{1,0:T(8,128)(2,1)S(1)} %bitcast.59), kind=kOutput, calls=%fused_computation.41 | convolution fusion | flops 210370304 | bytes 2130944 | tf_op jit(solution)/shard_map/dot_general | solution.py:153
  42.7 3.3 %collective-permute-start.8 = (bf16[2,128,640]{2,1,0:T(8,128)(2,1)S(1)}, bf16[2,128,640]{2,1,0:T(8,128)(2,1)S(1)}, u32[]{:S(2)}, u32[]{:S(2)}) collective-permute-start(bf16[2,128,640]{2,1,0:T(8,128)(2,1)S(1)} %bitcast.65), channel_id=1, source_target_pairs={{0,4},{4,8},{8,12},{1,5},{5,9},{9,13},{2,6},{6,10},{10,14},{3,7},{... | collective-permute-start | bytes 983048 | tf_op jit(solution)/shard_map/ppermute | solution.py:81
  46.0 2.1 %collective-permute-start.9 = (bf16[2,128,640]{2,1,0:T(8,128)(2,1)S(1)}, bf16[2,128,640]{2,1,0:T(8,128)(2,1)S(1)}, u32[]{:S(2)}, u32[]{:S(2)}) collective-permute-start(bf16[2,128,640]{2,1,0:T(8,128)(2,1)S(1)} %bitcast.66), channel_id=1, source_target_pairs={{4,0},{8,4},{12,8},{5,1},{9,5},{13,9},{6,2},{10,6},{14,10},{7,3},{... | collective-permute-start | bytes 983048 | tf_op jit(solution)/shard_map/ppermute | solution.py:82
  48.1 1.9 %collective-permute-done.8 = bf16[2,128,640]{2,1,0:T(8,128)(2,1)S(1)} collective-permute-done((bf16[2,128,640]{2,1,0:T(8,128)(2,1)S(1)}, bf16[2,128,640]{2,1,0:T(8,128)(2,1)S(1)}, u32[]{:S(2)}, u32[]{:S(2)}) %collective-permute-start.8) | collective-permute-done | bytes 327712 | tf_op jit(solution)/shard_map/ppermute | solution.py:81
  50.0 4.4 %collective-permute-done.9 = bf16[2,128,640]{2,1,0:T(8,128)(2,1)S(1)} collective-permute-done((bf16[2,128,640]{2,1,0:T(8,128)(2,1)S(1)}, bf16[2,128,640]{2,1,0:T(8,128)(2,1)S(1)}, u32[]{:S(2)}, u32[]{:S(2)}) %collective-permute-start.9) | collective-permute-done | bytes 327712 | tf_op jit(solution)/shard_map/ppermute | solution.py:82
  54.7 0.7 %fusion.11 = f32[512,640]{1,0:T(8,128)S(1)} fusion(bf16[512,640]{1,0:T(8,128)(2,1)S(1)} %bitcast.61, bf16[3,640,640]{2,1,0:T(8,128)(2,1)S(1)} %copy-done.3), kind=kOutput, calls=%fused_computation.25 | convolution fusion | flops 419430400 | bytes 2785280 | tf_op jit(solution)/shard_map/dot_general | solution.py:90
  55.4 0.7 %fusion.13 = f32[512,640]{1,0:T(8,128)S(1)} fusion(bf16[512,640]{1,0:T(8,128)(2,1)S(1)} %bitcast.60, bf16[3,640,640]{2,1,0:T(8,128)(2,1)S(1)} %copy-done.3), kind=kOutput, calls=%fused_computation.27 | convolution fusion | flops 419430400 | bytes 2785280 | tf_op jit(solution)/shard_map/dot_general | solution.py:90
  56.2 0.8 %multiply_convert_fusion = bf16[512,640]{1,0:T(8,128)(2,1)S(1)} fusion(f32[512,640]{1,0:T(8,128)S(1)} %fusion.11, f32[512,640]{1,0:T(8,128)S(1)} %fusion.13, bf16[512,640]{1,0:T(8,128)(2,1)S(1)} %bitcast.68, bf16[3,640,640]{2,1,0:T(8,128)(2,1)S(1)} %copy-done.3), kind=kOutput, calls=%fused_computation.2 | convolution fusion | flops 421724160 | bytes 4751360 | tf_op jit(solution)/shard_map/dot_general | solution.py:90
  57.2 1.5 %copy-done.2 = bf16[3,640,640]{2,1,0:T(8,128)(2,1)S(1)} copy-done((bf16[3,640,640]{2,1,0:T(8,128)(2,1)S(1)}, bf16[3,640,640]{2,1,0:T(8,128)(2,1)}, u32[]{:S(2)}) %copy-start.2) | copy-done | bytes 2457624
  59.6 1.2 %fusion.3 = bf16[256,640]{1,0:T(8,128)(2,1)} fusion(f32[256,640]{1,0:T(8,128)S(1)} %get-tuple-element.40, f32[256,640]{1,0:T(8,128)S(1)} %convolution_add_fusion.2, bf16[256,640]{1,0:T(8,128)(2,1)S(1)} %bitcast.64, bf16[3,640,640]{2,1,0:T(8,128)(2,1)S(1)} %copy-done.2), kind=kOutput, calls=%fused_computation.13 | convolution fusion | flops 210206720 | bytes 2785280 | tf_op jit(solution)/shard_map/dot_general | solution.py:90
  (32 shorter events, 3.0 us)
Async XLA Ops:
  0.0 40.9 %copy-start = (bf16[640,640]{1,0:T(8,128)(2,1)S(1)}, bf16[640,640]{1,0:T(8,128)(2,1)}, u32[]{:S(2)}) copy-start(bf16[640,640]{1,0:T(8,128)(2,1)} %param.12) | copy-start | bytes 2457604
  0.0 10.7 %copy-start.1 = (bf16[2,128,640]{2,1,0:T(8,128)(2,1)S(1)}, bf16[2,128,640]{2,1,0:T(8,128)(2,1)}, u32[]{:S(2)}) copy-start(bf16[2,128,640]{2,1,0:T(8,128)(2,1)} %param.8) | copy-start | bytes 983044
  1.2 8.5 %collective-permute-start = (bf16[2,64,640]{2,1,0:T(8,128)(2,1)S(1)}, bf16[2,64,640]{2,1,0:T(8,128)(2,1)S(1)}, u32[]{:S(2)}, u32[]{:S(2)}) collective-permute-start(bf16[2,64,640]{2,1,0:T(8,128)(2,1)S(1)} %get-tuple-element.34), channel_id=1, source_target_pairs={{0,12},{4,0},{8,4},{12,8},{1,13},{5,1},{9,5},{13,9},{2,14},{6,2},{... | collective-permute-start | bytes 491528 | tf_op jit(solution)/shard_map/ppermute | solution.py:115
  1.9 7.8 %collective-permute-start.1 = (bf16[2,64,640]{2,1,0:T(8,128)(2,1)S(1)}, bf16[2,64,640]{2,1,0:T(8,128)(2,1)S(1)}, u32[]{:S(2)}, u32[]{:S(2)}) collective-permute-start(bf16[2,64,640]{2,1,0:T(8,128)(2,1)S(1)} %get-tuple-element.36), channel_id=1, source_target_pairs={{0,8},{4,12},{8,0},{12,4},{1,9},{5,13},{9,1},{13,5},{2,10},{6,14},... | collective-permute-start | bytes 491528 | tf_op jit(solution)/shard_map/ppermute | solution.py:115
  3.2 7.5 %collective-permute-start.2 = (bf16[2,64,640]{2,1,0:T(8,128)(2,1)S(1)}, bf16[2,64,640]{2,1,0:T(8,128)(2,1)S(1)}, u32[]{:S(2)}, u32[]{:S(2)}) collective-permute-start(bf16[2,64,640]{2,1,0:T(8,128)(2,1)S(1)} %get-tuple-element.35), channel_id=1, source_target_pairs={{0,4},{4,8},{8,12},{12,0},{1,5},{5,9},{9,13},{13,1},{2,6},{6,10},{... | collective-permute-start | bytes 491528 | tf_op jit(solution)/shard_map/ppermute | solution.py:115
  7.2 8.8 %copy-start.5 = (bf16[640,1280]{1,0:T(8,128)(2,1)S(1)}, bf16[640,1280]{1,0:T(8,128)(2,1)}, u32[]{:S(2)}) copy-start(bf16[640,1280]{1,0:T(8,128)(2,1)} %param.11) | copy-start | bytes 4915204
  10.8 5.2 %collective-permute-start.6 = (bf16[2,64,640]{2,1,0:T(8,128)(2,1)S(1)}, bf16[2,64,640]{2,1,0:T(8,128)(2,1)S(1)}, u32[]{:S(2)}, u32[]{:S(2)}) collective-permute-start(bf16[2,64,640]{2,1,0:T(8,128)(2,1)S(1)} %pad_maximum_fusion.10), channel_id=1, source_target_pairs={{0,4},{4,0},{8,12},{12,8},{1,5},{5,1},{9,13},{13,9},{2,6},{6,2},{1... | collective-permute-start | bytes 491528 | tf_op jit(solution)/shard_map/ppermute | solution.py:122
  12.2 9.5 %collective-permute-start.3 = (bf16[2,64,640]{2,1,0:T(8,128)(2,1)S(1)}, bf16[2,64,640]{2,1,0:T(8,128)(2,1)S(1)}, u32[]{:S(2)}, u32[]{:S(2)}) collective-permute-start(bf16[2,64,640]{2,1,0:T(8,128)(2,1)S(1)} %pad_maximum_fusion.10), channel_id=1, source_target_pairs={{0,1},{1,2},{2,3},{3,0},{4,5},{5,6},{6,7},{7,4},{8,9},{9,10},{10,1... | collective-permute-start | bytes 491528 | tf_op jit(solution)/shard_map/ppermute | solution.py:125
  13.5 14.1 %collective-permute-start.4 = (bf16[2,64,640]{2,1,0:T(8,128)(2,1)S(1)}, bf16[2,64,640]{2,1,0:T(8,128)(2,1)S(1)}, u32[]{:S(2)}, u32[]{:S(2)}) collective-permute-start(bf16[2,64,640]{2,1,0:T(8,128)(2,1)S(1)} %pad_maximum_fusion.10), channel_id=1, source_target_pairs={{0,2},{1,3},{2,0},{3,1},{4,6},{5,7},{6,4},{7,5},{8,10},{9,11},{10,... | collective-permute-start | bytes 491528 | tf_op jit(solution)/shard_map/ppermute | solution.py:125
  14.5 15.2 %collective-permute-start.5 = (bf16[2,64,640]{2,1,0:T(8,128)(2,1)S(1)}, bf16[2,64,640]{2,1,0:T(8,128)(2,1)S(1)}, u32[]{:S(2)}, u32[]{:S(2)}) collective-permute-start(bf16[2,64,640]{2,1,0:T(8,128)(2,1)S(1)} %pad_maximum_fusion.10), channel_id=1, source_target_pairs={{0,3},{1,0},{2,1},{3,2},{4,7},{5,4},{6,5},{7,6},{8,11},{9,8},{10,9... | collective-permute-start | bytes 491528 | tf_op jit(solution)/shard_map/ppermute | solution.py:125
  17.2 13.1 %copy-start.6 = (bf16[640,1280]{1,0:T(8,128)(2,1)S(1)}, bf16[640,1280]{1,0:T(8,128)(2,1)}, u32[]{:S(2)}) copy-start(bf16[640,1280]{1,0:T(8,128)(2,1)} %param.11) | copy-start | bytes 4915204
  29.8 2.0 %collective-permute-start.7 = (bf16[384,640]{1,0:T(8,128)(2,1)S(1)}, bf16[384,640]{1,0:T(8,128)(2,1)S(1)}, u32[]{:S(2)}, u32[]{:S(2)}) collective-permute-start(bf16[384,640]{1,0:T(8,128)(2,1)S(1)} %bitcast.69), channel_id=1, source_target_pairs={{0,4},{4,0},{8,12},{12,8},{1,5},{5,1},{9,13},{13,9},{2,6},{6,2},{1... | collective-permute-start | bytes 1474568 | tf_op jit(solution)/shard_map/ppermute | solution.py:147
  40.9 1.6 %copy-start.4 = (f32[640]{0:T(1024)S(1)}, f32[640]{0:T(1024)}, u32[]{:S(2)}) copy-start(f32[640]{0:T(1024)} %param.13) | copy-start | bytes 7684
  42.7 7.3 %collective-permute-start.8 = (bf16[2,128,640]{2,1,0:T(8,128)(2,1)S(1)}, bf16[2,128,640]{2,1,0:T(8,128)(2,1)S(1)}, u32[]{:S(2)}, u32[]{:S(2)}) collective-permute-start(bf16[2,128,640]{2,1,0:T(8,128)(2,1)S(1)} %bitcast.65), channel_id=1, source_target_pairs={{0,4},{4,8},{8,12},{1,5},{5,9},{9,13},{2,6},{6,10},{10,14},{3,7},{... | collective-permute-start | bytes 983048 | tf_op jit(solution)/shard_map/ppermute | solution.py:81
  46.0 8.4 %collective-permute-start.9 = (bf16[2,128,640]{2,1,0:T(8,128)(2,1)S(1)}, bf16[2,128,640]{2,1,0:T(8,128)(2,1)S(1)}, u32[]{:S(2)}, u32[]{:S(2)}) collective-permute-start(bf16[2,128,640]{2,1,0:T(8,128)(2,1)S(1)} %bitcast.66), channel_id=1, source_target_pairs={{4,0},{8,4},{12,8},{5,1},{9,5},{13,9},{6,2},{10,6},{14,10},{7,3},{... | collective-permute-start | bytes 983048 | tf_op jit(solution)/shard_map/ppermute | solution.py:82
  48.1 6.5 %copy-start.3 = (bf16[3,640,640]{2,1,0:T(8,128)(2,1)S(1)}, bf16[3,640,640]{2,1,0:T(8,128)(2,1)}, u32[]{:S(2)}) copy-start(bf16[3,640,640]{2,1,0:T(8,128)(2,1)} %param.14) | copy-start | bytes 7372804
  57.0 1.7 %copy-start.2 = (bf16[3,640,640]{2,1,0:T(8,128)(2,1)S(1)}, bf16[3,640,640]{2,1,0:T(8,128)(2,1)}, u32[]{:S(2)}) copy-start(bf16[3,640,640]{2,1,0:T(8,128)(2,1)} %param.15) | copy-start | bytes 7372804

commit v18 on v14

--- a/solution.py
+++ b/solution.py
@@ -36,6 +36,35 @@
         out_specs=pl.BlockSpec((width, total), lambda j: (j, 0)),
         out_shape=jax.ShapeDtypeStruct((channels, total), jnp.bfloat16),
     )(keys, queries_t, values_t)
+
+
+def attention_block_kernel(k_ref, qt_ref, vt_ref, x_ref, w_ref, g_ref, r_ref, n_ref):
+    heads = [slice(h * HEAD_DIM, (h + 1) * HEAD_DIM) for h in range(qt_ref.shape[0] // HEAD_DIM)]
+    scores = [jnp.dot(k_ref[:, c], qt_ref[c, :], preferred_element_type=jnp.float32) for c in heads]
+    highest = [jnp.max(s, axis=0, keepdims=True) for s in scores]
+    exponent = [jnp.exp(s - m) for s, m in zip(scores, highest)]
+    denominator = [jnp.sum(e, axis=0, keepdims=True) for e in exponent]
+    mixed = [
+        jnp.dot(vt_ref[c, :], e.astype(jnp.bfloat16), preferred_element_type=jnp.float32)
+        for e, c in zip(exponent, heads)
+    ]
+    attended_t = jnp.concatenate([m / d for m, d in zip(mixed, denominator)], axis=0).astype(jnp.bfloat16)
+    projected = lax.dot_general(attended_t, w_ref[...], (((0,), (0,)), ((), ())), preferred_element_type=jnp.float32)
+    residual = x_ref[...].astype(jnp.float32) + projected
+    mean_square = jnp.mean(residual * residual, axis=1, keepdims=True)
+    r_ref[...] = residual
+    n_ref[...] = (residual * lax.rsqrt(mean_square + 1e-06) * g_ref[...]).astype(n_ref.dtype)
+
+
+def attention_block(keys, queries_t, values_t, tokens, w_out, norm_gain):
+    total, channels = tokens.shape
+    return pl.pallas_call(
+        attention_block_kernel,
+        out_shape=[
+            jax.ShapeDtypeStruct((total, channels), jnp.float32),
+            jax.ShapeDtypeStruct((total, channels), jnp.bfloat16),
+        ],
+    )(keys, queries_t, values_t, tokens, w_out, norm_gain.reshape(1, channels))
 
 
 def extended(array, axis, width):
@@ -92,6 +121,11 @@
     return mine, sibling
 
 
+def query_total_fits(queries_t, keys):
+    channels, total = queries_t.shape
+    return total * keys.shape[0] * channels <= 256 * 1024 * 640
+
+
 def shards(frames, key_index, w_query, w_keyval, w_out, norm_gain, w_first, w_second):
     frame_count, row_count, channels = frames.shape
     assert frame_count >= 2
@@ -111,12 +145,15 @@
     keys_sib, values_sib = project(sibling)
     keys = jnp.concatenate([keys_mine, keys_sib], axis=0)
     values_t = jnp.concatenate([values_mine, values_sib], axis=1)
-    attended_t = attend(keys, queries_t, values_t)
-    residual = flattened.astype(jnp.float32) + lax.dot_general(
-        attended_t, w_out, (((0,), (0,)), ((), ())), preferred_element_type=jnp.float32
-    )
-    mean_square = jnp.mean(residual * residual, axis=-1, keepdims=True)
-    normed = (residual * lax.rsqrt(mean_square + 1e-06) * norm_gain).astype(jnp.bfloat16)
+    if query_total_fits(queries_t, keys):
+        residual, normed = attention_block(keys, queries_t, values_t, flattened, w_out, norm_gain)
+    else:
+        attended_t = attend(keys, queries_t, values_t)
+        residual = flattened.astype(jnp.float32) + lax.dot_general(
+            attended_t, w_out, (((0,), (0,)), ((), ())), preferred_element_type=jnp.float32
+        )
+        mean_square = jnp.mean(residual * residual, axis=-1, keepdims=True)
+        normed = (residual * lax.rsqrt(mean_square + 1e-06) * norm_gain).astype(jnp.bfloat16)
     normed = normed.reshape(frame_count, row_count, channels)
     padded = extended(normed, "frame", 2)
     hidden = jax.nn.silu(temporal_mix(padded, w_first, frame_count + 2)).astype(jnp.bfloat16)

time: 59.8 us -> 63.2 us (1.057)
  the two profiles are of different devices: /device:TPU:9 before, /device:TPU:1 now
where the time goes in v18:
time: 63.2 us; the launch traced here: 62.9 us
  waiting for transfers between devices  21.6 us (34%)
  starting transfers between devices  13.5 us (21%)
  matrix products  9.52 us (15%)
  Pallas kernels  6.87 us (11%)
  local copies, waits for them, and re-layouts  5.3 us (8%)
  other arithmetic  4.5 us (7%)
  between operations  1.59 us (3%)
    ppermute x3, waiting for transfers between devices, gather_keyframes(): lax.ppermute(piece, 'row', [(i, (i + s) % rsize) for i in range(rsize)])  13.8 us
    pallas_call x1, Pallas kernels, attention_block(): pl.pallas_call(attention_block_kernel, out_shape=[jax.ShapeDtypeStruct((t...  6.87 us
    ppermute x3, starting transfers between devices, gather_keyframes(): lax.ppermute(piece, 'row', [(i, (i + s) % rsize) for i in range(rsize)])  4.64 us
    dot_general x6, matrix products, temporal_mix(): jnp.dot(window, weights[offset], preferred_element_type=jnp.float32)  4.41 us
    ppermute x1, waiting for transfers between devices, extended(): after = lax.ppermute(first, axis, down)  4.4 us
    ppermute x3, starting transfers between devices, gather_keyframes(): lax.ppermute(halves((me + s) % 2), 'frame', [(i, (i + s) % fsize) for i i...  3.13 us
    ppermute x1, starting transfers between devices, extended(): after = lax.ppermute(first, axis, down)  3.01 us
    dot_general x1, matrix products, shards(): lax.dot_general(w_query, flattened, (((0,), (1,)), ((), ())), preferred_e...  2.17 us
  transfers between devices with their start and end apart: 9, of which 6 were waited for; matrix products, arithmetic and copies ran while one was open for 9% of the time, Pallas kernels for 0%

profile of v18, /device:TPU:1, one launch (start us, length us, event | category | flops | bytes accessed | tf_op | source)
XLA Modules:
  0.0 62.9 jit_solution(1465955199682970176)
XLA Ops:
  0.0 1.2 %constant_dynamic-slice_fusion.2 = (bf16[2,64,640]{2,1,0:T(8,128)(2,1)S(1)}, bf16[2,64,640]{2,1,0:T(8,128)(2,1)S(1)}, bf16[2,64,640]{2,1,0:T(8,128)(2,1)S(1)}) fusion(bf16[2,128,640]{2,1,0:T(8,128)(2,1)} %param.8, s32[]{:T(128)S(6)} %select_n.137, s32[]{:T(128)S(6)} %select_n.147, s32[]{:T(128)S(6)} %select_n.143), kind=kLoop, calls=%fused_computation.54 | loop fusion | bytes 983052 | tf_op jit(solution)/shard_map/dynamic_slice | solution.py:102
  1.2 2.7 %collective-permute-start.2 = (bf16[2,64,640]{2,1,0:T(8,128)(2,1)S(1)}, bf16[2,64,640]{2,1,0:T(8,128)(2,1)S(1)}, u32[]{:S(2)}, u32[]{:S(2)}) collective-permute-start(bf16[2,64,640]{2,1,0:T(8,128)(2,1)S(1)} %get-tuple-element.21), channel_id=1, source_target_pairs={{0,4},{4,8},{8,12},{12,0},{1,5},{5,9},{9,13},{13,1},{2,6},{6,10},{... | collective-permute-start | bytes 491528 | tf_op jit(solution)/shard_map/ppermute | solution.py:110
  3.9 0.5 collective-permute-start
  4.3 1.3 %fusion.34 = (s32[1]{0:T(128)}, s32[1]{0:T(128)}) fusion(s32[2]{0:T(128)} %param.9), kind=kLoop, calls=%fused_computation.56 | loop fusion | bytes 16 | tf_op jit(solution)/shard_map/slice | solution.py:95
  7.1 2.2 %fusion.3.qt_ref = bf16[640,256]{1,0:T(8,128)(2,1)} fusion(bf16[640,640]{1,0:T(8,128)(2,1)S(1)} %copy-done, bf16[256,640]{1,0:T(8,128)(2,1)} %bitcast.56), kind=kOutput, calls=%fused_computation.14 | convolution fusion | flops 210042880 | bytes 1474560 | tf_op jit(solution)/shard_map/dot_general | solution.py:133
  9.3 1.5 %collective-permute-done.1 = bf16[2,64,640]{2,1,0:T(8,128)(2,1)S(1)} collective-permute-done((bf16[2,64,640]{2,1,0:T(8,128)(2,1)S(1)}, bf16[2,64,640]{2,1,0:T(8,128)(2,1)S(1)}, u32[]{:S(2)}, u32[]{:S(2)}) %collective-permute-start.1) | collective-permute-done | bytes 163872 | tf_op jit(solution)/shard_map/ppermute | solution.py:110
  10.8 0.5 collective-permute-done
  11.4 4.2 %collective-permute-start.5 = (bf16[2,64,640]{2,1,0:T(8,128)(2,1)S(1)}, bf16[2,64,640]{2,1,0:T(8,128)(2,1)S(1)}, u32[]{:S(2)}, u32[]{:S(2)}) collective-permute-start(bf16[2,64,640]{2,1,0:T(8,128)(2,1)S(1)} %pad_maximum_fusion.9), channel_id=1, source_target_pairs={{0,3},{1,0},{2,1},{3,2},{4,7},{5,4},{6,5},{7,6},{8,11},{9,8},{10,9... | collective-permute-start | bytes 491528 | tf_op jit(solution)/shard_map/ppermute | solution.py:118
  16.1 3.5 %collective-permute-done.5 = bf16[2,64,640]{2,1,0:T(8,128)(2,1)S(1)} collective-permute-done((bf16[2,64,640]{2,1,0:T(8,128)(2,1)S(1)}, bf16[2,64,640]{2,1,0:T(8,128)(2,1)S(1)}, u32[]{:S(2)}, u32[]{:S(2)}) %collective-permute-start.5) | collective-permute-done | bytes 163872 | tf_op jit(solution)/shard_map/ppermute | solution.py:118
  19.6 10.3 %collective-permute-done.4 = bf16[2,64,640]{2,1,0:T(8,128)(2,1)S(1)} collective-permute-done((bf16[2,64,640]{2,1,0:T(8,128)(2,1)S(1)}, bf16[2,64,640]{2,1,0:T(8,128)(2,1)S(1)}, u32[]{:S(2)}, u32[]{:S(2)}) %collective-permute-start.4) | collective-permute-done | bytes 163872 | tf_op jit(solution)/shard_map/ppermute | solution.py:118
  30.0 0.6 collective-permute-start.6
  30.6 0.6 reshape.43.g_ref
  31.2 0.7 %convolution_convert_fusion.3 = bf16[512,640]{1,0:T(8,128)(2,1)S(1)} fusion(bf16[512,640]{1,0:T(8,128)(2,1)S(1)} %bitcast.65, bf16[640,1280]{1,0:T(8,128)(2,1)S(1)} %copy-done.6), kind=kOutput, calls=%fused_computation.5 | convolution fusion | flops 419758080 | bytes 2129920 | tf_op jit(solution)/shard_map/dot_general | solution.py:138
  32.0 0.7 %fusion.1 = bf16[640,512]{1,0:T(8,128)(2,1)S(1)} fusion(bf16[512,640]{1,0:T(8,128)(2,1)S(1)} %bitcast.66, bf16[640,1280]{1,0:T(8,128)(2,1)S(1)} %copy-done.6), kind=kOutput, calls=%fused_computation.9 | convolution fusion | flops 419758080 | bytes 2129920 | tf_op jit(solution)/shard_map/dot_general | solution.py:139
  32.7 0.8 %convolution_convert_fusion.2 = bf16[512,640]{1,0:T(8,128)(2,1)S(1)} fusion(bf16[512,640]{1,0:T(8,128)(2,1)S(1)} %collective-permute-done.6, bf16[640,1280]{1,0:T(8,128)(2,1)S(1)} %copy-done.6), kind=kOutput, calls=%fused_computation.4 | convolution fusion | flops 419758080 | bytes 2129920 | tf_op jit(solution)/shard_map/dot_general | solution.py:138
  33.5 1.2 %pad_maximum_fusion.k_ref = bf16[1024,640]{1,0:T(8,128)(2,1)} fusion(bf16[512,640]{1,0:T(8,128)(2,1)S(1)} %convolution_convert_fusion.2, bf16[512,640]{1,0:T(8,128)(2,1)S(1)} %convolution_convert_fusion.3), kind=kLoop, calls=%fused_computation.6 | loop fusion | flops 2621440 | bytes 2621440 | tf_op jit(solution)/shard_map/concatenate | solution.py:146
  34.7 0.7 %fusion.2 = bf16[640,512]{1,0:T(8,128)(2,1)S(1)} fusion(bf16[512,640]{1,0:T(8,128)(2,1)S(1)} %collective-permute-done.6, bf16[640,1280]{1,0:T(8,128)(2,1)S(1)} %copy-done.6), kind=kOutput, calls=%fused_computation.10 | convolution fusion | flops 419758080 | bytes 2129920 | tf_op jit(solution)/shard_map/dot_general | solution.py:139
  35.4 1.2 %pad_maximum_fusion.1.vt_ref = bf16[640,1024]{1,0:T(8,128)(2,1)} fusion(bf16[640,512]{1,0:T(8,128)(2,1)S(1)} %fusion.2, bf16[640,512]{1,0:T(8,128)(2,1)S(1)} %fusion.1), kind=kLoop, calls=%fused_computation.7 | loop fusion | flops 2621440 | bytes 2621440 | tf_op jit(solution)/shard_map/concatenate | solution.py:147
  36.6 6.9 %shard_map.82 = (f32[256,640]{1,0:T(8,128)}, bf16[256,640]{1,0:T(8,128)(2,1)}) custom-call(bf16[1024,640]{1,0:T(8,128)(2,1)} %pad_maximum_fusion.k_ref, bf16[640,256]{1,0:T(8,128)(2,1)} %fusion.3.qt_ref, bf16[640,1024]{1,0:T(8,128)(2,1)} %pad_maximum_fusion.1.vt_ref, bf16[256,640]{1,0:T(8,128)(2,1)} %bitcast.57, bf16[640,640]{1,0:T(8,128)(2,1)} %w_ref.1, ...), custom_call_target="tpu_custom_call" | custom-call | tf_op jit(solution)/shard_map/pallas_call | solution.py:61
  43.5 2.1 %collective-permute-start.7 = (bf16[2,128,640]{2,1,0:T(8,128)(2,1)}, bf16[2,128,640]{2,1,0:T(8,128)(2,1)}, u32[]{:S(2)}, u32[]{:S(2)}) collective-permute-start(bf16[2,128,640]{2,1,0:T(8,128)(2,1)} %bitcast.68), channel_id=1, source_target_pairs={{0,4},{4,8},{8,12},{1,5},{5,9},{9,13},{2,6},{6,10},{10,14},{3,7},{... | collective-permute-start | bytes 983048 | tf_op jit(solution)/shard_map/ppermute | solution.py:76
  45.6 3.0 %collective-permute-start.8 = (bf16[2,128,640]{2,1,0:T(8,128)(2,1)}, bf16[2,128,640]{2,1,0:T(8,128)(2,1)}, u32[]{:S(2)}, u32[]{:S(2)}) collective-permute-start(bf16[2,128,640]{2,1,0:T(8,128)(2,1)} %bitcast.69), channel_id=1, source_target_pairs={{4,0},{8,4},{12,8},{5,1},{9,5},{13,9},{6,2},{10,6},{14,10},{7,3},{... | collective-permute-start | bytes 983048 | tf_op jit(solution)/shard_map/ppermute | solution.py:77
  48.7 1.3 %collective-permute-done.7 = bf16[2,128,640]{2,1,0:T(8,128)(2,1)} collective-permute-done((bf16[2,128,640]{2,1,0:T(8,128)(2,1)}, bf16[2,128,640]{2,1,0:T(8,128)(2,1)}, u32[]{:S(2)}, u32[]{:S(2)}) %collective-permute-start.7) | collective-permute-done | bytes 327712 | tf_op jit(solution)/shard_map/ppermute | solution.py:76
  49.9 4.4 %collective-permute-done.8 = bf16[2,128,640]{2,1,0:T(8,128)(2,1)} collective-permute-done((bf16[2,128,640]{2,1,0:T(8,128)(2,1)}, bf16[2,128,640]{2,1,0:T(8,128)(2,1)}, u32[]{:S(2)}, u32[]{:S(2)}) %collective-permute-start.8) | collective-permute-done | bytes 327712 | tf_op jit(solution)/shard_map/ppermute | solution.py:77
  54.3 1.7 %pad_maximum_fusion.5 = (bf16[4,128,640]{2,1,0:T(8,128)(2,1)S(1)}, bf16[4,128,640]{2,1,0:T(8,128)(2,1)S(1)}, bf16[4,128,640]{2,1,0:T(8,128)(2,1)S(1)}) fusion(bf16[2,128,640]{2,1,0:T(8,128)(2,1)} %bitcast.70, bf16[2,128,640]{2,1,0:T(8,128)(2,1)} %collective-permute-done.7, bf16[2,128,640]{2,1,0:T(8,128)(2,1)} %collective-permute-done.8), kind=kLoop, calls=%fused_computation.39 | loop fusion | flops 1310720 | bytes 2949120 | tf_op jit(solution)/shard_map/concatenate | solution.py:78
  56.1 0.8 %fusion.14 = f32[512,640]{1,0:T(8,128)S(1)} fusion(bf16[512,640]{1,0:T(8,128)(2,1)S(1)} %bitcast.59, bf16[3,640,640]{2,1,0:T(8,128)(2,1)S(1)} %copy-done.3), kind=kOutput, calls=%fused_computation.21 | convolution fusion | flops 419430400 | bytes 2785280 | tf_op jit(solution)/shard_map/dot_general | solution.py:85
  56.9 0.8 %fusion.16 = f32[512,640]{1,0:T(8,128)S(1)} fusion(bf16[512,640]{1,0:T(8,128)(2,1)S(1)} %bitcast.58, bf16[3,640,640]{2,1,0:T(8,128)(2,1)S(1)} %copy-done.3), kind=kOutput, calls=%fused_computation.23 | convolution fusion | flops 419430400 | bytes 2785280 | tf_op jit(solution)/shard_map/dot_general | solution.py:85
  57.6 0.8 %multiply_convert_fusion = bf16[512,640]{1,0:T(8,128)(2,1)S(1)} fusion(f32[512,640]{1,0:T(8,128)S(1)} %fusion.14, f32[512,640]{1,0:T(8,128)S(1)} %fusion.16, bf16[512,640]{1,0:T(8,128)(2,1)S(1)} %bitcast.67, bf16[3,640,640]{2,1,0:T(8,128)(2,1)S(1)} %copy-done.3), kind=kOutput, calls=%fused_computation.8 | convolution fusion | flops 421724160 | bytes 4751360 | tf_op jit(solution)/shard_map/dot_general | solution.py:85
  58.6 1.5 %copy-done.2 = bf16[3,640,640]{2,1,0:T(8,128)(2,1)S(1)} copy-done((bf16[3,640,640]{2,1,0:T(8,128)(2,1)S(1)}, bf16[3,640,640]{2,1,0:T(8,128)(2,1)}, u32[]{:S(2)}) %copy-start.2) | copy-done | bytes 2457624
  60.1 0.5 fusion.12
  60.6 0.5 convolution_add_fusion.2
  61.1 0.6 copy-done.4
  61.7 1.2 %fusion.8 = bf16[256,640]{1,0:T(8,128)(2,1)} fusion(f32[256,640]{1,0:T(8,128)S(1)} %copy-done.4, f32[256,640]{1,0:T(8,128)S(1)} %convolution_add_fusion.2, bf16[256,640]{1,0:T(8,128)(2,1)S(1)} %bitcast.62, bf16[3,640,640]{2,1,0:T(8,128)(2,1)S(1)} %copy-done.2), kind=kOutput, calls=%fused_computation.17 | convolution fusion | flops 210206720 | bytes 2785280 | tf_op jit(solution)/shard_map/dot_general | solution.py:85
  (24 shorter events, 0.9 us)
Async XLA Ops:
  0.0 7.1 %copy-start = (bf16[640,640]{1,0:T(8,128)(2,1)S(1)}, bf16[640,640]{1,0:T(8,128)(2,1)}, u32[]{:S(2)}) copy-start(bf16[640,640]{1,0:T(8,128)(2,1)} %param.10) | copy-start | bytes 2457604
  0.0 11.3 %copy-start.1 = (bf16[2,128,640]{2,1,0:T(8,128)(2,1)S(1)}, bf16[2,128,640]{2,1,0:T(8,128)(2,1)}, u32[]{:S(2)}) copy-start(bf16[2,128,640]{2,1,0:T(8,128)(2,1)} %param.8) | copy-start | bytes 983044
  1.2 8.0 %collective-permute-start.2 = (bf16[2,64,640]{2,1,0:T(8,128)(2,1)S(1)}, bf16[2,64,640]{2,1,0:T(8,128)(2,1)S(1)}, u32[]{:S(2)}, u32[]{:S(2)}) collective-permute-start(bf16[2,64,640]{2,1,0:T(8,128)(2,1)S(1)} %get-tuple-element.21), channel_id=1, source_target_pairs={{0,4},{4,8},{8,12},{12,0},{1,5},{5,9},{9,13},{13,1},{2,6},{6,10},{... | collective-permute-start | bytes 491528 | tf_op jit(solution)/shard_map/ppermute | solution.py:110
  3.9 6.9 %collective-permute-start.1 = (bf16[2,64,640]{2,1,0:T(8,128)(2,1)S(1)}, bf16[2,64,640]{2,1,0:T(8,128)(2,1)S(1)}, u32[]{:S(2)}, u32[]{:S(2)}) collective-permute-start(bf16[2,64,640]{2,1,0:T(8,128)(2,1)S(1)} %get-tuple-element.22), channel_id=1, source_target_pairs={{0,8},{4,12},{8,0},{12,4},{1,9},{5,13},{9,1},{13,5},{2,10},{6,14},... | collective-permute-start | bytes 491528 | tf_op jit(solution)/shard_map/ppermute | solution.py:110
  3.9 7.4 %collective-permute-start = (bf16[2,64,640]{2,1,0:T(8,128)(2,1)S(1)}, bf16[2,64,640]{2,1,0:T(8,128)(2,1)S(1)}, u32[]{:S(2)}, u32[]{:S(2)}) collective-permute-start(bf16[2,64,640]{2,1,0:T(8,128)(2,1)S(1)} %get-tuple-element.20), channel_id=1, source_target_pairs={{0,12},{4,0},{8,4},{12,8},{1,13},{5,1},{9,5},{13,9},{2,14},{6,2},{... | collective-permute-start | bytes 491528 | tf_op jit(solution)/shard_map/ppermute | solution.py:110
  7.1 23.6 %copy-start.5 = (f32[640]{0:T(1024)S(1)}, f32[640]{0:T(1024)}, u32[]{:S(2)}) copy-start(f32[640]{0:T(1024)} %param.13) | copy-start | bytes 7684
  9.2 22.0 %copy-start.6 = (bf16[640,1280]{1,0:T(8,128)(2,1)S(1)}, bf16[640,1280]{1,0:T(8,128)(2,1)}, u32[]{:S(2)}) copy-start(bf16[640,1280]{1,0:T(8,128)(2,1)} %param.11) | copy-start | bytes 4915204
  11.4 8.1 %collective-permute-start.5 = (bf16[2,64,640]{2,1,0:T(8,128)(2,1)S(1)}, bf16[2,64,640]{2,1,0:T(8,128)(2,1)S(1)}, u32[]{:S(2)}, u32[]{:S(2)}) collective-permute-start(bf16[2,64,640]{2,1,0:T(8,128)(2,1)S(1)} %pad_maximum_fusion.9), channel_id=1, source_target_pairs={{0,3},{1,0},{2,1},{3,2},{4,7},{5,4},{6,5},{7,6},{8,11},{9,8},{10,9... | collective-permute-start | bytes 491528 | tf_op jit(solution)/shard_map/ppermute | solution.py:118
  15.6 14.3 %collective-permute-start.4 = (bf16[2,64,640]{2,1,0:T(8,128)(2,1)S(1)}, bf16[2,64,640]{2,1,0:T(8,128)(2,1)S(1)}, u32[]{:S(2)}, u32[]{:S(2)}) collective-permute-start(bf16[2,64,640]{2,1,0:T(8,128)(2,1)S(1)} %pad_maximum_fusion.9), channel_id=1, source_target_pairs={{0,2},{1,3},{2,0},{3,1},{4,6},{5,7},{6,4},{7,5},{8,10},{9,11},{10,... | collective-permute-start | bytes 491528 | tf_op jit(solution)/shard_map/ppermute | solution.py:118
  15.6 14.3 %collective-permute-start.3 = (bf16[2,64,640]{2,1,0:T(8,128)(2,1)S(1)}, bf16[2,64,640]{2,1,0:T(8,128)(2,1)S(1)}, u32[]{:S(2)}, u32[]{:S(2)}) collective-permute-start(bf16[2,64,640]{2,1,0:T(8,128)(2,1)S(1)} %pad_maximum_fusion.9), channel_id=1, source_target_pairs={{0,1},{1,2},{2,3},{3,0},{4,5},{5,6},{6,7},{7,4},{8,9},{9,10},{10,1... | collective-permute-start | bytes 491528 | tf_op jit(solution)/shard_map/ppermute | solution.py:118
  30.0 2.7 %collective-permute-start.6 = (bf16[512,640]{1,0:T(8,128)(2,1)S(1)}, bf16[512,640]{1,0:T(8,128)(2,1)S(1)}, u32[]{:S(2)}, u32[]{:S(2)}) collective-permute-start(bf16[512,640]{1,0:T(8,128)(2,1)S(1)} %bitcast.64), channel_id=1, source_target_pairs={{0,4},{4,0},{8,12},{12,8},{1,5},{5,1},{9,13},{13,9},{2,6},{6,2},{1... | collective-permute-start | bytes 1966088 | tf_op jit(solution)/shard_map/ppermute | solution.py:120
  43.5 12.6 %copy-start.3 = (bf16[3,640,640]{2,1,0:T(8,128)(2,1)S(1)}, bf16[3,640,640]{2,1,0:T(8,128)(2,1)}, u32[]{:S(2)}) copy-start(bf16[3,640,640]{2,1,0:T(8,128)(2,1)} %param.14) | copy-start | bytes 7372804
  43.5 6.5 %collective-permute-start.7 = (bf16[2,128,640]{2,1,0:T(8,128)(2,1)}, bf16[2,128,640]{2,1,0:T(8,128)(2,1)}, u32[]{:S(2)}, u32[]{:S(2)}) collective-permute-start(bf16[2,128,640]{2,1,0:T(8,128)(2,1)} %bitcast.68), channel_id=1, source_target_pairs={{0,4},{4,8},{8,12},{1,5},{5,9},{9,13},{2,6},{6,10},{10,14},{3,7},{... | collective-permute-start | bytes 983048 | tf_op jit(solution)/shard_map/ppermute | solution.py:76
  45.6 8.7 %collective-permute-start.8 = (bf16[2,128,640]{2,1,0:T(8,128)(2,1)}, bf16[2,128,640]{2,1,0:T(8,128)(2,1)}, u32[]{:S(2)}, u32[]{:S(2)}) collective-permute-start(bf16[2,128,640]{2,1,0:T(8,128)(2,1)} %bitcast.69), channel_id=1, source_target_pairs={{4,0},{8,4},{12,8},{5,1},{9,5},{13,9},{6,2},{10,6},{14,10},{7,3},{... | collective-permute-start | bytes 983048 | tf_op jit(solution)/shard_map/ppermute | solution.py:77
  58.4 1.7 %copy-start.2 = (bf16[3,640,640]{2,1,0:T(8,128)(2,1)S(1)}, bf16[3,640,640]{2,1,0:T(8,128)(2,1)}, u32[]{:S(2)}) copy-start(bf16[3,640,640]{2,1,0:T(8,128)(2,1)} %param.15) | copy-start | bytes 7372804
  60.6 1.1 %copy-start.4 = (f32[256,640]{1,0:T(8,128)S(1)}, f32[256,640]{1,0:T(8,128)}, u32[]{:S(2)}) copy-start(f32[256,640]{1,0:T(8,128)} %get-tuple-element.9) | copy-start | bytes 1966084

commit v19 on v14

--- a/solution.py
+++ b/solution.py
@@ -84,12 +84,11 @@
         got_b = jnp.where(source == owner_b, recv[n_loc - 1], got_b)
     piece = jnp.stack([got_a, got_b])
     piece, early = lax.optimization_barrier((piece, early))
-    pieces = [piece]
+    pieces = []
     for s in range(1, rsize):
         pieces.append(lax.ppermute(piece, "row", [(i, (i + s) % rsize) for i in range(rsize)]))
-    mine = jnp.stack(pieces).reshape(-1, channels)
-    sibling = lax.ppermute(mine, "frame", [(i, i ^ 1) for i in range(fsize)])
-    return mine, sibling
+    own_row = jnp.concatenate([piece, lax.ppermute(piece, "frame", [(i, i ^ 1) for i in range(fsize)])], axis=0)
+    return own_row.reshape(-1, channels), pieces
 
 
 def shards(frames, key_index, w_query, w_keyval, w_out, norm_gain, w_first, w_second):
@@ -98,7 +97,7 @@
     flattened = frames.reshape(-1, channels)
     queries_t = lax.dot_general(w_query, flattened, (((0,), (1,)), ((), ())), preferred_element_type=jnp.float32)
     queries_t = (queries_t * HEAD_DIM ** (-0.5)).astype(jnp.bfloat16)
-    mine, sibling = gather_keyframes(frames, key_index, queries_t)
+    own_row, pieces = gather_keyframes(frames, key_index, queries_t)
 
     def project(tokens):
         keys = jnp.dot(tokens, w_keyval[:, :channels], preferred_element_type=jnp.float32).astype(jnp.bfloat16)
@@ -107,10 +106,14 @@
         ).astype(jnp.bfloat16)
         return keys, values_t
 
+    keys_own, values_own = project(own_row)
+    pieces, keys_own, values_own = lax.optimization_barrier((pieces, keys_own, values_own))
+    mine = jnp.stack(pieces).reshape(-1, channels)
+    sibling = lax.ppermute(mine, "frame", [(i, i ^ 1) for i in range(lax.axis_size("frame"))])
     keys_mine, values_mine = project(mine)
     keys_sib, values_sib = project(sibling)
-    keys = jnp.concatenate([keys_mine, keys_sib], axis=0)
-    values_t = jnp.concatenate([values_mine, values_sib], axis=1)
+    keys = jnp.concatenate([keys_own, keys_mine, keys_sib], axis=0)
+    values_t = jnp.concatenate([values_own, values_mine, values_sib], axis=1)
     attended_t = attend(keys, queries_t, values_t)
     residual = flattened.astype(jnp.float32) + lax.dot_general(
         attended_t, w_out, (((0,), (0,)), ((), ())), preferred_element_type=jnp.float32

time: 59.8 us -> 61.7 us (1.032)
  starting transfers between devices: 12 us -> 14.4 us
  waiting for transfers between devices: 21.2 us -> 20.1 us
    ppermute x1 -> x2, starting transfers between devices: 0.56 us -> 1.94 us  [the longest x1 1.4 us: gather_keyframes(): lax.ppermute(piece, 'frame', [(i, i ^ 1) for i in range(fsize)])]
    ppermute x3, waiting for transfers between devices: 13.7 us -> 12.7 us  [gather_keyframes(): lax.ppermute(piece, 'row', [(i, (i + s) % rsize) for i in range(rsize)])]
    ppermute x1, starting transfers between devices: 2.44 us -> 3.34 us  [extended(): before = lax.ppermute(last, axis, up)]
    dot_general x2 -> x3, matrix products: 1.44 us -> 1.89 us  [project(): lax.dot_general(w_keyval[:, channels:], tokens, (((0,), (1,)), ((), ())),...]
    dot_general x2 -> x3, matrix products: 1.5 us -> 1.68 us  [project(): jnp.dot(tokens, w_keyval[:, :channels], preferred_element_type=jnp.float32)]
    concatenate x2 -> x3, other arithmetic: 2.43 us -> 2.48 us  [the longest x1 1.25 us: shards(): values_t = jnp.concatenate([values_own, values_mine, values_sib], axis=1)]
  transfers between devices with their start and end apart: 9 -> 10, of which waited for: 7 -> 7; matrix products, arithmetic and copies ran while one was open for 9% -> 10% of each run, Pallas kernels for 0% -> 0%
where the time goes in v19:
time: 61.7 us; the launch traced here: 61.3 us
  waiting for transfers between devices  20.1 us (33%)
  starting transfers between devices  14.4 us (23%)
  matrix products  12.1 us (20%)
  Pallas kernels  5.84 us (9%)
  local copies, waits for them, and re-layouts  4.1 us (7%)
  other arithmetic  3.18 us (5%)
  between operations  1.54 us (2%)
    ppermute x3, waiting for transfers between devices, gather_keyframes(): lax.ppermute(piece, 'row', [(i, (i + s) % rsize) for i in range(rsize)])  12.7 us
    pallas_call x1, Pallas kernels, attend(): pl.pallas_call(attention_kernel, grid=(channels // width,), in_specs=[pl....  5.84 us
    dot_general x6, matrix products, temporal_mix(): jnp.dot(window, weights[offset], preferred_element_type=jnp.float32)  4.43 us
    ppermute x1, waiting for transfers between devices, extended(): after = lax.ppermute(first, axis, down)  4.4 us
    ppermute x3, starting transfers between devices, gather_keyframes(): lax.ppermute(piece, 'row', [(i, (i + s) % rsize) for i in range(rsize)])  3.78 us
    ppermute x1, starting transfers between devices, extended(): before = lax.ppermute(last, axis, up)  3.34 us
    ppermute x3, starting transfers between devices, gather_keyframes(): lax.ppermute(halves((me + s) % 2), 'frame', [(i, (i + s) % fsize) for i i...  3.29 us
    dot_general x1, matrix products, shards(): lax.dot_general(w_query, flattened, (((0,), (1,)), ((), ())), preferred_e...  2.54 us
  transfers between devices with their start and end apart: 10, of which 7 were waited for; matrix products, arithmetic and copies ran while one was open for 10% of the time, Pallas kernels for 0%

profile of v19, /device:TPU:9, one launch (start us, length us, event | category | flops | bytes accessed | tf_op | source)
XLA Modules:
  0.0 61.3 jit_solution(16375063154483458610)
XLA Ops:
  0.0 1.2 %constant_dynamic-slice_fusion.2 = (bf16[2,64,640]{2,1,0:T(8,128)(2,1)S(1)}, bf16[2,64,640]{2,1,0:T(8,128)(2,1)S(1)}, bf16[2,64,640]{2,1,0:T(8,128)(2,1)S(1)}) fusion(bf16[2,128,640]{2,1,0:T(8,128)(2,1)} %param.8, s32[]{:T(128)S(6)} %select_n.137, s32[]{:T(128)S(6)} %select_n.147, s32[]{:T(128)S(6)} %select_n.143), kind=kLoop, calls=%fused_computation.63 | loop fusion | bytes 983052 | tf_op jit(solution)/shard_map/dynamic_slice | solution.py:73
  1.2 0.7 %collective-permute-start = (bf16[2,64,640]{2,1,0:T(8,128)(2,1)S(1)}, bf16[2,64,640]{2,1,0:T(8,128)(2,1)S(1)}, u32[]{:S(2)}, u32[]{:S(2)}) collective-permute-start(bf16[2,64,640]{2,1,0:T(8,128)(2,1)S(1)} %get-tuple-element.26), channel_id=1, source_target_pairs={{0,12},{4,0},{8,4},{12,8},{1,13},{5,1},{9,5},{13,9},{2,14},{6,2},{... | collective-permute-start | bytes 491528 | tf_op jit(solution)/shard_map/ppermute | solution.py:81
  1.9 1.2 %collective-permute-start.1 = (bf16[2,64,640]{2,1,0:T(8,128)(2,1)S(1)}, bf16[2,64,640]{2,1,0:T(8,128)(2,1)S(1)}, u32[]{:S(2)}, u32[]{:S(2)}) collective-permute-start(bf16[2,64,640]{2,1,0:T(8,128)(2,1)S(1)} %get-tuple-element.28), channel_id=1, source_target_pairs={{0,8},{4,12},{8,0},{12,4},{1,9},{5,13},{9,1},{13,5},{2,10},{6,14},... | collective-permute-start | bytes 491528 | tf_op jit(solution)/shard_map/ppermute | solution.py:81
  3.2 1.3 %collective-permute-start.2 = (bf16[2,64,640]{2,1,0:T(8,128)(2,1)S(1)}, bf16[2,64,640]{2,1,0:T(8,128)(2,1)S(1)}, u32[]{:S(2)}, u32[]{:S(2)}) collective-permute-start(bf16[2,64,640]{2,1,0:T(8,128)(2,1)S(1)} %get-tuple-element.27), channel_id=1, source_target_pairs={{0,4},{4,8},{8,12},{12,0},{1,5},{5,9},{9,13},{13,1},{2,6},{6,10},{... | collective-permute-start | bytes 491528 | tf_op jit(solution)/shard_map/ppermute | solution.py:81
  4.5 1.3 %fusion.33 = (s32[1]{0:T(128)}, s32[1]{0:T(128)}) fusion(s32[2]{0:T(128)} %param.9), kind=kLoop, calls=%fused_computation.66 | loop fusion | bytes 16 | tf_op jit(solution)/shard_map/slice | solution.py:66
  7.2 2.5 %fusion.2.qt_ref = bf16[640,256]{1,0:T(8,128)(2,1)} fusion(bf16[640,640]{1,0:T(8,128)(2,1)} %param.10, bf16[256,640]{1,0:T(8,128)(2,1)} %bitcast.58), kind=kOutput, calls=%fused_computation.14 | convolution fusion | flops 210042880 | bytes 1474560 | tf_op jit(solution)/shard_map/dot_general | solution.py:98
  9.7 1.0 %collective-permute-done.2 = bf16[2,64,640]{2,1,0:T(8,128)(2,1)S(1)} collective-permute-done((bf16[2,64,640]{2,1,0:T(8,128)(2,1)S(1)}, bf16[2,64,640]{2,1,0:T(8,128)(2,1)S(1)}, u32[]{:S(2)}, u32[]{:S(2)}) %collective-permute-start.2) | collective-permute-done | bytes 163872 | tf_op jit(solution)/shard_map/ppermute | solution.py:81
  10.8 1.4 %collective-permute-start.6 = (bf16[2,64,640]{2,1,0:T(8,128)(2,1)S(1)}, bf16[2,64,640]{2,1,0:T(8,128)(2,1)S(1)}, u32[]{:S(2)}, u32[]{:S(2)}) collective-permute-start(bf16[2,64,640]{2,1,0:T(8,128)(2,1)S(1)} %pad_maximum_fusion.10), channel_id=1, source_target_pairs={{0,4},{4,0},{8,12},{12,8},{1,5},{5,1},{9,13},{13,9},{2,6},{6,2},{1... | collective-permute-start | bytes 491528 | tf_op jit(solution)/shard_map/ppermute | solution.py:90
  12.2 1.3 %collective-permute-start.3 = (bf16[2,64,640]{2,1,0:T(8,128)(2,1)S(1)}, bf16[2,64,640]{2,1,0:T(8,128)(2,1)S(1)}, u32[]{:S(2)}, u32[]{:S(2)}) collective-permute-start(bf16[2,64,640]{2,1,0:T(8,128)(2,1)S(1)} %pad_maximum_fusion.10), channel_id=1, source_target_pairs={{0,1},{1,2},{2,3},{3,0},{4,5},{5,6},{6,7},{7,4},{8,9},{9,10},{10,1... | collective-permute-start | bytes 491528 | tf_op jit(solution)/shard_map/ppermute | solution.py:89
  13.5 1.0 %collective-permute-start.4 = (bf16[2,64,640]{2,1,0:T(8,128)(2,1)S(1)}, bf16[2,64,640]{2,1,0:T(8,128)(2,1)S(1)}, u32[]{:S(2)}, u32[]{:S(2)}) collective-permute-start(bf16[2,64,640]{2,1,0:T(8,128)(2,1)S(1)} %pad_maximum_fusion.10), channel_id=1, source_target_pairs={{0,2},{1,3},{2,0},{3,1},{4,6},{5,7},{6,4},{7,5},{8,10},{9,11},{10,... | collective-permute-start | bytes 491528 | tf_op jit(solution)/shard_map/ppermute | solution.py:89
  14.5 1.5 %collective-permute-start.5 = (bf16[2,64,640]{2,1,0:T(8,128)(2,1)S(1)}, bf16[2,64,640]{2,1,0:T(8,128)(2,1)S(1)}, u32[]{:S(2)}, u32[]{:S(2)}) collective-permute-start(bf16[2,64,640]{2,1,0:T(8,128)(2,1)S(1)} %pad_maximum_fusion.10), channel_id=1, source_target_pairs={{0,3},{1,0},{2,1},{3,2},{4,7},{5,4},{6,5},{7,6},{8,11},{9,8},{10,9... | collective-permute-start | bytes 491528 | tf_op jit(solution)/shard_map/ppermute | solution.py:89
  17.0 1.0 %collective-permute-done.3 = bf16[2,64,640]{2,1,0:T(8,128)(2,1)S(1)} collective-permute-done((bf16[2,64,640]{2,1,0:T(8,128)(2,1)S(1)}, bf16[2,64,640]{2,1,0:T(8,128)(2,1)S(1)}, u32[]{:S(2)}, u32[]{:S(2)}) %collective-permute-start.3) | collective-permute-done | bytes 163872 | tf_op jit(solution)/shard_map/ppermute | solution.py:89
  18.0 9.6 %collective-permute-done.4 = bf16[2,64,640]{2,1,0:T(8,128)(2,1)S(1)} collective-permute-done((bf16[2,64,640]{2,1,0:T(8,128)(2,1)S(1)}, bf16[2,64,640]{2,1,0:T(8,128)(2,1)S(1)}, u32[]{:S(2)}, u32[]{:S(2)}) %collective-permute-start.4) | collective-permute-done | bytes 163872 | tf_op jit(solution)/shard_map/ppermute | solution.py:89
  27.6 2.1 %collective-permute-done.5 = bf16[2,64,640]{2,1,0:T(8,128)(2,1)S(1)} collective-permute-done((bf16[2,64,640]{2,1,0:T(8,128)(2,1)S(1)}, bf16[2,64,640]{2,1,0:T(8,128)(2,1)S(1)}, u32[]{:S(2)}, u32[]{:S(2)}) %collective-permute-start.5) | collective-permute-done | bytes 163872 | tf_op jit(solution)/shard_map/ppermute | solution.py:89
  29.8 0.5 collective-permute-start.7
  30.4 0.7 %fusion.4 = bf16[640,384]{1,0:T(8,128)(2,1)S(1)} fusion(bf16[384,640]{1,0:T(8,128)(2,1)S(1)} %bitcast.70, bf16[640,1280]{1,0:T(8,128)(2,1)S(1)} %copy-done.5), kind=kOutput, calls=%fused_computation.16 | convolution fusion | flops 314818560 | bytes 1802240 | tf_op jit(solution)/shard_map/dot_general | solution.py:104
  31.1 0.6 convolution_convert_fusion.3
  31.9 0.7 %fusion.5 = bf16[640,384]{1,0:T(8,128)(2,1)S(1)} fusion(bf16[384,640]{1,0:T(8,128)(2,1)S(1)} %collective-permute-done.7, bf16[640,1280]{1,0:T(8,128)(2,1)S(1)} %copy-done.5), kind=kOutput, calls=%fused_computation.17 | convolution fusion | flops 314818560 | bytes 1802240 | tf_op jit(solution)/shard_map/dot_general | solution.py:104
  32.6 1.2 %pad_maximum_fusion.1.vt_ref = bf16[640,1024]{1,0:T(8,128)(2,1)} fusion(bf16[640,384]{1,0:T(8,128)(2,1)S(1)} %fusion.5, bf16[640,384]{1,0:T(8,128)(2,1)S(1)} %fusion.4, bf16[640,256]{1,0:T(8,128)(2,1)S(1)} %fusion.6), kind=kLoop, calls=%fused_computation.3 | loop fusion | flops 3932160 | bytes 2621440 | tf_op jit(solution)/shard_map/concatenate | solution.py:116
  33.8 0.6 convolution_convert_fusion.2
  34.4 1.2 %pad_maximum_fusion.k_ref = bf16[1024,640]{1,0:T(8,128)(2,1)} fusion(bf16[384,640]{1,0:T(8,128)(2,1)S(1)} %convolution_convert_fusion.2, bf16[384,640]{1,0:T(8,128)(2,1)S(1)} %convolution_convert_fusion.3, bf16[256,640]{1,0:T(8,128)(2,1)S(1)} %convolution_convert_fusion.5), kind=kLoop, calls=%fused_computation.2 | loop fusion | flops 3932160 | bytes 2621440 | tf_op jit(solution)/shard_map/concatenate | solution.py:115
  35.6 5.8 %shard_map.82 = bf16[640,256]{1,0:T(8,128)(2,1)} custom-call(bf16[1024,640]{1,0:T(8,128)(2,1)} %pad_maximum_fusion.k_ref, bf16[640,256]{1,0:T(8,128)(2,1)} %fusion.2.qt_ref, bf16[640,1024]{1,0:T(8,128)(2,1)} %pad_maximum_fusion.1.vt_ref), custom_call_target="tpu_custom_call" | custom-call | tf_op jit(solution)/shard_map/pallas_call | solution.py:28
  41.5 1.6 %multiply_reduce_fusion = (f32[256]{0:T(256)S(1)}, f32[256,640]{1,0:T(8,128)S(1)}) fusion(bf16[640,256]{1,0:T(8,128)(2,1)} %shard_map.82, bf16[640,640]{1,0:T(8,128)(2,1)S(1)} %copy-done, bf16[256,640]{1,0:T(8,128)(2,1)S(1)} %bitcast.59), kind=kOutput, calls=%fused_computation.41 | convolution fusion | flops 210370304 | bytes 2130944 | tf_op jit(solution)/shard_map/dot_general | solution.py:118
  43.2 3.3 %collective-permute-start.8 = (bf16[2,128,640]{2,1,0:T(8,128)(2,1)S(1)}, bf16[2,128,640]{2,1,0:T(8,128)(2,1)S(1)}, u32[]{:S(2)}, u32[]{:S(2)}) collective-permute-start(bf16[2,128,640]{2,1,0:T(8,128)(2,1)S(1)} %bitcast.65), channel_id=1, source_target_pairs={{0,4},{4,8},{8,12},{1,5},{5,9},{9,13},{2,6},{6,10},{10,14},{3,7},{... | collective-permute-start | bytes 983048 | tf_op jit(solution)/shard_map/ppermute | solution.py:47
  46.5 2.1 %collective-permute-start.9 = (bf16[2,128,640]{2,1,0:T(8,128)(2,1)S(1)}, bf16[2,128,640]{2,1,0:T(8,128)(2,1)S(1)}, u32[]{:S(2)}, u32[]{:S(2)}) collective-permute-start(bf16[2,128,640]{2,1,0:T(8,128)(2,1)S(1)} %bitcast.66), channel_id=1, source_target_pairs={{4,0},{8,4},{12,8},{5,1},{9,5},{13,9},{6,2},{10,6},{14,10},{7,3},{... | collective-permute-start | bytes 983048 | tf_op jit(solution)/shard_map/ppermute | solution.py:48
  48.7 1.9 %collective-permute-done.8 = bf16[2,128,640]{2,1,0:T(8,128)(2,1)S(1)} collective-permute-done((bf16[2,128,640]{2,1,0:T(8,128)(2,1)S(1)}, bf16[2,128,640]{2,1,0:T(8,128)(2,1)S(1)}, u32[]{:S(2)}, u32[]{:S(2)}) %collective-permute-start.8) | collective-permute-done | bytes 327712 | tf_op jit(solution)/shard_map/ppermute | solution.py:47
  50.5 4.4 %collective-permute-done.9 = bf16[2,128,640]{2,1,0:T(8,128)(2,1)S(1)} collective-permute-done((bf16[2,128,640]{2,1,0:T(8,128)(2,1)S(1)}, bf16[2,128,640]{2,1,0:T(8,128)(2,1)S(1)}, u32[]{:S(2)}, u32[]{:S(2)}) %collective-permute-start.9) | collective-permute-done | bytes 327712 | tf_op jit(solution)/shard_map/ppermute | solution.py:48
  55.2 0.7 %fusion.11 = f32[512,640]{1,0:T(8,128)S(1)} fusion(bf16[512,640]{1,0:T(8,128)(2,1)S(1)} %bitcast.61, bf16[3,640,640]{2,1,0:T(8,128)(2,1)S(1)} %copy-done.3), kind=kOutput, calls=%fused_computation.25 | convolution fusion | flops 419430400 | bytes 2785280 | tf_op jit(solution)/shard_map/dot_general | solution.py:56
  55.9 0.7 %fusion.13 = f32[512,640]{1,0:T(8,128)S(1)} fusion(bf16[512,640]{1,0:T(8,128)(2,1)S(1)} %bitcast.60, bf16[3,640,640]{2,1,0:T(8,128)(2,1)S(1)} %copy-done.3), kind=kOutput, calls=%fused_computation.27 | convolution fusion | flops 419430400 | bytes 2785280 | tf_op jit(solution)/shard_map/dot_general | solution.py:56
  56.7 0.8 %multiply_convert_fusion = bf16[512,640]{1,0:T(8,128)(2,1)S(1)} fusion(f32[512,640]{1,0:T(8,128)S(1)} %fusion.11, f32[512,640]{1,0:T(8,128)S(1)} %fusion.13, bf16[512,640]{1,0:T(8,128)(2,1)S(1)} %bitcast.68, bf16[3,640,640]{2,1,0:T(8,128)(2,1)S(1)} %copy-done.3), kind=kOutput, calls=%fused_computation.4 | convolution fusion | flops 421724160 | bytes 4751360 | tf_op jit(solution)/shard_map/dot_general | solution.py:56
  57.7 1.5 %copy-done.2 = bf16[3,640,640]{2,1,0:T(8,128)(2,1)S(1)} copy-done((bf16[3,640,640]{2,1,0:T(8,128)(2,1)S(1)}, bf16[3,640,640]{2,1,0:T(8,128)(2,1)}, u32[]{:S(2)}) %copy-start.2) | copy-done | bytes 2457624
  60.2 1.2 %fusion.3 = bf16[256,640]{1,0:T(8,128)(2,1)} fusion(f32[256,640]{1,0:T(8,128)S(1)} %get-tuple-element.32, f32[256,640]{1,0:T(8,128)S(1)} %convolution_add_fusion.2, bf16[256,640]{1,0:T(8,128)(2,1)S(1)} %bitcast.64, bf16[3,640,640]{2,1,0:T(8,128)(2,1)S(1)} %copy-done.2), kind=kOutput, calls=%fused_computation.15 | convolution fusion | flops 210206720 | bytes 2785280 | tf_op jit(solution)/shard_map/dot_general | solution.py:56
  (29 shorter events, 2.8 us)
Async XLA Ops:
  0.0 41.5 %copy-start = (bf16[640,640]{1,0:T(8,128)(2,1)S(1)}, bf16[640,640]{1,0:T(8,128)(2,1)}, u32[]{:S(2)}) copy-start(bf16[640,640]{1,0:T(8,128)(2,1)} %param.12) | copy-start | bytes 2457604
  0.0 10.7 %copy-start.1 = (bf16[2,128,640]{2,1,0:T(8,128)(2,1)S(1)}, bf16[2,128,640]{2,1,0:T(8,128)(2,1)}, u32[]{:S(2)}) copy-start(bf16[2,128,640]{2,1,0:T(8,128)(2,1)} %param.8) | copy-start | bytes 983044
  1.2 8.5 %collective-permute-start = (bf16[2,64,640]{2,1,0:T(8,128)(2,1)S(1)}, bf16[2,64,640]{2,1,0:T(8,128)(2,1)S(1)}, u32[]{:S(2)}, u32[]{:S(2)}) collective-permute-start(bf16[2,64,640]{2,1,0:T(8,128)(2,1)S(1)} %get-tuple-element.26), channel_id=1, source_target_pairs={{0,12},{4,0},{8,4},{12,8},{1,13},{5,1},{9,5},{13,9},{2,14},{6,2},{... | collective-permute-start | bytes 491528 | tf_op jit(solution)/shard_map/ppermute | solution.py:81
  1.9 7.8 %collective-permute-start.1 = (bf16[2,64,640]{2,1,0:T(8,128)(2,1)S(1)}, bf16[2,64,640]{2,1,0:T(8,128)(2,1)S(1)}, u32[]{:S(2)}, u32[]{:S(2)}) collective-permute-start(bf16[2,64,640]{2,1,0:T(8,128)(2,1)S(1)} %get-tuple-element.28), channel_id=1, source_target_pairs={{0,8},{4,12},{8,0},{12,4},{1,9},{5,13},{9,1},{13,5},{2,10},{6,14},... | collective-permute-start | bytes 491528 | tf_op jit(solution)/shard_map/ppermute | solution.py:81
  3.2 7.5 %collective-permute-start.2 = (bf16[2,64,640]{2,1,0:T(8,128)(2,1)S(1)}, bf16[2,64,640]{2,1,0:T(8,128)(2,1)S(1)}, u32[]{:S(2)}, u32[]{:S(2)}) collective-permute-start(bf16[2,64,640]{2,1,0:T(8,128)(2,1)S(1)} %get-tuple-element.27), channel_id=1, source_target_pairs={{0,4},{4,8},{8,12},{12,0},{1,5},{5,9},{9,13},{13,1},{2,6},{6,10},{... | collective-permute-start | bytes 491528 | tf_op jit(solution)/shard_map/ppermute | solution.py:81
  7.1 8.9 %copy-start.5 = (bf16[640,1280]{1,0:T(8,128)(2,1)S(1)}, bf16[640,1280]{1,0:T(8,128)(2,1)}, u32[]{:S(2)}) copy-start(bf16[640,1280]{1,0:T(8,128)(2,1)} %param.11) | copy-start | bytes 4915204
  10.8 5.2 %collective-permute-start.6 = (bf16[2,64,640]{2,1,0:T(8,128)(2,1)S(1)}, bf16[2,64,640]{2,1,0:T(8,128)(2,1)S(1)}, u32[]{:S(2)}, u32[]{:S(2)}) collective-permute-start(bf16[2,64,640]{2,1,0:T(8,128)(2,1)S(1)} %pad_maximum_fusion.10), channel_id=1, source_target_pairs={{0,4},{4,0},{8,12},{12,8},{1,5},{5,1},{9,13},{13,9},{2,6},{6,2},{1... | collective-permute-start | bytes 491528 | tf_op jit(solution)/shard_map/ppermute | solution.py:90
  12.2 5.8 %collective-permute-start.3 = (bf16[2,64,640]{2,1,0:T(8,128)(2,1)S(1)}, bf16[2,64,640]{2,1,0:T(8,128)(2,1)S(1)}, u32[]{:S(2)}, u32[]{:S(2)}) collective-permute-start(bf16[2,64,640]{2,1,0:T(8,128)(2,1)S(1)} %pad_maximum_fusion.10), channel_id=1, source_target_pairs={{0,1},{1,2},{2,3},{3,0},{4,5},{5,6},{6,7},{7,4},{8,9},{9,10},{10,1... | collective-permute-start | bytes 491528 | tf_op jit(solution)/shard_map/ppermute | solution.py:89
  13.5 14.1 %collective-permute-start.4 = (bf16[2,64,640]{2,1,0:T(8,128)(2,1)S(1)}, bf16[2,64,640]{2,1,0:T(8,128)(2,1)S(1)}, u32[]{:S(2)}, u32[]{:S(2)}) collective-permute-start(bf16[2,64,640]{2,1,0:T(8,128)(2,1)S(1)} %pad_maximum_fusion.10), channel_id=1, source_target_pairs={{0,2},{1,3},{2,0},{3,1},{4,6},{5,7},{6,4},{7,5},{8,10},{9,11},{10,... | collective-permute-start | bytes 491528 | tf_op jit(solution)/shard_map/ppermute | solution.py:89
  14.5 15.2 %collective-permute-start.5 = (bf16[2,64,640]{2,1,0:T(8,128)(2,1)S(1)}, bf16[2,64,640]{2,1,0:T(8,128)(2,1)S(1)}, u32[]{:S(2)}, u32[]{:S(2)}) collective-permute-start(bf16[2,64,640]{2,1,0:T(8,128)(2,1)S(1)} %pad_maximum_fusion.10), channel_id=1, source_target_pairs={{0,3},{1,0},{2,1},{3,2},{4,7},{5,4},{6,5},{7,6},{8,11},{9,8},{10,9... | collective-permute-start | bytes 491528 | tf_op jit(solution)/shard_map/ppermute | solution.py:89
  29.8 2.0 %collective-permute-start.7 = (bf16[384,640]{1,0:T(8,128)(2,1)S(1)}, bf16[384,640]{1,0:T(8,128)(2,1)S(1)}, u32[]{:S(2)}, u32[]{:S(2)}) collective-permute-start(bf16[384,640]{1,0:T(8,128)(2,1)S(1)} %bitcast.69), channel_id=1, source_target_pairs={{0,4},{4,0},{8,12},{12,8},{1,5},{5,1},{9,13},{13,9},{2,6},{6,2},{1... | collective-permute-start | bytes 1474568 | tf_op jit(solution)/shard_map/ppermute | solution.py:112
  41.5 1.6 %copy-start.4 = (f32[640]{0:T(1024)S(1)}, f32[640]{0:T(1024)}, u32[]{:S(2)}) copy-start(f32[640]{0:T(1024)} %param.13) | copy-start | bytes 7684
  43.2 7.3 %collective-permute-start.8 = (bf16[2,128,640]{2,1,0:T(8,128)(2,1)S(1)}, bf16[2,128,640]{2,1,0:T(8,128)(2,1)S(1)}, u32[]{:S(2)}, u32[]{:S(2)}) collective-permute-start(bf16[2,128,640]{2,1,0:T(8,128)(2,1)S(1)} %bitcast.65), channel_id=1, source_target_pairs={{0,4},{4,8},{8,12},{1,5},{5,9},{9,13},{2,6},{6,10},{10,14},{3,7},{... | collective-permute-start | bytes 983048 | tf_op jit(solution)/shard_map/ppermute | solution.py:47
  46.5 8.4 %collective-permute-start.9 = (bf16[2,128,640]{2,1,0:T(8,128)(2,1)S(1)}, bf16[2,128,640]{2,1,0:T(8,128)(2,1)S(1)}, u32[]{:S(2)}, u32[]{:S(2)}) collective-permute-start(bf16[2,128,640]{2,1,0:T(8,128)(2,1)S(1)} %bitcast.66), channel_id=1, source_target_pairs={{4,0},{8,4},{12,8},{5,1},{9,5},{13,9},{6,2},{10,6},{14,10},{7,3},{... | collective-permute-start | bytes 983048 | tf_op jit(solution)/shard_map/ppermute | solution.py:48
  48.7 6.5 %copy-start.3 = (bf16[3,640,640]{2,1,0:T(8,128)(2,1)S(1)}, bf16[3,640,640]{2,1,0:T(8,128)(2,1)}, u32[]{:S(2)}) copy-start(bf16[3,640,640]{2,1,0:T(8,128)(2,1)} %param.14) | copy-start | bytes 7372804
  57.5 1.7 %copy-start.2 = (bf16[3,640,640]{2,1,0:T(8,128)(2,1)S(1)}, bf16[3,640,640]{2,1,0:T(8,128)(2,1)}, u32[]{:S(2)}) copy-start(bf16[3,640,640]{2,1,0:T(8,128)(2,1)} %param.15) | copy-start | bytes 7372804

commit v20 on v14

--- a/solution.py
+++ b/solution.py
@@ -84,10 +84,19 @@
         got_b = jnp.where(source == owner_b, recv[n_loc - 1], got_b)
     piece = jnp.stack([got_a, got_b])
     piece, early = lax.optimization_barrier((piece, early))
-    pieces = [piece]
-    for s in range(1, rsize):
-        pieces.append(lax.ppermute(piece, "row", [(i, (i + s) % rsize) for i in range(rsize)]))
-    mine = jnp.stack(pieces).reshape(-1, channels)
+    if rsize & (rsize - 1) == 0:
+        gathered = piece[None]
+        stride = 1
+        while stride < rsize:
+            moved = lax.ppermute(gathered, "row", [(i, (i + stride) % rsize) for i in range(rsize)])
+            gathered = jnp.concatenate([gathered, moved], axis=0)
+            stride *= 2
+        mine = gathered.reshape(-1, channels)
+    else:
+        pieces = [piece]
+        for s in range(1, rsize):
+            pieces.append(lax.ppermute(piece, "row", [(i, (i + s) % rsize) for i in range(rsize)]))
+        mine = jnp.stack(pieces).reshape(-1, channels)
     sibling = lax.ppermute(mine, "frame", [(i, i ^ 1) for i in range(fsize)])
     return mine, sibling
 

time: 59.8 us -> 66 us (1.10)
  the two profiles are of different devices: /device:TPU:9 before, /device:TPU:1 now
where the time goes in v20:
time: 66 us; the launch traced here: 65.7 us
  waiting for transfers between devices  29.1 us (44%)
  matrix products  11.3 us (17%)
  starting transfers between devices  10.5 us (16%)
  Pallas kernels  5.85 us (9%)
  local copies, waits for them, and re-layouts  4.11 us (6%)
  other arithmetic  3.19 us (5%)
  between operations  1.64 us (2%)
    ppermute x2, waiting for transfers between devices, gather_keyframes(): lax.ppermute(gathered, 'row', [(i, (i + stride) % rsize) for i in range(r...  21.4 us
    pallas_call x1, Pallas kernels, attend(): pl.pallas_call(attention_kernel, grid=(channels // width,), in_specs=[pl....  5.85 us
    dot_general x6, matrix products, temporal_mix(): jnp.dot(window, weights[offset], preferred_element_type=jnp.float32)  4.43 us
    ppermute x1, waiting for transfers between devices, extended(): after = lax.ppermute(first, axis, down)  4.4 us
    ppermute x3, starting transfers between devices, gather_keyframes(): lax.ppermute(halves((me + s) % 2), 'frame', [(i, (i + s) % fsize) for i i...  4.12 us
    ppermute x1, starting transfers between devices, extended(): before = lax.ppermute(last, axis, up)  2.51 us
    dot_general x1, matrix products, shards(): lax.dot_general(w_query, flattened, (((0,), (1,)), ((), ())), preferred_e...  2.42 us
    ppermute x1, waiting for transfers between devices, extended(): before = lax.ppermute(last, axis, up)  2.05 us
  transfers between devices with their start and end apart: 8, of which 6 were waited for; matrix products, arithmetic and copies ran while one was open for 8% of the time, Pallas kernels for 0%

profile of v20, /device:TPU:1, one launch (start us, length us, event | category | flops | bytes accessed | tf_op | source)
XLA Modules:
  0.0 65.7 jit_solution(6415204099079380374)
XLA Ops:
  0.0 1.2 %constant_dynamic-slice_fusion.2 = (bf16[2,64,640]{2,1,0:T(8,128)(2,1)S(1)}, bf16[2,64,640]{2,1,0:T(8,128)(2,1)S(1)}, bf16[2,64,640]{2,1,0:T(8,128)(2,1)S(1)}) fusion(bf16[2,128,640]{2,1,0:T(8,128)(2,1)} %param.8, s32[]{:T(128)S(6)} %select_n.137, s32[]{:T(128)S(6)} %select_n.147, s32[]{:T(128)S(6)} %select_n.143), kind=kLoop, calls=%fused_computation.58 | loop fusion | bytes 983052 | tf_op jit(solution)/shard_map/dynamic_slice | solution.py:73
  1.3 2.7 %collective-permute-start.1 = (bf16[2,64,640]{2,1,0:T(8,128)(2,1)S(1)}, bf16[2,64,640]{2,1,0:T(8,128)(2,1)S(1)}, u32[]{:S(2)}, u32[]{:S(2)}) collective-permute-start(bf16[2,64,640]{2,1,0:T(8,128)(2,1)S(1)} %get-tuple-element.18), channel_id=1, source_target_pairs={{0,8},{4,12},{8,0},{12,4},{1,9},{5,13},{9,1},{13,5},{2,10},{6,14},... | collective-permute-start | bytes 491528 | tf_op jit(solution)/shard_map/ppermute | solution.py:81
  4.0 1.3 %collective-permute-start.2 = (bf16[2,64,640]{2,1,0:T(8,128)(2,1)S(1)}, bf16[2,64,640]{2,1,0:T(8,128)(2,1)S(1)}, u32[]{:S(2)}, u32[]{:S(2)}) collective-permute-start(bf16[2,64,640]{2,1,0:T(8,128)(2,1)S(1)} %get-tuple-element.17), channel_id=1, source_target_pairs={{0,4},{4,8},{8,12},{12,0},{1,5},{5,9},{9,13},{13,1},{2,6},{6,10},{... | collective-permute-start | bytes 491528 | tf_op jit(solution)/shard_map/ppermute | solution.py:81
  5.3 1.3 %fusion.30 = (s32[1]{0:T(128)}, s32[1]{0:T(128)}) fusion(s32[2]{0:T(128)} %param.9), kind=kLoop, calls=%fused_computation.61 | loop fusion | bytes 16 | tf_op jit(solution)/shard_map/slice | solution.py:66
  8.1 2.4 %fusion.4.qt_ref = bf16[640,256]{1,0:T(8,128)(2,1)} fusion(bf16[640,640]{1,0:T(8,128)(2,1)} %param.10, bf16[256,640]{1,0:T(8,128)(2,1)} %bitcast.51), kind=kOutput, calls=%fused_computation.16 | convolution fusion | flops 210042880 | bytes 1474560 | tf_op jit(solution)/shard_map/dot_general | solution.py:108
  10.5 1.0 %collective-permute-done.2 = bf16[2,64,640]{2,1,0:T(8,128)(2,1)S(1)} collective-permute-done((bf16[2,64,640]{2,1,0:T(8,128)(2,1)S(1)}, bf16[2,64,640]{2,1,0:T(8,128)(2,1)S(1)}, u32[]{:S(2)}, u32[]{:S(2)}) %collective-permute-start.2) | collective-permute-done | bytes 163872 | tf_op jit(solution)/shard_map/ppermute | solution.py:81
  11.7 1.3 %collective-permute-start.3 = (bf16[1,2,64,640]{3,2,1,0:T(8,128)(2,1)S(1)}, bf16[1,2,64,640]{3,2,1,0:T(8,128)(2,1)S(1)}, u32[]{:S(2)}, u32[]{:S(2)}) collective-permute-start(bf16[1,2,64,640]{3,2,1,0:T(8,128)(2,1)S(1)} %bitcast.55), channel_id=1, source_target_pairs={{0,1},{1,2},{2,3},{3,0},{4,5},{5,6},{6,7},{7,4},{8,9},{9,10},{10,1... | collective-permute-start | bytes 491528 | tf_op jit(solution)/shard_map/ppermute | solution.py:91
  13.0 5.2 %collective-permute-done.3 = bf16[1,2,64,640]{3,2,1,0:T(8,128)(2,1)S(1)} collective-permute-done((bf16[1,2,64,640]{3,2,1,0:T(8,128)(2,1)S(1)}, bf16[1,2,64,640]{3,2,1,0:T(8,128)(2,1)S(1)}, u32[]{:S(2)}, u32[]{:S(2)}) %collective-permute-start.3) | collective-permute-done | bytes 163872 | tf_op jit(solution)/shard_map/ppermute | solution.py:91
  18.3 16.3 %collective-permute-done.4 = bf16[2,2,64,640]{3,2,1,0:T(8,128)(2,1)S(1)} collective-permute-done((bf16[2,2,64,640]{3,2,1,0:T(8,128)(2,1)S(1)}, bf16[2,2,64,640]{3,2,1,0:T(8,128)(2,1)S(1)}, u32[]{:S(2)}, u32[]{:S(2)}) %collective-permute-start.4) | collective-permute-done | bytes 327712 | tf_op jit(solution)/shard_map/ppermute | solution.py:91
  34.6 0.6 collective-permute-start.5
  35.2 0.7 %fusion.1 = bf16[640,512]{1,0:T(8,128)(2,1)S(1)} fusion(bf16[512,640]{1,0:T(8,128)(2,1)S(1)} %bitcast.65, bf16[640,1280]{1,0:T(8,128)(2,1)S(1)} %copy-done.5), kind=kOutput, calls=%fused_computation.9 | convolution fusion | flops 419758080 | bytes 2129920 | tf_op jit(solution)/shard_map/dot_general | solution.py:114
  35.9 0.7 %convolution_convert_fusion.3 = bf16[512,640]{1,0:T(8,128)(2,1)S(1)} fusion(bf16[512,640]{1,0:T(8,128)(2,1)S(1)} %bitcast.66, bf16[640,1280]{1,0:T(8,128)(2,1)S(1)} %copy-done.5), kind=kOutput, calls=%fused_computation.5 | convolution fusion | flops 419758080 | bytes 2129920 | tf_op jit(solution)/shard_map/dot_general | solution.py:113
  36.7 0.2 collective-permute-done.5
  36.9 0.7 %fusion.2 = bf16[640,512]{1,0:T(8,128)(2,1)S(1)} fusion(bf16[512,640]{1,0:T(8,128)(2,1)S(1)} %collective-permute-done.5, bf16[640,1280]{1,0:T(8,128)(2,1)S(1)} %copy-done.5), kind=kOutput, calls=%fused_computation.10 | convolution fusion | flops 419758080 | bytes 2129920 | tf_op jit(solution)/shard_map/dot_general | solution.py:114
  37.6 1.2 %pad_maximum_fusion.1.vt_ref = bf16[640,1024]{1,0:T(8,128)(2,1)} fusion(bf16[640,512]{1,0:T(8,128)(2,1)S(1)} %fusion.2, bf16[640,512]{1,0:T(8,128)(2,1)S(1)} %fusion.1), kind=kLoop, calls=%fused_computation.7 | loop fusion | flops 2621440 | bytes 2621440 | tf_op jit(solution)/shard_map/concatenate | solution.py:122
  38.9 0.7 %convolution_convert_fusion.2 = bf16[512,640]{1,0:T(8,128)(2,1)S(1)} fusion(bf16[512,640]{1,0:T(8,128)(2,1)S(1)} %collective-permute-done.5, bf16[640,1280]{1,0:T(8,128)(2,1)S(1)} %copy-done.5), kind=kOutput, calls=%fused_computation.4 | convolution fusion | flops 419758080 | bytes 2129920 | tf_op jit(solution)/shard_map/dot_general | solution.py:113
  39.6 1.2 %pad_maximum_fusion.k_ref = bf16[1024,640]{1,0:T(8,128)(2,1)} fusion(bf16[512,640]{1,0:T(8,128)(2,1)S(1)} %convolution_convert_fusion.2, bf16[512,640]{1,0:T(8,128)(2,1)S(1)} %convolution_convert_fusion.3), kind=kLoop, calls=%fused_computation.6 | loop fusion | flops 2621440 | bytes 2621440 | tf_op jit(solution)/shard_map/concatenate | solution.py:121
  40.8 5.8 %shard_map.82 = bf16[640,256]{1,0:T(8,128)(2,1)} custom-call(bf16[1024,640]{1,0:T(8,128)(2,1)} %pad_maximum_fusion.k_ref, bf16[640,256]{1,0:T(8,128)(2,1)} %fusion.4.qt_ref, bf16[640,1024]{1,0:T(8,128)(2,1)} %pad_maximum_fusion.1.vt_ref), custom_call_target="tpu_custom_call" | custom-call | tf_op jit(solution)/shard_map/pallas_call | solution.py:28
  46.7 1.6 %multiply_reduce_fusion = (f32[256]{0:T(256)S(1)}, f32[256,640]{1,0:T(8,128)S(1)}) fusion(bf16[640,256]{1,0:T(8,128)(2,1)} %shard_map.82, bf16[640,640]{1,0:T(8,128)(2,1)S(1)} %copy-done, bf16[256,640]{1,0:T(8,128)(2,1)S(1)} %bitcast.52), kind=kOutput, calls=%fused_computation.43 | convolution fusion | flops 210370304 | bytes 2130944 | tf_op jit(solution)/shard_map/dot_general | solution.py:124
  48.3 0.1 multiply_convert_fusion.1
  48.4 2.5 %collective-permute-start.6 = (bf16[2,128,640]{2,1,0:T(8,128)(2,1)S(1)}, bf16[2,128,640]{2,1,0:T(8,128)(2,1)S(1)}, u32[]{:S(2)}, u32[]{:S(2)}) collective-permute-start(bf16[2,128,640]{2,1,0:T(8,128)(2,1)S(1)} %bitcast.61), channel_id=1, source_target_pairs={{0,4},{4,8},{8,12},{1,5},{5,9},{9,13},{2,6},{6,10},{10,14},{3,7},{... | collective-permute-start | bytes 983048 | tf_op jit(solution)/shard_map/ppermute | solution.py:47
  50.9 1.9 %collective-permute-start.7 = (bf16[2,128,640]{2,1,0:T(8,128)(2,1)S(1)}, bf16[2,128,640]{2,1,0:T(8,128)(2,1)S(1)}, u32[]{:S(2)}, u32[]{:S(2)}) collective-permute-start(bf16[2,128,640]{2,1,0:T(8,128)(2,1)S(1)} %bitcast.62), channel_id=1, source_target_pairs={{4,0},{8,4},{12,8},{5,1},{9,5},{13,9},{6,2},{10,6},{14,10},{7,3},{... | collective-permute-start | bytes 983048 | tf_op jit(solution)/shard_map/ppermute | solution.py:48
  52.9 2.0 %collective-permute-done.6 = bf16[2,128,640]{2,1,0:T(8,128)(2,1)S(1)} collective-permute-done((bf16[2,128,640]{2,1,0:T(8,128)(2,1)S(1)}, bf16[2,128,640]{2,1,0:T(8,128)(2,1)S(1)}, u32[]{:S(2)}, u32[]{:S(2)}) %collective-permute-start.6) | collective-permute-done | bytes 327712 | tf_op jit(solution)/shard_map/ppermute | solution.py:47
  54.9 4.4 %collective-permute-done.7 = bf16[2,128,640]{2,1,0:T(8,128)(2,1)S(1)} collective-permute-done((bf16[2,128,640]{2,1,0:T(8,128)(2,1)S(1)}, bf16[2,128,640]{2,1,0:T(8,128)(2,1)S(1)}, u32[]{:S(2)}, u32[]{:S(2)}) %collective-permute-start.7) | collective-permute-done | bytes 327712 | tf_op jit(solution)/shard_map/ppermute | solution.py:48
  59.3 0.2 pad_maximum_fusion.5
  59.6 0.7 %fusion.10 = f32[512,640]{1,0:T(8,128)S(1)} fusion(bf16[512,640]{1,0:T(8,128)(2,1)S(1)} %bitcast.54, bf16[3,640,640]{2,1,0:T(8,128)(2,1)S(1)} %copy-done.3), kind=kOutput, calls=%fused_computation.22 | convolution fusion | flops 419430400 | bytes 2785280 | tf_op jit(solution)/shard_map/dot_general | solution.py:56
  60.3 0.7 %fusion.12 = f32[512,640]{1,0:T(8,128)S(1)} fusion(bf16[512,640]{1,0:T(8,128)(2,1)S(1)} %bitcast.53, bf16[3,640,640]{2,1,0:T(8,128)(2,1)S(1)} %copy-done.3), kind=kOutput, calls=%fused_computation.24 | convolution fusion | flops 419430400 | bytes 2785280 | tf_op jit(solution)/shard_map/dot_general | solution.py:56
  61.1 0.8 %multiply_convert_fusion = bf16[512,640]{1,0:T(8,128)(2,1)S(1)} fusion(f32[512,640]{1,0:T(8,128)S(1)} %fusion.10, f32[512,640]{1,0:T(8,128)S(1)} %fusion.12, bf16[512,640]{1,0:T(8,128)(2,1)S(1)} %bitcast.67, bf16[3,640,640]{2,1,0:T(8,128)(2,1)S(1)} %copy-done.3), kind=kOutput, calls=%fused_computation.8 | convolution fusion | flops 421724160 | bytes 4751360 | tf_op jit(solution)/shard_map/dot_general | solution.py:56
  62.1 1.5 %copy-done.2 = bf16[3,640,640]{2,1,0:T(8,128)(2,1)S(1)} copy-done((bf16[3,640,640]{2,1,0:T(8,128)(2,1)S(1)}, bf16[3,640,640]{2,1,0:T(8,128)(2,1)}, u32[]{:S(2)}) %copy-start.2) | copy-done | bytes 2457624
  63.6 0.5 fusion.8
  64.1 0.5 convolution_add_fusion.2
  64.6 1.2 %fusion.5 = bf16[256,640]{1,0:T(8,128)(2,1)} fusion(f32[256,640]{1,0:T(8,128)S(1)} %get-tuple-element.22, f32[256,640]{1,0:T(8,128)S(1)} %convolution_add_fusion.2, bf16[256,640]{1,0:T(8,128)(2,1)S(1)} %bitcast.60, bf16[3,640,640]{2,1,0:T(8,128)(2,1)S(1)} %copy-done.2), kind=kOutput, calls=%fused_computation.17 | convolution fusion | flops 210206720 | bytes 2785280 | tf_op jit(solution)/shard_map/dot_general | solution.py:56
  (23 shorter events, 0.6 us)
Async XLA Ops:
  0.0 46.7 %copy-start = (bf16[640,640]{1,0:T(8,128)(2,1)S(1)}, bf16[640,640]{1,0:T(8,128)(2,1)}, u32[]{:S(2)}) copy-start(bf16[640,640]{1,0:T(8,128)(2,1)} %param.12) | copy-start | bytes 2457604
  0.0 11.5 %copy-start.1 = (bf16[2,128,640]{2,1,0:T(8,128)(2,1)S(1)}, bf16[2,128,640]{2,1,0:T(8,128)(2,1)}, u32[]{:S(2)}) copy-start(bf16[2,128,640]{2,1,0:T(8,128)(2,1)} %param.8) | copy-start | bytes 983044
  1.2 9.3 %collective-permute-start = (bf16[2,64,640]{2,1,0:T(8,128)(2,1)S(1)}, bf16[2,64,640]{2,1,0:T(8,128)(2,1)S(1)}, u32[]{:S(2)}, u32[]{:S(2)}) collective-permute-start(bf16[2,64,640]{2,1,0:T(8,128)(2,1)S(1)} %get-tuple-element.16), channel_id=1, source_target_pairs={{0,12},{4,0},{8,4},{12,8},{1,13},{5,1},{9,5},{13,9},{2,14},{6,2},{... | collective-permute-start | bytes 491528 | tf_op jit(solution)/shard_map/ppermute | solution.py:81
  1.3 9.2 %collective-permute-start.1 = (bf16[2,64,640]{2,1,0:T(8,128)(2,1)S(1)}, bf16[2,64,640]{2,1,0:T(8,128)(2,1)S(1)}, u32[]{:S(2)}, u32[]{:S(2)}) collective-permute-start(bf16[2,64,640]{2,1,0:T(8,128)(2,1)S(1)} %get-tuple-element.18), channel_id=1, source_target_pairs={{0,8},{4,12},{8,0},{12,4},{1,9},{5,13},{9,1},{13,5},{2,10},{6,14},... | collective-permute-start | bytes 491528 | tf_op jit(solution)/shard_map/ppermute | solution.py:81
  4.0 7.5 %collective-permute-start.2 = (bf16[2,64,640]{2,1,0:T(8,128)(2,1)S(1)}, bf16[2,64,640]{2,1,0:T(8,128)(2,1)S(1)}, u32[]{:S(2)}, u32[]{:S(2)}) collective-permute-start(bf16[2,64,640]{2,1,0:T(8,128)(2,1)S(1)} %get-tuple-element.17), channel_id=1, source_target_pairs={{0,4},{4,8},{8,12},{12,0},{1,5},{5,9},{9,13},{13,1},{2,6},{6,10},{... | collective-permute-start | bytes 491528 | tf_op jit(solution)/shard_map/ppermute | solution.py:81
  10.5 24.7 %copy-start.5 = (bf16[640,1280]{1,0:T(8,128)(2,1)S(1)}, bf16[640,1280]{1,0:T(8,128)(2,1)}, u32[]{:S(2)}) copy-start(bf16[640,1280]{1,0:T(8,128)(2,1)} %param.11) | copy-start | bytes 4915204
  11.7 6.5 %collective-permute-start.3 = (bf16[1,2,64,640]{3,2,1,0:T(8,128)(2,1)S(1)}, bf16[1,2,64,640]{3,2,1,0:T(8,128)(2,1)S(1)}, u32[]{:S(2)}, u32[]{:S(2)}) collective-permute-start(bf16[1,2,64,640]{3,2,1,0:T(8,128)(2,1)S(1)} %bitcast.55), channel_id=1, source_target_pairs={{0,1},{1,2},{2,3},{3,0},{4,5},{5,6},{6,7},{7,4},{8,9},{9,10},{10,1... | collective-permute-start | bytes 491528 | tf_op jit(solution)/shard_map/ppermute | solution.py:91
  18.2 16.3 %collective-permute-start.4 = (bf16[2,2,64,640]{3,2,1,0:T(8,128)(2,1)S(1)}, bf16[2,2,64,640]{3,2,1,0:T(8,128)(2,1)S(1)}, u32[]{:S(2)}, u32[]{:S(2)}) collective-permute-start(bf16[2,2,64,640]{3,2,1,0:T(8,128)(2,1)S(1)} %pad_maximum_fusion.9), channel_id=1, source_target_pairs={{0,2},{1,3},{2,0},{3,1},{4,6},{5,7},{6,4},{7,5},{8,10},{9,11},{10,... | collective-permute-start | bytes 983048 | tf_op jit(solution)/shard_map/ppermute | solution.py:91
  34.6 2.3 %collective-permute-start.5 = (bf16[512,640]{1,0:T(8,128)(2,1)S(1)}, bf16[512,640]{1,0:T(8,128)(2,1)S(1)}, u32[]{:S(2)}, u32[]{:S(2)}) collective-permute-start(bf16[512,640]{1,0:T(8,128)(2,1)S(1)} %bitcast.64), channel_id=1, source_target_pairs={{0,4},{4,0},{8,12},{12,8},{1,5},{5,1},{9,13},{13,9},{2,6},{6,2},{1... | collective-permute-start | bytes 1966088 | tf_op jit(solution)/shard_map/ppermute | solution.py:100
  46.7 1.6 %copy-start.4 = (f32[640]{0:T(1024)S(1)}, f32[640]{0:T(1024)}, u32[]{:S(2)}) copy-start(f32[640]{0:T(1024)} %param.13) | copy-start | bytes 7684
  48.4 6.5 %collective-permute-start.6 = (bf16[2,128,640]{2,1,0:T(8,128)(2,1)S(1)}, bf16[2,128,640]{2,1,0:T(8,128)(2,1)S(1)}, u32[]{:S(2)}, u32[]{:S(2)}) collective-permute-start(bf16[2,128,640]{2,1,0:T(8,128)(2,1)S(1)} %bitcast.61), channel_id=1, source_target_pairs={{0,4},{4,8},{8,12},{1,5},{5,9},{9,13},{2,6},{6,10},{10,14},{3,7},{... | collective-permute-start | bytes 983048 | tf_op jit(solution)/shard_map/ppermute | solution.py:47
  50.9 8.4 %collective-permute-start.7 = (bf16[2,128,640]{2,1,0:T(8,128)(2,1)S(1)}, bf16[2,128,640]{2,1,0:T(8,128)(2,1)S(1)}, u32[]{:S(2)}, u32[]{:S(2)}) collective-permute-start(bf16[2,128,640]{2,1,0:T(8,128)(2,1)S(1)} %bitcast.62), channel_id=1, source_target_pairs={{4,0},{8,4},{12,8},{5,1},{9,5},{13,9},{6,2},{10,6},{14,10},{7,3},{... | collective-permute-start | bytes 983048 | tf_op jit(solution)/shard_map/ppermute | solution.py:48
  52.9 6.7 %copy-start.3 = (bf16[3,640,640]{2,1,0:T(8,128)(2,1)S(1)}, bf16[3,640,640]{2,1,0:T(8,128)(2,1)}, u32[]{:S(2)}) copy-start(bf16[3,640,640]{2,1,0:T(8,128)(2,1)} %param.14) | copy-start | bytes 7372804
  61.9 1.7 %copy-start.2 = (bf16[3,640,640]{2,1,0:T(8,128)(2,1)S(1)}, bf16[3,640,640]{2,1,0:T(8,128)(2,1)}, u32[]{:S(2)}) copy-start(bf16[3,640,640]{2,1,0:T(8,128)(2,1)} %param.15) | copy-start | bytes 7372804

commit v21 on v14

--- a/solution.py
+++ b/solution.py
@@ -77,7 +77,7 @@
         me == owner_a, lax.dynamic_index_in_dim(own, slot_a, 0, keepdims=False), jnp.zeros_like(own[0])
     )
     got_b = own[n_loc - 1]
-    for s in range(1, fsize):
+    for s in sorted(range(1, fsize), key=lambda s: (s != fsize // 2, s)):
         recv = lax.ppermute(halves((me + s) % 2), "frame", [(i, (i + s) % fsize) for i in range(fsize)])
         source = (me - s) % fsize
         got_a = jnp.where(source == owner_a, lax.dynamic_index_in_dim(recv, slot_a, 0, keepdims=False), got_a)

time: 59.8 us -> 61.6 us (1.030)
  waiting for transfers between devices: 21.2 us -> 22.2 us
  starting transfers between devices: 12 us -> 12.9 us
    ppermute x1, starting transfers between devices: 2.44 us -> 3.58 us  [extended(): before = lax.ppermute(last, axis, up)]
    ppermute x3, waiting for transfers between devices: 0.84 us -> 1.76 us  [gather_keyframes(): lax.ppermute(halves((me + s) % 2), 'frame', [(i, (i + s) % fsize) for i i...]
where the time goes in v21:
time: 61.6 us; the launch traced here: 61.3 us
  waiting for transfers between devices  22.2 us (36%)
  starting transfers between devices  12.9 us (21%)
  matrix products  11.5 us (19%)
  Pallas kernels  5.84 us (9%)
  local copies, waits for them, and re-layouts  4.11 us (7%)
  other arithmetic  3.16 us (5%)
  between operations  1.65 us (3%)
    ppermute x3, waiting for transfers between devices, gather_keyframes(): lax.ppermute(piece, 'row', [(i, (i + s) % rsize) for i in range(rsize)])  13.8 us
    pallas_call x1, Pallas kernels, attend(): pl.pallas_call(attention_kernel, grid=(channels // width,), in_specs=[pl....  5.84 us
    dot_general x6, matrix products, temporal_mix(): jnp.dot(window, weights[offset], preferred_element_type=jnp.float32)  4.44 us
    ppermute x1, waiting for transfers between devices, extended(): after = lax.ppermute(first, axis, down)  4.4 us
    ppermute x3, starting transfers between devices, gather_keyframes(): lax.ppermute(piece, 'row', [(i, (i + s) % rsize) for i in range(rsize)])  3.84 us
    ppermute x1, starting transfers between devices, extended(): before = lax.ppermute(last, axis, up)  3.58 us
    ppermute x3, starting transfers between devices, gather_keyframes(): lax.ppermute(halves((me + s) % 2), 'frame', [(i, (i + s) % fsize) for i i...  3.01 us
    dot_general x1, matrix products, shards(): lax.dot_general(w_query, flattened, (((0,), (1,)), ((), ())), preferred_e...  2.54 us
  transfers between devices with their start and end apart: 9, of which 7 were waited for; matrix products, arithmetic and copies ran while one was open for 9% of the time, Pallas kernels for 0%

profile of v21, /device:TPU:9, one launch (start us, length us, event | category | flops | bytes accessed | tf_op | source)
XLA Modules:
  0.0 61.3 jit_solution(12701363231100919709)
XLA Ops:
  0.0 1.2 %constant_dynamic-slice_fusion.2 = (bf16[2,64,640]{2,1,0:T(8,128)(2,1)S(1)}, bf16[2,64,640]{2,1,0:T(8,128)(2,1)S(1)}, bf16[2,64,640]{2,1,0:T(8,128)(2,1)S(1)}) fusion(bf16[2,128,640]{2,1,0:T(8,128)(2,1)} %param.8, s32[]{:T(128)S(6)} %select_n.137, s32[]{:T(128)S(6)} %select_n.147, s32[]{:T(128)S(6)} %select_n.143), kind=kLoop, calls=%fused_computation.57 | loop fusion | bytes 983052 | tf_op jit(solution)/shard_map/dynamic_slice | solution.py:73
  1.2 0.7 %collective-permute-start = (bf16[2,64,640]{2,1,0:T(8,128)(2,1)S(1)}, bf16[2,64,640]{2,1,0:T(8,128)(2,1)S(1)}, u32[]{:S(2)}, u32[]{:S(2)}) collective-permute-start(bf16[2,64,640]{2,1,0:T(8,128)(2,1)S(1)} %get-tuple-element.16), channel_id=1, source_target_pairs={{0,12},{4,0},{8,4},{12,8},{1,13},{5,1},{9,5},{13,9},{2,14},{6,2},{... | collective-permute-start | bytes 491528 | tf_op jit(solution)/shard_map/ppermute | solution.py:81
  1.9 1.2 %collective-permute-start.1 = (bf16[2,64,640]{2,1,0:T(8,128)(2,1)S(1)}, bf16[2,64,640]{2,1,0:T(8,128)(2,1)S(1)}, u32[]{:S(2)}, u32[]{:S(2)}) collective-permute-start(bf16[2,64,640]{2,1,0:T(8,128)(2,1)S(1)} %get-tuple-element.18), channel_id=1, source_target_pairs={{0,4},{4,8},{8,12},{12,0},{1,5},{5,9},{9,13},{13,1},{2,6},{6,10},{... | collective-permute-start | bytes 491528 | tf_op jit(solution)/shard_map/ppermute | solution.py:81
  3.1 1.1 %collective-permute-start.2 = (bf16[2,64,640]{2,1,0:T(8,128)(2,1)S(1)}, bf16[2,64,640]{2,1,0:T(8,128)(2,1)S(1)}, u32[]{:S(2)}, u32[]{:S(2)}) collective-permute-start(bf16[2,64,640]{2,1,0:T(8,128)(2,1)S(1)} %get-tuple-element.17), channel_id=1, source_target_pairs={{0,8},{4,12},{8,0},{12,4},{1,9},{5,13},{9,1},{13,5},{2,10},{6,14},... | collective-permute-start | bytes 491528 | tf_op jit(solution)/shard_map/ppermute | solution.py:81
  4.2 1.3 %fusion.30 = (s32[1]{0:T(128)}, s32[1]{0:T(128)}) fusion(s32[2]{0:T(128)} %param.9), kind=kLoop, calls=%fused_computation.60 | loop fusion | bytes 16 | tf_op jit(solution)/shard_map/slice | solution.py:66
  7.0 2.5 %fusion.4.qt_ref = bf16[640,256]{1,0:T(8,128)(2,1)} fusion(bf16[640,640]{1,0:T(8,128)(2,1)} %param.10, bf16[256,640]{1,0:T(8,128)(2,1)} %bitcast.54), kind=kOutput, calls=%fused_computation.16 | convolution fusion | flops 210042880 | bytes 1474560 | tf_op jit(solution)/shard_map/dot_general | solution.py:99
  9.6 1.8 %collective-permute-done.2 = bf16[2,64,640]{2,1,0:T(8,128)(2,1)S(1)} collective-permute-done((bf16[2,64,640]{2,1,0:T(8,128)(2,1)S(1)}, bf16[2,64,640]{2,1,0:T(8,128)(2,1)S(1)}, u32[]{:S(2)}, u32[]{:S(2)}) %collective-permute-start.2) | collective-permute-done | bytes 163872 | tf_op jit(solution)/shard_map/ppermute | solution.py:81
  11.5 1.4 %collective-permute-start.3 = (bf16[2,64,640]{2,1,0:T(8,128)(2,1)S(1)}, bf16[2,64,640]{2,1,0:T(8,128)(2,1)S(1)}, u32[]{:S(2)}, u32[]{:S(2)}) collective-permute-start(bf16[2,64,640]{2,1,0:T(8,128)(2,1)S(1)} %pad_maximum_fusion.9), channel_id=1, source_target_pairs={{0,1},{1,2},{2,3},{3,0},{4,5},{5,6},{6,7},{7,4},{8,9},{9,10},{10,1... | collective-permute-start | bytes 491528 | tf_op jit(solution)/shard_map/ppermute | solution.py:89
  12.8 1.1 %collective-permute-start.4 = (bf16[2,64,640]{2,1,0:T(8,128)(2,1)S(1)}, bf16[2,64,640]{2,1,0:T(8,128)(2,1)S(1)}, u32[]{:S(2)}, u32[]{:S(2)}) collective-permute-start(bf16[2,64,640]{2,1,0:T(8,128)(2,1)S(1)} %pad_maximum_fusion.9), channel_id=1, source_target_pairs={{0,2},{1,3},{2,0},{3,1},{4,6},{5,7},{6,4},{7,5},{8,10},{9,11},{10,... | collective-permute-start | bytes 491528 | tf_op jit(solution)/shard_map/ppermute | solution.py:89
  13.9 1.4 %collective-permute-start.5 = (bf16[2,64,640]{2,1,0:T(8,128)(2,1)S(1)}, bf16[2,64,640]{2,1,0:T(8,128)(2,1)S(1)}, u32[]{:S(2)}, u32[]{:S(2)}) collective-permute-start(bf16[2,64,640]{2,1,0:T(8,128)(2,1)S(1)} %pad_maximum_fusion.9), channel_id=1, source_target_pairs={{0,3},{1,0},{2,1},{3,2},{4,7},{5,4},{6,5},{7,6},{8,11},{9,8},{10,9... | collective-permute-start | bytes 491528 | tf_op jit(solution)/shard_map/ppermute | solution.py:89
  15.3 2.1 %collective-permute-done.3 = bf16[2,64,640]{2,1,0:T(8,128)(2,1)S(1)} collective-permute-done((bf16[2,64,640]{2,1,0:T(8,128)(2,1)S(1)}, bf16[2,64,640]{2,1,0:T(8,128)(2,1)S(1)}, u32[]{:S(2)}, u32[]{:S(2)}) %collective-permute-start.3) | collective-permute-done | bytes 163872 | tf_op jit(solution)/shard_map/ppermute | solution.py:89
  17.5 9.6 %collective-permute-done.4 = bf16[2,64,640]{2,1,0:T(8,128)(2,1)S(1)} collective-permute-done((bf16[2,64,640]{2,1,0:T(8,128)(2,1)S(1)}, bf16[2,64,640]{2,1,0:T(8,128)(2,1)S(1)}, u32[]{:S(2)}, u32[]{:S(2)}) %collective-permute-start.4) | collective-permute-done | bytes 163872 | tf_op jit(solution)/shard_map/ppermute | solution.py:89
  27.1 2.0 %collective-permute-done.5 = bf16[2,64,640]{2,1,0:T(8,128)(2,1)S(1)} collective-permute-done((bf16[2,64,640]{2,1,0:T(8,128)(2,1)S(1)}, bf16[2,64,640]{2,1,0:T(8,128)(2,1)S(1)}, u32[]{:S(2)}, u32[]{:S(2)}) %collective-permute-start.5) | collective-permute-done | bytes 163872 | tf_op jit(solution)/shard_map/ppermute | solution.py:89
  29.2 0.5 collective-permute-start.6
  29.7 0.7 %fusion.1 = bf16[640,512]{1,0:T(8,128)(2,1)S(1)} fusion(bf16[512,640]{1,0:T(8,128)(2,1)S(1)} %bitcast.66, bf16[640,1280]{1,0:T(8,128)(2,1)S(1)} %copy-done.5), kind=kOutput, calls=%fused_computation.9 | convolution fusion | flops 419758080 | bytes 2129920 | tf_op jit(solution)/shard_map/dot_general | solution.py:105
  30.4 0.7 %convolution_convert_fusion.3 = bf16[512,640]{1,0:T(8,128)(2,1)S(1)} fusion(bf16[512,640]{1,0:T(8,128)(2,1)S(1)} %bitcast.67, bf16[640,1280]{1,0:T(8,128)(2,1)S(1)} %copy-done.5), kind=kOutput, calls=%fused_computation.5 | convolution fusion | flops 419758080 | bytes 2129920 | tf_op jit(solution)/shard_map/dot_general | solution.py:104
  31.4 0.7 %fusion.2 = bf16[640,512]{1,0:T(8,128)(2,1)S(1)} fusion(bf16[512,640]{1,0:T(8,128)(2,1)S(1)} %collective-permute-done.6, bf16[640,1280]{1,0:T(8,128)(2,1)S(1)} %copy-done.5), kind=kOutput, calls=%fused_computation.10 | convolution fusion | flops 419758080 | bytes 2129920 | tf_op jit(solution)/shard_map/dot_general | solution.py:105
  32.2 1.2 %pad_maximum_fusion.1.vt_ref = bf16[640,1024]{1,0:T(8,128)(2,1)} fusion(bf16[640,512]{1,0:T(8,128)(2,1)S(1)} %fusion.2, bf16[640,512]{1,0:T(8,128)(2,1)S(1)} %fusion.1), kind=kLoop, calls=%fused_computation.7 | loop fusion | flops 2621440 | bytes 2621440 | tf_op jit(solution)/shard_map/concatenate | solution.py:113
  33.4 0.7 %convolution_convert_fusion.2 = bf16[512,640]{1,0:T(8,128)(2,1)S(1)} fusion(bf16[512,640]{1,0:T(8,128)(2,1)S(1)} %collective-permute-done.6, bf16[640,1280]{1,0:T(8,128)(2,1)S(1)} %copy-done.5), kind=kOutput, calls=%fused_computation.4 | convolution fusion | flops 419758080 | bytes 2129920 | tf_op jit(solution)/shard_map/dot_general | solution.py:104
  34.1 1.2 %pad_maximum_fusion.k_ref = bf16[1024,640]{1,0:T(8,128)(2,1)} fusion(bf16[512,640]{1,0:T(8,128)(2,1)S(1)} %convolution_convert_fusion.2, bf16[512,640]{1,0:T(8,128)(2,1)S(1)} %convolution_convert_fusion.3), kind=kLoop, calls=%fused_computation.6 | loop fusion | flops 2621440 | bytes 2621440 | tf_op jit(solution)/shard_map/concatenate | solution.py:112
  35.3 5.8 %shard_map.82 = bf16[640,256]{1,0:T(8,128)(2,1)} custom-call(bf16[1024,640]{1,0:T(8,128)(2,1)} %pad_maximum_fusion.k_ref, bf16[640,256]{1,0:T(8,128)(2,1)} %fusion.4.qt_ref, bf16[640,1024]{1,0:T(8,128)(2,1)} %pad_maximum_fusion.1.vt_ref), custom_call_target="tpu_custom_call" | custom-call | tf_op jit(solution)/shard_map/pallas_call | solution.py:28
  41.2 1.6 %multiply_reduce_fusion = (f32[256]{0:T(256)S(1)}, f32[256,640]{1,0:T(8,128)S(1)}) fusion(bf16[640,256]{1,0:T(8,128)(2,1)} %shard_map.82, bf16[640,640]{1,0:T(8,128)(2,1)S(1)} %copy-done, bf16[256,640]{1,0:T(8,128)(2,1)S(1)} %bitcast.55), kind=kOutput, calls=%fused_computation.43 | convolution fusion | flops 210370304 | bytes 2130944 | tf_op jit(solution)/shard_map/dot_general | solution.py:115
  42.9 3.6 %collective-permute-start.7 = (bf16[2,128,640]{2,1,0:T(8,128)(2,1)S(1)}, bf16[2,128,640]{2,1,0:T(8,128)(2,1)S(1)}, u32[]{:S(2)}, u32[]{:S(2)}) collective-permute-start(bf16[2,128,640]{2,1,0:T(8,128)(2,1)S(1)} %bitcast.61), channel_id=1, source_target_pairs={{0,4},{4,8},{8,12},{1,5},{5,9},{9,13},{2,6},{6,10},{10,14},{3,7},{... | collective-permute-start | bytes 983048 | tf_op jit(solution)/shard_map/ppermute | solution.py:47
  46.5 1.9 %collective-permute-start.8 = (bf16[2,128,640]{2,1,0:T(8,128)(2,1)S(1)}, bf16[2,128,640]{2,1,0:T(8,128)(2,1)S(1)}, u32[]{:S(2)}, u32[]{:S(2)}) collective-permute-start(bf16[2,128,640]{2,1,0:T(8,128)(2,1)S(1)} %bitcast.62), channel_id=1, source_target_pairs={{4,0},{8,4},{12,8},{5,1},{9,5},{13,9},{6,2},{10,6},{14,10},{7,3},{... | collective-permute-start | bytes 983048 | tf_op jit(solution)/shard_map/ppermute | solution.py:48
  48.4 2.0 %collective-permute-done.7 = bf16[2,128,640]{2,1,0:T(8,128)(2,1)S(1)} collective-permute-done((bf16[2,128,640]{2,1,0:T(8,128)(2,1)S(1)}, bf16[2,128,640]{2,1,0:T(8,128)(2,1)S(1)}, u32[]{:S(2)}, u32[]{:S(2)}) %collective-permute-start.7) | collective-permute-done | bytes 327712 | tf_op jit(solution)/shard_map/ppermute | solution.py:47
  50.5 4.4 %collective-permute-done.8 = bf16[2,128,640]{2,1,0:T(8,128)(2,1)S(1)} collective-permute-done((bf16[2,128,640]{2,1,0:T(8,128)(2,1)S(1)}, bf16[2,128,640]{2,1,0:T(8,128)(2,1)S(1)}, u32[]{:S(2)}, u32[]{:S(2)}) %collective-permute-start.8) | collective-permute-done | bytes 327712 | tf_op jit(solution)/shard_map/ppermute | solution.py:48
  55.1 0.7 %fusion.10 = f32[512,640]{1,0:T(8,128)S(1)} fusion(bf16[512,640]{1,0:T(8,128)(2,1)S(1)} %bitcast.57, bf16[3,640,640]{2,1,0:T(8,128)(2,1)S(1)} %copy-done.3), kind=kOutput, calls=%fused_computation.22 | convolution fusion | flops 419430400 | bytes 2785280 | tf_op jit(solution)/shard_map/dot_general | solution.py:56
  55.9 0.7 %fusion.12 = f32[512,640]{1,0:T(8,128)S(1)} fusion(bf16[512,640]{1,0:T(8,128)(2,1)S(1)} %bitcast.56, bf16[3,640,640]{2,1,0:T(8,128)(2,1)S(1)} %copy-done.3), kind=kOutput, calls=%fused_computation.24 | convolution fusion | flops 419430400 | bytes 2785280 | tf_op jit(solution)/shard_map/dot_general | solution.py:56
  56.6 0.8 %multiply_convert_fusion = bf16[512,640]{1,0:T(8,128)(2,1)S(1)} fusion(f32[512,640]{1,0:T(8,128)S(1)} %fusion.10, f32[512,640]{1,0:T(8,128)S(1)} %fusion.12, bf16[512,640]{1,0:T(8,128)(2,1)S(1)} %bitcast.68, bf16[3,640,640]{2,1,0:T(8,128)(2,1)S(1)} %copy-done.3), kind=kOutput, calls=%fused_computation.8 | convolution fusion | flops 421724160 | bytes 4751360 | tf_op jit(solution)/shard_map/dot_general | solution.py:56
  57.7 1.5 %copy-done.2 = bf16[3,640,640]{2,1,0:T(8,128)(2,1)S(1)} copy-done((bf16[3,640,640]{2,1,0:T(8,128)(2,1)S(1)}, bf16[3,640,640]{2,1,0:T(8,128)(2,1)}, u32[]{:S(2)}) %copy-start.2) | copy-done | bytes 2457624
  59.6 0.5 convolution_add_fusion.2
  60.1 1.2 %fusion.5 = bf16[256,640]{1,0:T(8,128)(2,1)} fusion(f32[256,640]{1,0:T(8,128)S(1)} %get-tuple-element.22, f32[256,640]{1,0:T(8,128)S(1)} %convolution_add_fusion.2, bf16[256,640]{1,0:T(8,128)(2,1)S(1)} %bitcast.60, bf16[3,640,640]{2,1,0:T(8,128)(2,1)S(1)} %copy-done.2), kind=kOutput, calls=%fused_computation.17 | convolution fusion | flops 210206720 | bytes 2785280 | tf_op jit(solution)/shard_map/dot_general | solution.py:56
  (24 shorter events, 1.5 us)
Async XLA Ops:
  0.0 41.2 %copy-start = (bf16[640,640]{1,0:T(8,128)(2,1)S(1)}, bf16[640,640]{1,0:T(8,128)(2,1)}, u32[]{:S(2)}) copy-start(bf16[640,640]{1,0:T(8,128)(2,1)} %param.12) | copy-start | bytes 2457604
  0.0 11.3 %copy-start.1 = (bf16[2,128,640]{2,1,0:T(8,128)(2,1)S(1)}, bf16[2,128,640]{2,1,0:T(8,128)(2,1)}, u32[]{:S(2)}) copy-start(bf16[2,128,640]{2,1,0:T(8,128)(2,1)} %param.8) | copy-start | bytes 983044
  1.2 8.3 %collective-permute-start = (bf16[2,64,640]{2,1,0:T(8,128)(2,1)S(1)}, bf16[2,64,640]{2,1,0:T(8,128)(2,1)S(1)}, u32[]{:S(2)}, u32[]{:S(2)}) collective-permute-start(bf16[2,64,640]{2,1,0:T(8,128)(2,1)S(1)} %get-tuple-element.16), channel_id=1, source_target_pairs={{0,12},{4,0},{8,4},{12,8},{1,13},{5,1},{9,5},{13,9},{2,14},{6,2},{... | collective-permute-start | bytes 491528 | tf_op jit(solution)/shard_map/ppermute | solution.py:81
  1.9 7.6 %collective-permute-start.1 = (bf16[2,64,640]{2,1,0:T(8,128)(2,1)S(1)}, bf16[2,64,640]{2,1,0:T(8,128)(2,1)S(1)}, u32[]{:S(2)}, u32[]{:S(2)}) collective-permute-start(bf16[2,64,640]{2,1,0:T(8,128)(2,1)S(1)} %get-tuple-element.18), channel_id=1, source_target_pairs={{0,4},{4,8},{8,12},{12,0},{1,5},{5,9},{9,13},{13,1},{2,6},{6,10},{... | collective-permute-start | bytes 491528 | tf_op jit(solution)/shard_map/ppermute | solution.py:81
  3.1 8.2 %collective-permute-start.2 = (bf16[2,64,640]{2,1,0:T(8,128)(2,1)S(1)}, bf16[2,64,640]{2,1,0:T(8,128)(2,1)S(1)}, u32[]{:S(2)}, u32[]{:S(2)}) collective-permute-start(bf16[2,64,640]{2,1,0:T(8,128)(2,1)S(1)} %get-tuple-element.17), channel_id=1, source_target_pairs={{0,8},{4,12},{8,0},{12,4},{1,9},{5,13},{9,1},{13,5},{2,10},{6,14},... | collective-permute-start | bytes 491528 | tf_op jit(solution)/shard_map/ppermute | solution.py:81
  7.0 22.7 %copy-start.5 = (bf16[640,1280]{1,0:T(8,128)(2,1)S(1)}, bf16[640,1280]{1,0:T(8,128)(2,1)}, u32[]{:S(2)}) copy-start(bf16[640,1280]{1,0:T(8,128)(2,1)} %param.11) | copy-start | bytes 4915204
  11.5 6.0 %collective-permute-start.3 = (bf16[2,64,640]{2,1,0:T(8,128)(2,1)S(1)}, bf16[2,64,640]{2,1,0:T(8,128)(2,1)S(1)}, u32[]{:S(2)}, u32[]{:S(2)}) collective-permute-start(bf16[2,64,640]{2,1,0:T(8,128)(2,1)S(1)} %pad_maximum_fusion.9), channel_id=1, source_target_pairs={{0,1},{1,2},{2,3},{3,0},{4,5},{5,6},{6,7},{7,4},{8,9},{9,10},{10,1... | collective-permute-start | bytes 491528 | tf_op jit(solution)/shard_map/ppermute | solution.py:89
  12.8 14.3 %collective-permute-start.4 = (bf16[2,64,640]{2,1,0:T(8,128)(2,1)S(1)}, bf16[2,64,640]{2,1,0:T(8,128)(2,1)S(1)}, u32[]{:S(2)}, u32[]{:S(2)}) collective-permute-start(bf16[2,64,640]{2,1,0:T(8,128)(2,1)S(1)} %pad_maximum_fusion.9), channel_id=1, source_target_pairs={{0,2},{1,3},{2,0},{3,1},{4,6},{5,7},{6,4},{7,5},{8,10},{9,11},{10,... | collective-permute-start | bytes 491528 | tf_op jit(solution)/shard_map/ppermute | solution.py:89
  13.9 15.2 %collective-permute-start.5 = (bf16[2,64,640]{2,1,0:T(8,128)(2,1)S(1)}, bf16[2,64,640]{2,1,0:T(8,128)(2,1)S(1)}, u32[]{:S(2)}, u32[]{:S(2)}) collective-permute-start(bf16[2,64,640]{2,1,0:T(8,128)(2,1)S(1)} %pad_maximum_fusion.9), channel_id=1, source_target_pairs={{0,3},{1,0},{2,1},{3,2},{4,7},{5,4},{6,5},{7,6},{8,11},{9,8},{10,9... | collective-permute-start | bytes 491528 | tf_op jit(solution)/shard_map/ppermute | solution.py:89
  29.2 2.2 %collective-permute-start.6 = (bf16[512,640]{1,0:T(8,128)(2,1)S(1)}, bf16[512,640]{1,0:T(8,128)(2,1)S(1)}, u32[]{:S(2)}, u32[]{:S(2)}) collective-permute-start(bf16[512,640]{1,0:T(8,128)(2,1)S(1)} %bitcast.65), channel_id=1, source_target_pairs={{0,4},{4,0},{8,12},{12,8},{1,5},{5,1},{9,13},{13,9},{2,6},{6,2},{1... | collective-permute-start | bytes 1966088 | tf_op jit(solution)/shard_map/ppermute | solution.py:91
  41.2 1.6 %copy-start.4 = (f32[640]{0:T(1024)S(1)}, f32[640]{0:T(1024)}, u32[]{:S(2)}) copy-start(f32[640]{0:T(1024)} %param.13) | copy-start | bytes 7684
  42.9 7.6 %collective-permute-start.7 = (bf16[2,128,640]{2,1,0:T(8,128)(2,1)S(1)}, bf16[2,128,640]{2,1,0:T(8,128)(2,1)S(1)}, u32[]{:S(2)}, u32[]{:S(2)}) collective-permute-start(bf16[2,128,640]{2,1,0:T(8,128)(2,1)S(1)} %bitcast.61), channel_id=1, source_target_pairs={{0,4},{4,8},{8,12},{1,5},{5,9},{9,13},{2,6},{6,10},{10,14},{3,7},{... | collective-permute-start | bytes 983048 | tf_op jit(solution)/shard_map/ppermute | solution.py:47
  46.5 8.4 %collective-permute-start.8 = (bf16[2,128,640]{2,1,0:T(8,128)(2,1)S(1)}, bf16[2,128,640]{2,1,0:T(8,128)(2,1)S(1)}, u32[]{:S(2)}, u32[]{:S(2)}) collective-permute-start(bf16[2,128,640]{2,1,0:T(8,128)(2,1)S(1)} %bitcast.62), channel_id=1, source_target_pairs={{4,0},{8,4},{12,8},{5,1},{9,5},{13,9},{6,2},{10,6},{14,10},{7,3},{... | collective-permute-start | bytes 983048 | tf_op jit(solution)/shard_map/ppermute | solution.py:48
  48.4 6.7 %copy-start.3 = (bf16[3,640,640]{2,1,0:T(8,128)(2,1)S(1)}, bf16[3,640,640]{2,1,0:T(8,128)(2,1)}, u32[]{:S(2)}) copy-start(bf16[3,640,640]{2,1,0:T(8,128)(2,1)} %param.14) | copy-start | bytes 7372804
  57.5 1.7 %copy-start.2 = (bf16[3,640,640]{2,1,0:T(8,128)(2,1)S(1)}, bf16[3,640,640]{2,1,0:T(8,128)(2,1)}, u32[]{:S(2)}) copy-start(bf16[3,640,640]{2,1,0:T(8,128)(2,1)} %param.15) | copy-start | bytes 7372804

commit v22 on v21

--- a/solution.py
+++ b/solution.py
@@ -77,7 +77,7 @@
         me == owner_a, lax.dynamic_index_in_dim(own, slot_a, 0, keepdims=False), jnp.zeros_like(own[0])
     )
     got_b = own[n_loc - 1]
-    for s in sorted(range(1, fsize), key=lambda s: (s != fsize // 2, s)):
+    for s in sorted(range(1, fsize), key=lambda s: (s == fsize // 2, s)):
         recv = lax.ppermute(halves((me + s) % 2), "frame", [(i, (i + s) % fsize) for i in range(fsize)])
         source = (me - s) % fsize
         got_a = jnp.where(source == owner_a, lax.dynamic_index_in_dim(recv, slot_a, 0, keepdims=False), got_a)

time: 61.6 us -> 60.8 us (0.987)
  no operation moved by 1% of the time
where the time goes in v22:
time: 60.8 us; the launch traced here: 60.5 us
  waiting for transfers between devices  21.7 us (36%)
  starting transfers between devices  12.6 us (21%)
  matrix products  11.5 us (19%)
  Pallas kernels  5.84 us (10%)
  local copies, waits for them, and re-layouts  4.11 us (7%)
  other arithmetic  3.16 us (5%)
  between operations  1.65 us (3%)
    ppermute x3, waiting for transfers between devices, gather_keyframes(): lax.ppermute(piece, 'row', [(i, (i + s) % rsize) for i in range(rsize)])  13.8 us
    pallas_call x1, Pallas kernels, attend(): pl.pallas_call(attention_kernel, grid=(channels // width,), in_specs=[pl....  5.84 us
    dot_general x6, matrix products, temporal_mix(): jnp.dot(window, weights[offset], preferred_element_type=jnp.float32)  4.43 us
    ppermute x1, waiting for transfers between devices, extended(): after = lax.ppermute(first, axis, down)  4.4 us
    ppermute x3, starting transfers between devices, gather_keyframes(): lax.ppermute(piece, 'row', [(i, (i + s) % rsize) for i in range(rsize)])  3.83 us
    ppermute x1, starting transfers between devices, extended(): before = lax.ppermute(last, axis, up)  3.31 us
    ppermute x3, starting transfers between devices, gather_keyframes(): lax.ppermute(halves((me + s) % 2), 'frame', [(i, (i + s) % fsize) for i i...  3.02 us
    dot_general x1, matrix products, shards(): lax.dot_general(w_query, flattened, (((0,), (1,)), ((), ())), preferred_e...  2.54 us
  transfers between devices with their start and end apart: 9, of which 7 were waited for; matrix products, arithmetic and copies ran while one was open for 9% of the time, Pallas kernels for 0%

profile of v22, /device:TPU:9, one launch (start us, length us, event | category | flops | bytes accessed | tf_op | source)
XLA Modules:
  0.0 60.5 jit_solution(509309879415652062)
XLA Ops:
  0.0 1.2 %constant_dynamic-slice_fusion.2 = (bf16[2,64,640]{2,1,0:T(8,128)(2,1)S(1)}, bf16[2,64,640]{2,1,0:T(8,128)(2,1)S(1)}, bf16[2,64,640]{2,1,0:T(8,128)(2,1)S(1)}) fusion(bf16[2,128,640]{2,1,0:T(8,128)(2,1)} %param.8, s32[]{:T(128)S(6)} %select_n.137, s32[]{:T(128)S(6)} %select_n.147, s32[]{:T(128)S(6)} %select_n.143), kind=kLoop, calls=%fused_computation.57 | loop fusion | bytes 983052 | tf_op jit(solution)/shard_map/dynamic_slice | solution.py:73
  1.2 1.3 %collective-permute-start = (bf16[2,64,640]{2,1,0:T(8,128)(2,1)S(1)}, bf16[2,64,640]{2,1,0:T(8,128)(2,1)S(1)}, u32[]{:S(2)}, u32[]{:S(2)}) collective-permute-start(bf16[2,64,640]{2,1,0:T(8,128)(2,1)S(1)} %get-tuple-element.16), channel_id=1, source_target_pairs={{0,8},{4,12},{8,0},{12,4},{1,9},{5,13},{9,1},{13,5},{2,10},{6,14},... | collective-permute-start | bytes 491528 | tf_op jit(solution)/shard_map/ppermute | solution.py:81
  2.5 1.0 %collective-permute-start.1 = (bf16[2,64,640]{2,1,0:T(8,128)(2,1)S(1)}, bf16[2,64,640]{2,1,0:T(8,128)(2,1)S(1)}, u32[]{:S(2)}, u32[]{:S(2)}) collective-permute-start(bf16[2,64,640]{2,1,0:T(8,128)(2,1)S(1)} %get-tuple-element.18), channel_id=1, source_target_pairs={{0,12},{4,0},{8,4},{12,8},{1,13},{5,1},{9,5},{13,9},{2,14},{6,2},{... | collective-permute-start | bytes 491528 | tf_op jit(solution)/shard_map/ppermute | solution.py:81
  3.5 0.8 %collective-permute-start.2 = (bf16[2,64,640]{2,1,0:T(8,128)(2,1)S(1)}, bf16[2,64,640]{2,1,0:T(8,128)(2,1)S(1)}, u32[]{:S(2)}, u32[]{:S(2)}) collective-permute-start(bf16[2,64,640]{2,1,0:T(8,128)(2,1)S(1)} %get-tuple-element.17), channel_id=1, source_target_pairs={{0,4},{4,8},{8,12},{12,0},{1,5},{5,9},{9,13},{13,1},{2,6},{6,10},{... | collective-permute-start | bytes 491528 | tf_op jit(solution)/shard_map/ppermute | solution.py:81
  4.2 1.3 %fusion.30 = (s32[1]{0:T(128)}, s32[1]{0:T(128)}) fusion(s32[2]{0:T(128)} %param.9), kind=kLoop, calls=%fused_computation.60 | loop fusion | bytes 16 | tf_op jit(solution)/shard_map/slice | solution.py:66
  7.0 2.5 %fusion.4.qt_ref = bf16[640,256]{1,0:T(8,128)(2,1)} fusion(bf16[640,640]{1,0:T(8,128)(2,1)} %param.10, bf16[256,640]{1,0:T(8,128)(2,1)} %bitcast.54), kind=kOutput, calls=%fused_computation.16 | convolution fusion | flops 210042880 | bytes 1474560 | tf_op jit(solution)/shard_map/dot_general | solution.py:99
  9.6 1.2 %collective-permute-done.1 = bf16[2,64,640]{2,1,0:T(8,128)(2,1)S(1)} collective-permute-done((bf16[2,64,640]{2,1,0:T(8,128)(2,1)S(1)}, bf16[2,64,640]{2,1,0:T(8,128)(2,1)S(1)}, u32[]{:S(2)}, u32[]{:S(2)}) %collective-permute-start.1) | collective-permute-done | bytes 163872 | tf_op jit(solution)/shard_map/ppermute | solution.py:81
  10.9 1.3 %collective-permute-start.3 = (bf16[2,64,640]{2,1,0:T(8,128)(2,1)S(1)}, bf16[2,64,640]{2,1,0:T(8,128)(2,1)S(1)}, u32[]{:S(2)}, u32[]{:S(2)}) collective-permute-start(bf16[2,64,640]{2,1,0:T(8,128)(2,1)S(1)} %pad_maximum_fusion.9), channel_id=1, source_target_pairs={{0,1},{1,2},{2,3},{3,0},{4,5},{5,6},{6,7},{7,4},{8,9},{9,10},{10,1... | collective-permute-start | bytes 491528 | tf_op jit(solution)/shard_map/ppermute | solution.py:89
  12.2 1.1 %collective-permute-start.4 = (bf16[2,64,640]{2,1,0:T(8,128)(2,1)S(1)}, bf16[2,64,640]{2,1,0:T(8,128)(2,1)S(1)}, u32[]{:S(2)}, u32[]{:S(2)}) collective-permute-start(bf16[2,64,640]{2,1,0:T(8,128)(2,1)S(1)} %pad_maximum_fusion.9), channel_id=1, source_target_pairs={{0,2},{1,3},{2,0},{3,1},{4,6},{5,7},{6,4},{7,5},{8,10},{9,11},{10,... | collective-permute-start | bytes 491528 | tf_op jit(solution)/shard_map/ppermute | solution.py:89
  13.3 1.4 %collective-permute-start.5 = (bf16[2,64,640]{2,1,0:T(8,128)(2,1)S(1)}, bf16[2,64,640]{2,1,0:T(8,128)(2,1)S(1)}, u32[]{:S(2)}, u32[]{:S(2)}) collective-permute-start(bf16[2,64,640]{2,1,0:T(8,128)(2,1)S(1)} %pad_maximum_fusion.9), channel_id=1, source_target_pairs={{0,3},{1,0},{2,1},{3,2},{4,7},{5,4},{6,5},{7,6},{8,11},{9,8},{10,9... | collective-permute-start | bytes 491528 | tf_op jit(solution)/shard_map/ppermute | solution.py:89
  14.7 2.3 %collective-permute-done.3 = bf16[2,64,640]{2,1,0:T(8,128)(2,1)S(1)} collective-permute-done((bf16[2,64,640]{2,1,0:T(8,128)(2,1)S(1)}, bf16[2,64,640]{2,1,0:T(8,128)(2,1)S(1)}, u32[]{:S(2)}, u32[]{:S(2)}) %collective-permute-start.3) | collective-permute-done | bytes 163872 | tf_op jit(solution)/shard_map/ppermute | solution.py:89
  17.0 9.6 %collective-permute-done.4 = bf16[2,64,640]{2,1,0:T(8,128)(2,1)S(1)} collective-permute-done((bf16[2,64,640]{2,1,0:T(8,128)(2,1)S(1)}, bf16[2,64,640]{2,1,0:T(8,128)(2,1)S(1)}, u32[]{:S(2)}, u32[]{:S(2)}) %collective-permute-start.4) | collective-permute-done | bytes 163872 | tf_op jit(solution)/shard_map/ppermute | solution.py:89
  26.6 1.9 %collective-permute-done.5 = bf16[2,64,640]{2,1,0:T(8,128)(2,1)S(1)} collective-permute-done((bf16[2,64,640]{2,1,0:T(8,128)(2,1)S(1)}, bf16[2,64,640]{2,1,0:T(8,128)(2,1)S(1)}, u32[]{:S(2)}, u32[]{:S(2)}) %collective-permute-start.5) | collective-permute-done | bytes 163872 | tf_op jit(solution)/shard_map/ppermute | solution.py:89
  28.6 0.5 collective-permute-start.6
  29.1 0.7 %fusion.1 = bf16[640,512]{1,0:T(8,128)(2,1)S(1)} fusion(bf16[512,640]{1,0:T(8,128)(2,1)S(1)} %bitcast.66, bf16[640,1280]{1,0:T(8,128)(2,1)S(1)} %copy-done.5), kind=kOutput, calls=%fused_computation.9 | convolution fusion | flops 419758080 | bytes 2129920 | tf_op jit(solution)/shard_map/dot_general | solution.py:105
  29.9 0.7 %convolution_convert_fusion.3 = bf16[512,640]{1,0:T(8,128)(2,1)S(1)} fusion(bf16[512,640]{1,0:T(8,128)(2,1)S(1)} %bitcast.67, bf16[640,1280]{1,0:T(8,128)(2,1)S(1)} %copy-done.5), kind=kOutput, calls=%fused_computation.5 | convolution fusion | flops 419758080 | bytes 2129920 | tf_op jit(solution)/shard_map/dot_general | solution.py:104
  30.9 0.7 %fusion.2 = bf16[640,512]{1,0:T(8,128)(2,1)S(1)} fusion(bf16[512,640]{1,0:T(8,128)(2,1)S(1)} %collective-permute-done.6, bf16[640,1280]{1,0:T(8,128)(2,1)S(1)} %copy-done.5), kind=kOutput, calls=%fused_computation.10 | convolution fusion | flops 419758080 | bytes 2129920 | tf_op jit(solution)/shard_map/dot_general | solution.py:105
  31.6 1.2 %pad_maximum_fusion.1.vt_ref = bf16[640,1024]{1,0:T(8,128)(2,1)} fusion(bf16[640,512]{1,0:T(8,128)(2,1)S(1)} %fusion.2, bf16[640,512]{1,0:T(8,128)(2,1)S(1)} %fusion.1), kind=kLoop, calls=%fused_computation.7 | loop fusion | flops 2621440 | bytes 2621440 | tf_op jit(solution)/shard_map/concatenate | solution.py:113
  32.8 0.7 %convolution_convert_fusion.2 = bf16[512,640]{1,0:T(8,128)(2,1)S(1)} fusion(bf16[512,640]{1,0:T(8,128)(2,1)S(1)} %collective-permute-done.6, bf16[640,1280]{1,0:T(8,128)(2,1)S(1)} %copy-done.5), kind=kOutput, calls=%fused_computation.4 | convolution fusion | flops 419758080 | bytes 2129920 | tf_op jit(solution)/shard_map/dot_general | solution.py:104
  33.6 1.2 %pad_maximum_fusion.k_ref = bf16[1024,640]{1,0:T(8,128)(2,1)} fusion(bf16[512,640]{1,0:T(8,128)(2,1)S(1)} %convolution_convert_fusion.2, bf16[512,640]{1,0:T(8,128)(2,1)S(1)} %convolution_convert_fusion.3), kind=kLoop, calls=%fused_computation.6 | loop fusion | flops 2621440 | bytes 2621440 | tf_op jit(solution)/shard_map/concatenate | solution.py:112
  34.8 5.8 %shard_map.82 = bf16[640,256]{1,0:T(8,128)(2,1)} custom-call(bf16[1024,640]{1,0:T(8,128)(2,1)} %pad_maximum_fusion.k_ref, bf16[640,256]{1,0:T(8,128)(2,1)} %fusion.4.qt_ref, bf16[640,1024]{1,0:T(8,128)(2,1)} %pad_maximum_fusion.1.vt_ref), custom_call_target="tpu_custom_call" | custom-call | tf_op jit(solution)/shard_map/pallas_call | solution.py:28
  40.6 1.6 %multiply_reduce_fusion = (f32[256]{0:T(256)S(1)}, f32[256,640]{1,0:T(8,128)S(1)}) fusion(bf16[640,256]{1,0:T(8,128)(2,1)} %shard_map.82, bf16[640,640]{1,0:T(8,128)(2,1)S(1)} %copy-done, bf16[256,640]{1,0:T(8,128)(2,1)S(1)} %bitcast.55), kind=kOutput, calls=%fused_computation.43 | convolution fusion | flops 210370304 | bytes 2130944 | tf_op jit(solution)/shard_map/dot_general | solution.py:115
  42.3 3.3 %collective-permute-start.7 = (bf16[2,128,640]{2,1,0:T(8,128)(2,1)S(1)}, bf16[2,128,640]{2,1,0:T(8,128)(2,1)S(1)}, u32[]{:S(2)}, u32[]{:S(2)}) collective-permute-start(bf16[2,128,640]{2,1,0:T(8,128)(2,1)S(1)} %bitcast.61), channel_id=1, source_target_pairs={{0,4},{4,8},{8,12},{1,5},{5,9},{9,13},{2,6},{6,10},{10,14},{3,7},{... | collective-permute-start | bytes 983048 | tf_op jit(solution)/shard_map/ppermute | solution.py:47
  45.7 1.9 %collective-permute-start.8 = (bf16[2,128,640]{2,1,0:T(8,128)(2,1)S(1)}, bf16[2,128,640]{2,1,0:T(8,128)(2,1)S(1)}, u32[]{:S(2)}, u32[]{:S(2)}) collective-permute-start(bf16[2,128,640]{2,1,0:T(8,128)(2,1)S(1)} %bitcast.62), channel_id=1, source_target_pairs={{4,0},{8,4},{12,8},{5,1},{9,5},{13,9},{6,2},{10,6},{14,10},{7,3},{... | collective-permute-start | bytes 983048 | tf_op jit(solution)/shard_map/ppermute | solution.py:48
  47.6 2.0 %collective-permute-done.7 = bf16[2,128,640]{2,1,0:T(8,128)(2,1)S(1)} collective-permute-done((bf16[2,128,640]{2,1,0:T(8,128)(2,1)S(1)}, bf16[2,128,640]{2,1,0:T(8,128)(2,1)S(1)}, u32[]{:S(2)}, u32[]{:S(2)}) %collective-permute-start.7) | collective-permute-done | bytes 327712 | tf_op jit(solution)/shard_map/ppermute | solution.py:47
  49.6 4.4 %collective-permute-done.8 = bf16[2,128,640]{2,1,0:T(8,128)(2,1)S(1)} collective-permute-done((bf16[2,128,640]{2,1,0:T(8,128)(2,1)S(1)}, bf16[2,128,640]{2,1,0:T(8,128)(2,1)S(1)}, u32[]{:S(2)}, u32[]{:S(2)}) %collective-permute-start.8) | collective-permute-done | bytes 327712 | tf_op jit(solution)/shard_map/ppermute | solution.py:48
  54.3 0.7 %fusion.10 = f32[512,640]{1,0:T(8,128)S(1)} fusion(bf16[512,640]{1,0:T(8,128)(2,1)S(1)} %bitcast.57, bf16[3,640,640]{2,1,0:T(8,128)(2,1)S(1)} %copy-done.3), kind=kOutput, calls=%fused_computation.22 | convolution fusion | flops 419430400 | bytes 2785280 | tf_op jit(solution)/shard_map/dot_general | solution.py:56
  55.0 0.7 %fusion.12 = f32[512,640]{1,0:T(8,128)S(1)} fusion(bf16[512,640]{1,0:T(8,128)(2,1)S(1)} %bitcast.56, bf16[3,640,640]{2,1,0:T(8,128)(2,1)S(1)} %copy-done.3), kind=kOutput, calls=%fused_computation.24 | convolution fusion | flops 419430400 | bytes 2785280 | tf_op jit(solution)/shard_map/dot_general | solution.py:56
  55.8 0.8 %multiply_convert_fusion = bf16[512,640]{1,0:T(8,128)(2,1)S(1)} fusion(f32[512,640]{1,0:T(8,128)S(1)} %fusion.10, f32[512,640]{1,0:T(8,128)S(1)} %fusion.12, bf16[512,640]{1,0:T(8,128)(2,1)S(1)} %bitcast.68, bf16[3,640,640]{2,1,0:T(8,128)(2,1)S(1)} %copy-done.3), kind=kOutput, calls=%fused_computation.8 | convolution fusion | flops 421724160 | bytes 4751360 | tf_op jit(solution)/shard_map/dot_general | solution.py:56
  56.8 1.5 %copy-done.2 = bf16[3,640,640]{2,1,0:T(8,128)(2,1)S(1)} copy-done((bf16[3,640,640]{2,1,0:T(8,128)(2,1)S(1)}, bf16[3,640,640]{2,1,0:T(8,128)(2,1)}, u32[]{:S(2)}) %copy-start.2) | copy-done | bytes 2457624
  58.8 0.5 convolution_add_fusion.2
  59.3 1.2 %fusion.5 = bf16[256,640]{1,0:T(8,128)(2,1)} fusion(f32[256,640]{1,0:T(8,128)S(1)} %get-tuple-element.22, f32[256,640]{1,0:T(8,128)S(1)} %convolution_add_fusion.2, bf16[256,640]{1,0:T(8,128)(2,1)S(1)} %bitcast.60, bf16[3,640,640]{2,1,0:T(8,128)(2,1)S(1)} %copy-done.2), kind=kOutput, calls=%fused_computation.17 | convolution fusion | flops 210206720 | bytes 2785280 | tf_op jit(solution)/shard_map/dot_general | solution.py:56
  (24 shorter events, 1.5 us)
Async XLA Ops:
  0.0 40.6 %copy-start = (bf16[640,640]{1,0:T(8,128)(2,1)S(1)}, bf16[640,640]{1,0:T(8,128)(2,1)}, u32[]{:S(2)}) copy-start(bf16[640,640]{1,0:T(8,128)(2,1)} %param.12) | copy-start | bytes 2457604
  0.0 10.7 %copy-start.1 = (bf16[2,128,640]{2,1,0:T(8,128)(2,1)S(1)}, bf16[2,128,640]{2,1,0:T(8,128)(2,1)}, u32[]{:S(2)}) copy-start(bf16[2,128,640]{2,1,0:T(8,128)(2,1)} %param.8) | copy-start | bytes 983044
  1.2 8.3 %collective-permute-start = (bf16[2,64,640]{2,1,0:T(8,128)(2,1)S(1)}, bf16[2,64,640]{2,1,0:T(8,128)(2,1)S(1)}, u32[]{:S(2)}, u32[]{:S(2)}) collective-permute-start(bf16[2,64,640]{2,1,0:T(8,128)(2,1)S(1)} %get-tuple-element.16), channel_id=1, source_target_pairs={{0,8},{4,12},{8,0},{12,4},{1,9},{5,13},{9,1},{13,5},{2,10},{6,14},... | collective-permute-start | bytes 491528 | tf_op jit(solution)/shard_map/ppermute | solution.py:81
  2.5 8.2 %collective-permute-start.1 = (bf16[2,64,640]{2,1,0:T(8,128)(2,1)S(1)}, bf16[2,64,640]{2,1,0:T(8,128)(2,1)S(1)}, u32[]{:S(2)}, u32[]{:S(2)}) collective-permute-start(bf16[2,64,640]{2,1,0:T(8,128)(2,1)S(1)} %get-tuple-element.18), channel_id=1, source_target_pairs={{0,12},{4,0},{8,4},{12,8},{1,13},{5,1},{9,5},{13,9},{2,14},{6,2},{... | collective-permute-start | bytes 491528 | tf_op jit(solution)/shard_map/ppermute | solution.py:81
  3.5 7.3 %collective-permute-start.2 = (bf16[2,64,640]{2,1,0:T(8,128)(2,1)S(1)}, bf16[2,64,640]{2,1,0:T(8,128)(2,1)S(1)}, u32[]{:S(2)}, u32[]{:S(2)}) collective-permute-start(bf16[2,64,640]{2,1,0:T(8,128)(2,1)S(1)} %get-tuple-element.17), channel_id=1, source_target_pairs={{0,4},{4,8},{8,12},{12,0},{1,5},{5,9},{9,13},{13,1},{2,6},{6,10},{... | collective-permute-start | bytes 491528 | tf_op jit(solution)/shard_map/ppermute | solution.py:81
  7.0 22.1 %copy-start.5 = (bf16[640,1280]{1,0:T(8,128)(2,1)S(1)}, bf16[640,1280]{1,0:T(8,128)(2,1)}, u32[]{:S(2)}) copy-start(bf16[640,1280]{1,0:T(8,128)(2,1)} %param.11) | copy-start | bytes 4915204
  10.9 6.1 %collective-permute-start.3 = (bf16[2,64,640]{2,1,0:T(8,128)(2,1)S(1)}, bf16[2,64,640]{2,1,0:T(8,128)(2,1)S(1)}, u32[]{:S(2)}, u32[]{:S(2)}) collective-permute-start(bf16[2,64,640]{2,1,0:T(8,128)(2,1)S(1)} %pad_maximum_fusion.9), channel_id=1, source_target_pairs={{0,1},{1,2},{2,3},{3,0},{4,5},{5,6},{6,7},{7,4},{8,9},{9,10},{10,1... | collective-permute-start | bytes 491528 | tf_op jit(solution)/shard_map/ppermute | solution.py:89
  12.2 14.4 %collective-permute-start.4 = (bf16[2,64,640]{2,1,0:T(8,128)(2,1)S(1)}, bf16[2,64,640]{2,1,0:T(8,128)(2,1)S(1)}, u32[]{:S(2)}, u32[]{:S(2)}) collective-permute-start(bf16[2,64,640]{2,1,0:T(8,128)(2,1)S(1)} %pad_maximum_fusion.9), channel_id=1, source_target_pairs={{0,2},{1,3},{2,0},{3,1},{4,6},{5,7},{6,4},{7,5},{8,10},{9,11},{10,... | collective-permute-start | bytes 491528 | tf_op jit(solution)/shard_map/ppermute | solution.py:89
  13.3 15.2 %collective-permute-start.5 = (bf16[2,64,640]{2,1,0:T(8,128)(2,1)S(1)}, bf16[2,64,640]{2,1,0:T(8,128)(2,1)S(1)}, u32[]{:S(2)}, u32[]{:S(2)}) collective-permute-start(bf16[2,64,640]{2,1,0:T(8,128)(2,1)S(1)} %pad_maximum_fusion.9), channel_id=1, source_target_pairs={{0,3},{1,0},{2,1},{3,2},{4,7},{5,4},{6,5},{7,6},{8,11},{9,8},{10,9... | collective-permute-start | bytes 491528 | tf_op jit(solution)/shard_map/ppermute | solution.py:89
  28.6 2.2 %collective-permute-start.6 = (bf16[512,640]{1,0:T(8,128)(2,1)S(1)}, bf16[512,640]{1,0:T(8,128)(2,1)S(1)}, u32[]{:S(2)}, u32[]{:S(2)}) collective-permute-start(bf16[512,640]{1,0:T(8,128)(2,1)S(1)} %bitcast.65), channel_id=1, source_target_pairs={{0,4},{4,0},{8,12},{12,8},{1,5},{5,1},{9,13},{13,9},{2,6},{6,2},{1... | collective-permute-start | bytes 1966088 | tf_op jit(solution)/shard_map/ppermute | solution.py:91
  40.6 1.6 %copy-start.4 = (f32[640]{0:T(1024)S(1)}, f32[640]{0:T(1024)}, u32[]{:S(2)}) copy-start(f32[640]{0:T(1024)} %param.13) | copy-start | bytes 7684
  42.3 7.3 %collective-permute-start.7 = (bf16[2,128,640]{2,1,0:T(8,128)(2,1)S(1)}, bf16[2,128,640]{2,1,0:T(8,128)(2,1)S(1)}, u32[]{:S(2)}, u32[]{:S(2)}) collective-permute-start(bf16[2,128,640]{2,1,0:T(8,128)(2,1)S(1)} %bitcast.61), channel_id=1, source_target_pairs={{0,4},{4,8},{8,12},{1,5},{5,9},{9,13},{2,6},{6,10},{10,14},{3,7},{... | collective-permute-start | bytes 983048 | tf_op jit(solution)/shard_map/ppermute | solution.py:47
  45.7 8.4 %collective-permute-start.8 = (bf16[2,128,640]{2,1,0:T(8,128)(2,1)S(1)}, bf16[2,128,640]{2,1,0:T(8,128)(2,1)S(1)}, u32[]{:S(2)}, u32[]{:S(2)}) collective-permute-start(bf16[2,128,640]{2,1,0:T(8,128)(2,1)S(1)} %bitcast.62), channel_id=1, source_target_pairs={{4,0},{8,4},{12,8},{5,1},{9,5},{13,9},{6,2},{10,6},{14,10},{7,3},{... | collective-permute-start | bytes 983048 | tf_op jit(solution)/shard_map/ppermute | solution.py:48
  47.6 6.7 %copy-start.3 = (bf16[3,640,640]{2,1,0:T(8,128)(2,1)S(1)}, bf16[3,640,640]{2,1,0:T(8,128)(2,1)}, u32[]{:S(2)}) copy-start(bf16[3,640,640]{2,1,0:T(8,128)(2,1)} %param.14) | copy-start | bytes 7372804
  56.6 1.7 %copy-start.2 = (bf16[3,640,640]{2,1,0:T(8,128)(2,1)S(1)}, bf16[3,640,640]{2,1,0:T(8,128)(2,1)}, u32[]{:S(2)}) copy-start(bf16[3,640,640]{2,1,0:T(8,128)(2,1)} %param.15) | copy-start | bytes 7372804

commit v23 on v22

--- a/solution.py
+++ b/solution.py
@@ -77,7 +77,7 @@
         me == owner_a, lax.dynamic_index_in_dim(own, slot_a, 0, keepdims=False), jnp.zeros_like(own[0])
     )
     got_b = own[n_loc - 1]
-    for s in sorted(range(1, fsize), key=lambda s: (s == fsize // 2, s)):
+    for s in reversed(range(1, fsize)):
         recv = lax.ppermute(halves((me + s) % 2), "frame", [(i, (i + s) % fsize) for i in range(fsize)])
         source = (me - s) % fsize
         got_a = jnp.where(source == owner_a, lax.dynamic_index_in_dim(recv, slot_a, 0, keepdims=False), got_a)

time: 60.8 us -> 60.4 us (level)
  starting transfers between devices: 12.6 us -> 11 us
  waiting for transfers between devices: 21.7 us -> 22.7 us
    ppermute x3, waiting for transfers between devices: 1.16 us -> 2.43 us  [gather_keyframes(): lax.ppermute(halves((me + s) % 2), 'frame', [(i, (i + s) % fsize) for i i...]
    ppermute x1, starting transfers between devices: 3.31 us -> 2.22 us  [extended(): before = lax.ppermute(last, axis, up)]
    ppermute x3, starting transfers between devices: 3.02 us -> 2.3 us  [gather_keyframes(): lax.ppermute(halves((me + s) % 2), 'frame', [(i, (i + s) % fsize) for i i...]
  transfers between devices with their start and end apart: 9 -> 9, of which waited for: 7 -> 8; matrix products, arithmetic and copies ran while one was open for 9% -> 9% of each run, Pallas kernels for 0% -> 0%
where the time goes in v23:
time: 60.4 us; the launch traced here: 59.9 us
  waiting for transfers between devices  22.7 us (38%)
  matrix products  11.5 us (19%)
  starting transfers between devices  11 us (18%)
  Pallas kernels  5.85 us (10%)
  local copies, waits for them, and re-layouts  4.11 us (7%)
  other arithmetic  3.16 us (5%)
  between operations  1.65 us (3%)
    ppermute x3, waiting for transfers between devices, gather_keyframes(): lax.ppermute(piece, 'row', [(i, (i + s) % rsize) for i in range(rsize)])  13.8 us
    pallas_call x1, Pallas kernels, attend(): pl.pallas_call(attention_kernel, grid=(channels // width,), in_specs=[pl....  5.85 us
    dot_general x6, matrix products, temporal_mix(): jnp.dot(window, weights[offset], preferred_element_type=jnp.float32)  4.43 us
    ppermute x1, waiting for transfers between devices, extended(): after = lax.ppermute(first, axis, down)  4.4 us
    ppermute x3, starting transfers between devices, gather_keyframes(): lax.ppermute(piece, 'row', [(i, (i + s) % rsize) for i in range(rsize)])  3.83 us
    dot_general x1, matrix products, shards(): lax.dot_general(w_query, flattened, (((0,), (1,)), ((), ())), preferred_e...  2.53 us
    ppermute x3, waiting for transfers between devices, gather_keyframes(): lax.ppermute(halves((me + s) % 2), 'frame', [(i, (i + s) % fsize) for i i...  2.43 us
    ppermute x3, starting transfers between devices, gather_keyframes(): lax.ppermute(halves((me + s) % 2), 'frame', [(i, (i + s) % fsize) for i i...  2.3 us
  transfers between devices with their start and end apart: 9, of which 8 were waited for; matrix products, arithmetic and copies ran while one was open for 9% of the time, Pallas kernels for 0%

profile of v23, /device:TPU:9, one launch (start us, length us, event | category | flops | bytes accessed | tf_op | source)
XLA Modules:
  0.0 59.9 jit_solution(7373992153002979393)
XLA Ops:
  0.0 1.2 %constant_dynamic-slice_fusion.2 = (bf16[2,64,640]{2,1,0:T(8,128)(2,1)S(1)}, bf16[2,64,640]{2,1,0:T(8,128)(2,1)S(1)}, bf16[2,64,640]{2,1,0:T(8,128)(2,1)S(1)}) fusion(bf16[2,128,640]{2,1,0:T(8,128)(2,1)} %param.8, s32[]{:T(128)S(6)} %select_n.137, s32[]{:T(128)S(6)} %select_n.147, s32[]{:T(128)S(6)} %select_n.143), kind=kLoop, calls=%fused_computation.57 | loop fusion | bytes 983052 | tf_op jit(solution)/shard_map/dynamic_slice | solution.py:73
  1.2 1.8 %collective-permute-start = (bf16[2,64,640]{2,1,0:T(8,128)(2,1)S(1)}, bf16[2,64,640]{2,1,0:T(8,128)(2,1)S(1)}, u32[]{:S(2)}, u32[]{:S(2)}) collective-permute-start(bf16[2,64,640]{2,1,0:T(8,128)(2,1)S(1)} %get-tuple-element.16), channel_id=1, source_target_pairs={{0,4},{4,8},{8,12},{12,0},{1,5},{5,9},{9,13},{13,1},{2,6},{6,10},{... | collective-permute-start | bytes 491528 | tf_op jit(solution)/shard_map/ppermute | solution.py:81
  3.5 1.3 %fusion.30 = (s32[1]{0:T(128)}, s32[1]{0:T(128)}) fusion(s32[2]{0:T(128)} %param.9), kind=kLoop, calls=%fused_computation.60 | loop fusion | bytes 16 | tf_op jit(solution)/shard_map/slice | solution.py:66
  6.3 2.5 %fusion.4.qt_ref = bf16[640,256]{1,0:T(8,128)(2,1)} fusion(bf16[640,640]{1,0:T(8,128)(2,1)} %param.10, bf16[256,640]{1,0:T(8,128)(2,1)} %bitcast.54), kind=kOutput, calls=%fused_computation.16 | convolution fusion | flops 210042880 | bytes 1474560 | tf_op jit(solution)/shard_map/dot_general | solution.py:99
  8.8 1.8 %collective-permute-done.1 = bf16[2,64,640]{2,1,0:T(8,128)(2,1)S(1)} collective-permute-done((bf16[2,64,640]{2,1,0:T(8,128)(2,1)S(1)}, bf16[2,64,640]{2,1,0:T(8,128)(2,1)S(1)}, u32[]{:S(2)}, u32[]{:S(2)}) %collective-permute-start.1) | collective-permute-done | bytes 163872 | tf_op jit(solution)/shard_map/ppermute | solution.py:81
  10.7 0.6 %collective-permute-done.2 = bf16[2,64,640]{2,1,0:T(8,128)(2,1)S(1)} collective-permute-done((bf16[2,64,640]{2,1,0:T(8,128)(2,1)S(1)}, bf16[2,64,640]{2,1,0:T(8,128)(2,1)S(1)}, u32[]{:S(2)}, u32[]{:S(2)}) %collective-permute-start.2) | collective-permute-done | bytes 163872 | tf_op jit(solution)/shard_map/ppermute | solution.py:81
  11.4 1.4 %collective-permute-start.3 = (bf16[2,64,640]{2,1,0:T(8,128)(2,1)S(1)}, bf16[2,64,640]{2,1,0:T(8,128)(2,1)S(1)}, u32[]{:S(2)}, u32[]{:S(2)}) collective-permute-start(bf16[2,64,640]{2,1,0:T(8,128)(2,1)S(1)} %pad_maximum_fusion.9), channel_id=1, source_target_pairs={{0,1},{1,2},{2,3},{3,0},{4,5},{5,6},{6,7},{7,4},{8,9},{9,10},{10,1... | collective-permute-start | bytes 491528 | tf_op jit(solution)/shard_map/ppermute | solution.py:89
  12.8 1.1 %collective-permute-start.4 = (bf16[2,64,640]{2,1,0:T(8,128)(2,1)S(1)}, bf16[2,64,640]{2,1,0:T(8,128)(2,1)S(1)}, u32[]{:S(2)}, u32[]{:S(2)}) collective-permute-start(bf16[2,64,640]{2,1,0:T(8,128)(2,1)S(1)} %pad_maximum_fusion.9), channel_id=1, source_target_pairs={{0,2},{1,3},{2,0},{3,1},{4,6},{5,7},{6,4},{7,5},{8,10},{9,11},{10,... | collective-permute-start | bytes 491528 | tf_op jit(solution)/shard_map/ppermute | solution.py:89
  13.9 1.4 %collective-permute-start.5 = (bf16[2,64,640]{2,1,0:T(8,128)(2,1)S(1)}, bf16[2,64,640]{2,1,0:T(8,128)(2,1)S(1)}, u32[]{:S(2)}, u32[]{:S(2)}) collective-permute-start(bf16[2,64,640]{2,1,0:T(8,128)(2,1)S(1)} %pad_maximum_fusion.9), channel_id=1, source_target_pairs={{0,3},{1,0},{2,1},{3,2},{4,7},{5,4},{6,5},{7,6},{8,11},{9,8},{10,9... | collective-permute-start | bytes 491528 | tf_op jit(solution)/shard_map/ppermute | solution.py:89
  15.3 2.3 %collective-permute-done.3 = bf16[2,64,640]{2,1,0:T(8,128)(2,1)S(1)} collective-permute-done((bf16[2,64,640]{2,1,0:T(8,128)(2,1)S(1)}, bf16[2,64,640]{2,1,0:T(8,128)(2,1)S(1)}, u32[]{:S(2)}, u32[]{:S(2)}) %collective-permute-start.3) | collective-permute-done | bytes 163872 | tf_op jit(solution)/shard_map/ppermute | solution.py:89
  17.5 9.6 %collective-permute-done.4 = bf16[2,64,640]{2,1,0:T(8,128)(2,1)S(1)} collective-permute-done((bf16[2,64,640]{2,1,0:T(8,128)(2,1)S(1)}, bf16[2,64,640]{2,1,0:T(8,128)(2,1)S(1)}, u32[]{:S(2)}, u32[]{:S(2)}) %collective-permute-start.4) | collective-permute-done | bytes 163872 | tf_op jit(solution)/shard_map/ppermute | solution.py:89
  27.2 1.9 %collective-permute-done.5 = bf16[2,64,640]{2,1,0:T(8,128)(2,1)S(1)} collective-permute-done((bf16[2,64,640]{2,1,0:T(8,128)(2,1)S(1)}, bf16[2,64,640]{2,1,0:T(8,128)(2,1)S(1)}, u32[]{:S(2)}, u32[]{:S(2)}) %collective-permute-start.5) | collective-permute-done | bytes 163872 | tf_op jit(solution)/shard_map/ppermute | solution.py:89
  29.2 0.5 collective-permute-start.6
  29.7 0.7 %fusion.1 = bf16[640,512]{1,0:T(8,128)(2,1)S(1)} fusion(bf16[512,640]{1,0:T(8,128)(2,1)S(1)} %bitcast.66, bf16[640,1280]{1,0:T(8,128)(2,1)S(1)} %copy-done.5), kind=kOutput, calls=%fused_computation.9 | convolution fusion | flops 419758080 | bytes 2129920 | tf_op jit(solution)/shard_map/dot_general | solution.py:105
  30.4 0.8 %convolution_convert_fusion.3 = bf16[512,640]{1,0:T(8,128)(2,1)S(1)} fusion(bf16[512,640]{1,0:T(8,128)(2,1)S(1)} %bitcast.67, bf16[640,1280]{1,0:T(8,128)(2,1)S(1)} %copy-done.5), kind=kOutput, calls=%fused_computation.5 | convolution fusion | flops 419758080 | bytes 2129920 | tf_op jit(solution)/shard_map/dot_general | solution.py:104
  31.4 0.7 %fusion.2 = bf16[640,512]{1,0:T(8,128)(2,1)S(1)} fusion(bf16[512,640]{1,0:T(8,128)(2,1)S(1)} %collective-permute-done.6, bf16[640,1280]{1,0:T(8,128)(2,1)S(1)} %copy-done.5), kind=kOutput, calls=%fused_computation.10 | convolution fusion | flops 419758080 | bytes 2129920 | tf_op jit(solution)/shard_map/dot_general | solution.py:105
  32.1 1.2 %pad_maximum_fusion.1.vt_ref = bf16[640,1024]{1,0:T(8,128)(2,1)} fusion(bf16[640,512]{1,0:T(8,128)(2,1)S(1)} %fusion.2, bf16[640,512]{1,0:T(8,128)(2,1)S(1)} %fusion.1), kind=kLoop, calls=%fused_computation.7 | loop fusion | flops 2621440 | bytes 2621440 | tf_op jit(solution)/shard_map/concatenate | solution.py:113
  33.4 0.7 %convolution_convert_fusion.2 = bf16[512,640]{1,0:T(8,128)(2,1)S(1)} fusion(bf16[512,640]{1,0:T(8,128)(2,1)S(1)} %collective-permute-done.6, bf16[640,1280]{1,0:T(8,128)(2,1)S(1)} %copy-done.5), kind=kOutput, calls=%fused_computation.4 | convolution fusion | flops 419758080 | bytes 2129920 | tf_op jit(solution)/shard_map/dot_general | solution.py:104
  34.1 1.2 %pad_maximum_fusion.k_ref = bf16[1024,640]{1,0:T(8,128)(2,1)} fusion(bf16[512,640]{1,0:T(8,128)(2,1)S(1)} %convolution_convert_fusion.2, bf16[512,640]{1,0:T(8,128)(2,1)S(1)} %convolution_convert_fusion.3), kind=kLoop, calls=%fused_computation.6 | loop fusion | flops 2621440 | bytes 2621440 | tf_op jit(solution)/shard_map/concatenate | solution.py:112
  35.3 5.8 %shard_map.82 = bf16[640,256]{1,0:T(8,128)(2,1)} custom-call(bf16[1024,640]{1,0:T(8,128)(2,1)} %pad_maximum_fusion.k_ref, bf16[640,256]{1,0:T(8,128)(2,1)} %fusion.4.qt_ref, bf16[640,1024]{1,0:T(8,128)(2,1)} %pad_maximum_fusion.1.vt_ref), custom_call_target="tpu_custom_call" | custom-call | tf_op jit(solution)/shard_map/pallas_call | solution.py:28
  41.2 1.6 %multiply_reduce_fusion = (f32[256]{0:T(256)S(1)}, f32[256,640]{1,0:T(8,128)S(1)}) fusion(bf16[640,256]{1,0:T(8,128)(2,1)} %shard_map.82, bf16[640,640]{1,0:T(8,128)(2,1)S(1)} %copy-done, bf16[256,640]{1,0:T(8,128)(2,1)S(1)} %bitcast.55), kind=kOutput, calls=%fused_computation.43 | convolution fusion | flops 210370304 | bytes 2130944 | tf_op jit(solution)/shard_map/dot_general | solution.py:115
  42.9 2.2 %collective-permute-start.7 = (bf16[2,128,640]{2,1,0:T(8,128)(2,1)S(1)}, bf16[2,128,640]{2,1,0:T(8,128)(2,1)S(1)}, u32[]{:S(2)}, u32[]{:S(2)}) collective-permute-start(bf16[2,128,640]{2,1,0:T(8,128)(2,1)S(1)} %bitcast.61), channel_id=1, source_target_pairs={{0,4},{4,8},{8,12},{1,5},{5,9},{9,13},{2,6},{6,10},{10,14},{3,7},{... | collective-permute-start | bytes 983048 | tf_op jit(solution)/shard_map/ppermute | solution.py:47
  45.1 2.1 %collective-permute-start.8 = (bf16[2,128,640]{2,1,0:T(8,128)(2,1)S(1)}, bf16[2,128,640]{2,1,0:T(8,128)(2,1)S(1)}, u32[]{:S(2)}, u32[]{:S(2)}) collective-permute-start(bf16[2,128,640]{2,1,0:T(8,128)(2,1)S(1)} %bitcast.62), channel_id=1, source_target_pairs={{4,0},{8,4},{12,8},{5,1},{9,5},{13,9},{6,2},{10,6},{14,10},{7,3},{... | collective-permute-start | bytes 983048 | tf_op jit(solution)/shard_map/ppermute | solution.py:48
  47.3 1.8 %collective-permute-done.7 = bf16[2,128,640]{2,1,0:T(8,128)(2,1)S(1)} collective-permute-done((bf16[2,128,640]{2,1,0:T(8,128)(2,1)S(1)}, bf16[2,128,640]{2,1,0:T(8,128)(2,1)S(1)}, u32[]{:S(2)}, u32[]{:S(2)}) %collective-permute-start.7) | collective-permute-done | bytes 327712 | tf_op jit(solution)/shard_map/ppermute | solution.py:47
  49.1 4.4 %collective-permute-done.8 = bf16[2,128,640]{2,1,0:T(8,128)(2,1)S(1)} collective-permute-done((bf16[2,128,640]{2,1,0:T(8,128)(2,1)S(1)}, bf16[2,128,640]{2,1,0:T(8,128)(2,1)S(1)}, u32[]{:S(2)}, u32[]{:S(2)}) %collective-permute-start.8) | collective-permute-done | bytes 327712 | tf_op jit(solution)/shard_map/ppermute | solution.py:48
  53.8 0.7 %fusion.10 = f32[512,640]{1,0:T(8,128)S(1)} fusion(bf16[512,640]{1,0:T(8,128)(2,1)S(1)} %bitcast.57, bf16[3,640,640]{2,1,0:T(8,128)(2,1)S(1)} %copy-done.3), kind=kOutput, calls=%fused_computation.22 | convolution fusion | flops 419430400 | bytes 2785280 | tf_op jit(solution)/shard_map/dot_general | solution.py:56
  54.5 0.7 %fusion.12 = f32[512,640]{1,0:T(8,128)S(1)} fusion(bf16[512,640]{1,0:T(8,128)(2,1)S(1)} %bitcast.56, bf16[3,640,640]{2,1,0:T(8,128)(2,1)S(1)} %copy-done.3), kind=kOutput, calls=%fused_computation.24 | convolution fusion | flops 419430400 | bytes 2785280 | tf_op jit(solution)/shard_map/dot_general | solution.py:56
  55.3 0.8 %multiply_convert_fusion = bf16[512,640]{1,0:T(8,128)(2,1)S(1)} fusion(f32[512,640]{1,0:T(8,128)S(1)} %fusion.10, f32[512,640]{1,0:T(8,128)S(1)} %fusion.12, bf16[512,640]{1,0:T(8,128)(2,1)S(1)} %bitcast.68, bf16[3,640,640]{2,1,0:T(8,128)(2,1)S(1)} %copy-done.3), kind=kOutput, calls=%fused_computation.8 | convolution fusion | flops 421724160 | bytes 4751360 | tf_op jit(solution)/shard_map/dot_general | solution.py:56
  56.3 1.5 %copy-done.2 = bf16[3,640,640]{2,1,0:T(8,128)(2,1)S(1)} copy-done((bf16[3,640,640]{2,1,0:T(8,128)(2,1)S(1)}, bf16[3,640,640]{2,1,0:T(8,128)(2,1)}, u32[]{:S(2)}) %copy-start.2) | copy-done | bytes 2457624
  57.8 0.5 fusion.8
  58.3 0.5 convolution_add_fusion.2
  58.7 1.2 %fusion.5 = bf16[256,640]{1,0:T(8,128)(2,1)} fusion(f32[256,640]{1,0:T(8,128)S(1)} %get-tuple-element.22, f32[256,640]{1,0:T(8,128)S(1)} %convolution_add_fusion.2, bf16[256,640]{1,0:T(8,128)(2,1)S(1)} %bitcast.60, bf16[3,640,640]{2,1,0:T(8,128)(2,1)S(1)} %copy-done.2), kind=kOutput, calls=%fused_computation.17 | convolution fusion | flops 210206720 | bytes 2785280 | tf_op jit(solution)/shard_map/dot_general | solution.py:56
  (24 shorter events, 1.5 us)
Async XLA Ops:
  0.0 41.2 %copy-start = (bf16[640,640]{1,0:T(8,128)(2,1)S(1)}, bf16[640,640]{1,0:T(8,128)(2,1)}, u32[]{:S(2)}) copy-start(bf16[640,640]{1,0:T(8,128)(2,1)} %param.12) | copy-start | bytes 2457604
  0.0 11.3 %copy-start.1 = (bf16[2,128,640]{2,1,0:T(8,128)(2,1)S(1)}, bf16[2,128,640]{2,1,0:T(8,128)(2,1)}, u32[]{:S(2)}) copy-start(bf16[2,128,640]{2,1,0:T(8,128)(2,1)} %param.8) | copy-start | bytes 983044
  1.2 7.6 %collective-permute-start = (bf16[2,64,640]{2,1,0:T(8,128)(2,1)S(1)}, bf16[2,64,640]{2,1,0:T(8,128)(2,1)S(1)}, u32[]{:S(2)}, u32[]{:S(2)}) collective-permute-start(bf16[2,64,640]{2,1,0:T(8,128)(2,1)S(1)} %get-tuple-element.16), channel_id=1, source_target_pairs={{0,4},{4,8},{8,12},{12,0},{1,5},{5,9},{9,13},{13,1},{2,6},{6,10},{... | collective-permute-start | bytes 491528 | tf_op jit(solution)/shard_map/ppermute | solution.py:81
  3.0 7.6 %collective-permute-start.1 = (bf16[2,64,640]{2,1,0:T(8,128)(2,1)S(1)}, bf16[2,64,640]{2,1,0:T(8,128)(2,1)S(1)}, u32[]{:S(2)}, u32[]{:S(2)}) collective-permute-start(bf16[2,64,640]{2,1,0:T(8,128)(2,1)S(1)} %get-tuple-element.18), channel_id=1, source_target_pairs={{0,8},{4,12},{8,0},{12,4},{1,9},{5,13},{9,1},{13,5},{2,10},{6,14},... | collective-permute-start | bytes 491528 | tf_op jit(solution)/shard_map/ppermute | solution.py:81
  3.3 8.0 %collective-permute-start.2 = (bf16[2,64,640]{2,1,0:T(8,128)(2,1)S(1)}, bf16[2,64,640]{2,1,0:T(8,128)(2,1)S(1)}, u32[]{:S(2)}, u32[]{:S(2)}) collective-permute-start(bf16[2,64,640]{2,1,0:T(8,128)(2,1)S(1)} %get-tuple-element.17), channel_id=1, source_target_pairs={{0,12},{4,0},{8,4},{12,8},{1,13},{5,1},{9,5},{13,9},{2,14},{6,2},{... | collective-permute-start | bytes 491528 | tf_op jit(solution)/shard_map/ppermute | solution.py:81
  6.3 23.4 %copy-start.5 = (bf16[640,1280]{1,0:T(8,128)(2,1)S(1)}, bf16[640,1280]{1,0:T(8,128)(2,1)}, u32[]{:S(2)}) copy-start(bf16[640,1280]{1,0:T(8,128)(2,1)} %param.11) | copy-start | bytes 4915204
  11.4 6.1 %collective-permute-start.3 = (bf16[2,64,640]{2,1,0:T(8,128)(2,1)S(1)}, bf16[2,64,640]{2,1,0:T(8,128)(2,1)S(1)}, u32[]{:S(2)}, u32[]{:S(2)}) collective-permute-start(bf16[2,64,640]{2,1,0:T(8,128)(2,1)S(1)} %pad_maximum_fusion.9), channel_id=1, source_target_pairs={{0,1},{1,2},{2,3},{3,0},{4,5},{5,6},{6,7},{7,4},{8,9},{9,10},{10,1... | collective-permute-start | bytes 491528 | tf_op jit(solution)/shard_map/ppermute | solution.py:89
  12.8 14.4 %collective-permute-start.4 = (bf16[2,64,640]{2,1,0:T(8,128)(2,1)S(1)}, bf16[2,64,640]{2,1,0:T(8,128)(2,1)S(1)}, u32[]{:S(2)}, u32[]{:S(2)}) collective-permute-start(bf16[2,64,640]{2,1,0:T(8,128)(2,1)S(1)} %pad_maximum_fusion.9), channel_id=1, source_target_pairs={{0,2},{1,3},{2,0},{3,1},{4,6},{5,7},{6,4},{7,5},{8,10},{9,11},{10,... | collective-permute-start | bytes 491528 | tf_op jit(solution)/shard_map/ppermute | solution.py:89
  13.9 15.2 %collective-permute-start.5 = (bf16[2,64,640]{2,1,0:T(8,128)(2,1)S(1)}, bf16[2,64,640]{2,1,0:T(8,128)(2,1)S(1)}, u32[]{:S(2)}, u32[]{:S(2)}) collective-permute-start(bf16[2,64,640]{2,1,0:T(8,128)(2,1)S(1)} %pad_maximum_fusion.9), channel_id=1, source_target_pairs={{0,3},{1,0},{2,1},{3,2},{4,7},{5,4},{6,5},{7,6},{8,11},{9,8},{10,9... | collective-permute-start | bytes 491528 | tf_op jit(solution)/shard_map/ppermute | solution.py:89
  29.2 2.2 %collective-permute-start.6 = (bf16[512,640]{1,0:T(8,128)(2,1)S(1)}, bf16[512,640]{1,0:T(8,128)(2,1)S(1)}, u32[]{:S(2)}, u32[]{:S(2)}) collective-permute-start(bf16[512,640]{1,0:T(8,128)(2,1)S(1)} %bitcast.65), channel_id=1, source_target_pairs={{0,4},{4,0},{8,12},{12,8},{1,5},{5,1},{9,13},{13,9},{2,6},{6,2},{1... | collective-permute-start | bytes 1966088 | tf_op jit(solution)/shard_map/ppermute | solution.py:91
  41.2 1.6 %copy-start.4 = (f32[640]{0:T(1024)S(1)}, f32[640]{0:T(1024)}, u32[]{:S(2)}) copy-start(f32[640]{0:T(1024)} %param.13) | copy-start | bytes 7684
  42.9 6.2 %collective-permute-start.7 = (bf16[2,128,640]{2,1,0:T(8,128)(2,1)S(1)}, bf16[2,128,640]{2,1,0:T(8,128)(2,1)S(1)}, u32[]{:S(2)}, u32[]{:S(2)}) collective-permute-start(bf16[2,128,640]{2,1,0:T(8,128)(2,1)S(1)} %bitcast.61), channel_id=1, source_target_pairs={{0,4},{4,8},{8,12},{1,5},{5,9},{9,13},{2,6},{6,10},{10,14},{3,7},{... | collective-permute-start | bytes 983048 | tf_op jit(solution)/shard_map/ppermute | solution.py:47
  45.1 8.4 %collective-permute-start.8 = (bf16[2,128,640]{2,1,0:T(8,128)(2,1)S(1)}, bf16[2,128,640]{2,1,0:T(8,128)(2,1)S(1)}, u32[]{:S(2)}, u32[]{:S(2)}) collective-permute-start(bf16[2,128,640]{2,1,0:T(8,128)(2,1)S(1)} %bitcast.62), channel_id=1, source_target_pairs={{4,0},{8,4},{12,8},{5,1},{9,5},{13,9},{6,2},{10,6},{14,10},{7,3},{... | collective-permute-start | bytes 983048 | tf_op jit(solution)/shard_map/ppermute | solution.py:48
  47.3 6.5 %copy-start.3 = (bf16[3,640,640]{2,1,0:T(8,128)(2,1)S(1)}, bf16[3,640,640]{2,1,0:T(8,128)(2,1)}, u32[]{:S(2)}) copy-start(bf16[3,640,640]{2,1,0:T(8,128)(2,1)} %param.14) | copy-start | bytes 7372804
  56.1 1.7 %copy-start.2 = (bf16[3,640,640]{2,1,0:T(8,128)(2,1)S(1)}, bf16[3,640,640]{2,1,0:T(8,128)(2,1)}, u32[]{:S(2)}) copy-start(bf16[3,640,640]{2,1,0:T(8,128)(2,1)} %param.15) | copy-start | bytes 7372804

commit v24 on v23

--- a/solution.py
+++ b/solution.py
@@ -77,7 +77,7 @@
         me == owner_a, lax.dynamic_index_in_dim(own, slot_a, 0, keepdims=False), jnp.zeros_like(own[0])
     )
     got_b = own[n_loc - 1]
-    for s in reversed(range(1, fsize)):
+    for s in sorted(range(1, fsize), key=lambda s: (s == fsize // 2, -s)):
         recv = lax.ppermute(halves((me + s) % 2), "frame", [(i, (i + s) % fsize) for i in range(fsize)])
         source = (me - s) % fsize
         got_a = jnp.where(source == owner_a, lax.dynamic_index_in_dim(recv, slot_a, 0, keepdims=False), got_a)

time: 60.4 us -> 60.8 us (level)
  starting transfers between devices: 11 us -> 12 us
    ppermute x1, starting transfers between devices: 2.22 us -> 3.32 us  [extended(): before = lax.ppermute(last, axis, up)]
    ppermute x3, waiting for transfers between devices: 2.43 us -> 1.8 us  [gather_keyframes(): lax.ppermute(halves((me + s) % 2), 'frame', [(i, (i + s) % fsize) for i i...]
  transfers between devices with their start and end apart: 9 -> 9, of which waited for: 8 -> 7; matrix products, arithmetic and copies ran while one was open for 9% -> 9% of each run, Pallas kernels for 0% -> 0%
where the time goes in v24:
time: 60.8 us; the launch traced here: 60.5 us
  waiting for transfers between devices  22.2 us (37%)
  starting transfers between devices  12 us (20%)
  matrix products  11.5 us (19%)
  Pallas kernels  5.84 us (10%)
  local copies, waits for them, and re-layouts  4.11 us (7%)
  other arithmetic  3.16 us (5%)
  between operations  1.65 us (3%)
    ppermute x3, waiting for transfers between devices, gather_keyframes(): lax.ppermute(piece, 'row', [(i, (i + s) % rsize) for i in range(rsize)])  13.8 us
    pallas_call x1, Pallas kernels, attend(): pl.pallas_call(attention_kernel, grid=(channels // width,), in_specs=[pl....  5.84 us
    dot_general x6, matrix products, temporal_mix(): jnp.dot(window, weights[offset], preferred_element_type=jnp.float32)  4.43 us
    ppermute x1, waiting for transfers between devices, extended(): after = lax.ppermute(first, axis, down)  4.4 us
    ppermute x3, starting transfers between devices, gather_keyframes(): lax.ppermute(piece, 'row', [(i, (i + s) % rsize) for i in range(rsize)])  3.85 us
    ppermute x1, starting transfers between devices, extended(): before = lax.ppermute(last, axis, up)  3.32 us
    dot_general x1, matrix products, shards(): lax.dot_general(w_query, flattened, (((0,), (1,)), ((), ())), preferred_e...  2.54 us
    ppermute x3, starting transfers between devices, gather_keyframes(): lax.ppermute(halves((me + s) % 2), 'frame', [(i, (i + s) % fsize) for i i...  2.37 us
  transfers between devices with their start and end apart: 9, of which 7 were waited for; matrix products, arithmetic and copies ran while one was open for 9% of the time, Pallas kernels for 0%

profile of v24, /device:TPU:9, one launch (start us, length us, event | category | flops | bytes accessed | tf_op | source)
XLA Modules:
  0.0 60.5 jit_solution(11327494690358663957)
XLA Ops:
  0.0 1.2 %constant_dynamic-slice_fusion.2 = (bf16[2,64,640]{2,1,0:T(8,128)(2,1)S(1)}, bf16[2,64,640]{2,1,0:T(8,128)(2,1)S(1)}, bf16[2,64,640]{2,1,0:T(8,128)(2,1)S(1)}) fusion(bf16[2,128,640]{2,1,0:T(8,128)(2,1)} %param.8, s32[]{:T(128)S(6)} %select_n.137, s32[]{:T(128)S(6)} %select_n.147, s32[]{:T(128)S(6)} %select_n.143), kind=kLoop, calls=%fused_computation.57 | loop fusion | bytes 983052 | tf_op jit(solution)/shard_map/dynamic_slice | solution.py:73
  1.2 1.3 %collective-permute-start = (bf16[2,64,640]{2,1,0:T(8,128)(2,1)S(1)}, bf16[2,64,640]{2,1,0:T(8,128)(2,1)S(1)}, u32[]{:S(2)}, u32[]{:S(2)}) collective-permute-start(bf16[2,64,640]{2,1,0:T(8,128)(2,1)S(1)} %get-tuple-element.16), channel_id=1, source_target_pairs={{0,8},{4,12},{8,0},{12,4},{1,9},{5,13},{9,1},{13,5},{2,10},{6,14},... | collective-permute-start | bytes 491528 | tf_op jit(solution)/shard_map/ppermute | solution.py:81
  2.5 1.1 %collective-permute-start.1 = (bf16[2,64,640]{2,1,0:T(8,128)(2,1)S(1)}, bf16[2,64,640]{2,1,0:T(8,128)(2,1)S(1)}, u32[]{:S(2)}, u32[]{:S(2)}) collective-permute-start(bf16[2,64,640]{2,1,0:T(8,128)(2,1)S(1)} %get-tuple-element.18), channel_id=1, source_target_pairs={{0,4},{4,8},{8,12},{12,0},{1,5},{5,9},{9,13},{13,1},{2,6},{6,10},{... | collective-permute-start | bytes 491528 | tf_op jit(solution)/shard_map/ppermute | solution.py:81
  3.6 1.3 %fusion.30 = (s32[1]{0:T(128)}, s32[1]{0:T(128)}) fusion(s32[2]{0:T(128)} %param.9), kind=kLoop, calls=%fused_computation.60 | loop fusion | bytes 16 | tf_op jit(solution)/shard_map/slice | solution.py:66
  6.4 2.5 %fusion.4.qt_ref = bf16[640,256]{1,0:T(8,128)(2,1)} fusion(bf16[640,640]{1,0:T(8,128)(2,1)} %param.10, bf16[256,640]{1,0:T(8,128)(2,1)} %bitcast.54), kind=kOutput, calls=%fused_computation.16 | convolution fusion | flops 210042880 | bytes 1474560 | tf_op jit(solution)/shard_map/dot_general | solution.py:99
  8.9 1.8 %collective-permute-done.2 = bf16[2,64,640]{2,1,0:T(8,128)(2,1)S(1)} collective-permute-done((bf16[2,64,640]{2,1,0:T(8,128)(2,1)S(1)}, bf16[2,64,640]{2,1,0:T(8,128)(2,1)S(1)}, u32[]{:S(2)}, u32[]{:S(2)}) %collective-permute-start.2) | collective-permute-done | bytes 163872 | tf_op jit(solution)/shard_map/ppermute | solution.py:81
  10.9 1.3 %collective-permute-start.3 = (bf16[2,64,640]{2,1,0:T(8,128)(2,1)S(1)}, bf16[2,64,640]{2,1,0:T(8,128)(2,1)S(1)}, u32[]{:S(2)}, u32[]{:S(2)}) collective-permute-start(bf16[2,64,640]{2,1,0:T(8,128)(2,1)S(1)} %pad_maximum_fusion.9), channel_id=1, source_target_pairs={{0,1},{1,2},{2,3},{3,0},{4,5},{5,6},{6,7},{7,4},{8,9},{9,10},{10,1... | collective-permute-start | bytes 491528 | tf_op jit(solution)/shard_map/ppermute | solution.py:89
  12.2 1.1 %collective-permute-start.4 = (bf16[2,64,640]{2,1,0:T(8,128)(2,1)S(1)}, bf16[2,64,640]{2,1,0:T(8,128)(2,1)S(1)}, u32[]{:S(2)}, u32[]{:S(2)}) collective-permute-start(bf16[2,64,640]{2,1,0:T(8,128)(2,1)S(1)} %pad_maximum_fusion.9), channel_id=1, source_target_pairs={{0,2},{1,3},{2,0},{3,1},{4,6},{5,7},{6,4},{7,5},{8,10},{9,11},{10,... | collective-permute-start | bytes 491528 | tf_op jit(solution)/shard_map/ppermute | solution.py:89
  13.3 1.4 %collective-permute-start.5 = (bf16[2,64,640]{2,1,0:T(8,128)(2,1)S(1)}, bf16[2,64,640]{2,1,0:T(8,128)(2,1)S(1)}, u32[]{:S(2)}, u32[]{:S(2)}) collective-permute-start(bf16[2,64,640]{2,1,0:T(8,128)(2,1)S(1)} %pad_maximum_fusion.9), channel_id=1, source_target_pairs={{0,3},{1,0},{2,1},{3,2},{4,7},{5,4},{6,5},{7,6},{8,11},{9,8},{10,9... | collective-permute-start | bytes 491528 | tf_op jit(solution)/shard_map/ppermute | solution.py:89
  14.7 2.1 %collective-permute-done.3 = bf16[2,64,640]{2,1,0:T(8,128)(2,1)S(1)} collective-permute-done((bf16[2,64,640]{2,1,0:T(8,128)(2,1)S(1)}, bf16[2,64,640]{2,1,0:T(8,128)(2,1)S(1)}, u32[]{:S(2)}, u32[]{:S(2)}) %collective-permute-start.3) | collective-permute-done | bytes 163872 | tf_op jit(solution)/shard_map/ppermute | solution.py:89
  16.9 9.6 %collective-permute-done.4 = bf16[2,64,640]{2,1,0:T(8,128)(2,1)S(1)} collective-permute-done((bf16[2,64,640]{2,1,0:T(8,128)(2,1)S(1)}, bf16[2,64,640]{2,1,0:T(8,128)(2,1)S(1)}, u32[]{:S(2)}, u32[]{:S(2)}) %collective-permute-start.4) | collective-permute-done | bytes 163872 | tf_op jit(solution)/shard_map/ppermute | solution.py:89
  26.5 2.0 %collective-permute-done.5 = bf16[2,64,640]{2,1,0:T(8,128)(2,1)S(1)} collective-permute-done((bf16[2,64,640]{2,1,0:T(8,128)(2,1)S(1)}, bf16[2,64,640]{2,1,0:T(8,128)(2,1)S(1)}, u32[]{:S(2)}, u32[]{:S(2)}) %collective-permute-start.5) | collective-permute-done | bytes 163872 | tf_op jit(solution)/shard_map/ppermute | solution.py:89
  28.6 0.5 collective-permute-start.6
  29.1 0.7 %fusion.1 = bf16[640,512]{1,0:T(8,128)(2,1)S(1)} fusion(bf16[512,640]{1,0:T(8,128)(2,1)S(1)} %bitcast.66, bf16[640,1280]{1,0:T(8,128)(2,1)S(1)} %copy-done.5), kind=kOutput, calls=%fused_computation.9 | convolution fusion | flops 419758080 | bytes 2129920 | tf_op jit(solution)/shard_map/dot_general | solution.py:105
  29.8 0.8 %convolution_convert_fusion.3 = bf16[512,640]{1,0:T(8,128)(2,1)S(1)} fusion(bf16[512,640]{1,0:T(8,128)(2,1)S(1)} %bitcast.67, bf16[640,1280]{1,0:T(8,128)(2,1)S(1)} %copy-done.5), kind=kOutput, calls=%fused_computation.5 | convolution fusion | flops 419758080 | bytes 2129920 | tf_op jit(solution)/shard_map/dot_general | solution.py:104
  30.8 0.7 %fusion.2 = bf16[640,512]{1,0:T(8,128)(2,1)S(1)} fusion(bf16[512,640]{1,0:T(8,128)(2,1)S(1)} %collective-permute-done.6, bf16[640,1280]{1,0:T(8,128)(2,1)S(1)} %copy-done.5), kind=kOutput, calls=%fused_computation.10 | convolution fusion | flops 419758080 | bytes 2129920 | tf_op jit(solution)/shard_map/dot_general | solution.py:105
  31.6 1.2 %pad_maximum_fusion.1.vt_ref = bf16[640,1024]{1,0:T(8,128)(2,1)} fusion(bf16[640,512]{1,0:T(8,128)(2,1)S(1)} %fusion.2, bf16[640,512]{1,0:T(8,128)(2,1)S(1)} %fusion.1), kind=kLoop, calls=%fused_computation.7 | loop fusion | flops 2621440 | bytes 2621440 | tf_op jit(solution)/shard_map/concatenate | solution.py:113
  32.8 0.7 %convolution_convert_fusion.2 = bf16[512,640]{1,0:T(8,128)(2,1)S(1)} fusion(bf16[512,640]{1,0:T(8,128)(2,1)S(1)} %collective-permute-done.6, bf16[640,1280]{1,0:T(8,128)(2,1)S(1)} %copy-done.5), kind=kOutput, calls=%fused_computation.4 | convolution fusion | flops 419758080 | bytes 2129920 | tf_op jit(solution)/shard_map/dot_general | solution.py:104
  33.5 1.2 %pad_maximum_fusion.k_ref = bf16[1024,640]{1,0:T(8,128)(2,1)} fusion(bf16[512,640]{1,0:T(8,128)(2,1)S(1)} %convolution_convert_fusion.2, bf16[512,640]{1,0:T(8,128)(2,1)S(1)} %convolution_convert_fusion.3), kind=kLoop, calls=%fused_computation.6 | loop fusion | flops 2621440 | bytes 2621440 | tf_op jit(solution)/shard_map/concatenate | solution.py:112
  34.7 5.8 %shard_map.82 = bf16[640,256]{1,0:T(8,128)(2,1)} custom-call(bf16[1024,640]{1,0:T(8,128)(2,1)} %pad_maximum_fusion.k_ref, bf16[640,256]{1,0:T(8,128)(2,1)} %fusion.4.qt_ref, bf16[640,1024]{1,0:T(8,128)(2,1)} %pad_maximum_fusion.1.vt_ref), custom_call_target="tpu_custom_call" | custom-call | tf_op jit(solution)/shard_map/pallas_call | solution.py:28
  40.6 1.6 %multiply_reduce_fusion = (f32[256]{0:T(256)S(1)}, f32[256,640]{1,0:T(8,128)S(1)}) fusion(bf16[640,256]{1,0:T(8,128)(2,1)} %shard_map.82, bf16[640,640]{1,0:T(8,128)(2,1)S(1)} %copy-done, bf16[256,640]{1,0:T(8,128)(2,1)S(1)} %bitcast.55), kind=kOutput, calls=%fused_computation.43 | convolution fusion | flops 210370304 | bytes 2130944 | tf_op jit(solution)/shard_map/dot_general | solution.py:115
  42.3 3.3 %collective-permute-start.7 = (bf16[2,128,640]{2,1,0:T(8,128)(2,1)S(1)}, bf16[2,128,640]{2,1,0:T(8,128)(2,1)S(1)}, u32[]{:S(2)}, u32[]{:S(2)}) collective-permute-start(bf16[2,128,640]{2,1,0:T(8,128)(2,1)S(1)} %bitcast.61), channel_id=1, source_target_pairs={{0,4},{4,8},{8,12},{1,5},{5,9},{9,13},{2,6},{6,10},{10,14},{3,7},{... | collective-permute-start | bytes 983048 | tf_op jit(solution)/shard_map/ppermute | solution.py:47
  45.6 1.9 %collective-permute-start.8 = (bf16[2,128,640]{2,1,0:T(8,128)(2,1)S(1)}, bf16[2,128,640]{2,1,0:T(8,128)(2,1)S(1)}, u32[]{:S(2)}, u32[]{:S(2)}) collective-permute-start(bf16[2,128,640]{2,1,0:T(8,128)(2,1)S(1)} %bitcast.62), channel_id=1, source_target_pairs={{4,0},{8,4},{12,8},{5,1},{9,5},{13,9},{6,2},{10,6},{14,10},{7,3},{... | collective-permute-start | bytes 983048 | tf_op jit(solution)/shard_map/ppermute | solution.py:48
  47.6 2.0 %collective-permute-done.7 = bf16[2,128,640]{2,1,0:T(8,128)(2,1)S(1)} collective-permute-done((bf16[2,128,640]{2,1,0:T(8,128)(2,1)S(1)}, bf16[2,128,640]{2,1,0:T(8,128)(2,1)S(1)}, u32[]{:S(2)}, u32[]{:S(2)}) %collective-permute-start.7) | collective-permute-done | bytes 327712 | tf_op jit(solution)/shard_map/ppermute | solution.py:47
  49.6 4.4 %collective-permute-done.8 = bf16[2,128,640]{2,1,0:T(8,128)(2,1)S(1)} collective-permute-done((bf16[2,128,640]{2,1,0:T(8,128)(2,1)S(1)}, bf16[2,128,640]{2,1,0:T(8,128)(2,1)S(1)}, u32[]{:S(2)}, u32[]{:S(2)}) %collective-permute-start.8) | collective-permute-done | bytes 327712 | tf_op jit(solution)/shard_map/ppermute | solution.py:48
  54.3 0.7 %fusion.10 = f32[512,640]{1,0:T(8,128)S(1)} fusion(bf16[512,640]{1,0:T(8,128)(2,1)S(1)} %bitcast.57, bf16[3,640,640]{2,1,0:T(8,128)(2,1)S(1)} %copy-done.3), kind=kOutput, calls=%fused_computation.22 | convolution fusion | flops 419430400 | bytes 2785280 | tf_op jit(solution)/shard_map/dot_general | solution.py:56
  55.0 0.7 %fusion.12 = f32[512,640]{1,0:T(8,128)S(1)} fusion(bf16[512,640]{1,0:T(8,128)(2,1)S(1)} %bitcast.56, bf16[3,640,640]{2,1,0:T(8,128)(2,1)S(1)} %copy-done.3), kind=kOutput, calls=%fused_computation.24 | convolution fusion | flops 419430400 | bytes 2785280 | tf_op jit(solution)/shard_map/dot_general | solution.py:56
  55.8 0.8 %multiply_convert_fusion = bf16[512,640]{1,0:T(8,128)(2,1)S(1)} fusion(f32[512,640]{1,0:T(8,128)S(1)} %fusion.10, f32[512,640]{1,0:T(8,128)S(1)} %fusion.12, bf16[512,640]{1,0:T(8,128)(2,1)S(1)} %bitcast.68, bf16[3,640,640]{2,1,0:T(8,128)(2,1)S(1)} %copy-done.3), kind=kOutput, calls=%fused_computation.8 | convolution fusion | flops 421724160 | bytes 4751360 | tf_op jit(solution)/shard_map/dot_general | solution.py:56
  56.8 1.5 %copy-done.2 = bf16[3,640,640]{2,1,0:T(8,128)(2,1)S(1)} copy-done((bf16[3,640,640]{2,1,0:T(8,128)(2,1)S(1)}, bf16[3,640,640]{2,1,0:T(8,128)(2,1)}, u32[]{:S(2)}) %copy-start.2) | copy-done | bytes 2457624
  58.3 0.5 fusion.8
  58.8 0.5 convolution_add_fusion.2
  59.3 1.2 %fusion.5 = bf16[256,640]{1,0:T(8,128)(2,1)} fusion(f32[256,640]{1,0:T(8,128)S(1)} %get-tuple-element.22, f32[256,640]{1,0:T(8,128)S(1)} %convolution_add_fusion.2, bf16[256,640]{1,0:T(8,128)(2,1)S(1)} %bitcast.60, bf16[3,640,640]{2,1,0:T(8,128)(2,1)S(1)} %copy-done.2), kind=kOutput, calls=%fused_computation.17 | convolution fusion | flops 210206720 | bytes 2785280 | tf_op jit(solution)/shard_map/dot_general | solution.py:56
  (24 shorter events, 1.0 us)
Async XLA Ops:
  0.0 40.6 %copy-start = (bf16[640,640]{1,0:T(8,128)(2,1)S(1)}, bf16[640,640]{1,0:T(8,128)(2,1)}, u32[]{:S(2)}) copy-start(bf16[640,640]{1,0:T(8,128)(2,1)} %param.12) | copy-start | bytes 2457604
  0.0 10.7 %copy-start.1 = (bf16[2,128,640]{2,1,0:T(8,128)(2,1)S(1)}, bf16[2,128,640]{2,1,0:T(8,128)(2,1)}, u32[]{:S(2)}) copy-start(bf16[2,128,640]{2,1,0:T(8,128)(2,1)} %param.8) | copy-start | bytes 983044
  1.2 7.7 %collective-permute-start = (bf16[2,64,640]{2,1,0:T(8,128)(2,1)S(1)}, bf16[2,64,640]{2,1,0:T(8,128)(2,1)S(1)}, u32[]{:S(2)}, u32[]{:S(2)}) collective-permute-start(bf16[2,64,640]{2,1,0:T(8,128)(2,1)S(1)} %get-tuple-element.16), channel_id=1, source_target_pairs={{0,8},{4,12},{8,0},{12,4},{1,9},{5,13},{9,1},{13,5},{2,10},{6,14},... | collective-permute-start | bytes 491528 | tf_op jit(solution)/shard_map/ppermute | solution.py:81
  2.5 6.4 %collective-permute-start.1 = (bf16[2,64,640]{2,1,0:T(8,128)(2,1)S(1)}, bf16[2,64,640]{2,1,0:T(8,128)(2,1)S(1)}, u32[]{:S(2)}, u32[]{:S(2)}) collective-permute-start(bf16[2,64,640]{2,1,0:T(8,128)(2,1)S(1)} %get-tuple-element.18), channel_id=1, source_target_pairs={{0,4},{4,8},{8,12},{12,0},{1,5},{5,9},{9,13},{13,1},{2,6},{6,10},{... | collective-permute-start | bytes 491528 | tf_op jit(solution)/shard_map/ppermute | solution.py:81
  3.6 7.1 %collective-permute-start.2 = (bf16[2,64,640]{2,1,0:T(8,128)(2,1)S(1)}, bf16[2,64,640]{2,1,0:T(8,128)(2,1)S(1)}, u32[]{:S(2)}, u32[]{:S(2)}) collective-permute-start(bf16[2,64,640]{2,1,0:T(8,128)(2,1)S(1)} %get-tuple-element.17), channel_id=1, source_target_pairs={{0,12},{4,0},{8,4},{12,8},{1,13},{5,1},{9,5},{13,9},{2,14},{6,2},{... | collective-permute-start | bytes 491528 | tf_op jit(solution)/shard_map/ppermute | solution.py:81
  6.4 22.7 %copy-start.5 = (bf16[640,1280]{1,0:T(8,128)(2,1)S(1)}, bf16[640,1280]{1,0:T(8,128)(2,1)}, u32[]{:S(2)}) copy-start(bf16[640,1280]{1,0:T(8,128)(2,1)} %param.11) | copy-start | bytes 4915204
  10.9 6.0 %collective-permute-start.3 = (bf16[2,64,640]{2,1,0:T(8,128)(2,1)S(1)}, bf16[2,64,640]{2,1,0:T(8,128)(2,1)S(1)}, u32[]{:S(2)}, u32[]{:S(2)}) collective-permute-start(bf16[2,64,640]{2,1,0:T(8,128)(2,1)S(1)} %pad_maximum_fusion.9), channel_id=1, source_target_pairs={{0,1},{1,2},{2,3},{3,0},{4,5},{5,6},{6,7},{7,4},{8,9},{9,10},{10,1... | collective-permute-start | bytes 491528 | tf_op jit(solution)/shard_map/ppermute | solution.py:89
  12.2 14.3 %collective-permute-start.4 = (bf16[2,64,640]{2,1,0:T(8,128)(2,1)S(1)}, bf16[2,64,640]{2,1,0:T(8,128)(2,1)S(1)}, u32[]{:S(2)}, u32[]{:S(2)}) collective-permute-start(bf16[2,64,640]{2,1,0:T(8,128)(2,1)S(1)} %pad_maximum_fusion.9), channel_id=1, source_target_pairs={{0,2},{1,3},{2,0},{3,1},{4,6},{5,7},{6,4},{7,5},{8,10},{9,11},{10,... | collective-permute-start | bytes 491528 | tf_op jit(solution)/shard_map/ppermute | solution.py:89
  13.3 15.2 %collective-permute-start.5 = (bf16[2,64,640]{2,1,0:T(8,128)(2,1)S(1)}, bf16[2,64,640]{2,1,0:T(8,128)(2,1)S(1)}, u32[]{:S(2)}, u32[]{:S(2)}) collective-permute-start(bf16[2,64,640]{2,1,0:T(8,128)(2,1)S(1)} %pad_maximum_fusion.9), channel_id=1, source_target_pairs={{0,3},{1,0},{2,1},{3,2},{4,7},{5,4},{6,5},{7,6},{8,11},{9,8},{10,9... | collective-permute-start | bytes 491528 | tf_op jit(solution)/shard_map/ppermute | solution.py:89
  28.6 2.2 %collective-permute-start.6 = (bf16[512,640]{1,0:T(8,128)(2,1)S(1)}, bf16[512,640]{1,0:T(8,128)(2,1)S(1)}, u32[]{:S(2)}, u32[]{:S(2)}) collective-permute-start(bf16[512,640]{1,0:T(8,128)(2,1)S(1)} %bitcast.65), channel_id=1, source_target_pairs={{0,4},{4,0},{8,12},{12,8},{1,5},{5,1},{9,13},{13,9},{2,6},{6,2},{1... | collective-permute-start | bytes 1966088 | tf_op jit(solution)/shard_map/ppermute | solution.py:91
  40.6 1.6 %copy-start.4 = (f32[640]{0:T(1024)S(1)}, f32[640]{0:T(1024)}, u32[]{:S(2)}) copy-start(f32[640]{0:T(1024)} %param.13) | copy-start | bytes 7684
  42.3 7.3 %collective-permute-start.7 = (bf16[2,128,640]{2,1,0:T(8,128)(2,1)S(1)}, bf16[2,128,640]{2,1,0:T(8,128)(2,1)S(1)}, u32[]{:S(2)}, u32[]{:S(2)}) collective-permute-start(bf16[2,128,640]{2,1,0:T(8,128)(2,1)S(1)} %bitcast.61), channel_id=1, source_target_pairs={{0,4},{4,8},{8,12},{1,5},{5,9},{9,13},{2,6},{6,10},{10,14},{3,7},{... | collective-permute-start | bytes 983048 | tf_op jit(solution)/shard_map/ppermute | solution.py:47
  45.6 8.4 %collective-permute-start.8 = (bf16[2,128,640]{2,1,0:T(8,128)(2,1)S(1)}, bf16[2,128,640]{2,1,0:T(8,128)(2,1)S(1)}, u32[]{:S(2)}, u32[]{:S(2)}) collective-permute-start(bf16[2,128,640]{2,1,0:T(8,128)(2,1)S(1)} %bitcast.62), channel_id=1, source_target_pairs={{4,0},{8,4},{12,8},{5,1},{9,5},{13,9},{6,2},{10,6},{14,10},{7,3},{... | collective-permute-start | bytes 983048 | tf_op jit(solution)/shard_map/ppermute | solution.py:48
  47.6 6.7 %copy-start.3 = (bf16[3,640,640]{2,1,0:T(8,128)(2,1)S(1)}, bf16[3,640,640]{2,1,0:T(8,128)(2,1)}, u32[]{:S(2)}) copy-start(bf16[3,640,640]{2,1,0:T(8,128)(2,1)} %param.14) | copy-start | bytes 7372804
  56.6 1.7 %copy-start.2 = (bf16[3,640,640]{2,1,0:T(8,128)(2,1)S(1)}, bf16[3,640,640]{2,1,0:T(8,128)(2,1)}, u32[]{:S(2)}) copy-start(bf16[3,640,640]{2,1,0:T(8,128)(2,1)} %param.15) | copy-start | bytes 7372804

commit v25 on v24

--- a/solution.py
+++ b/solution.py
@@ -77,7 +77,7 @@
         me == owner_a, lax.dynamic_index_in_dim(own, slot_a, 0, keepdims=False), jnp.zeros_like(own[0])
     )
     got_b = own[n_loc - 1]
-    for s in sorted(range(1, fsize), key=lambda s: (s == fsize // 2, -s)):
+    for s in sorted(range(1, fsize), key=lambda s: (s != fsize // 2, -s)):
         recv = lax.ppermute(halves((me + s) % 2), "frame", [(i, (i + s) % fsize) for i in range(fsize)])
         source = (me - s) % fsize
         got_a = jnp.where(source == owner_a, lax.dynamic_index_in_dim(recv, slot_a, 0, keepdims=False), got_a)

time: 60.8 us -> 61.2 us (level)
  starting transfers between devices: 12 us -> 13.2 us
  waiting for transfers between devices: 22.2 us -> 21.5 us
    ppermute x1, starting transfers between devices: 3.32 us -> 4.39 us  [extended(): before = lax.ppermute(last, axis, up)]
    ppermute x3, waiting for transfers between devices: 1.8 us -> 1.11 us  [gather_keyframes(): lax.ppermute(halves((me + s) % 2), 'frame', [(i, (i + s) % fsize) for i i...]
  transfers between devices with their start and end apart: 9 -> 9, of which waited for: 7 -> 8; matrix products, arithmetic and copies ran while one was open for 9% -> 9% of each run, Pallas kernels for 0% -> 0%
where the time goes in v25:
time: 61.2 us; the launch traced here: 60.9 us
  waiting for transfers between devices  21.5 us (35%)
  starting transfers between devices  13.2 us (22%)
  matrix products  11.5 us (19%)
  Pallas kernels  5.84 us (10%)
  local copies, waits for them, and re-layouts  4.11 us (7%)
  other arithmetic  3.16 us (5%)
  between operations  1.65 us (3%)
    ppermute x3, waiting for transfers between devices, gather_keyframes(): lax.ppermute(piece, 'row', [(i, (i + s) % rsize) for i in range(rsize)])  13.7 us
    pallas_call x1, Pallas kernels, attend(): pl.pallas_call(attention_kernel, grid=(channels // width,), in_specs=[pl....  5.84 us
    dot_general x6, matrix products, temporal_mix(): jnp.dot(window, weights[offset], preferred_element_type=jnp.float32)  4.44 us
    ppermute x1, waiting for transfers between devices, extended(): after = lax.ppermute(first, axis, down)  4.4 us
    ppermute x1, starting transfers between devices, extended(): before = lax.ppermute(last, axis, up)  4.39 us
    ppermute x3, starting transfers between devices, gather_keyframes(): lax.ppermute(piece, 'row', [(i, (i + s) % rsize) for i in range(rsize)])  3.83 us
    dot_general x1, matrix products, shards(): lax.dot_general(w_query, flattened, (((0,), (1,)), ((), ())), preferred_e...  2.53 us
    ppermute x3, starting transfers between devices, gather_keyframes(): lax.ppermute(halves((me + s) % 2), 'frame', [(i, (i + s) % fsize) for i i...  2.11 us
  transfers between devices with their start and end apart: 9, of which 8 were waited for; matrix products, arithmetic and copies ran while one was open for 9% of the time, Pallas kernels for 0%

profile of v25, /device:TPU:9, one launch (start us, length us, event | category | flops | bytes accessed | tf_op | source)
XLA Modules:
  0.0 60.9 jit_solution(8630682207668800030)
XLA Ops:
  0.0 1.2 %constant_dynamic-slice_fusion.2 = (bf16[2,64,640]{2,1,0:T(8,128)(2,1)S(1)}, bf16[2,64,640]{2,1,0:T(8,128)(2,1)S(1)}, bf16[2,64,640]{2,1,0:T(8,128)(2,1)S(1)}) fusion(bf16[2,128,640]{2,1,0:T(8,128)(2,1)} %param.8, s32[]{:T(128)S(6)} %select_n.137, s32[]{:T(128)S(6)} %select_n.147, s32[]{:T(128)S(6)} %select_n.143), kind=kLoop, calls=%fused_computation.57 | loop fusion | bytes 983052 | tf_op jit(solution)/shard_map/dynamic_slice | solution.py:73
  1.2 1.8 %collective-permute-start = (bf16[2,64,640]{2,1,0:T(8,128)(2,1)S(1)}, bf16[2,64,640]{2,1,0:T(8,128)(2,1)S(1)}, u32[]{:S(2)}, u32[]{:S(2)}) collective-permute-start(bf16[2,64,640]{2,1,0:T(8,128)(2,1)S(1)} %get-tuple-element.16), channel_id=1, source_target_pairs={{0,4},{4,8},{8,12},{12,0},{1,5},{5,9},{9,13},{13,1},{2,6},{6,10},{... | collective-permute-start | bytes 491528 | tf_op jit(solution)/shard_map/ppermute | solution.py:81
  3.0 0.3 collective-permute-start.2
  3.3 1.3 %fusion.30 = (s32[1]{0:T(128)}, s32[1]{0:T(128)}) fusion(s32[2]{0:T(128)} %param.9), kind=kLoop, calls=%fused_computation.60 | loop fusion | bytes 16 | tf_op jit(solution)/shard_map/slice | solution.py:66
  6.1 2.5 %fusion.4.qt_ref = bf16[640,256]{1,0:T(8,128)(2,1)} fusion(bf16[640,640]{1,0:T(8,128)(2,1)} %param.10, bf16[256,640]{1,0:T(8,128)(2,1)} %bitcast.54), kind=kOutput, calls=%fused_computation.16 | convolution fusion | flops 210042880 | bytes 1474560 | tf_op jit(solution)/shard_map/dot_general | solution.py:99
  8.7 0.9 %collective-permute-done.1 = bf16[2,64,640]{2,1,0:T(8,128)(2,1)S(1)} collective-permute-done((bf16[2,64,640]{2,1,0:T(8,128)(2,1)S(1)}, bf16[2,64,640]{2,1,0:T(8,128)(2,1)S(1)}, u32[]{:S(2)}, u32[]{:S(2)}) %collective-permute-start.1) | collective-permute-done | bytes 163872 | tf_op jit(solution)/shard_map/ppermute | solution.py:81
  9.9 1.4 %collective-permute-start.3 = (bf16[2,64,640]{2,1,0:T(8,128)(2,1)S(1)}, bf16[2,64,640]{2,1,0:T(8,128)(2,1)S(1)}, u32[]{:S(2)}, u32[]{:S(2)}) collective-permute-start(bf16[2,64,640]{2,1,0:T(8,128)(2,1)S(1)} %pad_maximum_fusion.9), channel_id=1, source_target_pairs={{0,1},{1,2},{2,3},{3,0},{4,5},{5,6},{6,7},{7,4},{8,9},{9,10},{10,1... | collective-permute-start | bytes 491528 | tf_op jit(solution)/shard_map/ppermute | solution.py:89
  11.3 1.7 %collective-permute-start.4 = (bf16[2,64,640]{2,1,0:T(8,128)(2,1)S(1)}, bf16[2,64,640]{2,1,0:T(8,128)(2,1)S(1)}, u32[]{:S(2)}, u32[]{:S(2)}) collective-permute-start(bf16[2,64,640]{2,1,0:T(8,128)(2,1)S(1)} %pad_maximum_fusion.9), channel_id=1, source_target_pairs={{0,2},{1,3},{2,0},{3,1},{4,6},{5,7},{6,4},{7,5},{8,10},{9,11},{10,... | collective-permute-start | bytes 491528 | tf_op jit(solution)/shard_map/ppermute | solution.py:89
  13.0 0.8 %collective-permute-start.5 = (bf16[2,64,640]{2,1,0:T(8,128)(2,1)S(1)}, bf16[2,64,640]{2,1,0:T(8,128)(2,1)S(1)}, u32[]{:S(2)}, u32[]{:S(2)}) collective-permute-start(bf16[2,64,640]{2,1,0:T(8,128)(2,1)S(1)} %pad_maximum_fusion.9), channel_id=1, source_target_pairs={{0,3},{1,0},{2,1},{3,2},{4,7},{5,4},{6,5},{7,6},{8,11},{9,8},{10,9... | collective-permute-start | bytes 491528 | tf_op jit(solution)/shard_map/ppermute | solution.py:89
  13.8 0.4 collective-permute-done.3
  14.1 9.2 %collective-permute-done.4 = bf16[2,64,640]{2,1,0:T(8,128)(2,1)S(1)} collective-permute-done((bf16[2,64,640]{2,1,0:T(8,128)(2,1)S(1)}, bf16[2,64,640]{2,1,0:T(8,128)(2,1)S(1)}, u32[]{:S(2)}, u32[]{:S(2)}) %collective-permute-start.4) | collective-permute-done | bytes 163872 | tf_op jit(solution)/shard_map/ppermute | solution.py:89
  23.3 4.1 %collective-permute-done.5 = bf16[2,64,640]{2,1,0:T(8,128)(2,1)S(1)} collective-permute-done((bf16[2,64,640]{2,1,0:T(8,128)(2,1)S(1)}, bf16[2,64,640]{2,1,0:T(8,128)(2,1)S(1)}, u32[]{:S(2)}, u32[]{:S(2)}) %collective-permute-start.5) | collective-permute-done | bytes 163872 | tf_op jit(solution)/shard_map/ppermute | solution.py:89
  27.5 1.0 %collective-permute-start.6 = (bf16[512,640]{1,0:T(8,128)(2,1)S(1)}, bf16[512,640]{1,0:T(8,128)(2,1)S(1)}, u32[]{:S(2)}, u32[]{:S(2)}) collective-permute-start(bf16[512,640]{1,0:T(8,128)(2,1)S(1)} %bitcast.65), channel_id=1, source_target_pairs={{0,4},{4,0},{8,12},{12,8},{1,5},{5,1},{9,13},{13,9},{2,6},{6,2},{1... | collective-permute-start | bytes 1966088 | tf_op jit(solution)/shard_map/ppermute | solution.py:91
  28.5 0.7 %fusion.1 = bf16[640,512]{1,0:T(8,128)(2,1)S(1)} fusion(bf16[512,640]{1,0:T(8,128)(2,1)S(1)} %bitcast.66, bf16[640,1280]{1,0:T(8,128)(2,1)S(1)} %copy-done.5), kind=kOutput, calls=%fused_computation.9 | convolution fusion | flops 419758080 | bytes 2129920 | tf_op jit(solution)/shard_map/dot_general | solution.py:105
  29.2 0.7 %convolution_convert_fusion.3 = bf16[512,640]{1,0:T(8,128)(2,1)S(1)} fusion(bf16[512,640]{1,0:T(8,128)(2,1)S(1)} %bitcast.67, bf16[640,1280]{1,0:T(8,128)(2,1)S(1)} %copy-done.5), kind=kOutput, calls=%fused_computation.5 | convolution fusion | flops 419758080 | bytes 2129920 | tf_op jit(solution)/shard_map/dot_general | solution.py:104
  30.2 0.7 %fusion.2 = bf16[640,512]{1,0:T(8,128)(2,1)S(1)} fusion(bf16[512,640]{1,0:T(8,128)(2,1)S(1)} %collective-permute-done.6, bf16[640,1280]{1,0:T(8,128)(2,1)S(1)} %copy-done.5), kind=kOutput, calls=%fused_computation.10 | convolution fusion | flops 419758080 | bytes 2129920 | tf_op jit(solution)/shard_map/dot_general | solution.py:105
  30.9 1.2 %pad_maximum_fusion.1.vt_ref = bf16[640,1024]{1,0:T(8,128)(2,1)} fusion(bf16[640,512]{1,0:T(8,128)(2,1)S(1)} %fusion.2, bf16[640,512]{1,0:T(8,128)(2,1)S(1)} %fusion.1), kind=kLoop, calls=%fused_computation.7 | loop fusion | flops 2621440 | bytes 2621440 | tf_op jit(solution)/shard_map/concatenate | solution.py:113
  32.2 0.7 %convolution_convert_fusion.2 = bf16[512,640]{1,0:T(8,128)(2,1)S(1)} fusion(bf16[512,640]{1,0:T(8,128)(2,1)S(1)} %collective-permute-done.6, bf16[640,1280]{1,0:T(8,128)(2,1)S(1)} %copy-done.5), kind=kOutput, calls=%fused_computation.4 | convolution fusion | flops 419758080 | bytes 2129920 | tf_op jit(solution)/shard_map/dot_general | solution.py:104
  32.9 1.2 %pad_maximum_fusion.k_ref = bf16[1024,640]{1,0:T(8,128)(2,1)} fusion(bf16[512,640]{1,0:T(8,128)(2,1)S(1)} %convolution_convert_fusion.2, bf16[512,640]{1,0:T(8,128)(2,1)S(1)} %convolution_convert_fusion.3), kind=kLoop, calls=%fused_computation.6 | loop fusion | flops 2621440 | bytes 2621440 | tf_op jit(solution)/shard_map/concatenate | solution.py:112
  34.1 5.8 %shard_map.82 = bf16[640,256]{1,0:T(8,128)(2,1)} custom-call(bf16[1024,640]{1,0:T(8,128)(2,1)} %pad_maximum_fusion.k_ref, bf16[640,256]{1,0:T(8,128)(2,1)} %fusion.4.qt_ref, bf16[640,1024]{1,0:T(8,128)(2,1)} %pad_maximum_fusion.1.vt_ref), custom_call_target="tpu_custom_call" | custom-call | tf_op jit(solution)/shard_map/pallas_call | solution.py:28
  40.0 1.6 %multiply_reduce_fusion = (f32[256]{0:T(256)S(1)}, f32[256,640]{1,0:T(8,128)S(1)}) fusion(bf16[640,256]{1,0:T(8,128)(2,1)} %shard_map.82, bf16[640,640]{1,0:T(8,128)(2,1)S(1)} %copy-done, bf16[256,640]{1,0:T(8,128)(2,1)S(1)} %bitcast.55), kind=kOutput, calls=%fused_computation.43 | convolution fusion | flops 210370304 | bytes 2130944 | tf_op jit(solution)/shard_map/dot_general | solution.py:115
  41.7 4.4 %collective-permute-start.7 = (bf16[2,128,640]{2,1,0:T(8,128)(2,1)S(1)}, bf16[2,128,640]{2,1,0:T(8,128)(2,1)S(1)}, u32[]{:S(2)}, u32[]{:S(2)}) collective-permute-start(bf16[2,128,640]{2,1,0:T(8,128)(2,1)S(1)} %bitcast.61), channel_id=1, source_target_pairs={{0,4},{4,8},{8,12},{1,5},{5,9},{9,13},{2,6},{6,10},{10,14},{3,7},{... | collective-permute-start | bytes 983048 | tf_op jit(solution)/shard_map/ppermute | solution.py:47
  46.1 1.9 %collective-permute-start.8 = (bf16[2,128,640]{2,1,0:T(8,128)(2,1)S(1)}, bf16[2,128,640]{2,1,0:T(8,128)(2,1)S(1)}, u32[]{:S(2)}, u32[]{:S(2)}) collective-permute-start(bf16[2,128,640]{2,1,0:T(8,128)(2,1)S(1)} %bitcast.62), channel_id=1, source_target_pairs={{4,0},{8,4},{12,8},{5,1},{9,5},{13,9},{6,2},{10,6},{14,10},{7,3},{... | collective-permute-start | bytes 983048 | tf_op jit(solution)/shard_map/ppermute | solution.py:48
  48.0 2.0 %collective-permute-done.7 = bf16[2,128,640]{2,1,0:T(8,128)(2,1)S(1)} collective-permute-done((bf16[2,128,640]{2,1,0:T(8,128)(2,1)S(1)}, bf16[2,128,640]{2,1,0:T(8,128)(2,1)S(1)}, u32[]{:S(2)}, u32[]{:S(2)}) %collective-permute-start.7) | collective-permute-done | bytes 327712 | tf_op jit(solution)/shard_map/ppermute | solution.py:47
  50.1 4.4 %collective-permute-done.8 = bf16[2,128,640]{2,1,0:T(8,128)(2,1)S(1)} collective-permute-done((bf16[2,128,640]{2,1,0:T(8,128)(2,1)S(1)}, bf16[2,128,640]{2,1,0:T(8,128)(2,1)S(1)}, u32[]{:S(2)}, u32[]{:S(2)}) %collective-permute-start.8) | collective-permute-done | bytes 327712 | tf_op jit(solution)/shard_map/ppermute | solution.py:48
  54.7 0.7 %fusion.10 = f32[512,640]{1,0:T(8,128)S(1)} fusion(bf16[512,640]{1,0:T(8,128)(2,1)S(1)} %bitcast.57, bf16[3,640,640]{2,1,0:T(8,128)(2,1)S(1)} %copy-done.3), kind=kOutput, calls=%fused_computation.22 | convolution fusion | flops 419430400 | bytes 2785280 | tf_op jit(solution)/shard_map/dot_general | solution.py:56
  55.5 0.7 %fusion.12 = f32[512,640]{1,0:T(8,128)S(1)} fusion(bf16[512,640]{1,0:T(8,128)(2,1)S(1)} %bitcast.56, bf16[3,640,640]{2,1,0:T(8,128)(2,1)S(1)} %copy-done.3), kind=kOutput, calls=%fused_computation.24 | convolution fusion | flops 419430400 | bytes 2785280 | tf_op jit(solution)/shard_map/dot_general | solution.py:56
  56.2 0.8 %multiply_convert_fusion = bf16[512,640]{1,0:T(8,128)(2,1)S(1)} fusion(f32[512,640]{1,0:T(8,128)S(1)} %fusion.10, f32[512,640]{1,0:T(8,128)S(1)} %fusion.12, bf16[512,640]{1,0:T(8,128)(2,1)S(1)} %bitcast.68, bf16[3,640,640]{2,1,0:T(8,128)(2,1)S(1)} %copy-done.3), kind=kOutput, calls=%fused_computation.8 | convolution fusion | flops 421724160 | bytes 4751360 | tf_op jit(solution)/shard_map/dot_general | solution.py:56
  57.2 1.5 %copy-done.2 = bf16[3,640,640]{2,1,0:T(8,128)(2,1)S(1)} copy-done((bf16[3,640,640]{2,1,0:T(8,128)(2,1)S(1)}, bf16[3,640,640]{2,1,0:T(8,128)(2,1)}, u32[]{:S(2)}) %copy-start.2) | copy-done | bytes 2457624
  58.8 0.5 fusion.8
  59.2 0.5 convolution_add_fusion.2
  59.7 1.2 %fusion.5 = bf16[256,640]{1,0:T(8,128)(2,1)} fusion(f32[256,640]{1,0:T(8,128)S(1)} %get-tuple-element.22, f32[256,640]{1,0:T(8,128)S(1)} %convolution_add_fusion.2, bf16[256,640]{1,0:T(8,128)(2,1)S(1)} %bitcast.60, bf16[3,640,640]{2,1,0:T(8,128)(2,1)S(1)} %copy-done.2), kind=kOutput, calls=%fused_computation.17 | convolution fusion | flops 210206720 | bytes 2785280 | tf_op jit(solution)/shard_map/dot_general | solution.py:56
  (24 shorter events, 1.3 us)
Async XLA Ops:
  0.0 40.0 %copy-start = (bf16[640,640]{1,0:T(8,128)(2,1)S(1)}, bf16[640,640]{1,0:T(8,128)(2,1)}, u32[]{:S(2)}) copy-start(bf16[640,640]{1,0:T(8,128)(2,1)} %param.12) | copy-start | bytes 2457604
  0.0 9.8 %copy-start.1 = (bf16[2,128,640]{2,1,0:T(8,128)(2,1)S(1)}, bf16[2,128,640]{2,1,0:T(8,128)(2,1)}, u32[]{:S(2)}) copy-start(bf16[2,128,640]{2,1,0:T(8,128)(2,1)} %param.8) | copy-start | bytes 983044
  1.2 7.4 %collective-permute-start = (bf16[2,64,640]{2,1,0:T(8,128)(2,1)S(1)}, bf16[2,64,640]{2,1,0:T(8,128)(2,1)S(1)}, u32[]{:S(2)}, u32[]{:S(2)}) collective-permute-start(bf16[2,64,640]{2,1,0:T(8,128)(2,1)S(1)} %get-tuple-element.16), channel_id=1, source_target_pairs={{0,4},{4,8},{8,12},{12,0},{1,5},{5,9},{9,13},{13,1},{2,6},{6,10},{... | collective-permute-start | bytes 491528 | tf_op jit(solution)/shard_map/ppermute | solution.py:81
  3.0 6.5 %collective-permute-start.1 = (bf16[2,64,640]{2,1,0:T(8,128)(2,1)S(1)}, bf16[2,64,640]{2,1,0:T(8,128)(2,1)S(1)}, u32[]{:S(2)}, u32[]{:S(2)}) collective-permute-start(bf16[2,64,640]{2,1,0:T(8,128)(2,1)S(1)} %get-tuple-element.18), channel_id=1, source_target_pairs={{0,12},{4,0},{8,4},{12,8},{1,13},{5,1},{9,5},{13,9},{2,14},{6,2},{... | collective-permute-start | bytes 491528 | tf_op jit(solution)/shard_map/ppermute | solution.py:81
  3.0 6.7 %collective-permute-start.2 = (bf16[2,64,640]{2,1,0:T(8,128)(2,1)S(1)}, bf16[2,64,640]{2,1,0:T(8,128)(2,1)S(1)}, u32[]{:S(2)}, u32[]{:S(2)}) collective-permute-start(bf16[2,64,640]{2,1,0:T(8,128)(2,1)S(1)} %get-tuple-element.17), channel_id=1, source_target_pairs={{0,8},{4,12},{8,0},{12,4},{1,9},{5,13},{9,1},{13,5},{2,10},{6,14},... | collective-permute-start | bytes 491528 | tf_op jit(solution)/shard_map/ppermute | solution.py:81
  6.1 22.4 %copy-start.5 = (bf16[640,1280]{1,0:T(8,128)(2,1)S(1)}, bf16[640,1280]{1,0:T(8,128)(2,1)}, u32[]{:S(2)}) copy-start(bf16[640,1280]{1,0:T(8,128)(2,1)} %param.11) | copy-start | bytes 4915204
  9.9 4.2 %collective-permute-start.3 = (bf16[2,64,640]{2,1,0:T(8,128)(2,1)S(1)}, bf16[2,64,640]{2,1,0:T(8,128)(2,1)S(1)}, u32[]{:S(2)}, u32[]{:S(2)}) collective-permute-start(bf16[2,64,640]{2,1,0:T(8,128)(2,1)S(1)} %pad_maximum_fusion.9), channel_id=1, source_target_pairs={{0,1},{1,2},{2,3},{3,0},{4,5},{5,6},{6,7},{7,4},{8,9},{9,10},{10,1... | collective-permute-start | bytes 491528 | tf_op jit(solution)/shard_map/ppermute | solution.py:89
  11.3 12.0 %collective-permute-start.4 = (bf16[2,64,640]{2,1,0:T(8,128)(2,1)S(1)}, bf16[2,64,640]{2,1,0:T(8,128)(2,1)S(1)}, u32[]{:S(2)}, u32[]{:S(2)}) collective-permute-start(bf16[2,64,640]{2,1,0:T(8,128)(2,1)S(1)} %pad_maximum_fusion.9), channel_id=1, source_target_pairs={{0,2},{1,3},{2,0},{3,1},{4,6},{5,7},{6,4},{7,5},{8,10},{9,11},{10,... | collective-permute-start | bytes 491528 | tf_op jit(solution)/shard_map/ppermute | solution.py:89
  13.0 14.5 %collective-permute-start.5 = (bf16[2,64,640]{2,1,0:T(8,128)(2,1)S(1)}, bf16[2,64,640]{2,1,0:T(8,128)(2,1)S(1)}, u32[]{:S(2)}, u32[]{:S(2)}) collective-permute-start(bf16[2,64,640]{2,1,0:T(8,128)(2,1)S(1)} %pad_maximum_fusion.9), channel_id=1, source_target_pairs={{0,3},{1,0},{2,1},{3,2},{4,7},{5,4},{6,5},{7,6},{8,11},{9,8},{10,9... | collective-permute-start | bytes 491528 | tf_op jit(solution)/shard_map/ppermute | solution.py:89
  27.5 2.7 %collective-permute-start.6 = (bf16[512,640]{1,0:T(8,128)(2,1)S(1)}, bf16[512,640]{1,0:T(8,128)(2,1)S(1)}, u32[]{:S(2)}, u32[]{:S(2)}) collective-permute-start(bf16[512,640]{1,0:T(8,128)(2,1)S(1)} %bitcast.65), channel_id=1, source_target_pairs={{0,4},{4,0},{8,12},{12,8},{1,5},{5,1},{9,13},{13,9},{2,6},{6,2},{1... | collective-permute-start | bytes 1966088 | tf_op jit(solution)/shard_map/ppermute | solution.py:91
  40.0 1.6 %copy-start.4 = (f32[640]{0:T(1024)S(1)}, f32[640]{0:T(1024)}, u32[]{:S(2)}) copy-start(f32[640]{0:T(1024)} %param.13) | copy-start | bytes 7684
  41.7 8.4 %collective-permute-start.7 = (bf16[2,128,640]{2,1,0:T(8,128)(2,1)S(1)}, bf16[2,128,640]{2,1,0:T(8,128)(2,1)S(1)}, u32[]{:S(2)}, u32[]{:S(2)}) collective-permute-start(bf16[2,128,640]{2,1,0:T(8,128)(2,1)S(1)} %bitcast.61), channel_id=1, source_target_pairs={{0,4},{4,8},{8,12},{1,5},{5,9},{9,13},{2,6},{6,10},{10,14},{3,7},{... | collective-permute-start | bytes 983048 | tf_op jit(solution)/shard_map/ppermute | solution.py:47
  46.1 8.4 %collective-permute-start.8 = (bf16[2,128,640]{2,1,0:T(8,128)(2,1)S(1)}, bf16[2,128,640]{2,1,0:T(8,128)(2,1)S(1)}, u32[]{:S(2)}, u32[]{:S(2)}) collective-permute-start(bf16[2,128,640]{2,1,0:T(8,128)(2,1)S(1)} %bitcast.62), channel_id=1, source_target_pairs={{4,0},{8,4},{12,8},{5,1},{9,5},{13,9},{6,2},{10,6},{14,10},{7,3},{... | collective-permute-start | bytes 983048 | tf_op jit(solution)/shard_map/ppermute | solution.py:48
  48.0 6.7 %copy-start.3 = (bf16[3,640,640]{2,1,0:T(8,128)(2,1)S(1)}, bf16[3,640,640]{2,1,0:T(8,128)(2,1)}, u32[]{:S(2)}) copy-start(bf16[3,640,640]{2,1,0:T(8,128)(2,1)} %param.14) | copy-start | bytes 7372804
  57.1 1.7 %copy-start.2 = (bf16[3,640,640]{2,1,0:T(8,128)(2,1)S(1)}, bf16[3,640,640]{2,1,0:T(8,128)(2,1)}, u32[]{:S(2)}) copy-start(bf16[3,640,640]{2,1,0:T(8,128)(2,1)} %param.15) | copy-start | bytes 7372804

commit v26 on v14

--- a/solution.py
+++ b/solution.py
@@ -85,7 +85,7 @@
     piece = jnp.stack([got_a, got_b])
     piece, early = lax.optimization_barrier((piece, early))
     pieces = [piece]
-    for s in range(1, rsize):
+    for s in reversed(range(1, rsize)):
         pieces.append(lax.ppermute(piece, "row", [(i, (i + s) % rsize) for i in range(rsize)]))
     mine = jnp.stack(pieces).reshape(-1, channels)
     sibling = lax.ppermute(mine, "frame", [(i, i ^ 1) for i in range(fsize)])

time: 59.8 us -> 61.8 us (1.033)
  the two profiles are of different devices: /device:TPU:9 before, /device:TPU:1 now
where the time goes in v26:
time: 61.8 us; the launch traced here: 61.4 us
  waiting for transfers between devices  21 us (34%)
  starting transfers between devices  14.2 us (23%)
  matrix products  11.5 us (19%)
  Pallas kernels  5.84 us (9%)
  local copies, waits for them, and re-layouts  4.11 us (7%)
  other arithmetic  3.16 us (5%)
  between operations  1.65 us (3%)
    ppermute x3, waiting for transfers between devices, gather_keyframes(): lax.ppermute(piece, 'row', [(i, (i + s) % rsize) for i in range(rsize)])  13.5 us
    pallas_call x1, Pallas kernels, attend(): pl.pallas_call(attention_kernel, grid=(channels // width,), in_specs=[pl....  5.84 us
    dot_general x6, matrix products, temporal_mix(): jnp.dot(window, weights[offset], preferred_element_type=jnp.float32)  4.43 us
    ppermute x1, waiting for transfers between devices, extended(): after = lax.ppermute(first, axis, down)  4.4 us
    ppermute x3, starting transfers between devices, gather_keyframes(): lax.ppermute(halves((me + s) % 2), 'frame', [(i, (i + s) % fsize) for i i...  4.12 us
    ppermute x3, starting transfers between devices, gather_keyframes(): lax.ppermute(piece, 'row', [(i, (i + s) % rsize) for i in range(rsize)])  3.83 us
    ppermute x1, starting transfers between devices, extended(): before = lax.ppermute(last, axis, up)  3.35 us
    dot_general x1, matrix products, shards(): lax.dot_general(w_query, flattened, (((0,), (1,)), ((), ())), preferred_e...  2.54 us
  transfers between devices with their start and end apart: 9, of which 6 were waited for; matrix products, arithmetic and copies ran while one was open for 9% of the time, Pallas kernels for 0%

profile of v26, /device:TPU:1, one launch (start us, length us, event | category | flops | bytes accessed | tf_op | source)
XLA Modules:
  0.0 61.4 jit_solution(14895857123530148372)
XLA Ops:
  0.0 1.2 %constant_dynamic-slice_fusion.2 = (bf16[2,64,640]{2,1,0:T(8,128)(2,1)S(1)}, bf16[2,64,640]{2,1,0:T(8,128)(2,1)S(1)}, bf16[2,64,640]{2,1,0:T(8,128)(2,1)S(1)}) fusion(bf16[2,128,640]{2,1,0:T(8,128)(2,1)} %param.8, s32[]{:T(128)S(6)} %select_n.137, s32[]{:T(128)S(6)} %select_n.147, s32[]{:T(128)S(6)} %select_n.143), kind=kLoop, calls=%fused_computation.57 | loop fusion | bytes 983052 | tf_op jit(solution)/shard_map/dynamic_slice | solution.py:73
  1.3 2.7 %collective-permute-start.1 = (bf16[2,64,640]{2,1,0:T(8,128)(2,1)S(1)}, bf16[2,64,640]{2,1,0:T(8,128)(2,1)S(1)}, u32[]{:S(2)}, u32[]{:S(2)}) collective-permute-start(bf16[2,64,640]{2,1,0:T(8,128)(2,1)S(1)} %get-tuple-element.18), channel_id=1, source_target_pairs={{0,8},{4,12},{8,0},{12,4},{1,9},{5,13},{9,1},{13,5},{2,10},{6,14},... | collective-permute-start | bytes 491528 | tf_op jit(solution)/shard_map/ppermute | solution.py:81
  4.0 1.3 %collective-permute-start.2 = (bf16[2,64,640]{2,1,0:T(8,128)(2,1)S(1)}, bf16[2,64,640]{2,1,0:T(8,128)(2,1)S(1)}, u32[]{:S(2)}, u32[]{:S(2)}) collective-permute-start(bf16[2,64,640]{2,1,0:T(8,128)(2,1)S(1)} %get-tuple-element.17), channel_id=1, source_target_pairs={{0,4},{4,8},{8,12},{12,0},{1,5},{5,9},{9,13},{13,1},{2,6},{6,10},{... | collective-permute-start | bytes 491528 | tf_op jit(solution)/shard_map/ppermute | solution.py:81
  5.3 1.3 %fusion.30 = (s32[1]{0:T(128)}, s32[1]{0:T(128)}) fusion(s32[2]{0:T(128)} %param.9), kind=kLoop, calls=%fused_computation.60 | loop fusion | bytes 16 | tf_op jit(solution)/shard_map/slice | solution.py:66
  8.1 2.5 %fusion.4.qt_ref = bf16[640,256]{1,0:T(8,128)(2,1)} fusion(bf16[640,640]{1,0:T(8,128)(2,1)} %param.10, bf16[256,640]{1,0:T(8,128)(2,1)} %bitcast.54), kind=kOutput, calls=%fused_computation.16 | convolution fusion | flops 210042880 | bytes 1474560 | tf_op jit(solution)/shard_map/dot_general | solution.py:99
  10.7 0.8 %collective-permute-done.2 = bf16[2,64,640]{2,1,0:T(8,128)(2,1)S(1)} collective-permute-done((bf16[2,64,640]{2,1,0:T(8,128)(2,1)S(1)}, bf16[2,64,640]{2,1,0:T(8,128)(2,1)S(1)}, u32[]{:S(2)}, u32[]{:S(2)}) %collective-permute-start.2) | collective-permute-done | bytes 163872 | tf_op jit(solution)/shard_map/ppermute | solution.py:81
  11.7 3.4 %collective-permute-start.3 = (bf16[2,64,640]{2,1,0:T(8,128)(2,1)S(1)}, bf16[2,64,640]{2,1,0:T(8,128)(2,1)S(1)}, u32[]{:S(2)}, u32[]{:S(2)}) collective-permute-start(bf16[2,64,640]{2,1,0:T(8,128)(2,1)S(1)} %pad_maximum_fusion.9), channel_id=1, source_target_pairs={{0,3},{1,0},{2,1},{3,2},{4,7},{5,4},{6,5},{7,6},{8,11},{9,8},{10,9... | collective-permute-start | bytes 491528 | tf_op jit(solution)/shard_map/ppermute | solution.py:89
  15.0 0.5 collective-permute-start.5
  15.5 1.9 %collective-permute-done.3 = bf16[2,64,640]{2,1,0:T(8,128)(2,1)S(1)} collective-permute-done((bf16[2,64,640]{2,1,0:T(8,128)(2,1)S(1)}, bf16[2,64,640]{2,1,0:T(8,128)(2,1)S(1)}, u32[]{:S(2)}, u32[]{:S(2)}) %collective-permute-start.3) | collective-permute-done | bytes 163872 | tf_op jit(solution)/shard_map/ppermute | solution.py:89
  17.3 11.6 %collective-permute-done.4 = bf16[2,64,640]{2,1,0:T(8,128)(2,1)S(1)} collective-permute-done((bf16[2,64,640]{2,1,0:T(8,128)(2,1)S(1)}, bf16[2,64,640]{2,1,0:T(8,128)(2,1)S(1)}, u32[]{:S(2)}, u32[]{:S(2)}) %collective-permute-start.4) | collective-permute-done | bytes 163872 | tf_op jit(solution)/shard_map/ppermute | solution.py:89
  29.1 1.0 %collective-permute-start.6 = (bf16[512,640]{1,0:T(8,128)(2,1)S(1)}, bf16[512,640]{1,0:T(8,128)(2,1)S(1)}, u32[]{:S(2)}, u32[]{:S(2)}) collective-permute-start(bf16[512,640]{1,0:T(8,128)(2,1)S(1)} %bitcast.65), channel_id=1, source_target_pairs={{0,4},{4,0},{8,12},{12,8},{1,5},{5,1},{9,13},{13,9},{2,6},{6,2},{1... | collective-permute-start | bytes 1966088 | tf_op jit(solution)/shard_map/ppermute | solution.py:91
  30.1 0.7 %fusion.1 = bf16[640,512]{1,0:T(8,128)(2,1)S(1)} fusion(bf16[512,640]{1,0:T(8,128)(2,1)S(1)} %bitcast.66, bf16[640,1280]{1,0:T(8,128)(2,1)S(1)} %copy-done.5), kind=kOutput, calls=%fused_computation.9 | convolution fusion | flops 419758080 | bytes 2129920 | tf_op jit(solution)/shard_map/dot_general | solution.py:105
  30.8 0.7 %convolution_convert_fusion.3 = bf16[512,640]{1,0:T(8,128)(2,1)S(1)} fusion(bf16[512,640]{1,0:T(8,128)(2,1)S(1)} %bitcast.67, bf16[640,1280]{1,0:T(8,128)(2,1)S(1)} %copy-done.5), kind=kOutput, calls=%fused_computation.5 | convolution fusion | flops 419758080 | bytes 2129920 | tf_op jit(solution)/shard_map/dot_general | solution.py:104
  31.6 0.2 collective-permute-done.6
  31.8 0.7 %fusion.2 = bf16[640,512]{1,0:T(8,128)(2,1)S(1)} fusion(bf16[512,640]{1,0:T(8,128)(2,1)S(1)} %collective-permute-done.6, bf16[640,1280]{1,0:T(8,128)(2,1)S(1)} %copy-done.5), kind=kOutput, calls=%fused_computation.10 | convolution fusion | flops 419758080 | bytes 2129920 | tf_op jit(solution)/shard_map/dot_general | solution.py:105
  32.5 1.2 %pad_maximum_fusion.1.vt_ref = bf16[640,1024]{1,0:T(8,128)(2,1)} fusion(bf16[640,512]{1,0:T(8,128)(2,1)S(1)} %fusion.2, bf16[640,512]{1,0:T(8,128)(2,1)S(1)} %fusion.1), kind=kLoop, calls=%fused_computation.7 | loop fusion | flops 2621440 | bytes 2621440 | tf_op jit(solution)/shard_map/concatenate | solution.py:113
  33.8 0.7 %convolution_convert_fusion.2 = bf16[512,640]{1,0:T(8,128)(2,1)S(1)} fusion(bf16[512,640]{1,0:T(8,128)(2,1)S(1)} %collective-permute-done.6, bf16[640,1280]{1,0:T(8,128)(2,1)S(1)} %copy-done.5), kind=kOutput, calls=%fused_computation.4 | convolution fusion | flops 419758080 | bytes 2129920 | tf_op jit(solution)/shard_map/dot_general | solution.py:104
  34.5 1.2 %pad_maximum_fusion.k_ref = bf16[1024,640]{1,0:T(8,128)(2,1)} fusion(bf16[512,640]{1,0:T(8,128)(2,1)S(1)} %convolution_convert_fusion.2, bf16[512,640]{1,0:T(8,128)(2,1)S(1)} %convolution_convert_fusion.3), kind=kLoop, calls=%fused_computation.6 | loop fusion | flops 2621440 | bytes 2621440 | tf_op jit(solution)/shard_map/concatenate | solution.py:112
  35.7 5.8 %shard_map.82 = bf16[640,256]{1,0:T(8,128)(2,1)} custom-call(bf16[1024,640]{1,0:T(8,128)(2,1)} %pad_maximum_fusion.k_ref, bf16[640,256]{1,0:T(8,128)(2,1)} %fusion.4.qt_ref, bf16[640,1024]{1,0:T(8,128)(2,1)} %pad_maximum_fusion.1.vt_ref), custom_call_target="tpu_custom_call" | custom-call | tf_op jit(solution)/shard_map/pallas_call | solution.py:28
  41.6 1.6 %multiply_reduce_fusion = (f32[256]{0:T(256)S(1)}, f32[256,640]{1,0:T(8,128)S(1)}) fusion(bf16[640,256]{1,0:T(8,128)(2,1)} %shard_map.82, bf16[640,640]{1,0:T(8,128)(2,1)S(1)} %copy-done, bf16[256,640]{1,0:T(8,128)(2,1)S(1)} %bitcast.55), kind=kOutput, calls=%fused_computation.43 | convolution fusion | flops 210370304 | bytes 2130944 | tf_op jit(solution)/shard_map/dot_general | solution.py:115
  43.3 3.3 %collective-permute-start.7 = (bf16[2,128,640]{2,1,0:T(8,128)(2,1)S(1)}, bf16[2,128,640]{2,1,0:T(8,128)(2,1)S(1)}, u32[]{:S(2)}, u32[]{:S(2)}) collective-permute-start(bf16[2,128,640]{2,1,0:T(8,128)(2,1)S(1)} %bitcast.61), channel_id=1, source_target_pairs={{0,4},{4,8},{8,12},{1,5},{5,9},{9,13},{2,6},{6,10},{10,14},{3,7},{... | collective-permute-start | bytes 983048 | tf_op jit(solution)/shard_map/ppermute | solution.py:47
  46.6 1.9 %collective-permute-start.8 = (bf16[2,128,640]{2,1,0:T(8,128)(2,1)S(1)}, bf16[2,128,640]{2,1,0:T(8,128)(2,1)S(1)}, u32[]{:S(2)}, u32[]{:S(2)}) collective-permute-start(bf16[2,128,640]{2,1,0:T(8,128)(2,1)S(1)} %bitcast.62), channel_id=1, source_target_pairs={{4,0},{8,4},{12,8},{5,1},{9,5},{13,9},{6,2},{10,6},{14,10},{7,3},{... | collective-permute-start | bytes 983048 | tf_op jit(solution)/shard_map/ppermute | solution.py:48
  48.6 2.0 %collective-permute-done.7 = bf16[2,128,640]{2,1,0:T(8,128)(2,1)S(1)} collective-permute-done((bf16[2,128,640]{2,1,0:T(8,128)(2,1)S(1)}, bf16[2,128,640]{2,1,0:T(8,128)(2,1)S(1)}, u32[]{:S(2)}, u32[]{:S(2)}) %collective-permute-start.7) | collective-permute-done | bytes 327712 | tf_op jit(solution)/shard_map/ppermute | solution.py:47
  50.6 4.4 %collective-permute-done.8 = bf16[2,128,640]{2,1,0:T(8,128)(2,1)S(1)} collective-permute-done((bf16[2,128,640]{2,1,0:T(8,128)(2,1)S(1)}, bf16[2,128,640]{2,1,0:T(8,128)(2,1)S(1)}, u32[]{:S(2)}, u32[]{:S(2)}) %collective-permute-start.8) | collective-permute-done | bytes 327712 | tf_op jit(solution)/shard_map/ppermute | solution.py:48
  55.0 0.2 pad_maximum_fusion.5
  55.3 0.7 %fusion.10 = f32[512,640]{1,0:T(8,128)S(1)} fusion(bf16[512,640]{1,0:T(8,128)(2,1)S(1)} %bitcast.57, bf16[3,640,640]{2,1,0:T(8,128)(2,1)S(1)} %copy-done.3), kind=kOutput, calls=%fused_computation.22 | convolution fusion | flops 419430400 | bytes 2785280 | tf_op jit(solution)/shard_map/dot_general | solution.py:56
  56.0 0.7 %fusion.12 = f32[512,640]{1,0:T(8,128)S(1)} fusion(bf16[512,640]{1,0:T(8,128)(2,1)S(1)} %bitcast.56, bf16[3,640,640]{2,1,0:T(8,128)(2,1)S(1)} %copy-done.3), kind=kOutput, calls=%fused_computation.24 | convolution fusion | flops 419430400 | bytes 2785280 | tf_op jit(solution)/shard_map/dot_general | solution.py:56
  56.8 0.8 %multiply_convert_fusion = bf16[512,640]{1,0:T(8,128)(2,1)S(1)} fusion(f32[512,640]{1,0:T(8,128)S(1)} %fusion.10, f32[512,640]{1,0:T(8,128)S(1)} %fusion.12, bf16[512,640]{1,0:T(8,128)(2,1)S(1)} %bitcast.68, bf16[3,640,640]{2,1,0:T(8,128)(2,1)S(1)} %copy-done.3), kind=kOutput, calls=%fused_computation.8 | convolution fusion | flops 421724160 | bytes 4751360 | tf_op jit(solution)/shard_map/dot_general | solution.py:56
  57.8 1.5 %copy-done.2 = bf16[3,640,640]{2,1,0:T(8,128)(2,1)S(1)} copy-done((bf16[3,640,640]{2,1,0:T(8,128)(2,1)S(1)}, bf16[3,640,640]{2,1,0:T(8,128)(2,1)}, u32[]{:S(2)}) %copy-start.2) | copy-done | bytes 2457624
  59.3 0.5 fusion.8
  59.8 0.5 convolution_add_fusion.2
  60.3 1.2 %fusion.5 = bf16[256,640]{1,0:T(8,128)(2,1)} fusion(f32[256,640]{1,0:T(8,128)S(1)} %get-tuple-element.22, f32[256,640]{1,0:T(8,128)S(1)} %convolution_add_fusion.2, bf16[256,640]{1,0:T(8,128)(2,1)S(1)} %bitcast.60, bf16[3,640,640]{2,1,0:T(8,128)(2,1)S(1)} %copy-done.2), kind=kOutput, calls=%fused_computation.17 | convolution fusion | flops 210206720 | bytes 2785280 | tf_op jit(solution)/shard_map/dot_general | solution.py:56
  (24 shorter events, 0.7 us)
Async XLA Ops:
  0.0 41.6 %copy-start = (bf16[640,640]{1,0:T(8,128)(2,1)S(1)}, bf16[640,640]{1,0:T(8,128)(2,1)}, u32[]{:S(2)}) copy-start(bf16[640,640]{1,0:T(8,128)(2,1)} %param.12) | copy-start | bytes 2457604
  0.0 11.5 %copy-start.1 = (bf16[2,128,640]{2,1,0:T(8,128)(2,1)S(1)}, bf16[2,128,640]{2,1,0:T(8,128)(2,1)}, u32[]{:S(2)}) copy-start(bf16[2,128,640]{2,1,0:T(8,128)(2,1)} %param.8) | copy-start | bytes 983044
  1.2 9.4 %collective-permute-start = (bf16[2,64,640]{2,1,0:T(8,128)(2,1)S(1)}, bf16[2,64,640]{2,1,0:T(8,128)(2,1)S(1)}, u32[]{:S(2)}, u32[]{:S(2)}) collective-permute-start(bf16[2,64,640]{2,1,0:T(8,128)(2,1)S(1)} %get-tuple-element.16), channel_id=1, source_target_pairs={{0,12},{4,0},{8,4},{12,8},{1,13},{5,1},{9,5},{13,9},{2,14},{6,2},{... | collective-permute-start | bytes 491528 | tf_op jit(solution)/shard_map/ppermute | solution.py:81
  1.3 9.3 %collective-permute-start.1 = (bf16[2,64,640]{2,1,0:T(8,128)(2,1)S(1)}, bf16[2,64,640]{2,1,0:T(8,128)(2,1)S(1)}, u32[]{:S(2)}, u32[]{:S(2)}) collective-permute-start(bf16[2,64,640]{2,1,0:T(8,128)(2,1)S(1)} %get-tuple-element.18), channel_id=1, source_target_pairs={{0,8},{4,12},{8,0},{12,4},{1,9},{5,13},{9,1},{13,5},{2,10},{6,14},... | collective-permute-start | bytes 491528 | tf_op jit(solution)/shard_map/ppermute | solution.py:81
  4.0 7.5 %collective-permute-start.2 = (bf16[2,64,640]{2,1,0:T(8,128)(2,1)S(1)}, bf16[2,64,640]{2,1,0:T(8,128)(2,1)S(1)}, u32[]{:S(2)}, u32[]{:S(2)}) collective-permute-start(bf16[2,64,640]{2,1,0:T(8,128)(2,1)S(1)} %get-tuple-element.17), channel_id=1, source_target_pairs={{0,4},{4,8},{8,12},{12,0},{1,5},{5,9},{9,13},{13,1},{2,6},{6,10},{... | collective-permute-start | bytes 491528 | tf_op jit(solution)/shard_map/ppermute | solution.py:81
  8.1 22.0 %copy-start.5 = (bf16[640,1280]{1,0:T(8,128)(2,1)S(1)}, bf16[640,1280]{1,0:T(8,128)(2,1)}, u32[]{:S(2)}) copy-start(bf16[640,1280]{1,0:T(8,128)(2,1)} %param.11) | copy-start | bytes 4915204
  11.7 5.7 %collective-permute-start.3 = (bf16[2,64,640]{2,1,0:T(8,128)(2,1)S(1)}, bf16[2,64,640]{2,1,0:T(8,128)(2,1)S(1)}, u32[]{:S(2)}, u32[]{:S(2)}) collective-permute-start(bf16[2,64,640]{2,1,0:T(8,128)(2,1)S(1)} %pad_maximum_fusion.9), channel_id=1, source_target_pairs={{0,3},{1,0},{2,1},{3,2},{4,7},{5,4},{6,5},{7,6},{8,11},{9,8},{10,9... | collective-permute-start | bytes 491528 | tf_op jit(solution)/shard_map/ppermute | solution.py:89
  15.0 13.9 %collective-permute-start.4 = (bf16[2,64,640]{2,1,0:T(8,128)(2,1)S(1)}, bf16[2,64,640]{2,1,0:T(8,128)(2,1)S(1)}, u32[]{:S(2)}, u32[]{:S(2)}) collective-permute-start(bf16[2,64,640]{2,1,0:T(8,128)(2,1)S(1)} %pad_maximum_fusion.9), channel_id=1, source_target_pairs={{0,2},{1,3},{2,0},{3,1},{4,6},{5,7},{6,4},{7,5},{8,10},{9,11},{10,... | collective-permute-start | bytes 491528 | tf_op jit(solution)/shard_map/ppermute | solution.py:89
  15.0 13.9 %collective-permute-start.5 = (bf16[2,64,640]{2,1,0:T(8,128)(2,1)S(1)}, bf16[2,64,640]{2,1,0:T(8,128)(2,1)S(1)}, u32[]{:S(2)}, u32[]{:S(2)}) collective-permute-start(bf16[2,64,640]{2,1,0:T(8,128)(2,1)S(1)} %pad_maximum_fusion.9), channel_id=1, source_target_pairs={{0,1},{1,2},{2,3},{3,0},{4,5},{5,6},{6,7},{7,4},{8,9},{9,10},{10,1... | collective-permute-start | bytes 491528 | tf_op jit(solution)/shard_map/ppermute | solution.py:89
  29.1 2.7 %collective-permute-start.6 = (bf16[512,640]{1,0:T(8,128)(2,1)S(1)}, bf16[512,640]{1,0:T(8,128)(2,1)S(1)}, u32[]{:S(2)}, u32[]{:S(2)}) collective-permute-start(bf16[512,640]{1,0:T(8,128)(2,1)S(1)} %bitcast.65), channel_id=1, source_target_pairs={{0,4},{4,0},{8,12},{12,8},{1,5},{5,1},{9,13},{13,9},{2,6},{6,2},{1... | collective-permute-start | bytes 1966088 | tf_op jit(solution)/shard_map/ppermute | solution.py:91
  41.6 1.6 %copy-start.4 = (f32[640]{0:T(1024)S(1)}, f32[640]{0:T(1024)}, u32[]{:S(2)}) copy-start(f32[640]{0:T(1024)} %param.13) | copy-start | bytes 7684
  43.3 7.4 %collective-permute-start.7 = (bf16[2,128,640]{2,1,0:T(8,128)(2,1)S(1)}, bf16[2,128,640]{2,1,0:T(8,128)(2,1)S(1)}, u32[]{:S(2)}, u32[]{:S(2)}) collective-permute-start(bf16[2,128,640]{2,1,0:T(8,128)(2,1)S(1)} %bitcast.61), channel_id=1, source_target_pairs={{0,4},{4,8},{8,12},{1,5},{5,9},{9,13},{2,6},{6,10},{10,14},{3,7},{... | collective-permute-start | bytes 983048 | tf_op jit(solution)/shard_map/ppermute | solution.py:47
  46.6 8.4 %collective-permute-start.8 = (bf16[2,128,640]{2,1,0:T(8,128)(2,1)S(1)}, bf16[2,128,640]{2,1,0:T(8,128)(2,1)S(1)}, u32[]{:S(2)}, u32[]{:S(2)}) collective-permute-start(bf16[2,128,640]{2,1,0:T(8,128)(2,1)S(1)} %bitcast.62), channel_id=1, source_target_pairs={{4,0},{8,4},{12,8},{5,1},{9,5},{13,9},{6,2},{10,6},{14,10},{7,3},{... | collective-permute-start | bytes 983048 | tf_op jit(solution)/shard_map/ppermute | solution.py:48
  48.6 6.7 %copy-start.3 = (bf16[3,640,640]{2,1,0:T(8,128)(2,1)S(1)}, bf16[3,640,640]{2,1,0:T(8,128)(2,1)}, u32[]{:S(2)}) copy-start(bf16[3,640,640]{2,1,0:T(8,128)(2,1)} %param.14) | copy-start | bytes 7372804
  57.6 1.7 %copy-start.2 = (bf16[3,640,640]{2,1,0:T(8,128)(2,1)S(1)}, bf16[3,640,640]{2,1,0:T(8,128)(2,1)}, u32[]{:S(2)}) copy-start(bf16[3,640,640]{2,1,0:T(8,128)(2,1)} %param.15) | copy-start | bytes 7372804
